TPU v7x, 256 devices: a whole 4x4x8 slice. The times are simulated.
256 devices in a mesh: grp: 16 (over y_hi, z), blk: 16 (over x, y_lo, core).
Axes of the slice: x: 4, y: 4 (y_hi: 2, y_lo: 2; y = y_hi * 2 + y_lo), z: 8, core: 2. Of those that a mesh axis runs over, the one named last changes fastest.
Arguments:
- src_codes: int32 [262144, 1024], P(('grp', 'blk')), may hold values from -119 to 119
- src_exps: int32 [262144, 8], P(('grp', 'blk')), may hold values from 0 to 3
- signs: int32 [262144, 256], P(('grp', 'blk')), may hold values from 0 to 1
- tgt_codes: int32 [4096, 1024], P('blk'), may hold values from -119 to 119
- tgt_exps: int32 [4096, 8], P('blk'), may hold values from 0 to 3
Outputs:
- kernel_product: float32 [4096, 256], P('blk', 'grp')
All inputs are finite; a program needn't handle non-finite values.
Results may differ from a plain program's by a relative error of at most 0.003.
Values may be sent and summed in bfloat16 or wider, within the bound.
No kernel may reach another device: no remote copies, remote signals or barrier semaphores. Data moves between devices by JAX's collectives and lax.ppermute only.
A program may use at most 64 MiB of HBM per device.

v0:
```python
import math

import jax
import jax.numpy as jnp
from jax import lax
from jax.sharding import PartitionSpec as P

kernel_rate = 20.0


def shifted(block, axis, distance):
    devices = range(lax.axis_size(axis))
    route = [((i - distance) % len(devices), i) for i in devices]
    return lax.ppermute(block, axis, route)


def dequantize(codes, exponents):
    points, columns = codes.shape
    blocks = exponents.shape[1]
    factor = jnp.zeros(exponents.shape, jnp.float32)
    for level_index in range(4):
        factor = factor + jnp.where(exponents == level_index, 2.0 ** (level_index - 9), 0.0)
    scaled_codes = (
        codes.reshape(points, blocks, columns // blocks).astype(jnp.float32) * factor[:, :, None]
    )
    return scaled_codes.reshape(points, columns).astype(jnp.bfloat16)


def squares(points_bf):
    widened = points_bf.astype(jnp.float32)
    return jnp.sum(widened * widened, axis=1)


def kernel_block(targets_bf, sources_bf, source_sq, rhs_values):
    target_sq = squares(targets_bf)
    inner_products = lax.dot_general(
        targets_bf, sources_bf, (((1,), (1,)), ((), ())), preferred_element_type=jnp.float32
    )
    squared = target_sq[:, None] + source_sq[None, :] - 2.0 * inner_products
    scaled = kernel_rate * jnp.sqrt(squared) / math.sqrt(targets_bf.shape[1])
    matern = ((1.0 + scaled + scaled * scaled / 3.0) * jnp.exp(-scaled)).astype(jnp.bfloat16)
    return jnp.dot(matern, rhs_values, preferred_element_type=jnp.float32)


def per_device(src_codes, src_exps, signs, tgt_codes, tgt_exps):
    sources_bf = dequantize(src_codes, src_exps)
    targets_bf = dequantize(tgt_codes, tgt_exps)
    rhs_values = (2 * signs - 1).astype(jnp.bfloat16)
    source_sq = squares(sources_bf)
    cycle_size = lax.axis_size("blk")
    group_size = lax.axis_size("grp")
    block_rows = targets_bf.shape[0]
    rhs_count = rhs_values.shape[1]

    def contribution(points_bf):
        return kernel_block(points_bf, sources_bf, source_sq, rhs_values)

    def advance(counter, carried):
        points_bf, running = carried
        running = running + contribution(points_bf)
        points_bf = shifted(points_bf, "blk", 1)
        running = shifted(running, "blk", 1)
        return (points_bf, running)

    start_sums = jnp.zeros((block_rows, rhs_count), jnp.float32)
    points_bf, running = lax.fori_loop(0, cycle_size - 1, advance, (targets_bf, start_sums))
    running = running + contribution(points_bf)
    gathered_sums = shifted(running, "blk", 1)
    owned_sums = lax.psum_scatter(gathered_sums, "grp", scatter_dimension=1, tiled=True)
    source_total = src_codes.shape[0] * group_size * cycle_size
    return owned_sums * (4.0 / math.sqrt(source_total))


def solution(mesh):
    placed = (
        P(("grp", "blk"), None),
        P(("grp", "blk"), None),
        P(("grp", "blk"), None),
        P("blk", None),
        P("blk", None),
    )
    return jax.shard_map(
        per_device, mesh=mesh, in_specs=placed, out_specs=P("blk", "grp"), check_vma=False
    )
```

profile of v0, /device:TPU:1, one launch (start us, length us, event | category | flops | bytes accessed | tf_op | source)
XLA Modules:
  0.0 436.2 jit_solution(4848804595270039178)
XLA Ops:
  6.5 0.8 select_add_fusion
  7.5 2.1 add_convert_fusion
  9.8 1.1 mul.78
  11.0 1.0 copy-done
  12.0 0.9 multiply_reduce_fusion.1
  13.6 198.9 %while.14 = (s32[]{:T(128)}, bf16[256,1024]{1,0:T(8,128)(2,1)S(1)}, f32[256,256]{1,0:T(8,128)S(1)}, f32[1024]{0:T(1024)S(1)}, bf16[1024,1024]{1,0:T(8,128)(2,1)S(1)}, /*index=5*/bf16[1024,256]{1,0:T(8,128)(2,1)}, s32[]{:T(128)}) while((s32[]{:T(128)}, bf16[256,1024]{1,0:T(8,128)(2,1)S(1)}, f32[256,256]{1,0:T(8,128)S(1)}, f32[1024]{0:T(1024)S(1)}, ...), condition=%wide.region_3.4_spmd, body=%wide.region_1.3_spmd.sunk | while | flops 674823936 | bytes 8394909 | solution.py:66
  13.7 2.8 collective-permute-start
  16.6 3.1 convolution_add_fusion.3
  19.7 5.8 %collective-permute-done.1 = f32[256,256]{1,0:T(8,128)S(1)} collective-permute-done((f32[256,256]{1,0:T(8,128)}, f32[256,256]{1,0:T(8,128)S(1)}, u32[]{:S(2)}, u32[]{:S(2)}) %collective-permute-start.1) | collective-permute-done | bytes 262176 | tf_op jit(solution)/shard_map/while/body/eval_jaxpr/ppermute | solution.py:14
  25.5 2.5 collective-permute-start
  28.1 3.1 convolution_add_fusion.3
  31.2 5.8 %collective-permute-done.1 = f32[256,256]{1,0:T(8,128)S(1)} collective-permute-done((f32[256,256]{1,0:T(8,128)}, f32[256,256]{1,0:T(8,128)S(1)}, u32[]{:S(2)}, u32[]{:S(2)}) %collective-permute-start.1) | collective-permute-done | bytes 262176 | tf_op jit(solution)/shard_map/while/body/eval_jaxpr/ppermute | solution.py:14
  37.0 2.5 collective-permute-start
  39.7 3.1 convolution_add_fusion.3
  42.8 6.0 %collective-permute-done.1 = f32[256,256]{1,0:T(8,128)S(1)} collective-permute-done((f32[256,256]{1,0:T(8,128)}, f32[256,256]{1,0:T(8,128)S(1)}, u32[]{:S(2)}, u32[]{:S(2)}) %collective-permute-start.1) | collective-permute-done | bytes 262176 | tf_op jit(solution)/shard_map/while/body/eval_jaxpr/ppermute | solution.py:14
  48.8 2.2 collective-permute-start
  51.2 3.1 convolution_add_fusion.3
  54.3 0.9 collective-permute-start.1
  55.2 7.2 %collective-permute-done.1 = f32[256,256]{1,0:T(8,128)S(1)} collective-permute-done((f32[256,256]{1,0:T(8,128)}, f32[256,256]{1,0:T(8,128)S(1)}, u32[]{:S(2)}, u32[]{:S(2)}) %collective-permute-start.1) | collective-permute-done | bytes 262176 | tf_op jit(solution)/shard_map/while/body/eval_jaxpr/ppermute | solution.py:14
  62.7 3.1 convolution_add_fusion.3
  65.8 1.8 collective-permute-start.1
  67.6 8.4 %collective-permute-done.1 = f32[256,256]{1,0:T(8,128)S(1)} collective-permute-done((f32[256,256]{1,0:T(8,128)}, f32[256,256]{1,0:T(8,128)S(1)}, u32[]{:S(2)}, u32[]{:S(2)}) %collective-permute-start.1) | collective-permute-done | bytes 262176 | tf_op jit(solution)/shard_map/while/body/eval_jaxpr/ppermute | solution.py:14
  76.4 3.1 convolution_add_fusion.3
  79.4 0.6 collective-permute-start.1
  80.1 9.6 %collective-permute-done.1 = f32[256,256]{1,0:T(8,128)S(1)} collective-permute-done((f32[256,256]{1,0:T(8,128)}, f32[256,256]{1,0:T(8,128)S(1)}, u32[]{:S(2)}, u32[]{:S(2)}) %collective-permute-start.1) | collective-permute-done | bytes 262176 | tf_op jit(solution)/shard_map/while/body/eval_jaxpr/ppermute | solution.py:14
  90.0 3.1 convolution_add_fusion.3
  93.1 10.2 %collective-permute-done.1 = f32[256,256]{1,0:T(8,128)S(1)} collective-permute-done((f32[256,256]{1,0:T(8,128)}, f32[256,256]{1,0:T(8,128)S(1)}, u32[]{:S(2)}, u32[]{:S(2)}) %collective-permute-start.1) | collective-permute-done | bytes 262176 | tf_op jit(solution)/shard_map/while/body/eval_jaxpr/ppermute | solution.py:14
  103.6 3.1 convolution_add_fusion.3
  106.7 10.3 %collective-permute-done.1 = f32[256,256]{1,0:T(8,128)S(1)} collective-permute-done((f32[256,256]{1,0:T(8,128)}, f32[256,256]{1,0:T(8,128)S(1)}, u32[]{:S(2)}, u32[]{:S(2)}) %collective-permute-start.1) | collective-permute-done | bytes 262176 | tf_op jit(solution)/shard_map/while/body/eval_jaxpr/ppermute | solution.py:14
  117.3 3.1 convolution_add_fusion.3
  120.4 10.2 %collective-permute-done.1 = f32[256,256]{1,0:T(8,128)S(1)} collective-permute-done((f32[256,256]{1,0:T(8,128)}, f32[256,256]{1,0:T(8,128)S(1)}, u32[]{:S(2)}, u32[]{:S(2)}) %collective-permute-start.1) | collective-permute-done | bytes 262176 | tf_op jit(solution)/shard_map/while/body/eval_jaxpr/ppermute | solution.py:14
  130.9 3.1 convolution_add_fusion.3
  134.0 10.3 %collective-permute-done.1 = f32[256,256]{1,0:T(8,128)S(1)} collective-permute-done((f32[256,256]{1,0:T(8,128)}, f32[256,256]{1,0:T(8,128)S(1)}, u32[]{:S(2)}, u32[]{:S(2)}) %collective-permute-start.1) | collective-permute-done | bytes 262176 | tf_op jit(solution)/shard_map/while/body/eval_jaxpr/ppermute | solution.py:14
  144.6 3.1 convolution_add_fusion.3
  147.7 10.2 %collective-permute-done.1 = f32[256,256]{1,0:T(8,128)S(1)} collective-permute-done((f32[256,256]{1,0:T(8,128)}, f32[256,256]{1,0:T(8,128)S(1)}, u32[]{:S(2)}, u32[]{:S(2)}) %collective-permute-start.1) | collective-permute-done | bytes 262176 | tf_op jit(solution)/shard_map/while/body/eval_jaxpr/ppermute | solution.py:14
  158.2 3.1 convolution_add_fusion.3
  161.3 10.2 %collective-permute-done.1 = f32[256,256]{1,0:T(8,128)S(1)} collective-permute-done((f32[256,256]{1,0:T(8,128)}, f32[256,256]{1,0:T(8,128)S(1)}, u32[]{:S(2)}, u32[]{:S(2)}) %collective-permute-start.1) | collective-permute-done | bytes 262176 | tf_op jit(solution)/shard_map/while/body/eval_jaxpr/ppermute | solution.py:14
  171.9 3.1 convolution_add_fusion.3
  174.9 10.3 %collective-permute-done.1 = f32[256,256]{1,0:T(8,128)S(1)} collective-permute-done((f32[256,256]{1,0:T(8,128)}, f32[256,256]{1,0:T(8,128)S(1)}, u32[]{:S(2)}, u32[]{:S(2)}) %collective-permute-start.1) | collective-permute-done | bytes 262176 | tf_op jit(solution)/shard_map/while/body/eval_jaxpr/ppermute | solution.py:14
  185.5 3.1 convolution_add_fusion.3
  188.6 10.2 %collective-permute-done.1 = f32[256,256]{1,0:T(8,128)S(1)} collective-permute-done((f32[256,256]{1,0:T(8,128)}, f32[256,256]{1,0:T(8,128)S(1)}, u32[]{:S(2)}, u32[]{:S(2)}) %collective-permute-start.1) | collective-permute-done | bytes 262176 | tf_op jit(solution)/shard_map/while/body/eval_jaxpr/ppermute | solution.py:14
  199.2 3.1 convolution_add_fusion.3
  202.2 10.2 %collective-permute-done.1 = f32[256,256]{1,0:T(8,128)S(1)} collective-permute-done((f32[256,256]{1,0:T(8,128)}, f32[256,256]{1,0:T(8,128)S(1)}, u32[]{:S(2)}, u32[]{:S(2)}) %collective-permute-start.1) | collective-permute-done | bytes 262176 | tf_op jit(solution)/shard_map/while/body/eval_jaxpr/ppermute | solution.py:14
  212.7 2.4 convolution_add_fusion.1
  215.1 10.0 %collective-permute-done.2 = f32[256,256]{1,0:T(8,128)S(1)} collective-permute-done((f32[256,256]{1,0:T(8,128)S(1)}, f32[256,256]{1,0:T(8,128)S(1)}, u32[]{:S(2)}, u32[]{:S(2)}) %collective-permute-start.2) | collective-permute-done | bytes 262176 | tf_op jit(solution)/shard_map/ppermute | solution.py:14
  225.2 0.8 copy.15
  226.0 202.0 %reduce-scatter.4.cloned.1.call-done = f32[16,256]{1,0:T(8,128)} async-done(((f32[256,256]{1,0:T(8,128)}), f32[16,256]{1,0:T(8,128)}) %reduce-scatter.4.cloned.1.call-update) | async-done | bytes 16400
  428.1 1.3 bitcast_multiply_fusion.2
  (83 shorter events, 5.6 us)
Async XLA Ops:
  6.5 3.1 copy-start.2
  6.5 421.5 %reduce-scatter.4.cloned.1.call-start = ((), (), s32[]{:S(2)}) async-start(), calls=%async_computation.1 | async-start | bytes 278528
  9.8 2.2 copy-start
  12.0 1.2 copy-start.1
  13.7 11.8 %collective-permute-start = (bf16[256,1024]{1,0:T(8,128)(2,1)S(1)}, bf16[256,1024]{1,0:T(8,128)(2,1)S(1)}, u32[]{:S(2)}, u32[]{:S(2)}) collective-permute-start(bf16[256,1024]{1,0:T(8,128)(2,1)S(1)} %copy.26), channel_id=1, source_target_pairs={{15,0},{0,1},{1,2},{2,3},{3,4},{4,5},{5,6},{6,7},{7,8},{8,9},{9,10... | collective-permute-start | bytes 1572872 | tf_op jit(solution)/shard_map/while/body/eval_jaxpr/ppermute | solution.py:14
  19.7 5.8 %collective-permute-start.1 = (f32[256,256]{1,0:T(8,128)}, f32[256,256]{1,0:T(8,128)S(1)}, u32[]{:S(2)}, u32[]{:S(2)}) collective-permute-start(f32[256,256]{1,0:T(8,128)} %convolution_add_fusion.3), channel_id=1, source_target_pairs={{15,0},{0,1},{1,2},{2,3},{3,4},{4,5},{5,6},{6,7},{7,8},{8,9},{9,10... | collective-permute-start | bytes 786440 | tf_op jit(solution)/shard_map/while/body/eval_jaxpr/ppermute | solution.py:14
  25.5 11.5 %collective-permute-start = (bf16[256,1024]{1,0:T(8,128)(2,1)S(1)}, bf16[256,1024]{1,0:T(8,128)(2,1)S(1)}, u32[]{:S(2)}, u32[]{:S(2)}) collective-permute-start(bf16[256,1024]{1,0:T(8,128)(2,1)S(1)} %copy.26), channel_id=1, source_target_pairs={{15,0},{0,1},{1,2},{2,3},{3,4},{4,5},{5,6},{6,7},{7,8},{8,9},{9,10... | collective-permute-start | bytes 1572872 | tf_op jit(solution)/shard_map/while/body/eval_jaxpr/ppermute | solution.py:14
  31.2 5.8 %collective-permute-start.1 = (f32[256,256]{1,0:T(8,128)}, f32[256,256]{1,0:T(8,128)S(1)}, u32[]{:S(2)}, u32[]{:S(2)}) collective-permute-start(f32[256,256]{1,0:T(8,128)} %convolution_add_fusion.3), channel_id=1, source_target_pairs={{15,0},{0,1},{1,2},{2,3},{3,4},{4,5},{5,6},{6,7},{7,8},{8,9},{9,10... | collective-permute-start | bytes 786440 | tf_op jit(solution)/shard_map/while/body/eval_jaxpr/ppermute | solution.py:14
  37.0 11.7 %collective-permute-start = (bf16[256,1024]{1,0:T(8,128)(2,1)S(1)}, bf16[256,1024]{1,0:T(8,128)(2,1)S(1)}, u32[]{:S(2)}, u32[]{:S(2)}) collective-permute-start(bf16[256,1024]{1,0:T(8,128)(2,1)S(1)} %copy.26), channel_id=1, source_target_pairs={{15,0},{0,1},{1,2},{2,3},{3,4},{4,5},{5,6},{6,7},{7,8},{8,9},{9,10... | collective-permute-start | bytes 1572872 | tf_op jit(solution)/shard_map/while/body/eval_jaxpr/ppermute | solution.py:14
  42.7 6.0 %collective-permute-start.1 = (f32[256,256]{1,0:T(8,128)}, f32[256,256]{1,0:T(8,128)S(1)}, u32[]{:S(2)}, u32[]{:S(2)}) collective-permute-start(f32[256,256]{1,0:T(8,128)} %convolution_add_fusion.3), channel_id=1, source_target_pairs={{15,0},{0,1},{1,2},{2,3},{3,4},{4,5},{5,6},{6,7},{7,8},{8,9},{9,10... | collective-permute-start | bytes 786440 | tf_op jit(solution)/shard_map/while/body/eval_jaxpr/ppermute | solution.py:14
  48.8 13.6 %collective-permute-start = (bf16[256,1024]{1,0:T(8,128)(2,1)S(1)}, bf16[256,1024]{1,0:T(8,128)(2,1)S(1)}, u32[]{:S(2)}, u32[]{:S(2)}) collective-permute-start(bf16[256,1024]{1,0:T(8,128)(2,1)S(1)} %copy.26), channel_id=1, source_target_pairs={{15,0},{0,1},{1,2},{2,3},{3,4},{4,5},{5,6},{6,7},{7,8},{8,9},{9,10... | collective-permute-start | bytes 1572872 | tf_op jit(solution)/shard_map/while/body/eval_jaxpr/ppermute | solution.py:14
  54.3 8.1 %collective-permute-start.1 = (f32[256,256]{1,0:T(8,128)}, f32[256,256]{1,0:T(8,128)S(1)}, u32[]{:S(2)}, u32[]{:S(2)}) collective-permute-start(f32[256,256]{1,0:T(8,128)} %convolution_add_fusion.3), channel_id=1, source_target_pairs={{15,0},{0,1},{1,2},{2,3},{3,4},{4,5},{5,6},{6,7},{7,8},{8,9},{9,10... | collective-permute-start | bytes 786440 | tf_op jit(solution)/shard_map/while/body/eval_jaxpr/ppermute | solution.py:14
  62.4 13.6 %collective-permute-start = (bf16[256,1024]{1,0:T(8,128)(2,1)S(1)}, bf16[256,1024]{1,0:T(8,128)(2,1)S(1)}, u32[]{:S(2)}, u32[]{:S(2)}) collective-permute-start(bf16[256,1024]{1,0:T(8,128)(2,1)S(1)} %copy.26), channel_id=1, source_target_pairs={{15,0},{0,1},{1,2},{2,3},{3,4},{4,5},{5,6},{6,7},{7,8},{8,9},{9,10... | collective-permute-start | bytes 1572872 | tf_op jit(solution)/shard_map/while/body/eval_jaxpr/ppermute | solution.py:14
  65.8 10.2 %collective-permute-start.1 = (f32[256,256]{1,0:T(8,128)}, f32[256,256]{1,0:T(8,128)S(1)}, u32[]{:S(2)}, u32[]{:S(2)}) collective-permute-start(f32[256,256]{1,0:T(8,128)} %convolution_add_fusion.3), channel_id=1, source_target_pairs={{15,0},{0,1},{1,2},{2,3},{3,4},{4,5},{5,6},{6,7},{7,8},{8,9},{9,10... | collective-permute-start | bytes 786440 | tf_op jit(solution)/shard_map/while/body/eval_jaxpr/ppermute | solution.py:14
  76.1 13.6 %collective-permute-start = (bf16[256,1024]{1,0:T(8,128)(2,1)S(1)}, bf16[256,1024]{1,0:T(8,128)(2,1)S(1)}, u32[]{:S(2)}, u32[]{:S(2)}) collective-permute-start(bf16[256,1024]{1,0:T(8,128)(2,1)S(1)} %copy.26), channel_id=1, source_target_pairs={{15,0},{0,1},{1,2},{2,3},{3,4},{4,5},{5,6},{6,7},{7,8},{8,9},{9,10... | collective-permute-start | bytes 1572872 | tf_op jit(solution)/shard_map/while/body/eval_jaxpr/ppermute | solution.py:14
  79.4 10.2 %collective-permute-start.1 = (f32[256,256]{1,0:T(8,128)}, f32[256,256]{1,0:T(8,128)S(1)}, u32[]{:S(2)}, u32[]{:S(2)}) collective-permute-start(f32[256,256]{1,0:T(8,128)} %convolution_add_fusion.3), channel_id=1, source_target_pairs={{15,0},{0,1},{1,2},{2,3},{3,4},{4,5},{5,6},{6,7},{7,8},{8,9},{9,10... | collective-permute-start | bytes 786440 | tf_op jit(solution)/shard_map/while/body/eval_jaxpr/ppermute | solution.py:14
  89.7 13.6 %collective-permute-start = (bf16[256,1024]{1,0:T(8,128)(2,1)S(1)}, bf16[256,1024]{1,0:T(8,128)(2,1)S(1)}, u32[]{:S(2)}, u32[]{:S(2)}) collective-permute-start(bf16[256,1024]{1,0:T(8,128)(2,1)S(1)} %copy.26), channel_id=1, source_target_pairs={{15,0},{0,1},{1,2},{2,3},{3,4},{4,5},{5,6},{6,7},{7,8},{8,9},{9,10... | collective-permute-start | bytes 1572872 | tf_op jit(solution)/shard_map/while/body/eval_jaxpr/ppermute | solution.py:14
  93.1 10.3 %collective-permute-start.1 = (f32[256,256]{1,0:T(8,128)}, f32[256,256]{1,0:T(8,128)S(1)}, u32[]{:S(2)}, u32[]{:S(2)}) collective-permute-start(f32[256,256]{1,0:T(8,128)} %convolution_add_fusion.3), channel_id=1, source_target_pairs={{15,0},{0,1},{1,2},{2,3},{3,4},{4,5},{5,6},{6,7},{7,8},{8,9},{9,10... | collective-permute-start | bytes 786440 | tf_op jit(solution)/shard_map/while/body/eval_jaxpr/ppermute | solution.py:14
  103.4 13.6 %collective-permute-start = (bf16[256,1024]{1,0:T(8,128)(2,1)S(1)}, bf16[256,1024]{1,0:T(8,128)(2,1)S(1)}, u32[]{:S(2)}, u32[]{:S(2)}) collective-permute-start(bf16[256,1024]{1,0:T(8,128)(2,1)S(1)} %copy.26), channel_id=1, source_target_pairs={{15,0},{0,1},{1,2},{2,3},{3,4},{4,5},{5,6},{6,7},{7,8},{8,9},{9,10... | collective-permute-start | bytes 1572872 | tf_op jit(solution)/shard_map/while/body/eval_jaxpr/ppermute | solution.py:14
  106.7 10.3 %collective-permute-start.1 = (f32[256,256]{1,0:T(8,128)}, f32[256,256]{1,0:T(8,128)S(1)}, u32[]{:S(2)}, u32[]{:S(2)}) collective-permute-start(f32[256,256]{1,0:T(8,128)} %convolution_add_fusion.3), channel_id=1, source_target_pairs={{15,0},{0,1},{1,2},{2,3},{3,4},{4,5},{5,6},{6,7},{7,8},{8,9},{9,10... | collective-permute-start | bytes 786440 | tf_op jit(solution)/shard_map/while/body/eval_jaxpr/ppermute | solution.py:14
  117.0 13.6 %collective-permute-start = (bf16[256,1024]{1,0:T(8,128)(2,1)S(1)}, bf16[256,1024]{1,0:T(8,128)(2,1)S(1)}, u32[]{:S(2)}, u32[]{:S(2)}) collective-permute-start(bf16[256,1024]{1,0:T(8,128)(2,1)S(1)} %copy.26), channel_id=1, source_target_pairs={{15,0},{0,1},{1,2},{2,3},{3,4},{4,5},{5,6},{6,7},{7,8},{8,9},{9,10... | collective-permute-start | bytes 1572872 | tf_op jit(solution)/shard_map/while/body/eval_jaxpr/ppermute | solution.py:14
  120.4 10.2 %collective-permute-start.1 = (f32[256,256]{1,0:T(8,128)}, f32[256,256]{1,0:T(8,128)S(1)}, u32[]{:S(2)}, u32[]{:S(2)}) collective-permute-start(f32[256,256]{1,0:T(8,128)} %convolution_add_fusion.3), channel_id=1, source_target_pairs={{15,0},{0,1},{1,2},{2,3},{3,4},{4,5},{5,6},{6,7},{7,8},{8,9},{9,10... | collective-permute-start | bytes 786440 | tf_op jit(solution)/shard_map/while/body/eval_jaxpr/ppermute | solution.py:14
  130.7 13.6 %collective-permute-start = (bf16[256,1024]{1,0:T(8,128)(2,1)S(1)}, bf16[256,1024]{1,0:T(8,128)(2,1)S(1)}, u32[]{:S(2)}, u32[]{:S(2)}) collective-permute-start(bf16[256,1024]{1,0:T(8,128)(2,1)S(1)} %copy.26), channel_id=1, source_target_pairs={{15,0},{0,1},{1,2},{2,3},{3,4},{4,5},{5,6},{6,7},{7,8},{8,9},{9,10... | collective-permute-start | bytes 1572872 | tf_op jit(solution)/shard_map/while/body/eval_jaxpr/ppermute | solution.py:14
  134.0 10.3 %collective-permute-start.1 = (f32[256,256]{1,0:T(8,128)}, f32[256,256]{1,0:T(8,128)S(1)}, u32[]{:S(2)}, u32[]{:S(2)}) collective-permute-start(f32[256,256]{1,0:T(8,128)} %convolution_add_fusion.3), channel_id=1, source_target_pairs={{15,0},{0,1},{1,2},{2,3},{3,4},{4,5},{5,6},{6,7},{7,8},{8,9},{9,10... | collective-permute-start | bytes 786440 | tf_op jit(solution)/shard_map/while/body/eval_jaxpr/ppermute | solution.py:14
  144.3 13.6 %collective-permute-start = (bf16[256,1024]{1,0:T(8,128)(2,1)S(1)}, bf16[256,1024]{1,0:T(8,128)(2,1)S(1)}, u32[]{:S(2)}, u32[]{:S(2)}) collective-permute-start(bf16[256,1024]{1,0:T(8,128)(2,1)S(1)} %copy.26), channel_id=1, source_target_pairs={{15,0},{0,1},{1,2},{2,3},{3,4},{4,5},{5,6},{6,7},{7,8},{8,9},{9,10... | collective-permute-start | bytes 1572872 | tf_op jit(solution)/shard_map/while/body/eval_jaxpr/ppermute | solution.py:14
  147.7 10.2 %collective-permute-start.1 = (f32[256,256]{1,0:T(8,128)}, f32[256,256]{1,0:T(8,128)S(1)}, u32[]{:S(2)}, u32[]{:S(2)}) collective-permute-start(f32[256,256]{1,0:T(8,128)} %convolution_add_fusion.3), channel_id=1, source_target_pairs={{15,0},{0,1},{1,2},{2,3},{3,4},{4,5},{5,6},{6,7},{7,8},{8,9},{9,10... | collective-permute-start | bytes 786440 | tf_op jit(solution)/shard_map/while/body/eval_jaxpr/ppermute | solution.py:14
  158.0 13.6 %collective-permute-start = (bf16[256,1024]{1,0:T(8,128)(2,1)S(1)}, bf16[256,1024]{1,0:T(8,128)(2,1)S(1)}, u32[]{:S(2)}, u32[]{:S(2)}) collective-permute-start(bf16[256,1024]{1,0:T(8,128)(2,1)S(1)} %copy.26), channel_id=1, source_target_pairs={{15,0},{0,1},{1,2},{2,3},{3,4},{4,5},{5,6},{6,7},{7,8},{8,9},{9,10... | collective-permute-start | bytes 1572872 | tf_op jit(solution)/shard_map/while/body/eval_jaxpr/ppermute | solution.py:14
  161.3 10.2 %collective-permute-start.1 = (f32[256,256]{1,0:T(8,128)}, f32[256,256]{1,0:T(8,128)S(1)}, u32[]{:S(2)}, u32[]{:S(2)}) collective-permute-start(f32[256,256]{1,0:T(8,128)} %convolution_add_fusion.3), channel_id=1, source_target_pairs={{15,0},{0,1},{1,2},{2,3},{3,4},{4,5},{5,6},{6,7},{7,8},{8,9},{9,10... | collective-permute-start | bytes 786440 | tf_op jit(solution)/shard_map/while/body/eval_jaxpr/ppermute | solution.py:14
  171.6 13.6 %collective-permute-start = (bf16[256,1024]{1,0:T(8,128)(2,1)S(1)}, bf16[256,1024]{1,0:T(8,128)(2,1)S(1)}, u32[]{:S(2)}, u32[]{:S(2)}) collective-permute-start(bf16[256,1024]{1,0:T(8,128)(2,1)S(1)} %copy.26), channel_id=1, source_target_pairs={{15,0},{0,1},{1,2},{2,3},{3,4},{4,5},{5,6},{6,7},{7,8},{8,9},{9,10... | collective-permute-start | bytes 1572872 | tf_op jit(solution)/shard_map/while/body/eval_jaxpr/ppermute | solution.py:14
  174.9 10.3 %collective-permute-start.1 = (f32[256,256]{1,0:T(8,128)}, f32[256,256]{1,0:T(8,128)S(1)}, u32[]{:S(2)}, u32[]{:S(2)}) collective-permute-start(f32[256,256]{1,0:T(8,128)} %convolution_add_fusion.3), channel_id=1, source_target_pairs={{15,0},{0,1},{1,2},{2,3},{3,4},{4,5},{5,6},{6,7},{7,8},{8,9},{9,10... | collective-permute-start | bytes 786440 | tf_op jit(solution)/shard_map/while/body/eval_jaxpr/ppermute | solution.py:14
  185.2 13.6 %collective-permute-start = (bf16[256,1024]{1,0:T(8,128)(2,1)S(1)}, bf16[256,1024]{1,0:T(8,128)(2,1)S(1)}, u32[]{:S(2)}, u32[]{:S(2)}) collective-permute-start(bf16[256,1024]{1,0:T(8,128)(2,1)S(1)} %copy.26), channel_id=1, source_target_pairs={{15,0},{0,1},{1,2},{2,3},{3,4},{4,5},{5,6},{6,7},{7,8},{8,9},{9,10... | collective-permute-start | bytes 1572872 | tf_op jit(solution)/shard_map/while/body/eval_jaxpr/ppermute | solution.py:14
  188.6 10.2 %collective-permute-start.1 = (f32[256,256]{1,0:T(8,128)}, f32[256,256]{1,0:T(8,128)S(1)}, u32[]{:S(2)}, u32[]{:S(2)}) collective-permute-start(f32[256,256]{1,0:T(8,128)} %convolution_add_fusion.3), channel_id=1, source_target_pairs={{15,0},{0,1},{1,2},{2,3},{3,4},{4,5},{5,6},{6,7},{7,8},{8,9},{9,10... | collective-permute-start | bytes 786440 | tf_op jit(solution)/shard_map/while/body/eval_jaxpr/ppermute | solution.py:14
  198.9 13.6 %collective-permute-start = (bf16[256,1024]{1,0:T(8,128)(2,1)S(1)}, bf16[256,1024]{1,0:T(8,128)(2,1)S(1)}, u32[]{:S(2)}, u32[]{:S(2)}) collective-permute-start(bf16[256,1024]{1,0:T(8,128)(2,1)S(1)} %copy.26), channel_id=1, source_target_pairs={{15,0},{0,1},{1,2},{2,3},{3,4},{4,5},{5,6},{6,7},{7,8},{8,9},{9,10... | collective-permute-start | bytes 1572872 | tf_op jit(solution)/shard_map/while/body/eval_jaxpr/ppermute | solution.py:14
  202.2 10.3 %collective-permute-start.1 = (f32[256,256]{1,0:T(8,128)}, f32[256,256]{1,0:T(8,128)S(1)}, u32[]{:S(2)}, u32[]{:S(2)}) collective-permute-start(f32[256,256]{1,0:T(8,128)} %convolution_add_fusion.3), channel_id=1, source_target_pairs={{15,0},{0,1},{1,2},{2,3},{3,4},{4,5},{5,6},{6,7},{7,8},{8,9},{9,10... | collective-permute-start | bytes 786440 | tf_op jit(solution)/shard_map/while/body/eval_jaxpr/ppermute | solution.py:14
  215.0 10.1 %collective-permute-start.2 = (f32[256,256]{1,0:T(8,128)S(1)}, f32[256,256]{1,0:T(8,128)S(1)}, u32[]{:S(2)}, u32[]{:S(2)}) collective-permute-start(f32[256,256]{1,0:T(8,128)S(1)} %convolution_add_fusion.1), channel_id=1, source_target_pairs={{15,0},{0,1},{1,2},{2,3},{3,4},{4,5},{5,6},{6,7},{7,8},{8,9},{9,10... | collective-permute-start | bytes 786440 | tf_op jit(solution)/shard_map/ppermute | solution.py:14
Sparse Core Ops, SparseCore 0:
  226.1 201.8 reduce-scatter.3
where the time goes:
time: 442 us; the launch traced here: 436 us
  waiting for transfers between devices  347 us (79%)
  matrix products  48.5 us (11%)
  starting transfers between devices  14.3 us (3%)
  between operations  13.4 us (3%)
  other arithmetic  8.37 us (2%)
    unnamed x2, waiting for transfers between devices  202 us
    ppermute x31, waiting for transfers between devices, shifted(): return lax.ppermute(block, axis, route)  145 us
    dot_general x16, matrix products, kernel_block(): return jnp.dot(matern, rhs_values, preferred_element_type=jnp.float32)  48.5 us
    ppermute x31, starting transfers between devices, shifted(): return lax.ppermute(block, axis, route)  14.3 us
  transfers between devices with their start and end apart: 32, of which 17 were waited for; matrix products, arithmetic and copies ran while one was open for 11% of the time, Pallas kernels for 0%

commit v1 on v0

--- a/solution.py
+++ b/solution.py
@@ -39,7 +39,29 @@
     squared = target_sq[:, None] + source_sq[None, :] - 2.0 * inner_products
     scaled = kernel_rate * jnp.sqrt(squared) / math.sqrt(targets_bf.shape[1])
     matern = ((1.0 + scaled + scaled * scaled / 3.0) * jnp.exp(-scaled)).astype(jnp.bfloat16)
-    return jnp.dot(matern, rhs_values, preferred_element_type=jnp.float32)
+    return lax.dot_general(
+        rhs_values, matern, (((0,), (1,)), ((), ())), preferred_element_type=jnp.float32
+    )
+
+
+def halving_scatter(sums, axis):
+    size = lax.axis_size(axis)
+    me = lax.axis_index(axis)
+    bits = size.bit_length() - 1
+    rows, cols = sums.shape
+    chunk = rows // size
+    parts = sums.reshape((2,) * bits + (chunk, cols))
+    order = [b for b in (0, 1, 3, 2) if b < bits] + [b for b in range(bits) if b not in (0, 1, 3, 2)]
+    remaining = list(range(bits - 1, -1, -1))
+    for bit in order:
+        position = remaining.index(bit)
+        mine = (me >> bit) & 1
+        kept = lax.dynamic_index_in_dim(parts, mine, position, keepdims=False)
+        sent = lax.dynamic_index_in_dim(parts, 1 - mine, position, keepdims=False)
+        route = [(i, i ^ (1 << bit)) for i in range(size)]
+        parts = kept + lax.ppermute(sent, axis, route)
+        remaining.pop(position)
+    return parts.reshape(chunk, cols)
 
 
 def per_device(src_codes, src_exps, signs, tgt_codes, tgt_exps):
@@ -62,13 +84,13 @@
         running = shifted(running, "blk", 1)
         return (points_bf, running)
 
-    start_sums = jnp.zeros((block_rows, rhs_count), jnp.float32)
+    start_sums = jnp.zeros((rhs_count, block_rows), jnp.float32)
     points_bf, running = lax.fori_loop(0, cycle_size - 1, advance, (targets_bf, start_sums))
     running = running + contribution(points_bf)
     gathered_sums = shifted(running, "blk", 1)
-    owned_sums = lax.psum_scatter(gathered_sums, "grp", scatter_dimension=1, tiled=True)
+    owned_sums = halving_scatter(gathered_sums, "grp")
     source_total = src_codes.shape[0] * group_size * cycle_size
-    return owned_sums * (4.0 / math.sqrt(source_total))
+    return owned_sums.T * (4.0 / math.sqrt(source_total))
 
 
 def solution(mesh):

time: 442 us -> 250 us (0.57)
  the two profiles are of different devices: /device:TPU:1 before, /device:TPU:16 now
where the time goes in v1:
time: 250 us; the launch traced here: 249 us
  waiting for transfers between devices  170 us (68%)
  matrix products  48.5 us (19%)
  starting transfers between devices  18.4 us (7%)
  other arithmetic  7.7 us (3%)
  local copies, waits for them, and re-layouts  3.58 us (1%)
    ppermute x31, waiting for transfers between devices, shifted(): return lax.ppermute(block, axis, route)  160 us
    dot_general x16, matrix products, kernel_block(): lax.dot_general(rhs_values, matern, (((0,), (1,)), ((), ())), preferred_e...  48.5 us
    ppermute x4, starting transfers between devices, halving_scatter(): parts = kept + lax.ppermute(sent, axis, route)  15.6 us
    ppermute x4, waiting for transfers between devices, halving_scatter(): parts = kept + lax.ppermute(sent, axis, route)  10.1 us
  transfers between devices with their start and end apart: 35, of which 20 were waited for; matrix products, arithmetic and copies ran while one was open for 20% of the time, Pallas kernels for 0%

profile of v1, /device:TPU:16, one launch (start us, length us, event | category | flops | bytes accessed | tf_op | source)
XLA Modules:
  0.0 249.0 jit_solution(3964614350548451622)
XLA Ops:
  0.0 0.8 select_add_fusion
  1.0 2.1 add_convert_fusion
  3.3 1.1 mul.81
  4.4 1.0 copy-done
  5.5 0.9 multiply_reduce_fusion.1
  7.1 204.7 %while.14 = (s32[]{:T(128)}, bf16[256,1024]{1,0:T(8,128)(2,1)S(1)}, f32[256,256]{0,1:T(8,128)S(1)}, f32[1024]{0:T(1024)S(1)}, bf16[1024,1024]{1,0:T(8,128)(2,1)S(1)}, /*index=5*/bf16[1024,256]{1,0:T(8,128)(2,1)}, s32[]{:T(128)}) while((s32[]{:T(128)}, bf16[256,1024]{1,0:T(8,128)(2,1)S(1)}, f32[256,256]{0,1:T(8,128)S(1)}, f32[1024]{0:T(1024)S(1)}, ...), condition=%wide.region_3.4_spmd, body=%wide.region_1.3_spmd.sunk | while | flops 674823936 | bytes 8394909 | solution.py:88
  7.4 3.1 %fusion.47 = f32[256,256]{0,1:T(8,128)} fusion(f32[256,256]{0,1:T(8,128)S(1)} %get-tuple-element.145, bf16[1024,256]{1,0:T(8,128)(2,1)} %get-tuple-element.155, bf16[256,1024]{1,0:T(8,128)(2,1)S(1)} %copy.18, bf16[1024,1024]{1,0:T(8,128)(2,1)S(1)} %get-tuple-element.154, f32[1024]{0:T(1024)S(1)} %get-tuple-element.153, f32[256]{0:T(256)S(1)} %multiply_reduce_fusion.4), kind=kOutput, calls=%fused_computation.5.clone.1 | convolution fusion | flops 674037760 | bytes 3675136 | tf_op jit(solution)/shard_map/while/body/eval_jaxpr/dot_general | solution.py:42
  10.5 1.4 collective-permute-start.1
  11.9 8.9 %collective-permute-done.1 = f32[256,256]{0,1:T(8,128)S(1)} collective-permute-done((f32[256,256]{0,1:T(8,128)}, f32[256,256]{0,1:T(8,128)S(1)}, u32[]{:S(2)}, u32[]{:S(2)}) %collective-permute-start.1) | collective-permute-done | bytes 262176 | tf_op jit(solution)/shard_map/while/body/eval_jaxpr/ppermute | solution.py:14
  21.0 3.1 %fusion.47 = f32[256,256]{0,1:T(8,128)} fusion(f32[256,256]{0,1:T(8,128)S(1)} %get-tuple-element.145, bf16[1024,256]{1,0:T(8,128)(2,1)} %get-tuple-element.155, bf16[256,1024]{1,0:T(8,128)(2,1)S(1)} %copy.18, bf16[1024,1024]{1,0:T(8,128)(2,1)S(1)} %get-tuple-element.154, f32[1024]{0:T(1024)S(1)} %get-tuple-element.153, f32[256]{0:T(256)S(1)} %multiply_reduce_fusion.4), kind=kOutput, calls=%fused_computation.5.clone.1 | convolution fusion | flops 674037760 | bytes 3675136 | tf_op jit(solution)/shard_map/while/body/eval_jaxpr/dot_general | solution.py:42
  24.1 10.3 %collective-permute-done.1 = f32[256,256]{0,1:T(8,128)S(1)} collective-permute-done((f32[256,256]{0,1:T(8,128)}, f32[256,256]{0,1:T(8,128)S(1)}, u32[]{:S(2)}, u32[]{:S(2)}) %collective-permute-start.1) | collective-permute-done | bytes 262176 | tf_op jit(solution)/shard_map/while/body/eval_jaxpr/ppermute | solution.py:14
  34.7 3.1 %fusion.47 = f32[256,256]{0,1:T(8,128)} fusion(f32[256,256]{0,1:T(8,128)S(1)} %get-tuple-element.145, bf16[1024,256]{1,0:T(8,128)(2,1)} %get-tuple-element.155, bf16[256,1024]{1,0:T(8,128)(2,1)S(1)} %copy.18, bf16[1024,1024]{1,0:T(8,128)(2,1)S(1)} %get-tuple-element.154, f32[1024]{0:T(1024)S(1)} %get-tuple-element.153, f32[256]{0:T(256)S(1)} %multiply_reduce_fusion.4), kind=kOutput, calls=%fused_computation.5.clone.1 | convolution fusion | flops 674037760 | bytes 3675136 | tf_op jit(solution)/shard_map/while/body/eval_jaxpr/dot_general | solution.py:42
  37.8 10.3 %collective-permute-done.1 = f32[256,256]{0,1:T(8,128)S(1)} collective-permute-done((f32[256,256]{0,1:T(8,128)}, f32[256,256]{0,1:T(8,128)S(1)}, u32[]{:S(2)}, u32[]{:S(2)}) %collective-permute-start.1) | collective-permute-done | bytes 262176 | tf_op jit(solution)/shard_map/while/body/eval_jaxpr/ppermute | solution.py:14
  48.3 3.1 %fusion.47 = f32[256,256]{0,1:T(8,128)} fusion(f32[256,256]{0,1:T(8,128)S(1)} %get-tuple-element.145, bf16[1024,256]{1,0:T(8,128)(2,1)} %get-tuple-element.155, bf16[256,1024]{1,0:T(8,128)(2,1)S(1)} %copy.18, bf16[1024,1024]{1,0:T(8,128)(2,1)S(1)} %get-tuple-element.154, f32[1024]{0:T(1024)S(1)} %get-tuple-element.153, f32[256]{0:T(256)S(1)} %multiply_reduce_fusion.4), kind=kOutput, calls=%fused_computation.5.clone.1 | convolution fusion | flops 674037760 | bytes 3675136 | tf_op jit(solution)/shard_map/while/body/eval_jaxpr/dot_general | solution.py:42
  51.4 10.3 %collective-permute-done.1 = f32[256,256]{0,1:T(8,128)S(1)} collective-permute-done((f32[256,256]{0,1:T(8,128)}, f32[256,256]{0,1:T(8,128)S(1)}, u32[]{:S(2)}, u32[]{:S(2)}) %collective-permute-start.1) | collective-permute-done | bytes 262176 | tf_op jit(solution)/shard_map/while/body/eval_jaxpr/ppermute | solution.py:14
  62.0 3.1 %fusion.47 = f32[256,256]{0,1:T(8,128)} fusion(f32[256,256]{0,1:T(8,128)S(1)} %get-tuple-element.145, bf16[1024,256]{1,0:T(8,128)(2,1)} %get-tuple-element.155, bf16[256,1024]{1,0:T(8,128)(2,1)S(1)} %copy.18, bf16[1024,1024]{1,0:T(8,128)(2,1)S(1)} %get-tuple-element.154, f32[1024]{0:T(1024)S(1)} %get-tuple-element.153, f32[256]{0:T(256)S(1)} %multiply_reduce_fusion.4), kind=kOutput, calls=%fused_computation.5.clone.1 | convolution fusion | flops 674037760 | bytes 3675136 | tf_op jit(solution)/shard_map/while/body/eval_jaxpr/dot_general | solution.py:42
  65.1 10.3 %collective-permute-done.1 = f32[256,256]{0,1:T(8,128)S(1)} collective-permute-done((f32[256,256]{0,1:T(8,128)}, f32[256,256]{0,1:T(8,128)S(1)}, u32[]{:S(2)}, u32[]{:S(2)}) %collective-permute-start.1) | collective-permute-done | bytes 262176 | tf_op jit(solution)/shard_map/while/body/eval_jaxpr/ppermute | solution.py:14
  75.6 3.1 %fusion.47 = f32[256,256]{0,1:T(8,128)} fusion(f32[256,256]{0,1:T(8,128)S(1)} %get-tuple-element.145, bf16[1024,256]{1,0:T(8,128)(2,1)} %get-tuple-element.155, bf16[256,1024]{1,0:T(8,128)(2,1)S(1)} %copy.18, bf16[1024,1024]{1,0:T(8,128)(2,1)S(1)} %get-tuple-element.154, f32[1024]{0:T(1024)S(1)} %get-tuple-element.153, f32[256]{0:T(256)S(1)} %multiply_reduce_fusion.4), kind=kOutput, calls=%fused_computation.5.clone.1 | convolution fusion | flops 674037760 | bytes 3675136 | tf_op jit(solution)/shard_map/while/body/eval_jaxpr/dot_general | solution.py:42
  78.7 10.3 %collective-permute-done.1 = f32[256,256]{0,1:T(8,128)S(1)} collective-permute-done((f32[256,256]{0,1:T(8,128)}, f32[256,256]{0,1:T(8,128)S(1)}, u32[]{:S(2)}, u32[]{:S(2)}) %collective-permute-start.1) | collective-permute-done | bytes 262176 | tf_op jit(solution)/shard_map/while/body/eval_jaxpr/ppermute | solution.py:14
  89.3 3.1 %fusion.47 = f32[256,256]{0,1:T(8,128)} fusion(f32[256,256]{0,1:T(8,128)S(1)} %get-tuple-element.145, bf16[1024,256]{1,0:T(8,128)(2,1)} %get-tuple-element.155, bf16[256,1024]{1,0:T(8,128)(2,1)S(1)} %copy.18, bf16[1024,1024]{1,0:T(8,128)(2,1)S(1)} %get-tuple-element.154, f32[1024]{0:T(1024)S(1)} %get-tuple-element.153, f32[256]{0:T(256)S(1)} %multiply_reduce_fusion.4), kind=kOutput, calls=%fused_computation.5.clone.1 | convolution fusion | flops 674037760 | bytes 3675136 | tf_op jit(solution)/shard_map/while/body/eval_jaxpr/dot_general | solution.py:42
  92.3 10.3 %collective-permute-done.1 = f32[256,256]{0,1:T(8,128)S(1)} collective-permute-done((f32[256,256]{0,1:T(8,128)}, f32[256,256]{0,1:T(8,128)S(1)}, u32[]{:S(2)}, u32[]{:S(2)}) %collective-permute-start.1) | collective-permute-done | bytes 262176 | tf_op jit(solution)/shard_map/while/body/eval_jaxpr/ppermute | solution.py:14
  102.9 3.1 %fusion.47 = f32[256,256]{0,1:T(8,128)} fusion(f32[256,256]{0,1:T(8,128)S(1)} %get-tuple-element.145, bf16[1024,256]{1,0:T(8,128)(2,1)} %get-tuple-element.155, bf16[256,1024]{1,0:T(8,128)(2,1)S(1)} %copy.18, bf16[1024,1024]{1,0:T(8,128)(2,1)S(1)} %get-tuple-element.154, f32[1024]{0:T(1024)S(1)} %get-tuple-element.153, f32[256]{0:T(256)S(1)} %multiply_reduce_fusion.4), kind=kOutput, calls=%fused_computation.5.clone.1 | convolution fusion | flops 674037760 | bytes 3675136 | tf_op jit(solution)/shard_map/while/body/eval_jaxpr/dot_general | solution.py:42
  106.0 10.3 %collective-permute-done.1 = f32[256,256]{0,1:T(8,128)S(1)} collective-permute-done((f32[256,256]{0,1:T(8,128)}, f32[256,256]{0,1:T(8,128)S(1)}, u32[]{:S(2)}, u32[]{:S(2)}) %collective-permute-start.1) | collective-permute-done | bytes 262176 | tf_op jit(solution)/shard_map/while/body/eval_jaxpr/ppermute | solution.py:14
  116.6 3.1 %fusion.47 = f32[256,256]{0,1:T(8,128)} fusion(f32[256,256]{0,1:T(8,128)S(1)} %get-tuple-element.145, bf16[1024,256]{1,0:T(8,128)(2,1)} %get-tuple-element.155, bf16[256,1024]{1,0:T(8,128)(2,1)S(1)} %copy.18, bf16[1024,1024]{1,0:T(8,128)(2,1)S(1)} %get-tuple-element.154, f32[1024]{0:T(1024)S(1)} %get-tuple-element.153, f32[256]{0:T(256)S(1)} %multiply_reduce_fusion.4), kind=kOutput, calls=%fused_computation.5.clone.1 | convolution fusion | flops 674037760 | bytes 3675136 | tf_op jit(solution)/shard_map/while/body/eval_jaxpr/dot_general | solution.py:42
  119.6 10.3 %collective-permute-done.1 = f32[256,256]{0,1:T(8,128)S(1)} collective-permute-done((f32[256,256]{0,1:T(8,128)}, f32[256,256]{0,1:T(8,128)S(1)}, u32[]{:S(2)}, u32[]{:S(2)}) %collective-permute-start.1) | collective-permute-done | bytes 262176 | tf_op jit(solution)/shard_map/while/body/eval_jaxpr/ppermute | solution.py:14
  130.2 3.1 %fusion.47 = f32[256,256]{0,1:T(8,128)} fusion(f32[256,256]{0,1:T(8,128)S(1)} %get-tuple-element.145, bf16[1024,256]{1,0:T(8,128)(2,1)} %get-tuple-element.155, bf16[256,1024]{1,0:T(8,128)(2,1)S(1)} %copy.18, bf16[1024,1024]{1,0:T(8,128)(2,1)S(1)} %get-tuple-element.154, f32[1024]{0:T(1024)S(1)} %get-tuple-element.153, f32[256]{0:T(256)S(1)} %multiply_reduce_fusion.4), kind=kOutput, calls=%fused_computation.5.clone.1 | convolution fusion | flops 674037760 | bytes 3675136 | tf_op jit(solution)/shard_map/while/body/eval_jaxpr/dot_general | solution.py:42
  133.3 10.3 %collective-permute-done.1 = f32[256,256]{0,1:T(8,128)S(1)} collective-permute-done((f32[256,256]{0,1:T(8,128)}, f32[256,256]{0,1:T(8,128)S(1)}, u32[]{:S(2)}, u32[]{:S(2)}) %collective-permute-start.1) | collective-permute-done | bytes 262176 | tf_op jit(solution)/shard_map/while/body/eval_jaxpr/ppermute | solution.py:14
  143.9 3.1 %fusion.47 = f32[256,256]{0,1:T(8,128)} fusion(f32[256,256]{0,1:T(8,128)S(1)} %get-tuple-element.145, bf16[1024,256]{1,0:T(8,128)(2,1)} %get-tuple-element.155, bf16[256,1024]{1,0:T(8,128)(2,1)S(1)} %copy.18, bf16[1024,1024]{1,0:T(8,128)(2,1)S(1)} %get-tuple-element.154, f32[1024]{0:T(1024)S(1)} %get-tuple-element.153, f32[256]{0:T(256)S(1)} %multiply_reduce_fusion.4), kind=kOutput, calls=%fused_computation.5.clone.1 | convolution fusion | flops 674037760 | bytes 3675136 | tf_op jit(solution)/shard_map/while/body/eval_jaxpr/dot_general | solution.py:42
  146.9 10.3 %collective-permute-done.1 = f32[256,256]{0,1:T(8,128)S(1)} collective-permute-done((f32[256,256]{0,1:T(8,128)}, f32[256,256]{0,1:T(8,128)S(1)}, u32[]{:S(2)}, u32[]{:S(2)}) %collective-permute-start.1) | collective-permute-done | bytes 262176 | tf_op jit(solution)/shard_map/while/body/eval_jaxpr/ppermute | solution.py:14
  157.5 3.1 %fusion.47 = f32[256,256]{0,1:T(8,128)} fusion(f32[256,256]{0,1:T(8,128)S(1)} %get-tuple-element.145, bf16[1024,256]{1,0:T(8,128)(2,1)} %get-tuple-element.155, bf16[256,1024]{1,0:T(8,128)(2,1)S(1)} %copy.18, bf16[1024,1024]{1,0:T(8,128)(2,1)S(1)} %get-tuple-element.154, f32[1024]{0:T(1024)S(1)} %get-tuple-element.153, f32[256]{0:T(256)S(1)} %multiply_reduce_fusion.4), kind=kOutput, calls=%fused_computation.5.clone.1 | convolution fusion | flops 674037760 | bytes 3675136 | tf_op jit(solution)/shard_map/while/body/eval_jaxpr/dot_general | solution.py:42
  160.6 10.3 %collective-permute-done.1 = f32[256,256]{0,1:T(8,128)S(1)} collective-permute-done((f32[256,256]{0,1:T(8,128)}, f32[256,256]{0,1:T(8,128)S(1)}, u32[]{:S(2)}, u32[]{:S(2)}) %collective-permute-start.1) | collective-permute-done | bytes 262176 | tf_op jit(solution)/shard_map/while/body/eval_jaxpr/ppermute | solution.py:14
  171.1 3.1 %fusion.47 = f32[256,256]{0,1:T(8,128)} fusion(f32[256,256]{0,1:T(8,128)S(1)} %get-tuple-element.145, bf16[1024,256]{1,0:T(8,128)(2,1)} %get-tuple-element.155, bf16[256,1024]{1,0:T(8,128)(2,1)S(1)} %copy.18, bf16[1024,1024]{1,0:T(8,128)(2,1)S(1)} %get-tuple-element.154, f32[1024]{0:T(1024)S(1)} %get-tuple-element.153, f32[256]{0:T(256)S(1)} %multiply_reduce_fusion.4), kind=kOutput, calls=%fused_computation.5.clone.1 | convolution fusion | flops 674037760 | bytes 3675136 | tf_op jit(solution)/shard_map/while/body/eval_jaxpr/dot_general | solution.py:42
  174.2 10.3 %collective-permute-done.1 = f32[256,256]{0,1:T(8,128)S(1)} collective-permute-done((f32[256,256]{0,1:T(8,128)}, f32[256,256]{0,1:T(8,128)S(1)}, u32[]{:S(2)}, u32[]{:S(2)}) %collective-permute-start.1) | collective-permute-done | bytes 262176 | tf_op jit(solution)/shard_map/while/body/eval_jaxpr/ppermute | solution.py:14
  184.8 3.1 %fusion.47 = f32[256,256]{0,1:T(8,128)} fusion(f32[256,256]{0,1:T(8,128)S(1)} %get-tuple-element.145, bf16[1024,256]{1,0:T(8,128)(2,1)} %get-tuple-element.155, bf16[256,1024]{1,0:T(8,128)(2,1)S(1)} %copy.18, bf16[1024,1024]{1,0:T(8,128)(2,1)S(1)} %get-tuple-element.154, f32[1024]{0:T(1024)S(1)} %get-tuple-element.153, f32[256]{0:T(256)S(1)} %multiply_reduce_fusion.4), kind=kOutput, calls=%fused_computation.5.clone.1 | convolution fusion | flops 674037760 | bytes 3675136 | tf_op jit(solution)/shard_map/while/body/eval_jaxpr/dot_general | solution.py:42
  187.9 10.3 %collective-permute-done.1 = f32[256,256]{0,1:T(8,128)S(1)} collective-permute-done((f32[256,256]{0,1:T(8,128)}, f32[256,256]{0,1:T(8,128)S(1)}, u32[]{:S(2)}, u32[]{:S(2)}) %collective-permute-start.1) | collective-permute-done | bytes 262176 | tf_op jit(solution)/shard_map/while/body/eval_jaxpr/ppermute | solution.py:14
  198.4 3.1 %fusion.47 = f32[256,256]{0,1:T(8,128)} fusion(f32[256,256]{0,1:T(8,128)S(1)} %get-tuple-element.145, bf16[1024,256]{1,0:T(8,128)(2,1)} %get-tuple-element.155, bf16[256,1024]{1,0:T(8,128)(2,1)S(1)} %copy.18, bf16[1024,1024]{1,0:T(8,128)(2,1)S(1)} %get-tuple-element.154, f32[1024]{0:T(1024)S(1)} %get-tuple-element.153, f32[256]{0:T(256)S(1)} %multiply_reduce_fusion.4), kind=kOutput, calls=%fused_computation.5.clone.1 | convolution fusion | flops 674037760 | bytes 3675136 | tf_op jit(solution)/shard_map/while/body/eval_jaxpr/dot_general | solution.py:42
  201.5 10.3 %collective-permute-done.1 = f32[256,256]{0,1:T(8,128)S(1)} collective-permute-done((f32[256,256]{0,1:T(8,128)}, f32[256,256]{0,1:T(8,128)S(1)}, u32[]{:S(2)}, u32[]{:S(2)}) %collective-permute-start.1) | collective-permute-done | bytes 262176 | tf_op jit(solution)/shard_map/while/body/eval_jaxpr/ppermute | solution.py:14
  212.1 2.5 %convolution_add_fusion = f32[256,256]{1,0:T(8,128)S(1)} fusion(f32[256,256]{1,0:T(8,128)S(1)} %copy.8, bf16[1024,256]{1,0:T(8,128)(2,1)} %get-tuple-element.161, bf16[256,1024]{1,0:T(8,128)(2,1)S(1)} %get-tuple-element.84, bf16[1024,1024]{1,0:T(8,128)(2,1)S(1)} %get-tuple-element.159, f32[1024]{0:T(1024)S(1)} %get-tuple-element.171, ...), kind=kOutput, calls=%fused_computation.26 | convolution fusion | flops 674037760 | bytes 3675136 | tf_op jit(solution)/shard_map/dot_general | solution.py:42
  214.7 7.9 %collective-permute-done.2 = f32[256,256]{1,0:T(8,128)S(1)} collective-permute-done((f32[256,256]{1,0:T(8,128)S(1)}, f32[256,256]{1,0:T(8,128)S(1)}, u32[]{:S(2)}, u32[]{:S(2)}) %collective-permute-start.2) | collective-permute-done | bytes 262176 | tf_op jit(solution)/shard_map/ppermute | solution.py:14
  222.6 2.0 collective-permute-start.3
  224.6 3.1 %collective-permute-done.3 = f32[2,2,2,16,256]{4,3,2,1,0:T(8,128)S(1)} collective-permute-done((f32[2,2,2,16,256]{4,3,2,1,0:T(8,128)S(1)}, f32[2,2,2,16,256]{4,3,2,1,0:T(8,128)S(1)}, u32[]{:S(2)}, u32[]{:S(2)}) %collective-permute-start.3) | collective-permute-done | bytes 131104 | tf_op jit(solution)/shard_map/ppermute | solution.py:62
  227.7 3.3 %collective-permute-start.4 = (f32[2,2,16,256]{3,2,1,0:T(8,128)S(1)}, f32[2,2,16,256]{3,2,1,0:T(8,128)S(1)}, u32[]{:S(2)}, u32[]{:S(2)}) collective-permute-start(f32[2,2,16,256]{3,2,1,0:T(8,128)S(1)} %dynamic-slice_bitcast_fusion.1), channel_id=1, source_target_pairs={{0,32},{16,48},{32,0},{48,16},{64,96},{80,112},{96,64},{112,80},{1... | collective-permute-start | bytes 196616 | tf_op jit(solution)/shard_map/ppermute | solution.py:62
  231.0 2.2 collective-permute-done.4
  233.3 2.5 collective-permute-start.5
  235.8 3.0 %collective-permute-done.5 = f32[2,16,256]{2,1,0:T(8,128)S(1)} collective-permute-done((f32[2,16,256]{2,1,0:T(8,128)S(1)}, f32[2,16,256]{2,1,0:T(8,128)S(1)}, u32[]{:S(2)}, u32[]{:S(2)}) %collective-permute-start.5) | collective-permute-done | bytes 32800 | tf_op jit(solution)/shard_map/ppermute | solution.py:62
  238.8 7.8 %collective-permute-start.6 = (f32[16,256]{1,0:T(8,128)S(1)}, f32[16,256]{1,0:T(8,128)S(1)}, u32[]{:S(2)}, u32[]{:S(2)}) collective-permute-start(f32[16,256]{1,0:T(8,128)S(1)} %dynamic-slice_bitcast_fusion.3), channel_id=1, source_target_pairs={{0,64},{16,80},{32,96},{48,112},{64,0},{80,16},{96,32},{112,48},{1... | collective-permute-start | bytes 49160 | tf_op jit(solution)/shard_map/ppermute | solution.py:62
  246.6 1.7 collective-permute-done.6
  248.4 0.6 fusion.28
  (95 shorter events, 6.1 us)
Async XLA Ops:
  0.0 3.1 %copy-start.2 = (s32[256,8]{0,1:T(8,128)S(1)}, s32[256,8]{0,1:T(8,128)}, u32[]{:S(2)}) copy-start(s32[256,8]{0,1:T(8,128)} %param.11) | copy-start | bytes 24580
  3.3 2.2 copy-start
  5.5 1.2 copy-start.1
  7.1 13.6 %collective-permute-start = (bf16[256,1024]{1,0:T(8,128)(2,1)S(1)}, bf16[256,1024]{1,0:T(8,128)(2,1)S(1)}, u32[]{:S(2)}, u32[]{:S(2)}) collective-permute-start(bf16[256,1024]{1,0:T(8,128)(2,1)S(1)} %copy.18), channel_id=1, source_target_pairs={{15,0},{0,1},{1,2},{2,3},{3,4},{4,5},{5,6},{6,7},{7,8},{8,9},{9,10... | collective-permute-start | bytes 1572872 | tf_op jit(solution)/shard_map/while/body/eval_jaxpr/ppermute | solution.py:14
  10.5 10.3 %collective-permute-start.1 = (f32[256,256]{0,1:T(8,128)}, f32[256,256]{0,1:T(8,128)S(1)}, u32[]{:S(2)}, u32[]{:S(2)}) collective-permute-start(f32[256,256]{0,1:T(8,128)} %fusion.47), channel_id=1, source_target_pairs={{15,0},{0,1},{1,2},{2,3},{3,4},{4,5},{5,6},{6,7},{7,8},{8,9},{9,10... | collective-permute-start | bytes 786440 | tf_op jit(solution)/shard_map/while/body/eval_jaxpr/ppermute | solution.py:14
  20.8 13.6 %collective-permute-start = (bf16[256,1024]{1,0:T(8,128)(2,1)S(1)}, bf16[256,1024]{1,0:T(8,128)(2,1)S(1)}, u32[]{:S(2)}, u32[]{:S(2)}) collective-permute-start(bf16[256,1024]{1,0:T(8,128)(2,1)S(1)} %copy.18), channel_id=1, source_target_pairs={{15,0},{0,1},{1,2},{2,3},{3,4},{4,5},{5,6},{6,7},{7,8},{8,9},{9,10... | collective-permute-start | bytes 1572872 | tf_op jit(solution)/shard_map/while/body/eval_jaxpr/ppermute | solution.py:14
  24.1 10.3 %collective-permute-start.1 = (f32[256,256]{0,1:T(8,128)}, f32[256,256]{0,1:T(8,128)S(1)}, u32[]{:S(2)}, u32[]{:S(2)}) collective-permute-start(f32[256,256]{0,1:T(8,128)} %fusion.47), channel_id=1, source_target_pairs={{15,0},{0,1},{1,2},{2,3},{3,4},{4,5},{5,6},{6,7},{7,8},{8,9},{9,10... | collective-permute-start | bytes 786440 | tf_op jit(solution)/shard_map/while/body/eval_jaxpr/ppermute | solution.py:14
  34.4 13.6 %collective-permute-start = (bf16[256,1024]{1,0:T(8,128)(2,1)S(1)}, bf16[256,1024]{1,0:T(8,128)(2,1)S(1)}, u32[]{:S(2)}, u32[]{:S(2)}) collective-permute-start(bf16[256,1024]{1,0:T(8,128)(2,1)S(1)} %copy.18), channel_id=1, source_target_pairs={{15,0},{0,1},{1,2},{2,3},{3,4},{4,5},{5,6},{6,7},{7,8},{8,9},{9,10... | collective-permute-start | bytes 1572872 | tf_op jit(solution)/shard_map/while/body/eval_jaxpr/ppermute | solution.py:14
  37.8 10.3 %collective-permute-start.1 = (f32[256,256]{0,1:T(8,128)}, f32[256,256]{0,1:T(8,128)S(1)}, u32[]{:S(2)}, u32[]{:S(2)}) collective-permute-start(f32[256,256]{0,1:T(8,128)} %fusion.47), channel_id=1, source_target_pairs={{15,0},{0,1},{1,2},{2,3},{3,4},{4,5},{5,6},{6,7},{7,8},{8,9},{9,10... | collective-permute-start | bytes 786440 | tf_op jit(solution)/shard_map/while/body/eval_jaxpr/ppermute | solution.py:14
  48.1 13.6 %collective-permute-start = (bf16[256,1024]{1,0:T(8,128)(2,1)S(1)}, bf16[256,1024]{1,0:T(8,128)(2,1)S(1)}, u32[]{:S(2)}, u32[]{:S(2)}) collective-permute-start(bf16[256,1024]{1,0:T(8,128)(2,1)S(1)} %copy.18), channel_id=1, source_target_pairs={{15,0},{0,1},{1,2},{2,3},{3,4},{4,5},{5,6},{6,7},{7,8},{8,9},{9,10... | collective-permute-start | bytes 1572872 | tf_op jit(solution)/shard_map/while/body/eval_jaxpr/ppermute | solution.py:14
  51.4 10.3 %collective-permute-start.1 = (f32[256,256]{0,1:T(8,128)}, f32[256,256]{0,1:T(8,128)S(1)}, u32[]{:S(2)}, u32[]{:S(2)}) collective-permute-start(f32[256,256]{0,1:T(8,128)} %fusion.47), channel_id=1, source_target_pairs={{15,0},{0,1},{1,2},{2,3},{3,4},{4,5},{5,6},{6,7},{7,8},{8,9},{9,10... | collective-permute-start | bytes 786440 | tf_op jit(solution)/shard_map/while/body/eval_jaxpr/ppermute | solution.py:14
  61.7 13.6 %collective-permute-start = (bf16[256,1024]{1,0:T(8,128)(2,1)S(1)}, bf16[256,1024]{1,0:T(8,128)(2,1)S(1)}, u32[]{:S(2)}, u32[]{:S(2)}) collective-permute-start(bf16[256,1024]{1,0:T(8,128)(2,1)S(1)} %copy.18), channel_id=1, source_target_pairs={{15,0},{0,1},{1,2},{2,3},{3,4},{4,5},{5,6},{6,7},{7,8},{8,9},{9,10... | collective-permute-start | bytes 1572872 | tf_op jit(solution)/shard_map/while/body/eval_jaxpr/ppermute | solution.py:14
  65.1 10.3 %collective-permute-start.1 = (f32[256,256]{0,1:T(8,128)}, f32[256,256]{0,1:T(8,128)S(1)}, u32[]{:S(2)}, u32[]{:S(2)}) collective-permute-start(f32[256,256]{0,1:T(8,128)} %fusion.47), channel_id=1, source_target_pairs={{15,0},{0,1},{1,2},{2,3},{3,4},{4,5},{5,6},{6,7},{7,8},{8,9},{9,10... | collective-permute-start | bytes 786440 | tf_op jit(solution)/shard_map/while/body/eval_jaxpr/ppermute | solution.py:14
  75.4 13.6 %collective-permute-start = (bf16[256,1024]{1,0:T(8,128)(2,1)S(1)}, bf16[256,1024]{1,0:T(8,128)(2,1)S(1)}, u32[]{:S(2)}, u32[]{:S(2)}) collective-permute-start(bf16[256,1024]{1,0:T(8,128)(2,1)S(1)} %copy.18), channel_id=1, source_target_pairs={{15,0},{0,1},{1,2},{2,3},{3,4},{4,5},{5,6},{6,7},{7,8},{8,9},{9,10... | collective-permute-start | bytes 1572872 | tf_op jit(solution)/shard_map/while/body/eval_jaxpr/ppermute | solution.py:14
  78.7 10.3 %collective-permute-start.1 = (f32[256,256]{0,1:T(8,128)}, f32[256,256]{0,1:T(8,128)S(1)}, u32[]{:S(2)}, u32[]{:S(2)}) collective-permute-start(f32[256,256]{0,1:T(8,128)} %fusion.47), channel_id=1, source_target_pairs={{15,0},{0,1},{1,2},{2,3},{3,4},{4,5},{5,6},{6,7},{7,8},{8,9},{9,10... | collective-permute-start | bytes 786440 | tf_op jit(solution)/shard_map/while/body/eval_jaxpr/ppermute | solution.py:14
  89.0 13.6 %collective-permute-start = (bf16[256,1024]{1,0:T(8,128)(2,1)S(1)}, bf16[256,1024]{1,0:T(8,128)(2,1)S(1)}, u32[]{:S(2)}, u32[]{:S(2)}) collective-permute-start(bf16[256,1024]{1,0:T(8,128)(2,1)S(1)} %copy.18), channel_id=1, source_target_pairs={{15,0},{0,1},{1,2},{2,3},{3,4},{4,5},{5,6},{6,7},{7,8},{8,9},{9,10... | collective-permute-start | bytes 1572872 | tf_op jit(solution)/shard_map/while/body/eval_jaxpr/ppermute | solution.py:14
  92.3 10.3 %collective-permute-start.1 = (f32[256,256]{0,1:T(8,128)}, f32[256,256]{0,1:T(8,128)S(1)}, u32[]{:S(2)}, u32[]{:S(2)}) collective-permute-start(f32[256,256]{0,1:T(8,128)} %fusion.47), channel_id=1, source_target_pairs={{15,0},{0,1},{1,2},{2,3},{3,4},{4,5},{5,6},{6,7},{7,8},{8,9},{9,10... | collective-permute-start | bytes 786440 | tf_op jit(solution)/shard_map/while/body/eval_jaxpr/ppermute | solution.py:14
  102.6 13.6 %collective-permute-start = (bf16[256,1024]{1,0:T(8,128)(2,1)S(1)}, bf16[256,1024]{1,0:T(8,128)(2,1)S(1)}, u32[]{:S(2)}, u32[]{:S(2)}) collective-permute-start(bf16[256,1024]{1,0:T(8,128)(2,1)S(1)} %copy.18), channel_id=1, source_target_pairs={{15,0},{0,1},{1,2},{2,3},{3,4},{4,5},{5,6},{6,7},{7,8},{8,9},{9,10... | collective-permute-start | bytes 1572872 | tf_op jit(solution)/shard_map/while/body/eval_jaxpr/ppermute | solution.py:14
  106.0 10.3 %collective-permute-start.1 = (f32[256,256]{0,1:T(8,128)}, f32[256,256]{0,1:T(8,128)S(1)}, u32[]{:S(2)}, u32[]{:S(2)}) collective-permute-start(f32[256,256]{0,1:T(8,128)} %fusion.47), channel_id=1, source_target_pairs={{15,0},{0,1},{1,2},{2,3},{3,4},{4,5},{5,6},{6,7},{7,8},{8,9},{9,10... | collective-permute-start | bytes 786440 | tf_op jit(solution)/shard_map/while/body/eval_jaxpr/ppermute | solution.py:14
  116.3 13.6 %collective-permute-start = (bf16[256,1024]{1,0:T(8,128)(2,1)S(1)}, bf16[256,1024]{1,0:T(8,128)(2,1)S(1)}, u32[]{:S(2)}, u32[]{:S(2)}) collective-permute-start(bf16[256,1024]{1,0:T(8,128)(2,1)S(1)} %copy.18), channel_id=1, source_target_pairs={{15,0},{0,1},{1,2},{2,3},{3,4},{4,5},{5,6},{6,7},{7,8},{8,9},{9,10... | collective-permute-start | bytes 1572872 | tf_op jit(solution)/shard_map/while/body/eval_jaxpr/ppermute | solution.py:14
  119.6 10.3 %collective-permute-start.1 = (f32[256,256]{0,1:T(8,128)}, f32[256,256]{0,1:T(8,128)S(1)}, u32[]{:S(2)}, u32[]{:S(2)}) collective-permute-start(f32[256,256]{0,1:T(8,128)} %fusion.47), channel_id=1, source_target_pairs={{15,0},{0,1},{1,2},{2,3},{3,4},{4,5},{5,6},{6,7},{7,8},{8,9},{9,10... | collective-permute-start | bytes 786440 | tf_op jit(solution)/shard_map/while/body/eval_jaxpr/ppermute | solution.py:14
  129.9 13.6 %collective-permute-start = (bf16[256,1024]{1,0:T(8,128)(2,1)S(1)}, bf16[256,1024]{1,0:T(8,128)(2,1)S(1)}, u32[]{:S(2)}, u32[]{:S(2)}) collective-permute-start(bf16[256,1024]{1,0:T(8,128)(2,1)S(1)} %copy.18), channel_id=1, source_target_pairs={{15,0},{0,1},{1,2},{2,3},{3,4},{4,5},{5,6},{6,7},{7,8},{8,9},{9,10... | collective-permute-start | bytes 1572872 | tf_op jit(solution)/shard_map/while/body/eval_jaxpr/ppermute | solution.py:14
  133.3 10.3 %collective-permute-start.1 = (f32[256,256]{0,1:T(8,128)}, f32[256,256]{0,1:T(8,128)S(1)}, u32[]{:S(2)}, u32[]{:S(2)}) collective-permute-start(f32[256,256]{0,1:T(8,128)} %fusion.47), channel_id=1, source_target_pairs={{15,0},{0,1},{1,2},{2,3},{3,4},{4,5},{5,6},{6,7},{7,8},{8,9},{9,10... | collective-permute-start | bytes 786440 | tf_op jit(solution)/shard_map/while/body/eval_jaxpr/ppermute | solution.py:14
  143.6 13.6 %collective-permute-start = (bf16[256,1024]{1,0:T(8,128)(2,1)S(1)}, bf16[256,1024]{1,0:T(8,128)(2,1)S(1)}, u32[]{:S(2)}, u32[]{:S(2)}) collective-permute-start(bf16[256,1024]{1,0:T(8,128)(2,1)S(1)} %copy.18), channel_id=1, source_target_pairs={{15,0},{0,1},{1,2},{2,3},{3,4},{4,5},{5,6},{6,7},{7,8},{8,9},{9,10... | collective-permute-start | bytes 1572872 | tf_op jit(solution)/shard_map/while/body/eval_jaxpr/ppermute | solution.py:14
  146.9 10.3 %collective-permute-start.1 = (f32[256,256]{0,1:T(8,128)}, f32[256,256]{0,1:T(8,128)S(1)}, u32[]{:S(2)}, u32[]{:S(2)}) collective-permute-start(f32[256,256]{0,1:T(8,128)} %fusion.47), channel_id=1, source_target_pairs={{15,0},{0,1},{1,2},{2,3},{3,4},{4,5},{5,6},{6,7},{7,8},{8,9},{9,10... | collective-permute-start | bytes 786440 | tf_op jit(solution)/shard_map/while/body/eval_jaxpr/ppermute | solution.py:14
  157.2 13.6 %collective-permute-start = (bf16[256,1024]{1,0:T(8,128)(2,1)S(1)}, bf16[256,1024]{1,0:T(8,128)(2,1)S(1)}, u32[]{:S(2)}, u32[]{:S(2)}) collective-permute-start(bf16[256,1024]{1,0:T(8,128)(2,1)S(1)} %copy.18), channel_id=1, source_target_pairs={{15,0},{0,1},{1,2},{2,3},{3,4},{4,5},{5,6},{6,7},{7,8},{8,9},{9,10... | collective-permute-start | bytes 1572872 | tf_op jit(solution)/shard_map/while/body/eval_jaxpr/ppermute | solution.py:14
  160.6 10.3 %collective-permute-start.1 = (f32[256,256]{0,1:T(8,128)}, f32[256,256]{0,1:T(8,128)S(1)}, u32[]{:S(2)}, u32[]{:S(2)}) collective-permute-start(f32[256,256]{0,1:T(8,128)} %fusion.47), channel_id=1, source_target_pairs={{15,0},{0,1},{1,2},{2,3},{3,4},{4,5},{5,6},{6,7},{7,8},{8,9},{9,10... | collective-permute-start | bytes 786440 | tf_op jit(solution)/shard_map/while/body/eval_jaxpr/ppermute | solution.py:14
  170.9 13.6 %collective-permute-start = (bf16[256,1024]{1,0:T(8,128)(2,1)S(1)}, bf16[256,1024]{1,0:T(8,128)(2,1)S(1)}, u32[]{:S(2)}, u32[]{:S(2)}) collective-permute-start(bf16[256,1024]{1,0:T(8,128)(2,1)S(1)} %copy.18), channel_id=1, source_target_pairs={{15,0},{0,1},{1,2},{2,3},{3,4},{4,5},{5,6},{6,7},{7,8},{8,9},{9,10... | collective-permute-start | bytes 1572872 | tf_op jit(solution)/shard_map/while/body/eval_jaxpr/ppermute | solution.py:14
  174.2 10.3 %collective-permute-start.1 = (f32[256,256]{0,1:T(8,128)}, f32[256,256]{0,1:T(8,128)S(1)}, u32[]{:S(2)}, u32[]{:S(2)}) collective-permute-start(f32[256,256]{0,1:T(8,128)} %fusion.47), channel_id=1, source_target_pairs={{15,0},{0,1},{1,2},{2,3},{3,4},{4,5},{5,6},{6,7},{7,8},{8,9},{9,10... | collective-permute-start | bytes 786440 | tf_op jit(solution)/shard_map/while/body/eval_jaxpr/ppermute | solution.py:14
  184.5 13.6 %collective-permute-start = (bf16[256,1024]{1,0:T(8,128)(2,1)S(1)}, bf16[256,1024]{1,0:T(8,128)(2,1)S(1)}, u32[]{:S(2)}, u32[]{:S(2)}) collective-permute-start(bf16[256,1024]{1,0:T(8,128)(2,1)S(1)} %copy.18), channel_id=1, source_target_pairs={{15,0},{0,1},{1,2},{2,3},{3,4},{4,5},{5,6},{6,7},{7,8},{8,9},{9,10... | collective-permute-start | bytes 1572872 | tf_op jit(solution)/shard_map/while/body/eval_jaxpr/ppermute | solution.py:14
  187.9 10.3 %collective-permute-start.1 = (f32[256,256]{0,1:T(8,128)}, f32[256,256]{0,1:T(8,128)S(1)}, u32[]{:S(2)}, u32[]{:S(2)}) collective-permute-start(f32[256,256]{0,1:T(8,128)} %fusion.47), channel_id=1, source_target_pairs={{15,0},{0,1},{1,2},{2,3},{3,4},{4,5},{5,6},{6,7},{7,8},{8,9},{9,10... | collective-permute-start | bytes 786440 | tf_op jit(solution)/shard_map/while/body/eval_jaxpr/ppermute | solution.py:14
  198.2 13.6 %collective-permute-start = (bf16[256,1024]{1,0:T(8,128)(2,1)S(1)}, bf16[256,1024]{1,0:T(8,128)(2,1)S(1)}, u32[]{:S(2)}, u32[]{:S(2)}) collective-permute-start(bf16[256,1024]{1,0:T(8,128)(2,1)S(1)} %copy.18), channel_id=1, source_target_pairs={{15,0},{0,1},{1,2},{2,3},{3,4},{4,5},{5,6},{6,7},{7,8},{8,9},{9,10... | collective-permute-start | bytes 1572872 | tf_op jit(solution)/shard_map/while/body/eval_jaxpr/ppermute | solution.py:14
  201.5 10.3 %collective-permute-start.1 = (f32[256,256]{0,1:T(8,128)}, f32[256,256]{0,1:T(8,128)S(1)}, u32[]{:S(2)}, u32[]{:S(2)}) collective-permute-start(f32[256,256]{0,1:T(8,128)} %fusion.47), channel_id=1, source_target_pairs={{15,0},{0,1},{1,2},{2,3},{3,4},{4,5},{5,6},{6,7},{7,8},{8,9},{9,10... | collective-permute-start | bytes 786440 | tf_op jit(solution)/shard_map/while/body/eval_jaxpr/ppermute | solution.py:14
  214.6 8.0 %collective-permute-start.2 = (f32[256,256]{1,0:T(8,128)S(1)}, f32[256,256]{1,0:T(8,128)S(1)}, u32[]{:S(2)}, u32[]{:S(2)}) collective-permute-start(f32[256,256]{1,0:T(8,128)S(1)} %convolution_add_fusion), channel_id=1, source_target_pairs={{15,0},{0,1},{1,2},{2,3},{3,4},{4,5},{5,6},{6,7},{7,8},{8,9},{9,10... | collective-permute-start | bytes 786440 | tf_op jit(solution)/shard_map/ppermute | solution.py:14
  222.6 5.1 %collective-permute-start.3 = (f32[2,2,2,16,256]{4,3,2,1,0:T(8,128)S(1)}, f32[2,2,2,16,256]{4,3,2,1,0:T(8,128)S(1)}, u32[]{:S(2)}, u32[]{:S(2)}) collective-permute-start(f32[2,2,2,16,256]{4,3,2,1,0:T(8,128)S(1)} %dynamic-slice_bitcast_fusion), channel_id=1, source_target_pairs={{0,16},{16,0},{32,48},{48,32},{64,80},{80,64},{96,112},{112,96},{1... | collective-permute-start | bytes 393224 | tf_op jit(solution)/shard_map/ppermute | solution.py:62
  227.7 5.6 %collective-permute-start.4 = (f32[2,2,16,256]{3,2,1,0:T(8,128)S(1)}, f32[2,2,16,256]{3,2,1,0:T(8,128)S(1)}, u32[]{:S(2)}, u32[]{:S(2)}) collective-permute-start(f32[2,2,16,256]{3,2,1,0:T(8,128)S(1)} %dynamic-slice_bitcast_fusion.1), channel_id=1, source_target_pairs={{0,32},{16,48},{32,0},{48,16},{64,96},{80,112},{96,64},{112,80},{1... | collective-permute-start | bytes 196616 | tf_op jit(solution)/shard_map/ppermute | solution.py:62
  233.3 5.5 %collective-permute-start.5 = (f32[2,16,256]{2,1,0:T(8,128)S(1)}, f32[2,16,256]{2,1,0:T(8,128)S(1)}, u32[]{:S(2)}, u32[]{:S(2)}) collective-permute-start(f32[2,16,256]{2,1,0:T(8,128)S(1)} %dynamic-slice_bitcast_fusion.2), channel_id=1, source_target_pairs={{0,128},{16,144},{32,160},{48,176},{64,192},{80,208},{96,224},{112... | collective-permute-start | bytes 98312 | tf_op jit(solution)/shard_map/ppermute | solution.py:62
  238.8 9.5 %collective-permute-start.6 = (f32[16,256]{1,0:T(8,128)S(1)}, f32[16,256]{1,0:T(8,128)S(1)}, u32[]{:S(2)}, u32[]{:S(2)}) collective-permute-start(f32[16,256]{1,0:T(8,128)S(1)} %dynamic-slice_bitcast_fusion.3), channel_id=1, source_target_pairs={{0,64},{16,80},{32,96},{48,112},{64,0},{80,16},{96,32},{112,48},{1... | collective-permute-start | bytes 49160 | tf_op jit(solution)/shard_map/ppermute | solution.py:62

commit v2 on v1

--- a/solution.py
+++ b/solution.py
@@ -64,6 +64,13 @@
     return parts.reshape(chunk, cols)
 
 
+def ring_order(size):
+    if size == 16:
+        chips = [(0, 0), (1, 0), (2, 0), (3, 0), (3, 1), (2, 1), (1, 1), (0, 1)]
+        return [(x * 2 + y) * 2 + core for x, y in chips for core in (0, 1)]
+    return list(range(size))
+
+
 def per_device(src_codes, src_exps, signs, tgt_codes, tgt_exps):
     sources_bf = dequantize(src_codes, src_exps)
     targets_bf = dequantize(tgt_codes, tgt_exps)
@@ -72,22 +79,35 @@
     cycle_size = lax.axis_size("blk")
     group_size = lax.axis_size("grp")
     block_rows = targets_bf.shape[0]
-    rhs_count = rhs_values.shape[1]
+    half = block_rows // 2
+    order = ring_order(cycle_size)
+    forward = [(order[i], order[(i + 1) % cycle_size]) for i in range(cycle_size)]
+    backward = [(b, a) for a, b in forward]
 
     def contribution(points_bf):
         return kernel_block(points_bf, sources_bf, source_sq, rhs_values)
 
+    def step(points_f, points_b, sums_f, sums_b):
+        both = contribution(jnp.concatenate([points_f, points_b], axis=0))
+        sums_f = lax.ppermute(sums_f + both[:, :half], "blk", forward)
+        sums_b = lax.ppermute(sums_b + both[:, half:], "blk", backward)
+        return sums_f, sums_b
+
     def advance(counter, carried):
-        points_bf, running = carried
-        running = running + contribution(points_bf)
-        points_bf = shifted(points_bf, "blk", 1)
-        running = shifted(running, "blk", 1)
-        return (points_bf, running)
+        points_f, points_b, sums_f, sums_b = carried
+        next_f = lax.ppermute(points_f, "blk", forward)
+        next_b = lax.ppermute(points_b, "blk", backward)
+        sums_f, sums_b = step(points_f, points_b, sums_f, sums_b)
+        return (next_f, next_b, sums_f, sums_b)
 
-    start_sums = jnp.zeros((rhs_count, block_rows), jnp.float32)
-    points_bf, running = lax.fori_loop(0, cycle_size - 1, advance, (targets_bf, start_sums))
-    running = running + contribution(points_bf)
-    gathered_sums = shifted(running, "blk", 1)
+    points_f = lax.ppermute(targets_bf[:half], "blk", forward)
+    points_b = lax.ppermute(targets_bf[half:], "blk", backward)
+    own = contribution(targets_bf)
+    rhs_count = rhs_values.shape[1]
+    zeros = jnp.zeros((rhs_count, half), jnp.float32)
+    carried = lax.fori_loop(0, cycle_size - 2, advance, (points_f, points_b, zeros, zeros))
+    sums_f, sums_b = step(*carried)
+    gathered_sums = own + jnp.concatenate([sums_f, sums_b], axis=1)
     owned_sums = halving_scatter(gathered_sums, "grp")
     source_total = src_codes.shape[0] * group_size * cycle_size
     return owned_sums.T * (4.0 / math.sqrt(source_total))

time: 250 us -> 188 us (0.75)
  the two profiles are of different devices: /device:TPU:16 before, /device:TPU:1 now
where the time goes in v2:
time: 188 us; the launch traced here: 186 us
  waiting for transfers between devices  67 us (36%)
  starting transfers between devices  54.7 us (29%)
  matrix products  47.2 us (25%)
  other arithmetic  10 us (5%)
  local copies, waits for them, and re-layouts  6.39 us (3%)
    dot_general x16, matrix products, kernel_block(): lax.dot_general(rhs_values, matern, (((0,), (1,)), ((), ())), preferred_e...  47.2 us
    ppermute x15, waiting for transfers between devices, step(): sums_b = lax.ppermute(sums_b + both[:, half:], 'blk', backward)  36.8 us
    ppermute x15, waiting for transfers between devices, step(): sums_f = lax.ppermute(sums_f + both[:, :half], 'blk', forward)  22 us
    ppermute x15, starting transfers between devices, step(): sums_f = lax.ppermute(sums_f + both[:, :half], 'blk', forward)  18.5 us
    ppermute x4, starting transfers between devices, halving_scatter(): parts = kept + lax.ppermute(sent, axis, route)  15.4 us
    ppermute x14, starting transfers between devices, advance(): next_b = lax.ppermute(points_b, 'blk', backward)  8.1 us
    ppermute x15, starting transfers between devices, step(): sums_b = lax.ppermute(sums_b + both[:, half:], 'blk', backward)  7.53 us
    ppermute x4, waiting for transfers between devices, halving_scatter(): parts = kept + lax.ppermute(sent, axis, route)  7.53 us
  transfers between devices with their start and end apart: 64, of which 35 were waited for; matrix products, arithmetic and copies ran while one was open for 26% of the time, Pallas kernels for 0%

profile of v2, /device:TPU:1, one launch (start us, length us, event | category | flops | bytes accessed | tf_op | source)
XLA Modules:
  0.0 186.0 jit_solution(1808948743416366092)
XLA Ops:
  1.2 1.5 multiply_reduce_fusion.3
  2.7 2.7 %collective-permute-start.4 = (bf16[128,1024]{1,0:T(8,128)(2,1)S(1)}, bf16[128,1024]{1,0:T(8,128)(2,1)S(1)}, u32[]{:S(2)}, u32[]{:S(2)}) collective-permute-start(bf16[128,1024]{1,0:T(8,128)(2,1)S(1)} %get-tuple-element.136), channel_id=1, source_target_pairs={{0,1},{1,4},{4,5},{5,8},{8,9},{9,12},{12,13},{13,14},{14,15},{15,1... | collective-permute-start | bytes 786440 | tf_op jit(solution)/shard_map/ppermute | solution.py:103
  8.5 2.1 %multiply_reduce_fusion.1 = (f32[1024]{0:T(1024)S(1)}, bf16[1024,1024]{1,0:T(8,128)(2,1)}) fusion(f32[128,8,8,128]{3,2,1,0:T(8,128)S(1)} %bitcast.54, s32[1024,1024]{1,0:T(8,128)S(1)} %copy-done), kind=kLoop, calls=%fused_computation.24 | loop fusion | flops 6290432 | bytes 10489856 | tf_op jit(solution)/shard_map/reduce_sum | solution.py:31
  11.5 135.5 %while.18 = (s32[]{:T(128)}, bf16[128,1024]{1,0:T(8,128)(2,1)S(1)}, bf16[128,1024]{1,0:T(8,128)(2,1)S(1)}, f32[256,128]{0,1:T(8,128)S(1)}, f32[256,128]{0,1:T(8,...) while((s32[]{:T(128)}, bf16[128,1024]{1,0:T(8,128)(2,1)S(1)}, ...), condition=%wide.region_4.5_spmd, body=%wide.region_2.4_spmd.sunk | while | flops 674823936 | bytes 9967869 | solution.py:108
  13.0 2.9 %convolution_bitcast_fusion.2 = f32[256,256]{0,1:T(8,128)S(1)} fusion(bf16[1024,256]{1,0:T(8,128)(2,1)S(1)} %get-tuple-element.217, bf16[256,1024]{1,0:T(8,128)(2,1)S(1)} %constant_dynamic-update-slice_fusion.7, bf16[1024,1024]{1,0:T(8,128)(2,1)} %get-tuple-element.216, f32[1024]{0:T(1024)S(1)} %get-tuple-element.215, f32[256]{0:T(256)S(1)} %multiply_reduce_fusion.5), kind=kOutput, calls=%fused_computation.4.clone.1 | convolution fusion | flops 673972224 | bytes 3412992 | tf_op jit(solution)/shard_map/while/body/eval_jaxpr/dot_general | solution.py:42
  19.1 2.7 %collective-permute-done.3 = f32[256,128]{0,1:T(8,128)S(1)} collective-permute-done((f32[256,128]{0,1:T(8,128)S(1)}, f32[256,128]{0,1:T(8,128)S(1)}, u32[]{:S(2)}, u32[]{:S(2)}) %collective-permute-start.3) | collective-permute-done | bytes 131104 | tf_op jit(solution)/shard_map/while/body/eval_jaxpr/ppermute | solution.py:93
  22.7 2.9 %convolution_bitcast_fusion.2 = f32[256,256]{0,1:T(8,128)S(1)} fusion(bf16[1024,256]{1,0:T(8,128)(2,1)S(1)} %get-tuple-element.217, bf16[256,1024]{1,0:T(8,128)(2,1)S(1)} %constant_dynamic-update-slice_fusion.7, bf16[1024,1024]{1,0:T(8,128)(2,1)} %get-tuple-element.216, f32[1024]{0:T(1024)S(1)} %get-tuple-element.215, f32[256]{0:T(256)S(1)} %multiply_reduce_fusion.5), kind=kOutput, calls=%fused_computation.4.clone.1 | convolution fusion | flops 673972224 | bytes 3412992 | tf_op jit(solution)/shard_map/while/body/eval_jaxpr/dot_general | solution.py:42
  27.5 1.5 collective-permute-done.2
  28.9 2.4 %collective-permute-done.3 = f32[256,128]{0,1:T(8,128)S(1)} collective-permute-done((f32[256,128]{0,1:T(8,128)S(1)}, f32[256,128]{0,1:T(8,128)S(1)}, u32[]{:S(2)}, u32[]{:S(2)}) %collective-permute-start.3) | collective-permute-done | bytes 131104 | tf_op jit(solution)/shard_map/while/body/eval_jaxpr/ppermute | solution.py:93
  32.3 2.9 %convolution_bitcast_fusion.2 = f32[256,256]{0,1:T(8,128)S(1)} fusion(bf16[1024,256]{1,0:T(8,128)(2,1)S(1)} %get-tuple-element.217, bf16[256,1024]{1,0:T(8,128)(2,1)S(1)} %constant_dynamic-update-slice_fusion.7, bf16[1024,1024]{1,0:T(8,128)(2,1)} %get-tuple-element.216, f32[1024]{0:T(1024)S(1)} %get-tuple-element.215, f32[256]{0:T(256)S(1)} %multiply_reduce_fusion.5), kind=kOutput, calls=%fused_computation.4.clone.1 | convolution fusion | flops 673972224 | bytes 3412992 | tf_op jit(solution)/shard_map/while/body/eval_jaxpr/dot_general | solution.py:42
  38.5 2.4 %collective-permute-done.3 = f32[256,128]{0,1:T(8,128)S(1)} collective-permute-done((f32[256,128]{0,1:T(8,128)S(1)}, f32[256,128]{0,1:T(8,128)S(1)}, u32[]{:S(2)}, u32[]{:S(2)}) %collective-permute-start.3) | collective-permute-done | bytes 131104 | tf_op jit(solution)/shard_map/while/body/eval_jaxpr/ppermute | solution.py:93
  41.9 2.9 %convolution_bitcast_fusion.2 = f32[256,256]{0,1:T(8,128)S(1)} fusion(bf16[1024,256]{1,0:T(8,128)(2,1)S(1)} %get-tuple-element.217, bf16[256,1024]{1,0:T(8,128)(2,1)S(1)} %constant_dynamic-update-slice_fusion.7, bf16[1024,1024]{1,0:T(8,128)(2,1)} %get-tuple-element.216, f32[1024]{0:T(1024)S(1)} %get-tuple-element.215, f32[256]{0:T(256)S(1)} %multiply_reduce_fusion.5), kind=kOutput, calls=%fused_computation.4.clone.1 | convolution fusion | flops 673972224 | bytes 3412992 | tf_op jit(solution)/shard_map/while/body/eval_jaxpr/dot_general | solution.py:42
  46.7 1.5 collective-permute-done.2
  48.2 2.4 %collective-permute-done.3 = f32[256,128]{0,1:T(8,128)S(1)} collective-permute-done((f32[256,128]{0,1:T(8,128)S(1)}, f32[256,128]{0,1:T(8,128)S(1)}, u32[]{:S(2)}, u32[]{:S(2)}) %collective-permute-start.3) | collective-permute-done | bytes 131104 | tf_op jit(solution)/shard_map/while/body/eval_jaxpr/ppermute | solution.py:93
  51.6 2.9 %convolution_bitcast_fusion.2 = f32[256,256]{0,1:T(8,128)S(1)} fusion(bf16[1024,256]{1,0:T(8,128)(2,1)S(1)} %get-tuple-element.217, bf16[256,1024]{1,0:T(8,128)(2,1)S(1)} %constant_dynamic-update-slice_fusion.7, bf16[1024,1024]{1,0:T(8,128)(2,1)} %get-tuple-element.216, f32[1024]{0:T(1024)S(1)} %get-tuple-element.215, f32[256]{0:T(256)S(1)} %multiply_reduce_fusion.5), kind=kOutput, calls=%fused_computation.4.clone.1 | convolution fusion | flops 673972224 | bytes 3412992 | tf_op jit(solution)/shard_map/while/body/eval_jaxpr/dot_general | solution.py:42
  56.3 1.5 collective-permute-done.2
  57.8 2.4 %collective-permute-done.3 = f32[256,128]{0,1:T(8,128)S(1)} collective-permute-done((f32[256,128]{0,1:T(8,128)S(1)}, f32[256,128]{0,1:T(8,128)S(1)}, u32[]{:S(2)}, u32[]{:S(2)}) %collective-permute-start.3) | collective-permute-done | bytes 131104 | tf_op jit(solution)/shard_map/while/body/eval_jaxpr/ppermute | solution.py:93
  61.2 2.9 %convolution_bitcast_fusion.2 = f32[256,256]{0,1:T(8,128)S(1)} fusion(bf16[1024,256]{1,0:T(8,128)(2,1)S(1)} %get-tuple-element.217, bf16[256,1024]{1,0:T(8,128)(2,1)S(1)} %constant_dynamic-update-slice_fusion.7, bf16[1024,1024]{1,0:T(8,128)(2,1)} %get-tuple-element.216, f32[1024]{0:T(1024)S(1)} %get-tuple-element.215, f32[256]{0:T(256)S(1)} %multiply_reduce_fusion.5), kind=kOutput, calls=%fused_computation.4.clone.1 | convolution fusion | flops 673972224 | bytes 3412992 | tf_op jit(solution)/shard_map/while/body/eval_jaxpr/dot_general | solution.py:42
  67.4 2.4 %collective-permute-done.3 = f32[256,128]{0,1:T(8,128)S(1)} collective-permute-done((f32[256,128]{0,1:T(8,128)S(1)}, f32[256,128]{0,1:T(8,128)S(1)}, u32[]{:S(2)}, u32[]{:S(2)}) %collective-permute-start.3) | collective-permute-done | bytes 131104 | tf_op jit(solution)/shard_map/while/body/eval_jaxpr/ppermute | solution.py:93
  70.8 2.9 %convolution_bitcast_fusion.2 = f32[256,256]{0,1:T(8,128)S(1)} fusion(bf16[1024,256]{1,0:T(8,128)(2,1)S(1)} %get-tuple-element.217, bf16[256,1024]{1,0:T(8,128)(2,1)S(1)} %constant_dynamic-update-slice_fusion.7, bf16[1024,1024]{1,0:T(8,128)(2,1)} %get-tuple-element.216, f32[1024]{0:T(1024)S(1)} %get-tuple-element.215, f32[256]{0:T(256)S(1)} %multiply_reduce_fusion.5), kind=kOutput, calls=%fused_computation.4.clone.1 | convolution fusion | flops 673972224 | bytes 3412992 | tf_op jit(solution)/shard_map/while/body/eval_jaxpr/dot_general | solution.py:42
  77.1 2.4 %collective-permute-done.3 = f32[256,128]{0,1:T(8,128)S(1)} collective-permute-done((f32[256,128]{0,1:T(8,128)S(1)}, f32[256,128]{0,1:T(8,128)S(1)}, u32[]{:S(2)}, u32[]{:S(2)}) %collective-permute-start.3) | collective-permute-done | bytes 131104 | tf_op jit(solution)/shard_map/while/body/eval_jaxpr/ppermute | solution.py:93
  80.5 2.9 %convolution_bitcast_fusion.2 = f32[256,256]{0,1:T(8,128)S(1)} fusion(bf16[1024,256]{1,0:T(8,128)(2,1)S(1)} %get-tuple-element.217, bf16[256,1024]{1,0:T(8,128)(2,1)S(1)} %constant_dynamic-update-slice_fusion.7, bf16[1024,1024]{1,0:T(8,128)(2,1)} %get-tuple-element.216, f32[1024]{0:T(1024)S(1)} %get-tuple-element.215, f32[256]{0:T(256)S(1)} %multiply_reduce_fusion.5), kind=kOutput, calls=%fused_computation.4.clone.1 | convolution fusion | flops 673972224 | bytes 3412992 | tf_op jit(solution)/shard_map/while/body/eval_jaxpr/dot_general | solution.py:42
  86.7 2.4 %collective-permute-done.3 = f32[256,128]{0,1:T(8,128)S(1)} collective-permute-done((f32[256,128]{0,1:T(8,128)S(1)}, f32[256,128]{0,1:T(8,128)S(1)}, u32[]{:S(2)}, u32[]{:S(2)}) %collective-permute-start.3) | collective-permute-done | bytes 131104 | tf_op jit(solution)/shard_map/while/body/eval_jaxpr/ppermute | solution.py:93
  90.1 2.9 %convolution_bitcast_fusion.2 = f32[256,256]{0,1:T(8,128)S(1)} fusion(bf16[1024,256]{1,0:T(8,128)(2,1)S(1)} %get-tuple-element.217, bf16[256,1024]{1,0:T(8,128)(2,1)S(1)} %constant_dynamic-update-slice_fusion.7, bf16[1024,1024]{1,0:T(8,128)(2,1)} %get-tuple-element.216, f32[1024]{0:T(1024)S(1)} %get-tuple-element.215, f32[256]{0:T(256)S(1)} %multiply_reduce_fusion.5), kind=kOutput, calls=%fused_computation.4.clone.1 | convolution fusion | flops 673972224 | bytes 3412992 | tf_op jit(solution)/shard_map/while/body/eval_jaxpr/dot_general | solution.py:42
  96.3 2.4 %collective-permute-done.3 = f32[256,128]{0,1:T(8,128)S(1)} collective-permute-done((f32[256,128]{0,1:T(8,128)S(1)}, f32[256,128]{0,1:T(8,128)S(1)}, u32[]{:S(2)}, u32[]{:S(2)}) %collective-permute-start.3) | collective-permute-done | bytes 131104 | tf_op jit(solution)/shard_map/while/body/eval_jaxpr/ppermute | solution.py:93
  99.7 2.9 %convolution_bitcast_fusion.2 = f32[256,256]{0,1:T(8,128)S(1)} fusion(bf16[1024,256]{1,0:T(8,128)(2,1)S(1)} %get-tuple-element.217, bf16[256,1024]{1,0:T(8,128)(2,1)S(1)} %constant_dynamic-update-slice_fusion.7, bf16[1024,1024]{1,0:T(8,128)(2,1)} %get-tuple-element.216, f32[1024]{0:T(1024)S(1)} %get-tuple-element.215, f32[256]{0:T(256)S(1)} %multiply_reduce_fusion.5), kind=kOutput, calls=%fused_computation.4.clone.1 | convolution fusion | flops 673972224 | bytes 3412992 | tf_op jit(solution)/shard_map/while/body/eval_jaxpr/dot_general | solution.py:42
  104.5 1.5 collective-permute-done.2
  105.9 2.4 %collective-permute-done.3 = f32[256,128]{0,1:T(8,128)S(1)} collective-permute-done((f32[256,128]{0,1:T(8,128)S(1)}, f32[256,128]{0,1:T(8,128)S(1)}, u32[]{:S(2)}, u32[]{:S(2)}) %collective-permute-start.3) | collective-permute-done | bytes 131104 | tf_op jit(solution)/shard_map/while/body/eval_jaxpr/ppermute | solution.py:93
  109.3 2.9 %convolution_bitcast_fusion.2 = f32[256,256]{0,1:T(8,128)S(1)} fusion(bf16[1024,256]{1,0:T(8,128)(2,1)S(1)} %get-tuple-element.217, bf16[256,1024]{1,0:T(8,128)(2,1)S(1)} %constant_dynamic-update-slice_fusion.7, bf16[1024,1024]{1,0:T(8,128)(2,1)} %get-tuple-element.216, f32[1024]{0:T(1024)S(1)} %get-tuple-element.215, f32[256]{0:T(256)S(1)} %multiply_reduce_fusion.5), kind=kOutput, calls=%fused_computation.4.clone.1 | convolution fusion | flops 673972224 | bytes 3412992 | tf_op jit(solution)/shard_map/while/body/eval_jaxpr/dot_general | solution.py:42
  114.1 1.5 collective-permute-done.2
  115.6 2.4 %collective-permute-done.3 = f32[256,128]{0,1:T(8,128)S(1)} collective-permute-done((f32[256,128]{0,1:T(8,128)S(1)}, f32[256,128]{0,1:T(8,128)S(1)}, u32[]{:S(2)}, u32[]{:S(2)}) %collective-permute-start.3) | collective-permute-done | bytes 131104 | tf_op jit(solution)/shard_map/while/body/eval_jaxpr/ppermute | solution.py:93
  119.0 2.9 %convolution_bitcast_fusion.2 = f32[256,256]{0,1:T(8,128)S(1)} fusion(bf16[1024,256]{1,0:T(8,128)(2,1)S(1)} %get-tuple-element.217, bf16[256,1024]{1,0:T(8,128)(2,1)S(1)} %constant_dynamic-update-slice_fusion.7, bf16[1024,1024]{1,0:T(8,128)(2,1)} %get-tuple-element.216, f32[1024]{0:T(1024)S(1)} %get-tuple-element.215, f32[256]{0:T(256)S(1)} %multiply_reduce_fusion.5), kind=kOutput, calls=%fused_computation.4.clone.1 | convolution fusion | flops 673972224 | bytes 3412992 | tf_op jit(solution)/shard_map/while/body/eval_jaxpr/dot_general | solution.py:42
  125.2 2.4 %collective-permute-done.3 = f32[256,128]{0,1:T(8,128)S(1)} collective-permute-done((f32[256,128]{0,1:T(8,128)S(1)}, f32[256,128]{0,1:T(8,128)S(1)}, u32[]{:S(2)}, u32[]{:S(2)}) %collective-permute-start.3) | collective-permute-done | bytes 131104 | tf_op jit(solution)/shard_map/while/body/eval_jaxpr/ppermute | solution.py:93
  128.6 2.9 %convolution_bitcast_fusion.2 = f32[256,256]{0,1:T(8,128)S(1)} fusion(bf16[1024,256]{1,0:T(8,128)(2,1)S(1)} %get-tuple-element.217, bf16[256,1024]{1,0:T(8,128)(2,1)S(1)} %constant_dynamic-update-slice_fusion.7, bf16[1024,1024]{1,0:T(8,128)(2,1)} %get-tuple-element.216, f32[1024]{0:T(1024)S(1)} %get-tuple-element.215, f32[256]{0:T(256)S(1)} %multiply_reduce_fusion.5), kind=kOutput, calls=%fused_computation.4.clone.1 | convolution fusion | flops 673972224 | bytes 3412992 | tf_op jit(solution)/shard_map/while/body/eval_jaxpr/dot_general | solution.py:42
  134.8 2.4 %collective-permute-done.3 = f32[256,128]{0,1:T(8,128)S(1)} collective-permute-done((f32[256,128]{0,1:T(8,128)S(1)}, f32[256,128]{0,1:T(8,128)S(1)}, u32[]{:S(2)}, u32[]{:S(2)}) %collective-permute-start.3) | collective-permute-done | bytes 131104 | tf_op jit(solution)/shard_map/while/body/eval_jaxpr/ppermute | solution.py:93
  138.2 2.9 %convolution_bitcast_fusion.2 = f32[256,256]{0,1:T(8,128)S(1)} fusion(bf16[1024,256]{1,0:T(8,128)(2,1)S(1)} %get-tuple-element.217, bf16[256,1024]{1,0:T(8,128)(2,1)S(1)} %constant_dynamic-update-slice_fusion.7, bf16[1024,1024]{1,0:T(8,128)(2,1)} %get-tuple-element.216, f32[1024]{0:T(1024)S(1)} %get-tuple-element.215, f32[256]{0:T(256)S(1)} %multiply_reduce_fusion.5), kind=kOutput, calls=%fused_computation.4.clone.1 | convolution fusion | flops 673972224 | bytes 3412992 | tf_op jit(solution)/shard_map/while/body/eval_jaxpr/dot_general | solution.py:42
  143.0 1.5 collective-permute-done.2
  144.5 2.4 %collective-permute-done.3 = f32[256,128]{0,1:T(8,128)S(1)} collective-permute-done((f32[256,128]{0,1:T(8,128)S(1)}, f32[256,128]{0,1:T(8,128)S(1)}, u32[]{:S(2)}, u32[]{:S(2)}) %collective-permute-start.3) | collective-permute-done | bytes 131104 | tf_op jit(solution)/shard_map/while/body/eval_jaxpr/ppermute | solution.py:93
  148.7 4.2 %fusion.22 = f32[256,256]{1,0:T(8,128)} fusion(bf16[1024,256]{1,0:T(8,128)(2,1)} %copy-done.4, bf16[256,1024]{1,0:T(8,128)(2,1)} %copy-done.2, bf16[1024,1024]{1,0:T(8,128)(2,1)} %get-tuple-element.229, f32[256]{0:T(256)S(1)} %multiply_reduce_fusion.2, f32[1024]{0:T(1024)S(1)} %get-tuple-element.242), kind=kOutput, calls=%fused_computation.36 | convolution fusion | flops 673972224 | bytes 3412992 | tf_op jit(solution)/shard_map/dot_general | solution.py:42
  153.1 1.6 slice_add_fusion.3
  155.2 1.8 collective-permute-done.6
  157.0 2.3 %collective-permute-done.7 = f32[256,128]{1,0:T(8,128)S(1)} collective-permute-done((f32[256,128]{1,0:T(8,128)S(1)}, f32[256,128]{1,0:T(8,128)S(1)}, u32[]{:S(2)}, u32[]{:S(2)}) %collective-permute-start.7) | collective-permute-done | bytes 131104 | tf_op jit(solution)/shard_map/ppermute | solution.py:93
  160.0 2.3 %maximum_add_fusion = f32[256,256]{1,0:T(8,128)S(1)} fusion(f32[256,128]{1,0:T(8,128)} %copy-done.7, f32[256,128]{1,0:T(8,128)S(1)} %collective-permute-done.6, bf16[1024,256]{1,0:T(8,128)(2,1)S(1)} %copy-done.5, bf16[256,1024]{1,0:T(8,128)(2,1)S(1)} %get-tuple-element.130, bf16[1024,1024]{1,0:T(8,128)(2,1)S(1)} %copy-done.1, ...), kind=kOutput, calls=%fused_computation.56 | convolution fusion | flops 674103296 | bytes 3675136 | tf_op jit(solution)/shard_map/dot_general | solution.py:42
  163.7 3.4 %collective-permute-done.8 = f32[2,2,2,16,256]{4,3,2,1,0:T(8,128)S(1)} collective-permute-done((f32[2,2,2,16,256]{4,3,2,1,0:T(8,128)S(1)}, f32[2,2,2,16,256]{4,3,2,1,0:T(8,128)S(1)}, u32[]{:S(2)}, u32[]{:S(2)}) %collective-permute-start.8) | collective-permute-done | bytes 131104 | tf_op jit(solution)/shard_map/ppermute | solution.py:62
  167.2 2.8 %collective-permute-start.9 = (f32[2,2,16,256]{3,2,1,0:T(8,128)S(1)}, f32[2,2,16,256]{3,2,1,0:T(8,128)S(1)}, u32[]{:S(2)}, u32[]{:S(2)}) collective-permute-start(f32[2,2,16,256]{3,2,1,0:T(8,128)S(1)} %dynamic-slice_bitcast_fusion.1), channel_id=1, source_target_pairs={{0,32},{16,48},{32,0},{48,16},{64,96},{80,112},{96,64},{112,80},{1... | collective-permute-start | bytes 196616 | tf_op jit(solution)/shard_map/ppermute | solution.py:62
  169.9 1.7 collective-permute-done.9
  171.6 3.7 %collective-permute-start.10 = (f32[2,16,256]{2,1,0:T(8,128)S(1)}, f32[2,16,256]{2,1,0:T(8,128)S(1)}, u32[]{:S(2)}, u32[]{:S(2)}) collective-permute-start(f32[2,16,256]{2,1,0:T(8,128)S(1)} %dynamic-slice_bitcast_fusion.2), channel_id=1, source_target_pairs={{0,128},{16,144},{32,160},{48,176},{64,192},{80,208},{96,224},{112... | collective-permute-start | bytes 98312 | tf_op jit(solution)/shard_map/ppermute | solution.py:62
  176.6 7.6 %collective-permute-start.11 = (f32[16,256]{1,0:T(8,128)S(1)}, f32[16,256]{1,0:T(8,128)S(1)}, u32[]{:S(2)}, u32[]{:S(2)}) collective-permute-start(f32[16,256]{1,0:T(8,128)S(1)} %dynamic-slice_bitcast_fusion.3), channel_id=1, source_target_pairs={{0,64},{16,80},{32,96},{48,112},{64,0},{80,16},{96,32},{112,48},{1... | collective-permute-start | bytes 49160 | tf_op jit(solution)/shard_map/ppermute | solution.py:62
  (223 shorter events, 63.6 us)
Async XLA Ops:
  2.7 8.1 %collective-permute-start.4 = (bf16[128,1024]{1,0:T(8,128)(2,1)S(1)}, bf16[128,1024]{1,0:T(8,128)(2,1)S(1)}, u32[]{:S(2)}, u32[]{:S(2)}) collective-permute-start(bf16[128,1024]{1,0:T(8,128)(2,1)S(1)} %get-tuple-element.136), channel_id=1, source_target_pairs={{0,1},{1,4},{4,5},{5,8},{8,9},{9,12},{12,13},{13,14},{14,15},{15,1... | collective-permute-start | bytes 786440 | tf_op jit(solution)/shard_map/ppermute | solution.py:103
  5.4 6.0 %collective-permute-start.5 = (bf16[128,1024]{1,0:T(8,128)(2,1)S(1)}, bf16[128,1024]{1,0:T(8,128)(2,1)S(1)}, u32[]{:S(2)}, u32[]{:S(2)}) collective-permute-start(bf16[128,1024]{1,0:T(8,128)(2,1)S(1)} %get-tuple-element.135), channel_id=1, source_target_pairs={{1,0},{4,1},{5,4},{8,5},{9,8},{12,9},{13,12},{14,13},{15,14},{10,1... | collective-permute-start | bytes 786440 | tf_op jit(solution)/shard_map/ppermute | solution.py:104
  11.5 10.2 %collective-permute-start = (bf16[128,1024]{1,0:T(8,128)(2,1)S(1)}, bf16[128,1024]{1,0:T(8,128)(2,1)S(1)}, u32[]{:S(2)}, u32[]{:S(2)}) collective-permute-start(bf16[128,1024]{1,0:T(8,128)(2,1)S(1)} %copy.23), channel_id=1, source_target_pairs={{0,1},{1,4},{4,5},{5,8},{8,9},{9,12},{12,13},{13,14},{14,15},{15,1... | collective-permute-start | bytes 786440 | tf_op jit(solution)/shard_map/while/body/eval_jaxpr/ppermute | solution.py:98
  12.0 9.7 %collective-permute-start.1 = (bf16[128,1024]{1,0:T(8,128)(2,1)S(1)}, bf16[128,1024]{1,0:T(8,128)(2,1)S(1)}, u32[]{:S(2)}, u32[]{:S(2)}) collective-permute-start(bf16[128,1024]{1,0:T(8,128)(2,1)S(1)} %copy.24), channel_id=1, source_target_pairs={{1,0},{4,1},{5,4},{8,5},{9,8},{12,9},{13,12},{14,13},{15,14},{10,1... | collective-permute-start | bytes 786440 | tf_op jit(solution)/shard_map/while/body/eval_jaxpr/ppermute | solution.py:99
  17.1 4.6 %collective-permute-start.3 = (f32[256,128]{0,1:T(8,128)S(1)}, f32[256,128]{0,1:T(8,128)S(1)}, u32[]{:S(2)}, u32[]{:S(2)}) collective-permute-start(f32[256,128]{0,1:T(8,128)S(1)} %get-tuple-element.191), channel_id=1, source_target_pairs={{1,0},{4,1},{5,4},{8,5},{9,8},{12,9},{13,12},{14,13},{15,14},{10,1... | collective-permute-start | bytes 393224 | tf_op jit(solution)/shard_map/while/body/eval_jaxpr/ppermute | solution.py:93
  21.8 9.6 %collective-permute-start = (bf16[128,1024]{1,0:T(8,128)(2,1)S(1)}, bf16[128,1024]{1,0:T(8,128)(2,1)S(1)}, u32[]{:S(2)}, u32[]{:S(2)}) collective-permute-start(bf16[128,1024]{1,0:T(8,128)(2,1)S(1)} %copy.23), channel_id=1, source_target_pairs={{0,1},{1,4},{4,5},{5,8},{8,9},{9,12},{12,13},{13,14},{14,15},{15,1... | collective-permute-start | bytes 786440 | tf_op jit(solution)/shard_map/while/body/eval_jaxpr/ppermute | solution.py:98
  21.9 9.5 %collective-permute-start.1 = (bf16[128,1024]{1,0:T(8,128)(2,1)S(1)}, bf16[128,1024]{1,0:T(8,128)(2,1)S(1)}, u32[]{:S(2)}, u32[]{:S(2)}) collective-permute-start(bf16[128,1024]{1,0:T(8,128)(2,1)S(1)} %copy.24), channel_id=1, source_target_pairs={{1,0},{4,1},{5,4},{8,5},{9,8},{12,9},{13,12},{14,13},{15,14},{10,1... | collective-permute-start | bytes 786440 | tf_op jit(solution)/shard_map/while/body/eval_jaxpr/ppermute | solution.py:99
  27.0 4.4 %collective-permute-start.3 = (f32[256,128]{0,1:T(8,128)S(1)}, f32[256,128]{0,1:T(8,128)S(1)}, u32[]{:S(2)}, u32[]{:S(2)}) collective-permute-start(f32[256,128]{0,1:T(8,128)S(1)} %get-tuple-element.191), channel_id=1, source_target_pairs={{1,0},{4,1},{5,4},{8,5},{9,8},{12,9},{13,12},{14,13},{15,14},{10,1... | collective-permute-start | bytes 393224 | tf_op jit(solution)/shard_map/while/body/eval_jaxpr/ppermute | solution.py:93
  31.4 9.6 %collective-permute-start = (bf16[128,1024]{1,0:T(8,128)(2,1)S(1)}, bf16[128,1024]{1,0:T(8,128)(2,1)S(1)}, u32[]{:S(2)}, u32[]{:S(2)}) collective-permute-start(bf16[128,1024]{1,0:T(8,128)(2,1)S(1)} %copy.23), channel_id=1, source_target_pairs={{0,1},{1,4},{4,5},{5,8},{8,9},{9,12},{12,13},{13,14},{14,15},{15,1... | collective-permute-start | bytes 786440 | tf_op jit(solution)/shard_map/while/body/eval_jaxpr/ppermute | solution.py:98
  31.5 9.5 %collective-permute-start.1 = (bf16[128,1024]{1,0:T(8,128)(2,1)S(1)}, bf16[128,1024]{1,0:T(8,128)(2,1)S(1)}, u32[]{:S(2)}, u32[]{:S(2)}) collective-permute-start(bf16[128,1024]{1,0:T(8,128)(2,1)S(1)} %copy.24), channel_id=1, source_target_pairs={{1,0},{4,1},{5,4},{8,5},{9,8},{12,9},{13,12},{14,13},{15,14},{10,1... | collective-permute-start | bytes 786440 | tf_op jit(solution)/shard_map/while/body/eval_jaxpr/ppermute | solution.py:99
  36.6 4.4 %collective-permute-start.3 = (f32[256,128]{0,1:T(8,128)S(1)}, f32[256,128]{0,1:T(8,128)S(1)}, u32[]{:S(2)}, u32[]{:S(2)}) collective-permute-start(f32[256,128]{0,1:T(8,128)S(1)} %get-tuple-element.191), channel_id=1, source_target_pairs={{1,0},{4,1},{5,4},{8,5},{9,8},{12,9},{13,12},{14,13},{15,14},{10,1... | collective-permute-start | bytes 393224 | tf_op jit(solution)/shard_map/while/body/eval_jaxpr/ppermute | solution.py:93
  41.0 9.6 %collective-permute-start = (bf16[128,1024]{1,0:T(8,128)(2,1)S(1)}, bf16[128,1024]{1,0:T(8,128)(2,1)S(1)}, u32[]{:S(2)}, u32[]{:S(2)}) collective-permute-start(bf16[128,1024]{1,0:T(8,128)(2,1)S(1)} %copy.23), channel_id=1, source_target_pairs={{0,1},{1,4},{4,5},{5,8},{8,9},{9,12},{12,13},{13,14},{14,15},{15,1... | collective-permute-start | bytes 786440 | tf_op jit(solution)/shard_map/while/body/eval_jaxpr/ppermute | solution.py:98
  41.1 9.5 %collective-permute-start.1 = (bf16[128,1024]{1,0:T(8,128)(2,1)S(1)}, bf16[128,1024]{1,0:T(8,128)(2,1)S(1)}, u32[]{:S(2)}, u32[]{:S(2)}) collective-permute-start(bf16[128,1024]{1,0:T(8,128)(2,1)S(1)} %copy.24), channel_id=1, source_target_pairs={{1,0},{4,1},{5,4},{8,5},{9,8},{12,9},{13,12},{14,13},{15,14},{10,1... | collective-permute-start | bytes 786440 | tf_op jit(solution)/shard_map/while/body/eval_jaxpr/ppermute | solution.py:99
  46.2 4.4 %collective-permute-start.3 = (f32[256,128]{0,1:T(8,128)S(1)}, f32[256,128]{0,1:T(8,128)S(1)}, u32[]{:S(2)}, u32[]{:S(2)}) collective-permute-start(f32[256,128]{0,1:T(8,128)S(1)} %get-tuple-element.191), channel_id=1, source_target_pairs={{1,0},{4,1},{5,4},{8,5},{9,8},{12,9},{13,12},{14,13},{15,14},{10,1... | collective-permute-start | bytes 393224 | tf_op jit(solution)/shard_map/while/body/eval_jaxpr/ppermute | solution.py:93
  50.6 9.6 %collective-permute-start = (bf16[128,1024]{1,0:T(8,128)(2,1)S(1)}, bf16[128,1024]{1,0:T(8,128)(2,1)S(1)}, u32[]{:S(2)}, u32[]{:S(2)}) collective-permute-start(bf16[128,1024]{1,0:T(8,128)(2,1)S(1)} %copy.23), channel_id=1, source_target_pairs={{0,1},{1,4},{4,5},{5,8},{8,9},{9,12},{12,13},{13,14},{14,15},{15,1... | collective-permute-start | bytes 786440 | tf_op jit(solution)/shard_map/while/body/eval_jaxpr/ppermute | solution.py:98
  50.8 9.5 %collective-permute-start.1 = (bf16[128,1024]{1,0:T(8,128)(2,1)S(1)}, bf16[128,1024]{1,0:T(8,128)(2,1)S(1)}, u32[]{:S(2)}, u32[]{:S(2)}) collective-permute-start(bf16[128,1024]{1,0:T(8,128)(2,1)S(1)} %copy.24), channel_id=1, source_target_pairs={{1,0},{4,1},{5,4},{8,5},{9,8},{12,9},{13,12},{14,13},{15,14},{10,1... | collective-permute-start | bytes 786440 | tf_op jit(solution)/shard_map/while/body/eval_jaxpr/ppermute | solution.py:99
  55.9 4.4 %collective-permute-start.3 = (f32[256,128]{0,1:T(8,128)S(1)}, f32[256,128]{0,1:T(8,128)S(1)}, u32[]{:S(2)}, u32[]{:S(2)}) collective-permute-start(f32[256,128]{0,1:T(8,128)S(1)} %get-tuple-element.191), channel_id=1, source_target_pairs={{1,0},{4,1},{5,4},{8,5},{9,8},{12,9},{13,12},{14,13},{15,14},{10,1... | collective-permute-start | bytes 393224 | tf_op jit(solution)/shard_map/while/body/eval_jaxpr/ppermute | solution.py:93
  60.3 9.6 %collective-permute-start = (bf16[128,1024]{1,0:T(8,128)(2,1)S(1)}, bf16[128,1024]{1,0:T(8,128)(2,1)S(1)}, u32[]{:S(2)}, u32[]{:S(2)}) collective-permute-start(bf16[128,1024]{1,0:T(8,128)(2,1)S(1)} %copy.23), channel_id=1, source_target_pairs={{0,1},{1,4},{4,5},{5,8},{8,9},{9,12},{12,13},{13,14},{14,15},{15,1... | collective-permute-start | bytes 786440 | tf_op jit(solution)/shard_map/while/body/eval_jaxpr/ppermute | solution.py:98
  60.4 9.5 %collective-permute-start.1 = (bf16[128,1024]{1,0:T(8,128)(2,1)S(1)}, bf16[128,1024]{1,0:T(8,128)(2,1)S(1)}, u32[]{:S(2)}, u32[]{:S(2)}) collective-permute-start(bf16[128,1024]{1,0:T(8,128)(2,1)S(1)} %copy.24), channel_id=1, source_target_pairs={{1,0},{4,1},{5,4},{8,5},{9,8},{12,9},{13,12},{14,13},{15,14},{10,1... | collective-permute-start | bytes 786440 | tf_op jit(solution)/shard_map/while/body/eval_jaxpr/ppermute | solution.py:99
  65.5 4.4 %collective-permute-start.3 = (f32[256,128]{0,1:T(8,128)S(1)}, f32[256,128]{0,1:T(8,128)S(1)}, u32[]{:S(2)}, u32[]{:S(2)}) collective-permute-start(f32[256,128]{0,1:T(8,128)S(1)} %get-tuple-element.191), channel_id=1, source_target_pairs={{1,0},{4,1},{5,4},{8,5},{9,8},{12,9},{13,12},{14,13},{15,14},{10,1... | collective-permute-start | bytes 393224 | tf_op jit(solution)/shard_map/while/body/eval_jaxpr/ppermute | solution.py:93
  69.9 9.6 %collective-permute-start = (bf16[128,1024]{1,0:T(8,128)(2,1)S(1)}, bf16[128,1024]{1,0:T(8,128)(2,1)S(1)}, u32[]{:S(2)}, u32[]{:S(2)}) collective-permute-start(bf16[128,1024]{1,0:T(8,128)(2,1)S(1)} %copy.23), channel_id=1, source_target_pairs={{0,1},{1,4},{4,5},{5,8},{8,9},{9,12},{12,13},{13,14},{14,15},{15,1... | collective-permute-start | bytes 786440 | tf_op jit(solution)/shard_map/while/body/eval_jaxpr/ppermute | solution.py:98
  70.0 9.5 %collective-permute-start.1 = (bf16[128,1024]{1,0:T(8,128)(2,1)S(1)}, bf16[128,1024]{1,0:T(8,128)(2,1)S(1)}, u32[]{:S(2)}, u32[]{:S(2)}) collective-permute-start(bf16[128,1024]{1,0:T(8,128)(2,1)S(1)} %copy.24), channel_id=1, source_target_pairs={{1,0},{4,1},{5,4},{8,5},{9,8},{12,9},{13,12},{14,13},{15,14},{10,1... | collective-permute-start | bytes 786440 | tf_op jit(solution)/shard_map/while/body/eval_jaxpr/ppermute | solution.py:99
  75.1 4.4 %collective-permute-start.3 = (f32[256,128]{0,1:T(8,128)S(1)}, f32[256,128]{0,1:T(8,128)S(1)}, u32[]{:S(2)}, u32[]{:S(2)}) collective-permute-start(f32[256,128]{0,1:T(8,128)S(1)} %get-tuple-element.191), channel_id=1, source_target_pairs={{1,0},{4,1},{5,4},{8,5},{9,8},{12,9},{13,12},{14,13},{15,14},{10,1... | collective-permute-start | bytes 393224 | tf_op jit(solution)/shard_map/while/body/eval_jaxpr/ppermute | solution.py:93
  79.5 9.6 %collective-permute-start = (bf16[128,1024]{1,0:T(8,128)(2,1)S(1)}, bf16[128,1024]{1,0:T(8,128)(2,1)S(1)}, u32[]{:S(2)}, u32[]{:S(2)}) collective-permute-start(bf16[128,1024]{1,0:T(8,128)(2,1)S(1)} %copy.23), channel_id=1, source_target_pairs={{0,1},{1,4},{4,5},{5,8},{8,9},{9,12},{12,13},{13,14},{14,15},{15,1... | collective-permute-start | bytes 786440 | tf_op jit(solution)/shard_map/while/body/eval_jaxpr/ppermute | solution.py:98
  79.7 9.5 %collective-permute-start.1 = (bf16[128,1024]{1,0:T(8,128)(2,1)S(1)}, bf16[128,1024]{1,0:T(8,128)(2,1)S(1)}, u32[]{:S(2)}, u32[]{:S(2)}) collective-permute-start(bf16[128,1024]{1,0:T(8,128)(2,1)S(1)} %copy.24), channel_id=1, source_target_pairs={{1,0},{4,1},{5,4},{8,5},{9,8},{12,9},{13,12},{14,13},{15,14},{10,1... | collective-permute-start | bytes 786440 | tf_op jit(solution)/shard_map/while/body/eval_jaxpr/ppermute | solution.py:99
  84.7 4.4 %collective-permute-start.3 = (f32[256,128]{0,1:T(8,128)S(1)}, f32[256,128]{0,1:T(8,128)S(1)}, u32[]{:S(2)}, u32[]{:S(2)}) collective-permute-start(f32[256,128]{0,1:T(8,128)S(1)} %get-tuple-element.191), channel_id=1, source_target_pairs={{1,0},{4,1},{5,4},{8,5},{9,8},{12,9},{13,12},{14,13},{15,14},{10,1... | collective-permute-start | bytes 393224 | tf_op jit(solution)/shard_map/while/body/eval_jaxpr/ppermute | solution.py:93
  89.2 9.6 %collective-permute-start = (bf16[128,1024]{1,0:T(8,128)(2,1)S(1)}, bf16[128,1024]{1,0:T(8,128)(2,1)S(1)}, u32[]{:S(2)}, u32[]{:S(2)}) collective-permute-start(bf16[128,1024]{1,0:T(8,128)(2,1)S(1)} %copy.23), channel_id=1, source_target_pairs={{0,1},{1,4},{4,5},{5,8},{8,9},{9,12},{12,13},{13,14},{14,15},{15,1... | collective-permute-start | bytes 786440 | tf_op jit(solution)/shard_map/while/body/eval_jaxpr/ppermute | solution.py:98
  89.3 9.5 %collective-permute-start.1 = (bf16[128,1024]{1,0:T(8,128)(2,1)S(1)}, bf16[128,1024]{1,0:T(8,128)(2,1)S(1)}, u32[]{:S(2)}, u32[]{:S(2)}) collective-permute-start(bf16[128,1024]{1,0:T(8,128)(2,1)S(1)} %copy.24), channel_id=1, source_target_pairs={{1,0},{4,1},{5,4},{8,5},{9,8},{12,9},{13,12},{14,13},{15,14},{10,1... | collective-permute-start | bytes 786440 | tf_op jit(solution)/shard_map/while/body/eval_jaxpr/ppermute | solution.py:99
  94.4 4.4 %collective-permute-start.3 = (f32[256,128]{0,1:T(8,128)S(1)}, f32[256,128]{0,1:T(8,128)S(1)}, u32[]{:S(2)}, u32[]{:S(2)}) collective-permute-start(f32[256,128]{0,1:T(8,128)S(1)} %get-tuple-element.191), channel_id=1, source_target_pairs={{1,0},{4,1},{5,4},{8,5},{9,8},{12,9},{13,12},{14,13},{15,14},{10,1... | collective-permute-start | bytes 393224 | tf_op jit(solution)/shard_map/while/body/eval_jaxpr/ppermute | solution.py:93
  98.8 9.6 %collective-permute-start = (bf16[128,1024]{1,0:T(8,128)(2,1)S(1)}, bf16[128,1024]{1,0:T(8,128)(2,1)S(1)}, u32[]{:S(2)}, u32[]{:S(2)}) collective-permute-start(bf16[128,1024]{1,0:T(8,128)(2,1)S(1)} %copy.23), channel_id=1, source_target_pairs={{0,1},{1,4},{4,5},{5,8},{8,9},{9,12},{12,13},{13,14},{14,15},{15,1... | collective-permute-start | bytes 786440 | tf_op jit(solution)/shard_map/while/body/eval_jaxpr/ppermute | solution.py:98
  98.9 9.5 %collective-permute-start.1 = (bf16[128,1024]{1,0:T(8,128)(2,1)S(1)}, bf16[128,1024]{1,0:T(8,128)(2,1)S(1)}, u32[]{:S(2)}, u32[]{:S(2)}) collective-permute-start(bf16[128,1024]{1,0:T(8,128)(2,1)S(1)} %copy.24), channel_id=1, source_target_pairs={{1,0},{4,1},{5,4},{8,5},{9,8},{12,9},{13,12},{14,13},{15,14},{10,1... | collective-permute-start | bytes 786440 | tf_op jit(solution)/shard_map/while/body/eval_jaxpr/ppermute | solution.py:99
  104.0 4.4 %collective-permute-start.3 = (f32[256,128]{0,1:T(8,128)S(1)}, f32[256,128]{0,1:T(8,128)S(1)}, u32[]{:S(2)}, u32[]{:S(2)}) collective-permute-start(f32[256,128]{0,1:T(8,128)S(1)} %get-tuple-element.191), channel_id=1, source_target_pairs={{1,0},{4,1},{5,4},{8,5},{9,8},{12,9},{13,12},{14,13},{15,14},{10,1... | collective-permute-start | bytes 393224 | tf_op jit(solution)/shard_map/while/body/eval_jaxpr/ppermute | solution.py:93
  108.4 9.6 %collective-permute-start = (bf16[128,1024]{1,0:T(8,128)(2,1)S(1)}, bf16[128,1024]{1,0:T(8,128)(2,1)S(1)}, u32[]{:S(2)}, u32[]{:S(2)}) collective-permute-start(bf16[128,1024]{1,0:T(8,128)(2,1)S(1)} %copy.23), channel_id=1, source_target_pairs={{0,1},{1,4},{4,5},{5,8},{8,9},{9,12},{12,13},{13,14},{14,15},{15,1... | collective-permute-start | bytes 786440 | tf_op jit(solution)/shard_map/while/body/eval_jaxpr/ppermute | solution.py:98
  108.5 9.5 %collective-permute-start.1 = (bf16[128,1024]{1,0:T(8,128)(2,1)S(1)}, bf16[128,1024]{1,0:T(8,128)(2,1)S(1)}, u32[]{:S(2)}, u32[]{:S(2)}) collective-permute-start(bf16[128,1024]{1,0:T(8,128)(2,1)S(1)} %copy.24), channel_id=1, source_target_pairs={{1,0},{4,1},{5,4},{8,5},{9,8},{12,9},{13,12},{14,13},{15,14},{10,1... | collective-permute-start | bytes 786440 | tf_op jit(solution)/shard_map/while/body/eval_jaxpr/ppermute | solution.py:99
  113.6 4.4 %collective-permute-start.3 = (f32[256,128]{0,1:T(8,128)S(1)}, f32[256,128]{0,1:T(8,128)S(1)}, u32[]{:S(2)}, u32[]{:S(2)}) collective-permute-start(f32[256,128]{0,1:T(8,128)S(1)} %get-tuple-element.191), channel_id=1, source_target_pairs={{1,0},{4,1},{5,4},{8,5},{9,8},{12,9},{13,12},{14,13},{15,14},{10,1... | collective-permute-start | bytes 393224 | tf_op jit(solution)/shard_map/while/body/eval_jaxpr/ppermute | solution.py:93
  118.1 9.6 %collective-permute-start = (bf16[128,1024]{1,0:T(8,128)(2,1)S(1)}, bf16[128,1024]{1,0:T(8,128)(2,1)S(1)}, u32[]{:S(2)}, u32[]{:S(2)}) collective-permute-start(bf16[128,1024]{1,0:T(8,128)(2,1)S(1)} %copy.23), channel_id=1, source_target_pairs={{0,1},{1,4},{4,5},{5,8},{8,9},{9,12},{12,13},{13,14},{14,15},{15,1... | collective-permute-start | bytes 786440 | tf_op jit(solution)/shard_map/while/body/eval_jaxpr/ppermute | solution.py:98
  118.2 9.5 %collective-permute-start.1 = (bf16[128,1024]{1,0:T(8,128)(2,1)S(1)}, bf16[128,1024]{1,0:T(8,128)(2,1)S(1)}, u32[]{:S(2)}, u32[]{:S(2)}) collective-permute-start(bf16[128,1024]{1,0:T(8,128)(2,1)S(1)} %copy.24), channel_id=1, source_target_pairs={{1,0},{4,1},{5,4},{8,5},{9,8},{12,9},{13,12},{14,13},{15,14},{10,1... | collective-permute-start | bytes 786440 | tf_op jit(solution)/shard_map/while/body/eval_jaxpr/ppermute | solution.py:99
  123.3 4.4 %collective-permute-start.3 = (f32[256,128]{0,1:T(8,128)S(1)}, f32[256,128]{0,1:T(8,128)S(1)}, u32[]{:S(2)}, u32[]{:S(2)}) collective-permute-start(f32[256,128]{0,1:T(8,128)S(1)} %get-tuple-element.191), channel_id=1, source_target_pairs={{1,0},{4,1},{5,4},{8,5},{9,8},{12,9},{13,12},{14,13},{15,14},{10,1... | collective-permute-start | bytes 393224 | tf_op jit(solution)/shard_map/while/body/eval_jaxpr/ppermute | solution.py:93
  127.7 9.6 %collective-permute-start = (bf16[128,1024]{1,0:T(8,128)(2,1)S(1)}, bf16[128,1024]{1,0:T(8,128)(2,1)S(1)}, u32[]{:S(2)}, u32[]{:S(2)}) collective-permute-start(bf16[128,1024]{1,0:T(8,128)(2,1)S(1)} %copy.23), channel_id=1, source_target_pairs={{0,1},{1,4},{4,5},{5,8},{8,9},{9,12},{12,13},{13,14},{14,15},{15,1... | collective-permute-start | bytes 786440 | tf_op jit(solution)/shard_map/while/body/eval_jaxpr/ppermute | solution.py:98
  127.8 9.5 %collective-permute-start.1 = (bf16[128,1024]{1,0:T(8,128)(2,1)S(1)}, bf16[128,1024]{1,0:T(8,128)(2,1)S(1)}, u32[]{:S(2)}, u32[]{:S(2)}) collective-permute-start(bf16[128,1024]{1,0:T(8,128)(2,1)S(1)} %copy.24), channel_id=1, source_target_pairs={{1,0},{4,1},{5,4},{8,5},{9,8},{12,9},{13,12},{14,13},{15,14},{10,1... | collective-permute-start | bytes 786440 | tf_op jit(solution)/shard_map/while/body/eval_jaxpr/ppermute | solution.py:99
  132.9 4.4 %collective-permute-start.3 = (f32[256,128]{0,1:T(8,128)S(1)}, f32[256,128]{0,1:T(8,128)S(1)}, u32[]{:S(2)}, u32[]{:S(2)}) collective-permute-start(f32[256,128]{0,1:T(8,128)S(1)} %get-tuple-element.191), channel_id=1, source_target_pairs={{1,0},{4,1},{5,4},{8,5},{9,8},{12,9},{13,12},{14,13},{15,14},{10,1... | collective-permute-start | bytes 393224 | tf_op jit(solution)/shard_map/while/body/eval_jaxpr/ppermute | solution.py:93
  137.3 9.6 %collective-permute-start = (bf16[128,1024]{1,0:T(8,128)(2,1)S(1)}, bf16[128,1024]{1,0:T(8,128)(2,1)S(1)}, u32[]{:S(2)}, u32[]{:S(2)}) collective-permute-start(bf16[128,1024]{1,0:T(8,128)(2,1)S(1)} %copy.23), channel_id=1, source_target_pairs={{0,1},{1,4},{4,5},{5,8},{8,9},{9,12},{12,13},{13,14},{14,15},{15,1... | collective-permute-start | bytes 786440 | tf_op jit(solution)/shard_map/while/body/eval_jaxpr/ppermute | solution.py:98
  137.4 9.5 %collective-permute-start.1 = (bf16[128,1024]{1,0:T(8,128)(2,1)S(1)}, bf16[128,1024]{1,0:T(8,128)(2,1)S(1)}, u32[]{:S(2)}, u32[]{:S(2)}) collective-permute-start(bf16[128,1024]{1,0:T(8,128)(2,1)S(1)} %copy.24), channel_id=1, source_target_pairs={{1,0},{4,1},{5,4},{8,5},{9,8},{12,9},{13,12},{14,13},{15,14},{10,1... | collective-permute-start | bytes 786440 | tf_op jit(solution)/shard_map/while/body/eval_jaxpr/ppermute | solution.py:99
  154.7 4.6 %collective-permute-start.7 = (f32[256,128]{1,0:T(8,128)S(1)}, f32[256,128]{1,0:T(8,128)S(1)}, u32[]{:S(2)}, u32[]{:S(2)}) collective-permute-start(f32[256,128]{1,0:T(8,128)S(1)} %get-tuple-element.138), channel_id=1, source_target_pairs={{1,0},{4,1},{5,4},{8,5},{9,8},{12,9},{13,12},{14,13},{15,14},{10,1... | collective-permute-start | bytes 393224 | tf_op jit(solution)/shard_map/ppermute | solution.py:93
  162.4 4.7 %collective-permute-start.8 = (f32[2,2,2,16,256]{4,3,2,1,0:T(8,128)S(1)}, f32[2,2,2,16,256]{4,3,2,1,0:T(8,128)S(1)}, u32[]{:S(2)}, u32[]{:S(2)}) collective-permute-start(f32[2,2,2,16,256]{4,3,2,1,0:T(8,128)S(1)} %dynamic-slice_bitcast_fusion), channel_id=1, source_target_pairs={{0,16},{16,0},{32,48},{48,32},{64,80},{80,64},{96,112},{112,96},{1... | collective-permute-start | bytes 393224 | tf_op jit(solution)/shard_map/ppermute | solution.py:62
  167.2 4.4 %collective-permute-start.9 = (f32[2,2,16,256]{3,2,1,0:T(8,128)S(1)}, f32[2,2,16,256]{3,2,1,0:T(8,128)S(1)}, u32[]{:S(2)}, u32[]{:S(2)}) collective-permute-start(f32[2,2,16,256]{3,2,1,0:T(8,128)S(1)} %dynamic-slice_bitcast_fusion.1), channel_id=1, source_target_pairs={{0,32},{16,48},{32,0},{48,16},{64,96},{80,112},{96,64},{112,80},{1... | collective-permute-start | bytes 196616 | tf_op jit(solution)/shard_map/ppermute | solution.py:62
  171.6 5.0 %collective-permute-start.10 = (f32[2,16,256]{2,1,0:T(8,128)S(1)}, f32[2,16,256]{2,1,0:T(8,128)S(1)}, u32[]{:S(2)}, u32[]{:S(2)}) collective-permute-start(f32[2,16,256]{2,1,0:T(8,128)S(1)} %dynamic-slice_bitcast_fusion.2), channel_id=1, source_target_pairs={{0,128},{16,144},{32,160},{48,176},{64,192},{80,208},{96,224},{112... | collective-permute-start | bytes 98312 | tf_op jit(solution)/shard_map/ppermute | solution.py:62
  176.6 8.8 %collective-permute-start.11 = (f32[16,256]{1,0:T(8,128)S(1)}, f32[16,256]{1,0:T(8,128)S(1)}, u32[]{:S(2)}, u32[]{:S(2)}) collective-permute-start(f32[16,256]{1,0:T(8,128)S(1)} %dynamic-slice_bitcast_fusion.3), channel_id=1, source_target_pairs={{0,64},{16,80},{32,96},{48,112},{64,0},{80,16},{96,32},{112,48},{1... | collective-permute-start | bytes 49160 | tf_op jit(solution)/shard_map/ppermute | solution.py:62
  (24 other events, 86.6 us)

commit v3 on v2

--- a/solution.py
+++ b/solution.py
@@ -87,26 +87,31 @@
     def contribution(points_bf):
         return kernel_block(points_bf, sources_bf, source_sq, rhs_values)
 
-    def step(points_f, points_b, sums_f, sums_b):
+    def halves(points_f, points_b):
         both = contribution(jnp.concatenate([points_f, points_b], axis=0))
-        sums_f = lax.ppermute(sums_f + both[:, :half], "blk", forward)
-        sums_b = lax.ppermute(sums_b + both[:, half:], "blk", backward)
-        return sums_f, sums_b
+        return both[:, :half], both[:, half:]
+
+    def send(points_f, points_b):
+        return lax.ppermute(points_f, "blk", forward), lax.ppermute(points_b, "blk", backward)
 
     def advance(counter, carried):
-        points_f, points_b, sums_f, sums_b = carried
-        next_f = lax.ppermute(points_f, "blk", forward)
-        next_b = lax.ppermute(points_b, "blk", backward)
-        sums_f, sums_b = step(points_f, points_b, sums_f, sums_b)
-        return (next_f, next_b, sums_f, sums_b)
+        points_f, points_b, sums_f, sums_b, part_f, part_b = carried
+        sums_f, sums_b = send(sums_f + part_f, sums_b + part_b)
+        next_f, next_b = send(points_f, points_b)
+        part_f, part_b = halves(points_f, points_b)
+        return (next_f, next_b, sums_f, sums_b, part_f, part_b)
 
-    points_f = lax.ppermute(targets_bf[:half], "blk", forward)
-    points_b = lax.ppermute(targets_bf[half:], "blk", backward)
+    points_f, points_b = send(targets_bf[:half], targets_bf[half:])
     own = contribution(targets_bf)
-    rhs_count = rhs_values.shape[1]
-    zeros = jnp.zeros((rhs_count, half), jnp.float32)
-    carried = lax.fori_loop(0, cycle_size - 2, advance, (points_f, points_b, zeros, zeros))
-    sums_f, sums_b = step(*carried)
+    next_f, next_b = send(points_f, points_b)
+    part_f, part_b = halves(points_f, points_b)
+    zeros = jnp.zeros_like(part_f)
+    carried = (next_f, next_b, zeros, zeros, part_f, part_b)
+    carried = lax.fori_loop(0, cycle_size - 3, advance, carried)
+    points_f, points_b, sums_f, sums_b, part_f, part_b = carried
+    sums_f, sums_b = send(sums_f + part_f, sums_b + part_b)
+    part_f, part_b = halves(points_f, points_b)
+    sums_f, sums_b = send(sums_f + part_f, sums_b + part_b)
     gathered_sums = own + jnp.concatenate([sums_f, sums_b], axis=1)
     owned_sums = halving_scatter(gathered_sums, "grp")
     source_total = src_codes.shape[0] * group_size * cycle_size

time: 188 us -> 157 us (0.84)
  the two profiles are of different devices: /device:TPU:1 before, /device:TPU:6 now
where the time goes in v3:
time: 157 us; the launch traced here: 156 us
  starting transfers between devices  72.2 us (46%)
  matrix products  46.1 us (29%)
  waiting for transfers between devices  19.7 us (13%)
  local copies, waits for them, and re-layouts  8.89 us (6%)
  other arithmetic  8.01 us (5%)
    dot_general x16, matrix products, kernel_block(): lax.dot_general(rhs_values, matern, (((0,), (1,)), ((), ())), preferred_e...  46.1 us
    ppermute x30, starting transfers between devices, send(): lax.ppermute(points_f, 'blk', forward)  31.4 us
    ppermute x30, starting transfers between devices, send(): lax.ppermute(points_b, 'blk', backward)  25.7 us
    ppermute x4, starting transfers between devices, halving_scatter(): parts = kept + lax.ppermute(sent, axis, route)  15.2 us
    ppermute x4, waiting for transfers between devices, halving_scatter(): parts = kept + lax.ppermute(sent, axis, route)  10.9 us
    ppermute x30, waiting for transfers between devices, send(): lax.ppermute(points_f, 'blk', forward)  6.64 us
    reduce_sum x17, other arithmetic, squares(): return jnp.sum(widened * widened, axis=1)  5.11 us
    unnamed x18, local copies, waits for them, and re-layouts  3.2 us
  transfers between devices with their start and end apart: 64, of which 20 were waited for; matrix products, arithmetic and copies ran while one was open for 34% of the time, Pallas kernels for 0%

profile of v3, /device:TPU:6, one launch (start us, length us, event | category | flops | bytes accessed | tf_op | source)
XLA Modules:
  0.0 156.2 jit_solution(487383885896833975)
XLA Ops:
  1.2 1.5 multiply_reduce_fusion.4
  2.8 1.7 %collective-permute-start.6 = (bf16[128,1024]{1,0:T(8,128)(2,1)S(1)}, bf16[128,1024]{1,0:T(8,128)(2,1)}, u32[]{:S(2)}, u32[]{:S(2)}) collective-permute-start(bf16[128,1024]{1,0:T(8,128)(2,1)S(1)} %get-tuple-element.177), channel_id=1, source_target_pairs={{1,0},{4,1},{5,4},{8,5},{9,8},{12,9},{13,12},{14,13},{15,14},{10,1... | collective-permute-start | bytes 786440 | tf_op jit(solution)/shard_map/ppermute | solution.py:95
  11.7 1.6 %collective-permute-start.7 = (bf16[128,1024]{1,0:T(8,128)(2,1)}, bf16[128,1024]{1,0:T(8,128)(2,1)S(1)}, u32[]{:S(2)}, u32[]{:S(2)}) collective-permute-start(bf16[128,1024]{1,0:T(8,128)(2,1)} %collective-permute-done.6), channel_id=1, source_target_pairs={{1,0},{4,1},{5,4},{8,5},{9,8},{12,9},{13,12},{14,13},{15,14},{10,1... | collective-permute-start | bytes 786440 | tf_op jit(solution)/shard_map/ppermute | solution.py:95
  13.2 3.2 %fusion.27 = f32[256,256]{1,0:T(8,128)} fusion(bf16[1024,256]{1,0:T(8,128)(2,1)} %add_convert_fusion, bf16[256,1024]{1,0:T(8,128)(2,1)S(1)} %constant_dynamic-update-slice_fusion.2, bf16[1024,1024]{1,0:T(8,128)(2,1)S(1)} %get-tuple-element.256, f32[256]{0:T(256)S(1)} %multiply_reduce_fusion.3, f32[1024]{0:T(1024)S(1)} %get-tuple-element.255), kind=kOutput, calls=%fused_computation.42 | convolution fusion | flops 673972224 | bytes 3412992 | tf_op jit(solution)/shard_map/dot_general | solution.py:42
  17.6 96.6 %while.22 = (s32[]{:T(128)}, bf16[128,1024]{1,0:T(8,128)(2,1)S(1)}, bf16[128,1024]{1,0:T(8,128)(2,1)S(1)}, f32[256,128]{0,1:T(8,128)S(1)}, f32[256,128]{0,1:T(8,...) while((s32[]{:T(128)}, bf16[128,1024]{1,0:T(8,128)(2,1)S(1)}, ...), condition=%wide.region_5.6_spmd, body=%wide.region_3.5_spmd.sunk | while | flops 674823936 | bytes 12589353 | solution.py:110
  17.7 1.6 %collective-permute-start = (bf16[128,1024]{1,0:T(8,128)(2,1)S(1)}, bf16[128,1024]{1,0:T(8,128)(2,1)S(1)}, u32[]{:S(2)}, u32[]{:S(2)}) collective-permute-start(bf16[128,1024]{1,0:T(8,128)(2,1)S(1)} %copy.30), channel_id=1, source_target_pairs={{0,1},{1,4},{4,5},{5,8},{8,9},{9,12},{12,13},{13,14},{14,15},{15,1... | collective-permute-start | bytes 786440 | tf_op jit(solution)/shard_map/while/body/eval_jaxpr/ppermute | solution.py:95
  20.1 1.5 collective-permute-start.3
  21.8 2.9 %convolution_bitcast_fusion.2 = f32[256,256]{0,1:T(8,128)S(1)} fusion(bf16[1024,256]{1,0:T(8,128)(2,1)S(1)} %copy-done.7, bf16[256,1024]{1,0:T(8,128)(2,1)S(1)} %constant_dynamic-update-slice_fusion.9, bf16[1024,1024]{1,0:T(8,128)(2,1)} %get-tuple-element.278, f32[1024]{0:T(1024)S(1)} %get-tuple-element.277, f32[256]{0:T(256)S(1)} %multiply_reduce_fusion.6), kind=kOutput, calls=%fused_computation.4.clone.1 | convolution fusion | flops 673972224 | bytes 3412992 | tf_op jit(solution)/shard_map/while/body/eval_jaxpr/dot_general | solution.py:42
  25.0 1.8 %collective-permute-start = (bf16[128,1024]{1,0:T(8,128)(2,1)S(1)}, bf16[128,1024]{1,0:T(8,128)(2,1)S(1)}, u32[]{:S(2)}, u32[]{:S(2)}) collective-permute-start(bf16[128,1024]{1,0:T(8,128)(2,1)S(1)} %copy.30), channel_id=1, source_target_pairs={{0,1},{1,4},{4,5},{5,8},{8,9},{9,12},{12,13},{13,14},{14,15},{15,1... | collective-permute-start | bytes 786440 | tf_op jit(solution)/shard_map/while/body/eval_jaxpr/ppermute | solution.py:95
  29.2 2.9 %convolution_bitcast_fusion.2 = f32[256,256]{0,1:T(8,128)S(1)} fusion(bf16[1024,256]{1,0:T(8,128)(2,1)S(1)} %copy-done.7, bf16[256,1024]{1,0:T(8,128)(2,1)S(1)} %constant_dynamic-update-slice_fusion.9, bf16[1024,1024]{1,0:T(8,128)(2,1)} %get-tuple-element.278, f32[1024]{0:T(1024)S(1)} %get-tuple-element.277, f32[256]{0:T(256)S(1)} %multiply_reduce_fusion.6), kind=kOutput, calls=%fused_computation.4.clone.1 | convolution fusion | flops 673972224 | bytes 3412992 | tf_op jit(solution)/shard_map/while/body/eval_jaxpr/dot_general | solution.py:42
  32.5 1.9 %collective-permute-start = (bf16[128,1024]{1,0:T(8,128)(2,1)S(1)}, bf16[128,1024]{1,0:T(8,128)(2,1)S(1)}, u32[]{:S(2)}, u32[]{:S(2)}) collective-permute-start(bf16[128,1024]{1,0:T(8,128)(2,1)S(1)} %copy.30), channel_id=1, source_target_pairs={{0,1},{1,4},{4,5},{5,8},{8,9},{9,12},{12,13},{13,14},{14,15},{15,1... | collective-permute-start | bytes 786440 | tf_op jit(solution)/shard_map/while/body/eval_jaxpr/ppermute | solution.py:95
  35.0 1.4 collective-permute-start.3
  36.7 2.9 %convolution_bitcast_fusion.2 = f32[256,256]{0,1:T(8,128)S(1)} fusion(bf16[1024,256]{1,0:T(8,128)(2,1)S(1)} %copy-done.7, bf16[256,1024]{1,0:T(8,128)(2,1)S(1)} %constant_dynamic-update-slice_fusion.9, bf16[1024,1024]{1,0:T(8,128)(2,1)} %get-tuple-element.278, f32[1024]{0:T(1024)S(1)} %get-tuple-element.277, f32[256]{0:T(256)S(1)} %multiply_reduce_fusion.6), kind=kOutput, calls=%fused_computation.4.clone.1 | convolution fusion | flops 673972224 | bytes 3412992 | tf_op jit(solution)/shard_map/while/body/eval_jaxpr/dot_general | solution.py:42
  39.9 1.9 %collective-permute-start = (bf16[128,1024]{1,0:T(8,128)(2,1)S(1)}, bf16[128,1024]{1,0:T(8,128)(2,1)S(1)}, u32[]{:S(2)}, u32[]{:S(2)}) collective-permute-start(bf16[128,1024]{1,0:T(8,128)(2,1)S(1)} %copy.30), channel_id=1, source_target_pairs={{0,1},{1,4},{4,5},{5,8},{8,9},{9,12},{12,13},{13,14},{14,15},{15,1... | collective-permute-start | bytes 786440 | tf_op jit(solution)/shard_map/while/body/eval_jaxpr/ppermute | solution.py:95
  44.1 2.9 %convolution_bitcast_fusion.2 = f32[256,256]{0,1:T(8,128)S(1)} fusion(bf16[1024,256]{1,0:T(8,128)(2,1)S(1)} %copy-done.7, bf16[256,1024]{1,0:T(8,128)(2,1)S(1)} %constant_dynamic-update-slice_fusion.9, bf16[1024,1024]{1,0:T(8,128)(2,1)} %get-tuple-element.278, f32[1024]{0:T(1024)S(1)} %get-tuple-element.277, f32[256]{0:T(256)S(1)} %multiply_reduce_fusion.6), kind=kOutput, calls=%fused_computation.4.clone.1 | convolution fusion | flops 673972224 | bytes 3412992 | tf_op jit(solution)/shard_map/while/body/eval_jaxpr/dot_general | solution.py:42
  47.3 1.9 %collective-permute-start = (bf16[128,1024]{1,0:T(8,128)(2,1)S(1)}, bf16[128,1024]{1,0:T(8,128)(2,1)S(1)}, u32[]{:S(2)}, u32[]{:S(2)}) collective-permute-start(bf16[128,1024]{1,0:T(8,128)(2,1)S(1)} %copy.30), channel_id=1, source_target_pairs={{0,1},{1,4},{4,5},{5,8},{8,9},{9,12},{12,13},{13,14},{14,15},{15,1... | collective-permute-start | bytes 786440 | tf_op jit(solution)/shard_map/while/body/eval_jaxpr/ppermute | solution.py:95
  49.9 1.4 collective-permute-start.3
  51.5 2.9 %convolution_bitcast_fusion.2 = f32[256,256]{0,1:T(8,128)S(1)} fusion(bf16[1024,256]{1,0:T(8,128)(2,1)S(1)} %copy-done.7, bf16[256,1024]{1,0:T(8,128)(2,1)S(1)} %constant_dynamic-update-slice_fusion.9, bf16[1024,1024]{1,0:T(8,128)(2,1)} %get-tuple-element.278, f32[1024]{0:T(1024)S(1)} %get-tuple-element.277, f32[256]{0:T(256)S(1)} %multiply_reduce_fusion.6), kind=kOutput, calls=%fused_computation.4.clone.1 | convolution fusion | flops 673972224 | bytes 3412992 | tf_op jit(solution)/shard_map/while/body/eval_jaxpr/dot_general | solution.py:42
  54.8 1.9 %collective-permute-start = (bf16[128,1024]{1,0:T(8,128)(2,1)S(1)}, bf16[128,1024]{1,0:T(8,128)(2,1)S(1)}, u32[]{:S(2)}, u32[]{:S(2)}) collective-permute-start(bf16[128,1024]{1,0:T(8,128)(2,1)S(1)} %copy.30), channel_id=1, source_target_pairs={{0,1},{1,4},{4,5},{5,8},{8,9},{9,12},{12,13},{13,14},{14,15},{15,1... | collective-permute-start | bytes 786440 | tf_op jit(solution)/shard_map/while/body/eval_jaxpr/ppermute | solution.py:95
  59.0 2.9 %convolution_bitcast_fusion.2 = f32[256,256]{0,1:T(8,128)S(1)} fusion(bf16[1024,256]{1,0:T(8,128)(2,1)S(1)} %copy-done.7, bf16[256,1024]{1,0:T(8,128)(2,1)S(1)} %constant_dynamic-update-slice_fusion.9, bf16[1024,1024]{1,0:T(8,128)(2,1)} %get-tuple-element.278, f32[1024]{0:T(1024)S(1)} %get-tuple-element.277, f32[256]{0:T(256)S(1)} %multiply_reduce_fusion.6), kind=kOutput, calls=%fused_computation.4.clone.1 | convolution fusion | flops 673972224 | bytes 3412992 | tf_op jit(solution)/shard_map/while/body/eval_jaxpr/dot_general | solution.py:42
  62.2 1.9 %collective-permute-start = (bf16[128,1024]{1,0:T(8,128)(2,1)S(1)}, bf16[128,1024]{1,0:T(8,128)(2,1)S(1)}, u32[]{:S(2)}, u32[]{:S(2)}) collective-permute-start(bf16[128,1024]{1,0:T(8,128)(2,1)S(1)} %copy.30), channel_id=1, source_target_pairs={{0,1},{1,4},{4,5},{5,8},{8,9},{9,12},{12,13},{13,14},{14,15},{15,1... | collective-permute-start | bytes 786440 | tf_op jit(solution)/shard_map/while/body/eval_jaxpr/ppermute | solution.py:95
  66.4 2.9 %convolution_bitcast_fusion.2 = f32[256,256]{0,1:T(8,128)S(1)} fusion(bf16[1024,256]{1,0:T(8,128)(2,1)S(1)} %copy-done.7, bf16[256,1024]{1,0:T(8,128)(2,1)S(1)} %constant_dynamic-update-slice_fusion.9, bf16[1024,1024]{1,0:T(8,128)(2,1)} %get-tuple-element.278, f32[1024]{0:T(1024)S(1)} %get-tuple-element.277, f32[256]{0:T(256)S(1)} %multiply_reduce_fusion.6), kind=kOutput, calls=%fused_computation.4.clone.1 | convolution fusion | flops 673972224 | bytes 3412992 | tf_op jit(solution)/shard_map/while/body/eval_jaxpr/dot_general | solution.py:42
  69.6 1.9 %collective-permute-start = (bf16[128,1024]{1,0:T(8,128)(2,1)S(1)}, bf16[128,1024]{1,0:T(8,128)(2,1)S(1)}, u32[]{:S(2)}, u32[]{:S(2)}) collective-permute-start(bf16[128,1024]{1,0:T(8,128)(2,1)S(1)} %copy.30), channel_id=1, source_target_pairs={{0,1},{1,4},{4,5},{5,8},{8,9},{9,12},{12,13},{13,14},{14,15},{15,1... | collective-permute-start | bytes 786440 | tf_op jit(solution)/shard_map/while/body/eval_jaxpr/ppermute | solution.py:95
  73.8 2.9 %convolution_bitcast_fusion.2 = f32[256,256]{0,1:T(8,128)S(1)} fusion(bf16[1024,256]{1,0:T(8,128)(2,1)S(1)} %copy-done.7, bf16[256,1024]{1,0:T(8,128)(2,1)S(1)} %constant_dynamic-update-slice_fusion.9, bf16[1024,1024]{1,0:T(8,128)(2,1)} %get-tuple-element.278, f32[1024]{0:T(1024)S(1)} %get-tuple-element.277, f32[256]{0:T(256)S(1)} %multiply_reduce_fusion.6), kind=kOutput, calls=%fused_computation.4.clone.1 | convolution fusion | flops 673972224 | bytes 3412992 | tf_op jit(solution)/shard_map/while/body/eval_jaxpr/dot_general | solution.py:42
  77.1 1.9 %collective-permute-start = (bf16[128,1024]{1,0:T(8,128)(2,1)S(1)}, bf16[128,1024]{1,0:T(8,128)(2,1)S(1)}, u32[]{:S(2)}, u32[]{:S(2)}) collective-permute-start(bf16[128,1024]{1,0:T(8,128)(2,1)S(1)} %copy.30), channel_id=1, source_target_pairs={{0,1},{1,4},{4,5},{5,8},{8,9},{9,12},{12,13},{13,14},{14,15},{15,1... | collective-permute-start | bytes 786440 | tf_op jit(solution)/shard_map/while/body/eval_jaxpr/ppermute | solution.py:95
  81.3 2.9 %convolution_bitcast_fusion.2 = f32[256,256]{0,1:T(8,128)S(1)} fusion(bf16[1024,256]{1,0:T(8,128)(2,1)S(1)} %copy-done.7, bf16[256,1024]{1,0:T(8,128)(2,1)S(1)} %constant_dynamic-update-slice_fusion.9, bf16[1024,1024]{1,0:T(8,128)(2,1)} %get-tuple-element.278, f32[1024]{0:T(1024)S(1)} %get-tuple-element.277, f32[256]{0:T(256)S(1)} %multiply_reduce_fusion.6), kind=kOutput, calls=%fused_computation.4.clone.1 | convolution fusion | flops 673972224 | bytes 3412992 | tf_op jit(solution)/shard_map/while/body/eval_jaxpr/dot_general | solution.py:42
  84.5 1.9 %collective-permute-start = (bf16[128,1024]{1,0:T(8,128)(2,1)S(1)}, bf16[128,1024]{1,0:T(8,128)(2,1)S(1)}, u32[]{:S(2)}, u32[]{:S(2)}) collective-permute-start(bf16[128,1024]{1,0:T(8,128)(2,1)S(1)} %copy.30), channel_id=1, source_target_pairs={{0,1},{1,4},{4,5},{5,8},{8,9},{9,12},{12,13},{13,14},{14,15},{15,1... | collective-permute-start | bytes 786440 | tf_op jit(solution)/shard_map/while/body/eval_jaxpr/ppermute | solution.py:95
  88.7 2.9 %convolution_bitcast_fusion.2 = f32[256,256]{0,1:T(8,128)S(1)} fusion(bf16[1024,256]{1,0:T(8,128)(2,1)S(1)} %copy-done.7, bf16[256,1024]{1,0:T(8,128)(2,1)S(1)} %constant_dynamic-update-slice_fusion.9, bf16[1024,1024]{1,0:T(8,128)(2,1)} %get-tuple-element.278, f32[1024]{0:T(1024)S(1)} %get-tuple-element.277, f32[256]{0:T(256)S(1)} %multiply_reduce_fusion.6), kind=kOutput, calls=%fused_computation.4.clone.1 | convolution fusion | flops 673972224 | bytes 3412992 | tf_op jit(solution)/shard_map/while/body/eval_jaxpr/dot_general | solution.py:42
  91.9 1.9 %collective-permute-start = (bf16[128,1024]{1,0:T(8,128)(2,1)S(1)}, bf16[128,1024]{1,0:T(8,128)(2,1)S(1)}, u32[]{:S(2)}, u32[]{:S(2)}) collective-permute-start(bf16[128,1024]{1,0:T(8,128)(2,1)S(1)} %copy.30), channel_id=1, source_target_pairs={{0,1},{1,4},{4,5},{5,8},{8,9},{9,12},{12,13},{13,14},{14,15},{15,1... | collective-permute-start | bytes 786440 | tf_op jit(solution)/shard_map/while/body/eval_jaxpr/ppermute | solution.py:95
  96.2 2.9 %convolution_bitcast_fusion.2 = f32[256,256]{0,1:T(8,128)S(1)} fusion(bf16[1024,256]{1,0:T(8,128)(2,1)S(1)} %copy-done.7, bf16[256,1024]{1,0:T(8,128)(2,1)S(1)} %constant_dynamic-update-slice_fusion.9, bf16[1024,1024]{1,0:T(8,128)(2,1)} %get-tuple-element.278, f32[1024]{0:T(1024)S(1)} %get-tuple-element.277, f32[256]{0:T(256)S(1)} %multiply_reduce_fusion.6), kind=kOutput, calls=%fused_computation.4.clone.1 | convolution fusion | flops 673972224 | bytes 3412992 | tf_op jit(solution)/shard_map/while/body/eval_jaxpr/dot_general | solution.py:42
  99.4 1.9 %collective-permute-start = (bf16[128,1024]{1,0:T(8,128)(2,1)S(1)}, bf16[128,1024]{1,0:T(8,128)(2,1)S(1)}, u32[]{:S(2)}, u32[]{:S(2)}) collective-permute-start(bf16[128,1024]{1,0:T(8,128)(2,1)S(1)} %copy.30), channel_id=1, source_target_pairs={{0,1},{1,4},{4,5},{5,8},{8,9},{9,12},{12,13},{13,14},{14,15},{15,1... | collective-permute-start | bytes 786440 | tf_op jit(solution)/shard_map/while/body/eval_jaxpr/ppermute | solution.py:95
  103.6 2.9 %convolution_bitcast_fusion.2 = f32[256,256]{0,1:T(8,128)S(1)} fusion(bf16[1024,256]{1,0:T(8,128)(2,1)S(1)} %copy-done.7, bf16[256,1024]{1,0:T(8,128)(2,1)S(1)} %constant_dynamic-update-slice_fusion.9, bf16[1024,1024]{1,0:T(8,128)(2,1)} %get-tuple-element.278, f32[1024]{0:T(1024)S(1)} %get-tuple-element.277, f32[256]{0:T(256)S(1)} %multiply_reduce_fusion.6), kind=kOutput, calls=%fused_computation.4.clone.1 | convolution fusion | flops 673972224 | bytes 3412992 | tf_op jit(solution)/shard_map/while/body/eval_jaxpr/dot_general | solution.py:42
  106.8 1.9 %collective-permute-start = (bf16[128,1024]{1,0:T(8,128)(2,1)S(1)}, bf16[128,1024]{1,0:T(8,128)(2,1)S(1)}, u32[]{:S(2)}, u32[]{:S(2)}) collective-permute-start(bf16[128,1024]{1,0:T(8,128)(2,1)S(1)} %copy.30), channel_id=1, source_target_pairs={{0,1},{1,4},{4,5},{5,8},{8,9},{9,12},{12,13},{13,14},{14,15},{15,1... | collective-permute-start | bytes 786440 | tf_op jit(solution)/shard_map/while/body/eval_jaxpr/ppermute | solution.py:95
  111.0 2.9 %convolution_bitcast_fusion.2 = f32[256,256]{0,1:T(8,128)S(1)} fusion(bf16[1024,256]{1,0:T(8,128)(2,1)S(1)} %copy-done.7, bf16[256,1024]{1,0:T(8,128)(2,1)S(1)} %constant_dynamic-update-slice_fusion.9, bf16[1024,1024]{1,0:T(8,128)(2,1)} %get-tuple-element.278, f32[1024]{0:T(1024)S(1)} %get-tuple-element.277, f32[256]{0:T(256)S(1)} %multiply_reduce_fusion.6), kind=kOutput, calls=%fused_computation.4.clone.1 | convolution fusion | flops 673972224 | bytes 3412992 | tf_op jit(solution)/shard_map/while/body/eval_jaxpr/dot_general | solution.py:42
  114.4 2.1 %collective-permute-start.10 = (f32[256,128]{1,0:T(8,128)S(1)}, f32[256,128]{1,0:T(8,128)S(1)}, u32[]{:S(2)}, u32[]{:S(2)}) collective-permute-start(f32[256,128]{1,0:T(8,128)S(1)} %add.204), channel_id=1, source_target_pairs={{1,0},{4,1},{5,4},{8,5},{9,8},{12,9},{13,12},{14,13},{15,14},{10,1... | collective-permute-start | bytes 393224 | tf_op jit(solution)/shard_map/ppermute | solution.py:95
  117.9 2.7 %fusion.25 = f32[256,256]{1,0:T(8,128)S(1)} fusion(bf16[1024,256]{1,0:T(8,128)(2,1)} %get-tuple-element.292, bf16[256,1024]{1,0:T(8,128)(2,1)} %copy-done.5, bf16[1024,1024]{1,0:T(8,128)(2,1)S(1)} %copy-done.2, f32[256]{0:T(256)S(1)} %multiply_reduce_fusion.2, f32[1024]{0:T(1024)S(1)} %get-tuple-element.309), kind=kOutput, calls=%fused_computation.38 | convolution fusion | flops 673972224 | bytes 3412992 | tf_op jit(solution)/shard_map/dot_general | solution.py:42
  120.6 1.7 %collective-permute-done.8 = f32[256,128]{1,0:T(8,128)S(1)} collective-permute-done((f32[256,128]{1,0:T(8,128)S(1)}, f32[256,128]{1,0:T(8,128)S(1)}, u32[]{:S(2)}, u32[]{:S(2)}) %collective-permute-start.8) | collective-permute-done | bytes 131104 | tf_op jit(solution)/shard_map/ppermute | solution.py:95
  122.9 2.0 %collective-permute-done.11 = f32[256,128]{1,0:T(8,128)S(1)} collective-permute-done((f32[256,128]{1,0:T(8,128)S(1)}, f32[256,128]{1,0:T(8,128)S(1)}, u32[]{:S(2)}, u32[]{:S(2)}) %collective-permute-start.11) | collective-permute-done | bytes 131104 | tf_op jit(solution)/shard_map/ppermute | solution.py:95
  124.9 1.9 %collective-permute-done.9 = f32[256,128]{1,0:T(8,128)S(1)} collective-permute-done((f32[256,128]{1,0:T(8,128)S(1)}, f32[256,128]{1,0:T(8,128)S(1)}, u32[]{:S(2)}, u32[]{:S(2)}) %collective-permute-start.9) | collective-permute-done | bytes 131104 | tf_op jit(solution)/shard_map/ppermute | solution.py:95
  126.9 2.5 %maximum_add_fusion = f32[256,256]{1,0:T(8,128)S(1)} fusion(f32[256,128]{1,0:T(8,128)S(1)} %collective-permute-done.11, f32[256,128]{1,0:T(8,128)S(1)} %collective-permute-done.9, bf16[1024,256]{1,0:T(8,128)(2,1)} %get-tuple-element.292, bf16[256,1024]{1,0:T(8,128)(2,1)S(1)} %copy-done.4, bf16[1024,1024]{1,0:T(8,128)(2,1)S(1)} %copy-done.2, ...), kind=kOutput, calls=%fused_computation.68 | convolution fusion | flops 674103296 | bytes 3675136 | tf_op jit(solution)/shard_map/dot_general | solution.py:42
  129.4 2.0 %collective-permute-start.12 = (f32[2,2,2,16,256]{4,3,2,1,0:T(8,128)S(1)}, f32[2,2,2,16,256]{4,3,2,1,0:T(8,128)S(1)}, u32[]{:S(2)}, u32[]{:S(2)}) collective-permute-start(f32[2,2,2,16,256]{4,3,2,1,0:T(8,128)S(1)} %dynamic-slice_bitcast_fusion), channel_id=1, source_target_pairs={{0,16},{16,0},{32,48},{48,32},{64,80},{80,64},{96,112},{112,96},{1... | collective-permute-start | bytes 393224 | tf_op jit(solution)/shard_map/ppermute | solution.py:62
  131.4 3.8 %collective-permute-done.12 = f32[2,2,2,16,256]{4,3,2,1,0:T(8,128)S(1)} collective-permute-done((f32[2,2,2,16,256]{4,3,2,1,0:T(8,128)S(1)}, f32[2,2,2,16,256]{4,3,2,1,0:T(8,128)S(1)}, u32[]{:S(2)}, u32[]{:S(2)}) %collective-permute-start.12) | collective-permute-done | bytes 131104 | tf_op jit(solution)/shard_map/ppermute | solution.py:62
  135.2 3.3 %collective-permute-start.13 = (f32[2,2,16,256]{3,2,1,0:T(8,128)S(1)}, f32[2,2,16,256]{3,2,1,0:T(8,128)S(1)}, u32[]{:S(2)}, u32[]{:S(2)}) collective-permute-start(f32[2,2,16,256]{3,2,1,0:T(8,128)S(1)} %dynamic-slice_bitcast_fusion.1), channel_id=1, source_target_pairs={{0,32},{16,48},{32,0},{48,16},{64,96},{80,112},{96,64},{112,80},{1... | collective-permute-start | bytes 196616 | tf_op jit(solution)/shard_map/ppermute | solution.py:62
  138.5 2.7 %collective-permute-done.13 = f32[2,2,16,256]{3,2,1,0:T(8,128)S(1)} collective-permute-done((f32[2,2,16,256]{3,2,1,0:T(8,128)S(1)}, f32[2,2,16,256]{3,2,1,0:T(8,128)S(1)}, u32[]{:S(2)}, u32[]{:S(2)}) %collective-permute-start.13) | collective-permute-done | bytes 65568 | tf_op jit(solution)/shard_map/ppermute | solution.py:62
  141.3 2.8 %collective-permute-start.14 = (f32[2,16,256]{2,1,0:T(8,128)S(1)}, f32[2,16,256]{2,1,0:T(8,128)S(1)}, u32[]{:S(2)}, u32[]{:S(2)}) collective-permute-start(f32[2,16,256]{2,1,0:T(8,128)S(1)} %dynamic-slice_bitcast_fusion.2), channel_id=1, source_target_pairs={{0,128},{16,144},{32,160},{48,176},{64,192},{80,208},{96,224},{112... | collective-permute-start | bytes 98312 | tf_op jit(solution)/shard_map/ppermute | solution.py:62
  144.0 2.7 %collective-permute-done.14 = f32[2,16,256]{2,1,0:T(8,128)S(1)} collective-permute-done((f32[2,16,256]{2,1,0:T(8,128)S(1)}, f32[2,16,256]{2,1,0:T(8,128)S(1)}, u32[]{:S(2)}, u32[]{:S(2)}) %collective-permute-start.14) | collective-permute-done | bytes 32800 | tf_op jit(solution)/shard_map/ppermute | solution.py:62
  146.8 7.0 %collective-permute-start.15 = (f32[16,256]{1,0:T(8,128)S(1)}, f32[16,256]{1,0:T(8,128)S(1)}, u32[]{:S(2)}, u32[]{:S(2)}) collective-permute-start(f32[16,256]{1,0:T(8,128)S(1)} %dynamic-slice_bitcast_fusion.3), channel_id=1, source_target_pairs={{0,64},{16,80},{32,96},{48,112},{64,0},{80,16},{96,32},{112,48},{1... | collective-permute-start | bytes 49160 | tf_op jit(solution)/shard_map/ppermute | solution.py:62
  153.8 1.7 %collective-permute-done.15 = f32[16,256]{1,0:T(8,128)S(1)} collective-permute-done((f32[16,256]{1,0:T(8,128)S(1)}, f32[16,256]{1,0:T(8,128)S(1)}, u32[]{:S(2)}, u32[]{:S(2)}) %collective-permute-start.15) | collective-permute-done | bytes 16416 | tf_op jit(solution)/shard_map/ppermute | solution.py:62
  (279 shorter events, 42.0 us)
Async XLA Ops:
  2.7 6.5 %collective-permute-start.4 = (bf16[128,1024]{1,0:T(8,128)(2,1)S(1)}, bf16[128,1024]{1,0:T(8,128)(2,1)}, u32[]{:S(2)}, u32[]{:S(2)}) collective-permute-start(bf16[128,1024]{1,0:T(8,128)(2,1)S(1)} %get-tuple-element.178), channel_id=1, source_target_pairs={{0,1},{1,4},{4,5},{5,8},{8,9},{9,12},{12,13},{13,14},{14,15},{15,1... | collective-permute-start | bytes 786440 | tf_op jit(solution)/shard_map/ppermute | solution.py:95
  2.8 7.4 %collective-permute-start.6 = (bf16[128,1024]{1,0:T(8,128)(2,1)S(1)}, bf16[128,1024]{1,0:T(8,128)(2,1)}, u32[]{:S(2)}, u32[]{:S(2)}) collective-permute-start(bf16[128,1024]{1,0:T(8,128)(2,1)S(1)} %get-tuple-element.177), channel_id=1, source_target_pairs={{1,0},{4,1},{5,4},{8,5},{9,8},{12,9},{13,12},{14,13},{15,14},{10,1... | collective-permute-start | bytes 786440 | tf_op jit(solution)/shard_map/ppermute | solution.py:95
  11.4 6.2 %collective-permute-start.5 = (bf16[128,1024]{1,0:T(8,128)(2,1)}, bf16[128,1024]{1,0:T(8,128)(2,1)S(1)}, u32[]{:S(2)}, u32[]{:S(2)}) collective-permute-start(bf16[128,1024]{1,0:T(8,128)(2,1)} %collective-permute-done.4), channel_id=1, source_target_pairs={{0,1},{1,4},{4,5},{5,8},{8,9},{9,12},{12,13},{13,14},{14,15},{15,1... | collective-permute-start | bytes 786440 | tf_op jit(solution)/shard_map/ppermute | solution.py:95
  11.7 5.9 %collective-permute-start.7 = (bf16[128,1024]{1,0:T(8,128)(2,1)}, bf16[128,1024]{1,0:T(8,128)(2,1)S(1)}, u32[]{:S(2)}, u32[]{:S(2)}) collective-permute-start(bf16[128,1024]{1,0:T(8,128)(2,1)} %collective-permute-done.6), channel_id=1, source_target_pairs={{1,0},{4,1},{5,4},{8,5},{9,8},{12,9},{13,12},{14,13},{15,14},{10,1... | collective-permute-start | bytes 786440 | tf_op jit(solution)/shard_map/ppermute | solution.py:95
  17.7 7.3 %collective-permute-start = (bf16[128,1024]{1,0:T(8,128)(2,1)S(1)}, bf16[128,1024]{1,0:T(8,128)(2,1)S(1)}, u32[]{:S(2)}, u32[]{:S(2)}) collective-permute-start(bf16[128,1024]{1,0:T(8,128)(2,1)S(1)} %copy.30), channel_id=1, source_target_pairs={{0,1},{1,4},{4,5},{5,8},{8,9},{9,12},{12,13},{13,14},{14,15},{15,1... | collective-permute-start | bytes 786440 | tf_op jit(solution)/shard_map/while/body/eval_jaxpr/ppermute | solution.py:95
  19.4 5.6 %collective-permute-start.1 = (bf16[128,1024]{1,0:T(8,128)(2,1)S(1)}, bf16[128,1024]{1,0:T(8,128)(2,1)S(1)}, u32[]{:S(2)}, u32[]{:S(2)}) collective-permute-start(bf16[128,1024]{1,0:T(8,128)(2,1)S(1)} %copy.31), channel_id=1, source_target_pairs={{1,0},{4,1},{5,4},{8,5},{9,8},{12,9},{13,12},{14,13},{15,14},{10,1... | collective-permute-start | bytes 786440 | tf_op jit(solution)/shard_map/while/body/eval_jaxpr/ppermute | solution.py:95
  19.6 5.3 %collective-permute-start.2 = (f32[256,128]{0,1:T(8,128)S(1)}, f32[256,128]{0,1:T(8,128)S(1)}, u32[]{:S(2)}, u32[]{:S(2)}) collective-permute-start(f32[256,128]{0,1:T(8,128)S(1)} %add.332), channel_id=1, source_target_pairs={{0,1},{1,4},{4,5},{5,8},{8,9},{9,12},{12,13},{13,14},{14,15},{15,1... | collective-permute-start | bytes 393224 | tf_op jit(solution)/shard_map/while/body/eval_jaxpr/ppermute | solution.py:95
  25.0 7.4 %collective-permute-start = (bf16[128,1024]{1,0:T(8,128)(2,1)S(1)}, bf16[128,1024]{1,0:T(8,128)(2,1)S(1)}, u32[]{:S(2)}, u32[]{:S(2)}) collective-permute-start(bf16[128,1024]{1,0:T(8,128)(2,1)S(1)} %copy.30), channel_id=1, source_target_pairs={{0,1},{1,4},{4,5},{5,8},{8,9},{9,12},{12,13},{13,14},{14,15},{15,1... | collective-permute-start | bytes 786440 | tf_op jit(solution)/shard_map/while/body/eval_jaxpr/ppermute | solution.py:95
  26.9 5.5 %collective-permute-start.1 = (bf16[128,1024]{1,0:T(8,128)(2,1)S(1)}, bf16[128,1024]{1,0:T(8,128)(2,1)S(1)}, u32[]{:S(2)}, u32[]{:S(2)}) collective-permute-start(bf16[128,1024]{1,0:T(8,128)(2,1)S(1)} %copy.31), channel_id=1, source_target_pairs={{1,0},{4,1},{5,4},{8,5},{9,8},{12,9},{13,12},{14,13},{15,14},{10,1... | collective-permute-start | bytes 786440 | tf_op jit(solution)/shard_map/while/body/eval_jaxpr/ppermute | solution.py:95
  27.1 5.3 %collective-permute-start.2 = (f32[256,128]{0,1:T(8,128)S(1)}, f32[256,128]{0,1:T(8,128)S(1)}, u32[]{:S(2)}, u32[]{:S(2)}) collective-permute-start(f32[256,128]{0,1:T(8,128)S(1)} %add.332), channel_id=1, source_target_pairs={{0,1},{1,4},{4,5},{5,8},{8,9},{9,12},{12,13},{13,14},{14,15},{15,1... | collective-permute-start | bytes 393224 | tf_op jit(solution)/shard_map/while/body/eval_jaxpr/ppermute | solution.py:95
  32.5 7.4 %collective-permute-start = (bf16[128,1024]{1,0:T(8,128)(2,1)S(1)}, bf16[128,1024]{1,0:T(8,128)(2,1)S(1)}, u32[]{:S(2)}, u32[]{:S(2)}) collective-permute-start(bf16[128,1024]{1,0:T(8,128)(2,1)S(1)} %copy.30), channel_id=1, source_target_pairs={{0,1},{1,4},{4,5},{5,8},{8,9},{9,12},{12,13},{13,14},{14,15},{15,1... | collective-permute-start | bytes 786440 | tf_op jit(solution)/shard_map/while/body/eval_jaxpr/ppermute | solution.py:95
  34.3 5.5 %collective-permute-start.1 = (bf16[128,1024]{1,0:T(8,128)(2,1)S(1)}, bf16[128,1024]{1,0:T(8,128)(2,1)S(1)}, u32[]{:S(2)}, u32[]{:S(2)}) collective-permute-start(bf16[128,1024]{1,0:T(8,128)(2,1)S(1)} %copy.31), channel_id=1, source_target_pairs={{1,0},{4,1},{5,4},{8,5},{9,8},{12,9},{13,12},{14,13},{15,14},{10,1... | collective-permute-start | bytes 786440 | tf_op jit(solution)/shard_map/while/body/eval_jaxpr/ppermute | solution.py:95
  34.5 5.3 %collective-permute-start.2 = (f32[256,128]{0,1:T(8,128)S(1)}, f32[256,128]{0,1:T(8,128)S(1)}, u32[]{:S(2)}, u32[]{:S(2)}) collective-permute-start(f32[256,128]{0,1:T(8,128)S(1)} %add.332), channel_id=1, source_target_pairs={{0,1},{1,4},{4,5},{5,8},{8,9},{9,12},{12,13},{13,14},{14,15},{15,1... | collective-permute-start | bytes 393224 | tf_op jit(solution)/shard_map/while/body/eval_jaxpr/ppermute | solution.py:95
  39.9 7.4 %collective-permute-start = (bf16[128,1024]{1,0:T(8,128)(2,1)S(1)}, bf16[128,1024]{1,0:T(8,128)(2,1)S(1)}, u32[]{:S(2)}, u32[]{:S(2)}) collective-permute-start(bf16[128,1024]{1,0:T(8,128)(2,1)S(1)} %copy.30), channel_id=1, source_target_pairs={{0,1},{1,4},{4,5},{5,8},{8,9},{9,12},{12,13},{13,14},{14,15},{15,1... | collective-permute-start | bytes 786440 | tf_op jit(solution)/shard_map/while/body/eval_jaxpr/ppermute | solution.py:95
  41.8 5.5 %collective-permute-start.1 = (bf16[128,1024]{1,0:T(8,128)(2,1)S(1)}, bf16[128,1024]{1,0:T(8,128)(2,1)S(1)}, u32[]{:S(2)}, u32[]{:S(2)}) collective-permute-start(bf16[128,1024]{1,0:T(8,128)(2,1)S(1)} %copy.31), channel_id=1, source_target_pairs={{1,0},{4,1},{5,4},{8,5},{9,8},{12,9},{13,12},{14,13},{15,14},{10,1... | collective-permute-start | bytes 786440 | tf_op jit(solution)/shard_map/while/body/eval_jaxpr/ppermute | solution.py:95
  41.9 5.3 %collective-permute-start.2 = (f32[256,128]{0,1:T(8,128)S(1)}, f32[256,128]{0,1:T(8,128)S(1)}, u32[]{:S(2)}, u32[]{:S(2)}) collective-permute-start(f32[256,128]{0,1:T(8,128)S(1)} %add.332), channel_id=1, source_target_pairs={{0,1},{1,4},{4,5},{5,8},{8,9},{9,12},{12,13},{13,14},{14,15},{15,1... | collective-permute-start | bytes 393224 | tf_op jit(solution)/shard_map/while/body/eval_jaxpr/ppermute | solution.py:95
  47.3 7.4 %collective-permute-start = (bf16[128,1024]{1,0:T(8,128)(2,1)S(1)}, bf16[128,1024]{1,0:T(8,128)(2,1)S(1)}, u32[]{:S(2)}, u32[]{:S(2)}) collective-permute-start(bf16[128,1024]{1,0:T(8,128)(2,1)S(1)} %copy.30), channel_id=1, source_target_pairs={{0,1},{1,4},{4,5},{5,8},{8,9},{9,12},{12,13},{13,14},{14,15},{15,1... | collective-permute-start | bytes 786440 | tf_op jit(solution)/shard_map/while/body/eval_jaxpr/ppermute | solution.py:95
  49.2 5.5 %collective-permute-start.1 = (bf16[128,1024]{1,0:T(8,128)(2,1)S(1)}, bf16[128,1024]{1,0:T(8,128)(2,1)S(1)}, u32[]{:S(2)}, u32[]{:S(2)}) collective-permute-start(bf16[128,1024]{1,0:T(8,128)(2,1)S(1)} %copy.31), channel_id=1, source_target_pairs={{1,0},{4,1},{5,4},{8,5},{9,8},{12,9},{13,12},{14,13},{15,14},{10,1... | collective-permute-start | bytes 786440 | tf_op jit(solution)/shard_map/while/body/eval_jaxpr/ppermute | solution.py:95
  49.4 5.3 %collective-permute-start.2 = (f32[256,128]{0,1:T(8,128)S(1)}, f32[256,128]{0,1:T(8,128)S(1)}, u32[]{:S(2)}, u32[]{:S(2)}) collective-permute-start(f32[256,128]{0,1:T(8,128)S(1)} %add.332), channel_id=1, source_target_pairs={{0,1},{1,4},{4,5},{5,8},{8,9},{9,12},{12,13},{13,14},{14,15},{15,1... | collective-permute-start | bytes 393224 | tf_op jit(solution)/shard_map/while/body/eval_jaxpr/ppermute | solution.py:95
  54.8 7.4 %collective-permute-start = (bf16[128,1024]{1,0:T(8,128)(2,1)S(1)}, bf16[128,1024]{1,0:T(8,128)(2,1)S(1)}, u32[]{:S(2)}, u32[]{:S(2)}) collective-permute-start(bf16[128,1024]{1,0:T(8,128)(2,1)S(1)} %copy.30), channel_id=1, source_target_pairs={{0,1},{1,4},{4,5},{5,8},{8,9},{9,12},{12,13},{13,14},{14,15},{15,1... | collective-permute-start | bytes 786440 | tf_op jit(solution)/shard_map/while/body/eval_jaxpr/ppermute | solution.py:95
  56.6 5.5 %collective-permute-start.1 = (bf16[128,1024]{1,0:T(8,128)(2,1)S(1)}, bf16[128,1024]{1,0:T(8,128)(2,1)S(1)}, u32[]{:S(2)}, u32[]{:S(2)}) collective-permute-start(bf16[128,1024]{1,0:T(8,128)(2,1)S(1)} %copy.31), channel_id=1, source_target_pairs={{1,0},{4,1},{5,4},{8,5},{9,8},{12,9},{13,12},{14,13},{15,14},{10,1... | collective-permute-start | bytes 786440 | tf_op jit(solution)/shard_map/while/body/eval_jaxpr/ppermute | solution.py:95
  56.8 5.3 %collective-permute-start.2 = (f32[256,128]{0,1:T(8,128)S(1)}, f32[256,128]{0,1:T(8,128)S(1)}, u32[]{:S(2)}, u32[]{:S(2)}) collective-permute-start(f32[256,128]{0,1:T(8,128)S(1)} %add.332), channel_id=1, source_target_pairs={{0,1},{1,4},{4,5},{5,8},{8,9},{9,12},{12,13},{13,14},{14,15},{15,1... | collective-permute-start | bytes 393224 | tf_op jit(solution)/shard_map/while/body/eval_jaxpr/ppermute | solution.py:95
  62.2 7.4 %collective-permute-start = (bf16[128,1024]{1,0:T(8,128)(2,1)S(1)}, bf16[128,1024]{1,0:T(8,128)(2,1)S(1)}, u32[]{:S(2)}, u32[]{:S(2)}) collective-permute-start(bf16[128,1024]{1,0:T(8,128)(2,1)S(1)} %copy.30), channel_id=1, source_target_pairs={{0,1},{1,4},{4,5},{5,8},{8,9},{9,12},{12,13},{13,14},{14,15},{15,1... | collective-permute-start | bytes 786440 | tf_op jit(solution)/shard_map/while/body/eval_jaxpr/ppermute | solution.py:95
  64.1 5.5 %collective-permute-start.1 = (bf16[128,1024]{1,0:T(8,128)(2,1)S(1)}, bf16[128,1024]{1,0:T(8,128)(2,1)S(1)}, u32[]{:S(2)}, u32[]{:S(2)}) collective-permute-start(bf16[128,1024]{1,0:T(8,128)(2,1)S(1)} %copy.31), channel_id=1, source_target_pairs={{1,0},{4,1},{5,4},{8,5},{9,8},{12,9},{13,12},{14,13},{15,14},{10,1... | collective-permute-start | bytes 786440 | tf_op jit(solution)/shard_map/while/body/eval_jaxpr/ppermute | solution.py:95
  64.2 5.3 %collective-permute-start.2 = (f32[256,128]{0,1:T(8,128)S(1)}, f32[256,128]{0,1:T(8,128)S(1)}, u32[]{:S(2)}, u32[]{:S(2)}) collective-permute-start(f32[256,128]{0,1:T(8,128)S(1)} %add.332), channel_id=1, source_target_pairs={{0,1},{1,4},{4,5},{5,8},{8,9},{9,12},{12,13},{13,14},{14,15},{15,1... | collective-permute-start | bytes 393224 | tf_op jit(solution)/shard_map/while/body/eval_jaxpr/ppermute | solution.py:95
  69.6 7.4 %collective-permute-start = (bf16[128,1024]{1,0:T(8,128)(2,1)S(1)}, bf16[128,1024]{1,0:T(8,128)(2,1)S(1)}, u32[]{:S(2)}, u32[]{:S(2)}) collective-permute-start(bf16[128,1024]{1,0:T(8,128)(2,1)S(1)} %copy.30), channel_id=1, source_target_pairs={{0,1},{1,4},{4,5},{5,8},{8,9},{9,12},{12,13},{13,14},{14,15},{15,1... | collective-permute-start | bytes 786440 | tf_op jit(solution)/shard_map/while/body/eval_jaxpr/ppermute | solution.py:95
  71.5 5.5 %collective-permute-start.1 = (bf16[128,1024]{1,0:T(8,128)(2,1)S(1)}, bf16[128,1024]{1,0:T(8,128)(2,1)S(1)}, u32[]{:S(2)}, u32[]{:S(2)}) collective-permute-start(bf16[128,1024]{1,0:T(8,128)(2,1)S(1)} %copy.31), channel_id=1, source_target_pairs={{1,0},{4,1},{5,4},{8,5},{9,8},{12,9},{13,12},{14,13},{15,14},{10,1... | collective-permute-start | bytes 786440 | tf_op jit(solution)/shard_map/while/body/eval_jaxpr/ppermute | solution.py:95
  71.7 5.3 %collective-permute-start.2 = (f32[256,128]{0,1:T(8,128)S(1)}, f32[256,128]{0,1:T(8,128)S(1)}, u32[]{:S(2)}, u32[]{:S(2)}) collective-permute-start(f32[256,128]{0,1:T(8,128)S(1)} %add.332), channel_id=1, source_target_pairs={{0,1},{1,4},{4,5},{5,8},{8,9},{9,12},{12,13},{13,14},{14,15},{15,1... | collective-permute-start | bytes 393224 | tf_op jit(solution)/shard_map/while/body/eval_jaxpr/ppermute | solution.py:95
  77.1 7.4 %collective-permute-start = (bf16[128,1024]{1,0:T(8,128)(2,1)S(1)}, bf16[128,1024]{1,0:T(8,128)(2,1)S(1)}, u32[]{:S(2)}, u32[]{:S(2)}) collective-permute-start(bf16[128,1024]{1,0:T(8,128)(2,1)S(1)} %copy.30), channel_id=1, source_target_pairs={{0,1},{1,4},{4,5},{5,8},{8,9},{9,12},{12,13},{13,14},{14,15},{15,1... | collective-permute-start | bytes 786440 | tf_op jit(solution)/shard_map/while/body/eval_jaxpr/ppermute | solution.py:95
  79.0 5.5 %collective-permute-start.1 = (bf16[128,1024]{1,0:T(8,128)(2,1)S(1)}, bf16[128,1024]{1,0:T(8,128)(2,1)S(1)}, u32[]{:S(2)}, u32[]{:S(2)}) collective-permute-start(bf16[128,1024]{1,0:T(8,128)(2,1)S(1)} %copy.31), channel_id=1, source_target_pairs={{1,0},{4,1},{5,4},{8,5},{9,8},{12,9},{13,12},{14,13},{15,14},{10,1... | collective-permute-start | bytes 786440 | tf_op jit(solution)/shard_map/while/body/eval_jaxpr/ppermute | solution.py:95
  79.1 5.3 %collective-permute-start.2 = (f32[256,128]{0,1:T(8,128)S(1)}, f32[256,128]{0,1:T(8,128)S(1)}, u32[]{:S(2)}, u32[]{:S(2)}) collective-permute-start(f32[256,128]{0,1:T(8,128)S(1)} %add.332), channel_id=1, source_target_pairs={{0,1},{1,4},{4,5},{5,8},{8,9},{9,12},{12,13},{13,14},{14,15},{15,1... | collective-permute-start | bytes 393224 | tf_op jit(solution)/shard_map/while/body/eval_jaxpr/ppermute | solution.py:95
  84.5 7.4 %collective-permute-start = (bf16[128,1024]{1,0:T(8,128)(2,1)S(1)}, bf16[128,1024]{1,0:T(8,128)(2,1)S(1)}, u32[]{:S(2)}, u32[]{:S(2)}) collective-permute-start(bf16[128,1024]{1,0:T(8,128)(2,1)S(1)} %copy.30), channel_id=1, source_target_pairs={{0,1},{1,4},{4,5},{5,8},{8,9},{9,12},{12,13},{13,14},{14,15},{15,1... | collective-permute-start | bytes 786440 | tf_op jit(solution)/shard_map/while/body/eval_jaxpr/ppermute | solution.py:95
  86.4 5.5 %collective-permute-start.1 = (bf16[128,1024]{1,0:T(8,128)(2,1)S(1)}, bf16[128,1024]{1,0:T(8,128)(2,1)S(1)}, u32[]{:S(2)}, u32[]{:S(2)}) collective-permute-start(bf16[128,1024]{1,0:T(8,128)(2,1)S(1)} %copy.31), channel_id=1, source_target_pairs={{1,0},{4,1},{5,4},{8,5},{9,8},{12,9},{13,12},{14,13},{15,14},{10,1... | collective-permute-start | bytes 786440 | tf_op jit(solution)/shard_map/while/body/eval_jaxpr/ppermute | solution.py:95
  86.6 5.3 %collective-permute-start.2 = (f32[256,128]{0,1:T(8,128)S(1)}, f32[256,128]{0,1:T(8,128)S(1)}, u32[]{:S(2)}, u32[]{:S(2)}) collective-permute-start(f32[256,128]{0,1:T(8,128)S(1)} %add.332), channel_id=1, source_target_pairs={{0,1},{1,4},{4,5},{5,8},{8,9},{9,12},{12,13},{13,14},{14,15},{15,1... | collective-permute-start | bytes 393224 | tf_op jit(solution)/shard_map/while/body/eval_jaxpr/ppermute | solution.py:95
  91.9 7.4 %collective-permute-start = (bf16[128,1024]{1,0:T(8,128)(2,1)S(1)}, bf16[128,1024]{1,0:T(8,128)(2,1)S(1)}, u32[]{:S(2)}, u32[]{:S(2)}) collective-permute-start(bf16[128,1024]{1,0:T(8,128)(2,1)S(1)} %copy.30), channel_id=1, source_target_pairs={{0,1},{1,4},{4,5},{5,8},{8,9},{9,12},{12,13},{13,14},{14,15},{15,1... | collective-permute-start | bytes 786440 | tf_op jit(solution)/shard_map/while/body/eval_jaxpr/ppermute | solution.py:95
  93.8 5.5 %collective-permute-start.1 = (bf16[128,1024]{1,0:T(8,128)(2,1)S(1)}, bf16[128,1024]{1,0:T(8,128)(2,1)S(1)}, u32[]{:S(2)}, u32[]{:S(2)}) collective-permute-start(bf16[128,1024]{1,0:T(8,128)(2,1)S(1)} %copy.31), channel_id=1, source_target_pairs={{1,0},{4,1},{5,4},{8,5},{9,8},{12,9},{13,12},{14,13},{15,14},{10,1... | collective-permute-start | bytes 786440 | tf_op jit(solution)/shard_map/while/body/eval_jaxpr/ppermute | solution.py:95
  94.0 5.3 %collective-permute-start.2 = (f32[256,128]{0,1:T(8,128)S(1)}, f32[256,128]{0,1:T(8,128)S(1)}, u32[]{:S(2)}, u32[]{:S(2)}) collective-permute-start(f32[256,128]{0,1:T(8,128)S(1)} %add.332), channel_id=1, source_target_pairs={{0,1},{1,4},{4,5},{5,8},{8,9},{9,12},{12,13},{13,14},{14,15},{15,1... | collective-permute-start | bytes 393224 | tf_op jit(solution)/shard_map/while/body/eval_jaxpr/ppermute | solution.py:95
  99.4 7.4 %collective-permute-start = (bf16[128,1024]{1,0:T(8,128)(2,1)S(1)}, bf16[128,1024]{1,0:T(8,128)(2,1)S(1)}, u32[]{:S(2)}, u32[]{:S(2)}) collective-permute-start(bf16[128,1024]{1,0:T(8,128)(2,1)S(1)} %copy.30), channel_id=1, source_target_pairs={{0,1},{1,4},{4,5},{5,8},{8,9},{9,12},{12,13},{13,14},{14,15},{15,1... | collective-permute-start | bytes 786440 | tf_op jit(solution)/shard_map/while/body/eval_jaxpr/ppermute | solution.py:95
  101.3 5.5 %collective-permute-start.1 = (bf16[128,1024]{1,0:T(8,128)(2,1)S(1)}, bf16[128,1024]{1,0:T(8,128)(2,1)S(1)}, u32[]{:S(2)}, u32[]{:S(2)}) collective-permute-start(bf16[128,1024]{1,0:T(8,128)(2,1)S(1)} %copy.31), channel_id=1, source_target_pairs={{1,0},{4,1},{5,4},{8,5},{9,8},{12,9},{13,12},{14,13},{15,14},{10,1... | collective-permute-start | bytes 786440 | tf_op jit(solution)/shard_map/while/body/eval_jaxpr/ppermute | solution.py:95
  101.4 5.3 %collective-permute-start.2 = (f32[256,128]{0,1:T(8,128)S(1)}, f32[256,128]{0,1:T(8,128)S(1)}, u32[]{:S(2)}, u32[]{:S(2)}) collective-permute-start(f32[256,128]{0,1:T(8,128)S(1)} %add.332), channel_id=1, source_target_pairs={{0,1},{1,4},{4,5},{5,8},{8,9},{9,12},{12,13},{13,14},{14,15},{15,1... | collective-permute-start | bytes 393224 | tf_op jit(solution)/shard_map/while/body/eval_jaxpr/ppermute | solution.py:95
  106.8 7.4 %collective-permute-start = (bf16[128,1024]{1,0:T(8,128)(2,1)S(1)}, bf16[128,1024]{1,0:T(8,128)(2,1)S(1)}, u32[]{:S(2)}, u32[]{:S(2)}) collective-permute-start(bf16[128,1024]{1,0:T(8,128)(2,1)S(1)} %copy.30), channel_id=1, source_target_pairs={{0,1},{1,4},{4,5},{5,8},{8,9},{9,12},{12,13},{13,14},{14,15},{15,1... | collective-permute-start | bytes 786440 | tf_op jit(solution)/shard_map/while/body/eval_jaxpr/ppermute | solution.py:95
  108.7 5.5 %collective-permute-start.1 = (bf16[128,1024]{1,0:T(8,128)(2,1)S(1)}, bf16[128,1024]{1,0:T(8,128)(2,1)S(1)}, u32[]{:S(2)}, u32[]{:S(2)}) collective-permute-start(bf16[128,1024]{1,0:T(8,128)(2,1)S(1)} %copy.31), channel_id=1, source_target_pairs={{1,0},{4,1},{5,4},{8,5},{9,8},{12,9},{13,12},{14,13},{15,14},{10,1... | collective-permute-start | bytes 786440 | tf_op jit(solution)/shard_map/while/body/eval_jaxpr/ppermute | solution.py:95
  108.9 5.3 %collective-permute-start.2 = (f32[256,128]{0,1:T(8,128)S(1)}, f32[256,128]{0,1:T(8,128)S(1)}, u32[]{:S(2)}, u32[]{:S(2)}) collective-permute-start(f32[256,128]{0,1:T(8,128)S(1)} %add.332), channel_id=1, source_target_pairs={{0,1},{1,4},{4,5},{5,8},{8,9},{9,12},{12,13},{13,14},{14,15},{15,1... | collective-permute-start | bytes 393224 | tf_op jit(solution)/shard_map/while/body/eval_jaxpr/ppermute | solution.py:95
  114.4 6.1 %collective-permute-start.10 = (f32[256,128]{1,0:T(8,128)S(1)}, f32[256,128]{1,0:T(8,128)S(1)}, u32[]{:S(2)}, u32[]{:S(2)}) collective-permute-start(f32[256,128]{1,0:T(8,128)S(1)} %add.204), channel_id=1, source_target_pairs={{1,0},{4,1},{5,4},{8,5},{9,8},{12,9},{13,12},{14,13},{15,14},{10,1... | collective-permute-start | bytes 393224 | tf_op jit(solution)/shard_map/ppermute | solution.py:95
  129.4 5.8 %collective-permute-start.12 = (f32[2,2,2,16,256]{4,3,2,1,0:T(8,128)S(1)}, f32[2,2,2,16,256]{4,3,2,1,0:T(8,128)S(1)}, u32[]{:S(2)}, u32[]{:S(2)}) collective-permute-start(f32[2,2,2,16,256]{4,3,2,1,0:T(8,128)S(1)} %dynamic-slice_bitcast_fusion), channel_id=1, source_target_pairs={{0,16},{16,0},{32,48},{48,32},{64,80},{80,64},{96,112},{112,96},{1... | collective-permute-start | bytes 393224 | tf_op jit(solution)/shard_map/ppermute | solution.py:62
  135.2 6.0 %collective-permute-start.13 = (f32[2,2,16,256]{3,2,1,0:T(8,128)S(1)}, f32[2,2,16,256]{3,2,1,0:T(8,128)S(1)}, u32[]{:S(2)}, u32[]{:S(2)}) collective-permute-start(f32[2,2,16,256]{3,2,1,0:T(8,128)S(1)} %dynamic-slice_bitcast_fusion.1), channel_id=1, source_target_pairs={{0,32},{16,48},{32,0},{48,16},{64,96},{80,112},{96,64},{112,80},{1... | collective-permute-start | bytes 196616 | tf_op jit(solution)/shard_map/ppermute | solution.py:62
  141.3 5.5 %collective-permute-start.14 = (f32[2,16,256]{2,1,0:T(8,128)S(1)}, f32[2,16,256]{2,1,0:T(8,128)S(1)}, u32[]{:S(2)}, u32[]{:S(2)}) collective-permute-start(f32[2,16,256]{2,1,0:T(8,128)S(1)} %dynamic-slice_bitcast_fusion.2), channel_id=1, source_target_pairs={{0,128},{16,144},{32,160},{48,176},{64,192},{80,208},{96,224},{112... | collective-permute-start | bytes 98312 | tf_op jit(solution)/shard_map/ppermute | solution.py:62
  146.8 8.8 %collective-permute-start.15 = (f32[16,256]{1,0:T(8,128)S(1)}, f32[16,256]{1,0:T(8,128)S(1)}, u32[]{:S(2)}, u32[]{:S(2)}) collective-permute-start(f32[16,256]{1,0:T(8,128)S(1)} %dynamic-slice_bitcast_fusion.3), channel_id=1, source_target_pairs={{0,64},{16,80},{32,96},{48,112},{64,0},{80,16},{96,32},{112,48},{1... | collective-permute-start | bytes 49160 | tf_op jit(solution)/shard_map/ppermute | solution.py:62
  (37 other events, 160.8 us)

commit v4 on v3

--- a/solution.py
+++ b/solution.py
@@ -94,24 +94,39 @@
     def send(points_f, points_b):
         return lax.ppermute(points_f, "blk", forward), lax.ppermute(points_b, "blk", backward)
 
+    width = targets_bf.shape[1]
+    rhs_count = rhs_values.shape[1]
+    sum_shape = (rhs_count, half)
+    sum_rows = rhs_count * half // width
+
+    def pack(points, sums):
+        high = lax.reduce_precision(sums, exponent_bits=8, mantissa_bits=7)
+        low = (sums - high).astype(jnp.bfloat16)
+        parts = [points, high.astype(jnp.bfloat16).reshape(-1, width), low.reshape(-1, width)]
+        return jnp.concatenate(parts, axis=0)
+
+    def unpack(packed):
+        points = packed[:half]
+        high = packed[half : half + sum_rows].reshape(sum_shape).astype(jnp.float32)
+        low = packed[half + sum_rows :].reshape(sum_shape).astype(jnp.float32)
+        return points, high + low
+
     def advance(counter, carried):
-        points_f, points_b, sums_f, sums_b, part_f, part_b = carried
-        sums_f, sums_b = send(sums_f + part_f, sums_b + part_b)
-        next_f, next_b = send(points_f, points_b)
+        packed_f, packed_b, part_f, part_b = carried
+        points_f, sums_f = unpack(packed_f)
+        points_b, sums_b = unpack(packed_b)
+        packed_f, packed_b = send(pack(points_f, sums_f + part_f), pack(points_b, sums_b + part_b))
         part_f, part_b = halves(points_f, points_b)
-        return (next_f, next_b, sums_f, sums_b, part_f, part_b)
+        return (packed_f, packed_b, part_f, part_b)
 
-    points_f, points_b = send(targets_bf[:half], targets_bf[half:])
+    zeros = jnp.zeros(sum_shape, jnp.float32)
+    packed_f, packed_b = send(pack(targets_bf[:half], zeros), pack(targets_bf[half:], zeros))
     own = contribution(targets_bf)
-    next_f, next_b = send(points_f, points_b)
-    part_f, part_b = halves(points_f, points_b)
-    zeros = jnp.zeros_like(part_f)
-    carried = (next_f, next_b, zeros, zeros, part_f, part_b)
-    carried = lax.fori_loop(0, cycle_size - 3, advance, carried)
-    points_f, points_b, sums_f, sums_b, part_f, part_b = carried
-    sums_f, sums_b = send(sums_f + part_f, sums_b + part_b)
-    part_f, part_b = halves(points_f, points_b)
-    sums_f, sums_b = send(sums_f + part_f, sums_b + part_b)
+    carried = lax.fori_loop(0, cycle_size - 1, advance, (packed_f, packed_b, zeros, zeros))
+    packed_f, packed_b, part_f, part_b = carried
+    sums_f = unpack(packed_f)[1] + part_f
+    sums_b = unpack(packed_b)[1] + part_b
+    sums_f, sums_b = send(sums_f, sums_b)
     gathered_sums = own + jnp.concatenate([sums_f, sums_b], axis=1)
     owned_sums = halving_scatter(gathered_sums, "grp")
     source_total = src_codes.shape[0] * group_size * cycle_size

time: 157 us -> 169 us (1.076)
  the two profiles are of different devices: /device:TPU:6 before, /device:TPU:1 now
where the time goes in v4:
time: 169 us; the launch traced here: 167 us
  starting transfers between devices  50.8 us (30%)
  matrix products  47.5 us (28%)
  waiting for transfers between devices  45.4 us (27%)
  other arithmetic  11.1 us (7%)
  local copies, waits for them, and re-layouts  9.54 us (6%)
  loops' own time  2 us (1%)
    dot_general x16, matrix products, kernel_block(): lax.dot_general(rhs_values, matern, (((0,), (1,)), ((), ())), preferred_e...  47.5 us
    ppermute x17, waiting for transfers between devices, send(): lax.ppermute(points_b, 'blk', backward)  34.8 us
    ppermute x17, starting transfers between devices, send(): lax.ppermute(points_b, 'blk', backward)  30 us
    ppermute x4, starting transfers between devices, halving_scatter(): parts = kept + lax.ppermute(sent, axis, route)  13.7 us
    ppermute x4, waiting for transfers between devices, halving_scatter(): parts = kept + lax.ppermute(sent, axis, route)  8.9 us
    ppermute x17, starting transfers between devices, send(): lax.ppermute(points_f, 'blk', forward)  7.19 us
    reduce_sum x17, other arithmetic, squares(): return jnp.sum(widened * widened, axis=1)  6.38 us
  transfers between devices with their start and end apart: 38, of which 22 were waited for; matrix products, arithmetic and copies ran while one was open for 34% of the time, Pallas kernels for 0%

profile of v4, /device:TPU:1, one launch (start us, length us, event | category | flops | bytes accessed | tf_op | source)
XLA Modules:
  0.0 166.6 jit_solution(6593609733487732118)
XLA Ops:
  2.9 2.7 %collective-permute-start.2 = (bf16[192,1024]{1,0:T(8,128)(2,1)S(1)}, bf16[192,1024]{1,0:T(8,128)(2,1)S(1)}, u32[]{:S(2)}, u32[]{:S(2)}) collective-permute-start(bf16[192,1024]{1,0:T(8,128)(2,1)S(1)} %get-tuple-element.142), channel_id=1, source_target_pairs={{0,1},{1,4},{4,5},{5,8},{8,9},{9,12},{12,13},{13,14},{14,15},{15,1... | collective-permute-start | bytes 1179656 | tf_op jit(solution)/shard_map/ppermute | solution.py:95
  10.0 2.1 %multiply_reduce_fusion.1 = (f32[1024]{0:T(1024)S(1)}, bf16[1024,1024]{1,0:T(8,128)(2,1)}) fusion(f32[128,8,8,128]{3,2,1,0:T(8,128)S(1)} %bitcast.48, s32[1024,1024]{1,0:T(8,128)S(1)} %copy-done), kind=kLoop, calls=%fused_computation.32 | loop fusion | flops 6290432 | bytes 10489856 | tf_op jit(solution)/shard_map/reduce_sum | solution.py:31
  13.0 120.9 %while.18 = (s32[]{:T(128)}, bf16[192,1024]{1,0:T(8,128)(2,1)S(1)}, bf16[192,1024]{1,0:T(8,128)(2,1)S(1)}, f32[256,128]{0,1:T(8,128)S(1)}, f32[256,128]{0,1:T(8,...) while((s32[]{:T(128)}, bf16[192,1024]{1,0:T(8,128)(2,1)S(1)}, ...), condition=%wide.region_4.5_spmd, body=%wide.region_2.4_spmd.sunk | while | flops 679476992 | bytes 13113517 | solution.py:125
  15.7 3.0 %convolution_bitcast_fusion.2 = f32[256,256]{0,1:T(8,128)S(1)} fusion(bf16[1024,256]{1,0:T(8,128)(2,1)} %get-tuple-element.229, bf16[1024,1024]{1,0:T(8,128)(2,1)} %get-tuple-element.228, f32[1024]{0:T(1024)S(1)} %get-tuple-element.227, f32[256]{0:T(256)S(1)} %multiply_reduce_fusion.4, bf16[128,1024]{1,0:T(8,128)(2,1)S(1)} %slice.103, ...), kind=kOutput, calls=%fused_computation.4.clone.1 | convolution fusion | flops 675020800 | bytes 3412992 | tf_op jit(solution)/shard_map/while/body/eval_jaxpr/dot_general | solution.py:42
  18.8 2.1 %collective-permute-done.1 = bf16[192,1024]{1,0:T(8,128)(2,1)S(1)} collective-permute-done((bf16[192,1024]{1,0:T(8,128)(2,1)S(1)}, bf16[192,1024]{1,0:T(8,128)(2,1)S(1)}, u32[]{:S(2)}, u32[]{:S(2)}) %collective-permute-start.1) | collective-permute-done | bytes 393248 | tf_op jit(solution)/shard_map/while/body/eval_jaxpr/ppermute | solution.py:95
  21.2 2.3 %collective-permute-start.1 = (bf16[192,1024]{1,0:T(8,128)(2,1)S(1)}, bf16[192,1024]{1,0:T(8,128)(2,1)S(1)}, u32[]{:S(2)}, u32[]{:S(2)}) collective-permute-start(bf16[192,1024]{1,0:T(8,128)(2,1)S(1)} %pad_maximum_fusion.14), channel_id=1, source_target_pairs={{1,0},{4,1},{5,4},{8,5},{9,8},{12,9},{13,12},{14,13},{15,14},{10,1... | collective-permute-start | bytes 1179656 | tf_op jit(solution)/shard_map/while/body/eval_jaxpr/ppermute | solution.py:95
  24.2 3.0 %convolution_bitcast_fusion.2 = f32[256,256]{0,1:T(8,128)S(1)} fusion(bf16[1024,256]{1,0:T(8,128)(2,1)} %get-tuple-element.229, bf16[1024,1024]{1,0:T(8,128)(2,1)} %get-tuple-element.228, f32[1024]{0:T(1024)S(1)} %get-tuple-element.227, f32[256]{0:T(256)S(1)} %multiply_reduce_fusion.4, bf16[128,1024]{1,0:T(8,128)(2,1)S(1)} %slice.103, ...), kind=kOutput, calls=%fused_computation.4.clone.1 | convolution fusion | flops 675020800 | bytes 3412992 | tf_op jit(solution)/shard_map/while/body/eval_jaxpr/dot_general | solution.py:42
  29.3 2.3 %collective-permute-start.1 = (bf16[192,1024]{1,0:T(8,128)(2,1)S(1)}, bf16[192,1024]{1,0:T(8,128)(2,1)S(1)}, u32[]{:S(2)}, u32[]{:S(2)}) collective-permute-start(bf16[192,1024]{1,0:T(8,128)(2,1)S(1)} %pad_maximum_fusion.14), channel_id=1, source_target_pairs={{1,0},{4,1},{5,4},{8,5},{9,8},{12,9},{13,12},{14,13},{15,14},{10,1... | collective-permute-start | bytes 1179656 | tf_op jit(solution)/shard_map/while/body/eval_jaxpr/ppermute | solution.py:95
  32.2 3.0 %convolution_bitcast_fusion.2 = f32[256,256]{0,1:T(8,128)S(1)} fusion(bf16[1024,256]{1,0:T(8,128)(2,1)} %get-tuple-element.229, bf16[1024,1024]{1,0:T(8,128)(2,1)} %get-tuple-element.228, f32[1024]{0:T(1024)S(1)} %get-tuple-element.227, f32[256]{0:T(256)S(1)} %multiply_reduce_fusion.4, bf16[128,1024]{1,0:T(8,128)(2,1)S(1)} %slice.103, ...), kind=kOutput, calls=%fused_computation.4.clone.1 | convolution fusion | flops 675020800 | bytes 3412992 | tf_op jit(solution)/shard_map/while/body/eval_jaxpr/dot_general | solution.py:42
  35.2 2.1 %collective-permute-done.1 = bf16[192,1024]{1,0:T(8,128)(2,1)S(1)} collective-permute-done((bf16[192,1024]{1,0:T(8,128)(2,1)S(1)}, bf16[192,1024]{1,0:T(8,128)(2,1)S(1)}, u32[]{:S(2)}, u32[]{:S(2)}) %collective-permute-start.1) | collective-permute-done | bytes 393248 | tf_op jit(solution)/shard_map/while/body/eval_jaxpr/ppermute | solution.py:95
  37.7 2.0 %collective-permute-start.1 = (bf16[192,1024]{1,0:T(8,128)(2,1)S(1)}, bf16[192,1024]{1,0:T(8,128)(2,1)S(1)}, u32[]{:S(2)}, u32[]{:S(2)}) collective-permute-start(bf16[192,1024]{1,0:T(8,128)(2,1)S(1)} %pad_maximum_fusion.14), channel_id=1, source_target_pairs={{1,0},{4,1},{5,4},{8,5},{9,8},{12,9},{13,12},{14,13},{15,14},{10,1... | collective-permute-start | bytes 1179656 | tf_op jit(solution)/shard_map/while/body/eval_jaxpr/ppermute | solution.py:95
  40.3 3.0 %convolution_bitcast_fusion.2 = f32[256,256]{0,1:T(8,128)S(1)} fusion(bf16[1024,256]{1,0:T(8,128)(2,1)} %get-tuple-element.229, bf16[1024,1024]{1,0:T(8,128)(2,1)} %get-tuple-element.228, f32[1024]{0:T(1024)S(1)} %get-tuple-element.227, f32[256]{0:T(256)S(1)} %multiply_reduce_fusion.4, bf16[128,1024]{1,0:T(8,128)(2,1)S(1)} %slice.103, ...), kind=kOutput, calls=%fused_computation.4.clone.1 | convolution fusion | flops 675020800 | bytes 3412992 | tf_op jit(solution)/shard_map/while/body/eval_jaxpr/dot_general | solution.py:42
  43.3 2.1 %collective-permute-done.1 = bf16[192,1024]{1,0:T(8,128)(2,1)S(1)} collective-permute-done((bf16[192,1024]{1,0:T(8,128)(2,1)S(1)}, bf16[192,1024]{1,0:T(8,128)(2,1)S(1)}, u32[]{:S(2)}, u32[]{:S(2)}) %collective-permute-start.1) | collective-permute-done | bytes 393248 | tf_op jit(solution)/shard_map/while/body/eval_jaxpr/ppermute | solution.py:95
  45.7 2.0 %collective-permute-start.1 = (bf16[192,1024]{1,0:T(8,128)(2,1)S(1)}, bf16[192,1024]{1,0:T(8,128)(2,1)S(1)}, u32[]{:S(2)}, u32[]{:S(2)}) collective-permute-start(bf16[192,1024]{1,0:T(8,128)(2,1)S(1)} %pad_maximum_fusion.14), channel_id=1, source_target_pairs={{1,0},{4,1},{5,4},{8,5},{9,8},{12,9},{13,12},{14,13},{15,14},{10,1... | collective-permute-start | bytes 1179656 | tf_op jit(solution)/shard_map/while/body/eval_jaxpr/ppermute | solution.py:95
  48.3 3.0 %convolution_bitcast_fusion.2 = f32[256,256]{0,1:T(8,128)S(1)} fusion(bf16[1024,256]{1,0:T(8,128)(2,1)} %get-tuple-element.229, bf16[1024,1024]{1,0:T(8,128)(2,1)} %get-tuple-element.228, f32[1024]{0:T(1024)S(1)} %get-tuple-element.227, f32[256]{0:T(256)S(1)} %multiply_reduce_fusion.4, bf16[128,1024]{1,0:T(8,128)(2,1)S(1)} %slice.103, ...), kind=kOutput, calls=%fused_computation.4.clone.1 | convolution fusion | flops 675020800 | bytes 3412992 | tf_op jit(solution)/shard_map/while/body/eval_jaxpr/dot_general | solution.py:42
  51.3 2.1 %collective-permute-done.1 = bf16[192,1024]{1,0:T(8,128)(2,1)S(1)} collective-permute-done((bf16[192,1024]{1,0:T(8,128)(2,1)S(1)}, bf16[192,1024]{1,0:T(8,128)(2,1)S(1)}, u32[]{:S(2)}, u32[]{:S(2)}) %collective-permute-start.1) | collective-permute-done | bytes 393248 | tf_op jit(solution)/shard_map/while/body/eval_jaxpr/ppermute | solution.py:95
  56.4 3.0 %convolution_bitcast_fusion.2 = f32[256,256]{0,1:T(8,128)S(1)} fusion(bf16[1024,256]{1,0:T(8,128)(2,1)} %get-tuple-element.229, bf16[1024,1024]{1,0:T(8,128)(2,1)} %get-tuple-element.228, f32[1024]{0:T(1024)S(1)} %get-tuple-element.227, f32[256]{0:T(256)S(1)} %multiply_reduce_fusion.4, bf16[128,1024]{1,0:T(8,128)(2,1)S(1)} %slice.103, ...), kind=kOutput, calls=%fused_computation.4.clone.1 | convolution fusion | flops 675020800 | bytes 3412992 | tf_op jit(solution)/shard_map/while/body/eval_jaxpr/dot_general | solution.py:42
  59.4 2.1 %collective-permute-done.1 = bf16[192,1024]{1,0:T(8,128)(2,1)S(1)} collective-permute-done((bf16[192,1024]{1,0:T(8,128)(2,1)S(1)}, bf16[192,1024]{1,0:T(8,128)(2,1)S(1)}, u32[]{:S(2)}, u32[]{:S(2)}) %collective-permute-start.1) | collective-permute-done | bytes 393248 | tf_op jit(solution)/shard_map/while/body/eval_jaxpr/ppermute | solution.py:95
  61.8 2.0 %collective-permute-start.1 = (bf16[192,1024]{1,0:T(8,128)(2,1)S(1)}, bf16[192,1024]{1,0:T(8,128)(2,1)S(1)}, u32[]{:S(2)}, u32[]{:S(2)}) collective-permute-start(bf16[192,1024]{1,0:T(8,128)(2,1)S(1)} %pad_maximum_fusion.14), channel_id=1, source_target_pairs={{1,0},{4,1},{5,4},{8,5},{9,8},{12,9},{13,12},{14,13},{15,14},{10,1... | collective-permute-start | bytes 1179656 | tf_op jit(solution)/shard_map/while/body/eval_jaxpr/ppermute | solution.py:95
  64.4 3.0 %convolution_bitcast_fusion.2 = f32[256,256]{0,1:T(8,128)S(1)} fusion(bf16[1024,256]{1,0:T(8,128)(2,1)} %get-tuple-element.229, bf16[1024,1024]{1,0:T(8,128)(2,1)} %get-tuple-element.228, f32[1024]{0:T(1024)S(1)} %get-tuple-element.227, f32[256]{0:T(256)S(1)} %multiply_reduce_fusion.4, bf16[128,1024]{1,0:T(8,128)(2,1)S(1)} %slice.103, ...), kind=kOutput, calls=%fused_computation.4.clone.1 | convolution fusion | flops 675020800 | bytes 3412992 | tf_op jit(solution)/shard_map/while/body/eval_jaxpr/dot_general | solution.py:42
  67.4 2.1 %collective-permute-done.1 = bf16[192,1024]{1,0:T(8,128)(2,1)S(1)} collective-permute-done((bf16[192,1024]{1,0:T(8,128)(2,1)S(1)}, bf16[192,1024]{1,0:T(8,128)(2,1)S(1)}, u32[]{:S(2)}, u32[]{:S(2)}) %collective-permute-start.1) | collective-permute-done | bytes 393248 | tf_op jit(solution)/shard_map/while/body/eval_jaxpr/ppermute | solution.py:95
  69.9 2.0 %collective-permute-start.1 = (bf16[192,1024]{1,0:T(8,128)(2,1)S(1)}, bf16[192,1024]{1,0:T(8,128)(2,1)S(1)}, u32[]{:S(2)}, u32[]{:S(2)}) collective-permute-start(bf16[192,1024]{1,0:T(8,128)(2,1)S(1)} %pad_maximum_fusion.14), channel_id=1, source_target_pairs={{1,0},{4,1},{5,4},{8,5},{9,8},{12,9},{13,12},{14,13},{15,14},{10,1... | collective-permute-start | bytes 1179656 | tf_op jit(solution)/shard_map/while/body/eval_jaxpr/ppermute | solution.py:95
  72.4 3.0 %convolution_bitcast_fusion.2 = f32[256,256]{0,1:T(8,128)S(1)} fusion(bf16[1024,256]{1,0:T(8,128)(2,1)} %get-tuple-element.229, bf16[1024,1024]{1,0:T(8,128)(2,1)} %get-tuple-element.228, f32[1024]{0:T(1024)S(1)} %get-tuple-element.227, f32[256]{0:T(256)S(1)} %multiply_reduce_fusion.4, bf16[128,1024]{1,0:T(8,128)(2,1)S(1)} %slice.103, ...), kind=kOutput, calls=%fused_computation.4.clone.1 | convolution fusion | flops 675020800 | bytes 3412992 | tf_op jit(solution)/shard_map/while/body/eval_jaxpr/dot_general | solution.py:42
  75.5 2.1 %collective-permute-done.1 = bf16[192,1024]{1,0:T(8,128)(2,1)S(1)} collective-permute-done((bf16[192,1024]{1,0:T(8,128)(2,1)S(1)}, bf16[192,1024]{1,0:T(8,128)(2,1)S(1)}, u32[]{:S(2)}, u32[]{:S(2)}) %collective-permute-start.1) | collective-permute-done | bytes 393248 | tf_op jit(solution)/shard_map/while/body/eval_jaxpr/ppermute | solution.py:95
  77.9 2.0 %collective-permute-start.1 = (bf16[192,1024]{1,0:T(8,128)(2,1)S(1)}, bf16[192,1024]{1,0:T(8,128)(2,1)S(1)}, u32[]{:S(2)}, u32[]{:S(2)}) collective-permute-start(bf16[192,1024]{1,0:T(8,128)(2,1)S(1)} %pad_maximum_fusion.14), channel_id=1, source_target_pairs={{1,0},{4,1},{5,4},{8,5},{9,8},{12,9},{13,12},{14,13},{15,14},{10,1... | collective-permute-start | bytes 1179656 | tf_op jit(solution)/shard_map/while/body/eval_jaxpr/ppermute | solution.py:95
  80.5 3.0 %convolution_bitcast_fusion.2 = f32[256,256]{0,1:T(8,128)S(1)} fusion(bf16[1024,256]{1,0:T(8,128)(2,1)} %get-tuple-element.229, bf16[1024,1024]{1,0:T(8,128)(2,1)} %get-tuple-element.228, f32[1024]{0:T(1024)S(1)} %get-tuple-element.227, f32[256]{0:T(256)S(1)} %multiply_reduce_fusion.4, bf16[128,1024]{1,0:T(8,128)(2,1)S(1)} %slice.103, ...), kind=kOutput, calls=%fused_computation.4.clone.1 | convolution fusion | flops 675020800 | bytes 3412992 | tf_op jit(solution)/shard_map/while/body/eval_jaxpr/dot_general | solution.py:42
  83.5 2.1 %collective-permute-done.1 = bf16[192,1024]{1,0:T(8,128)(2,1)S(1)} collective-permute-done((bf16[192,1024]{1,0:T(8,128)(2,1)S(1)}, bf16[192,1024]{1,0:T(8,128)(2,1)S(1)}, u32[]{:S(2)}, u32[]{:S(2)}) %collective-permute-start.1) | collective-permute-done | bytes 393248 | tf_op jit(solution)/shard_map/while/body/eval_jaxpr/ppermute | solution.py:95
  86.0 2.0 %collective-permute-start.1 = (bf16[192,1024]{1,0:T(8,128)(2,1)S(1)}, bf16[192,1024]{1,0:T(8,128)(2,1)S(1)}, u32[]{:S(2)}, u32[]{:S(2)}) collective-permute-start(bf16[192,1024]{1,0:T(8,128)(2,1)S(1)} %pad_maximum_fusion.14), channel_id=1, source_target_pairs={{1,0},{4,1},{5,4},{8,5},{9,8},{12,9},{13,12},{14,13},{15,14},{10,1... | collective-permute-start | bytes 1179656 | tf_op jit(solution)/shard_map/while/body/eval_jaxpr/ppermute | solution.py:95
  88.5 3.0 %convolution_bitcast_fusion.2 = f32[256,256]{0,1:T(8,128)S(1)} fusion(bf16[1024,256]{1,0:T(8,128)(2,1)} %get-tuple-element.229, bf16[1024,1024]{1,0:T(8,128)(2,1)} %get-tuple-element.228, f32[1024]{0:T(1024)S(1)} %get-tuple-element.227, f32[256]{0:T(256)S(1)} %multiply_reduce_fusion.4, bf16[128,1024]{1,0:T(8,128)(2,1)S(1)} %slice.103, ...), kind=kOutput, calls=%fused_computation.4.clone.1 | convolution fusion | flops 675020800 | bytes 3412992 | tf_op jit(solution)/shard_map/while/body/eval_jaxpr/dot_general | solution.py:42
  91.5 2.1 %collective-permute-done.1 = bf16[192,1024]{1,0:T(8,128)(2,1)S(1)} collective-permute-done((bf16[192,1024]{1,0:T(8,128)(2,1)S(1)}, bf16[192,1024]{1,0:T(8,128)(2,1)S(1)}, u32[]{:S(2)}, u32[]{:S(2)}) %collective-permute-start.1) | collective-permute-done | bytes 393248 | tf_op jit(solution)/shard_map/while/body/eval_jaxpr/ppermute | solution.py:95
  94.0 2.0 %collective-permute-start.1 = (bf16[192,1024]{1,0:T(8,128)(2,1)S(1)}, bf16[192,1024]{1,0:T(8,128)(2,1)S(1)}, u32[]{:S(2)}, u32[]{:S(2)}) collective-permute-start(bf16[192,1024]{1,0:T(8,128)(2,1)S(1)} %pad_maximum_fusion.14), channel_id=1, source_target_pairs={{1,0},{4,1},{5,4},{8,5},{9,8},{12,9},{13,12},{14,13},{15,14},{10,1... | collective-permute-start | bytes 1179656 | tf_op jit(solution)/shard_map/while/body/eval_jaxpr/ppermute | solution.py:95
  96.6 3.0 %convolution_bitcast_fusion.2 = f32[256,256]{0,1:T(8,128)S(1)} fusion(bf16[1024,256]{1,0:T(8,128)(2,1)} %get-tuple-element.229, bf16[1024,1024]{1,0:T(8,128)(2,1)} %get-tuple-element.228, f32[1024]{0:T(1024)S(1)} %get-tuple-element.227, f32[256]{0:T(256)S(1)} %multiply_reduce_fusion.4, bf16[128,1024]{1,0:T(8,128)(2,1)S(1)} %slice.103, ...), kind=kOutput, calls=%fused_computation.4.clone.1 | convolution fusion | flops 675020800 | bytes 3412992 | tf_op jit(solution)/shard_map/while/body/eval_jaxpr/dot_general | solution.py:42
  99.6 2.1 %collective-permute-done.1 = bf16[192,1024]{1,0:T(8,128)(2,1)S(1)} collective-permute-done((bf16[192,1024]{1,0:T(8,128)(2,1)S(1)}, bf16[192,1024]{1,0:T(8,128)(2,1)S(1)}, u32[]{:S(2)}, u32[]{:S(2)}) %collective-permute-start.1) | collective-permute-done | bytes 393248 | tf_op jit(solution)/shard_map/while/body/eval_jaxpr/ppermute | solution.py:95
  102.0 2.0 %collective-permute-start.1 = (bf16[192,1024]{1,0:T(8,128)(2,1)S(1)}, bf16[192,1024]{1,0:T(8,128)(2,1)S(1)}, u32[]{:S(2)}, u32[]{:S(2)}) collective-permute-start(bf16[192,1024]{1,0:T(8,128)(2,1)S(1)} %pad_maximum_fusion.14), channel_id=1, source_target_pairs={{1,0},{4,1},{5,4},{8,5},{9,8},{12,9},{13,12},{14,13},{15,14},{10,1... | collective-permute-start | bytes 1179656 | tf_op jit(solution)/shard_map/while/body/eval_jaxpr/ppermute | solution.py:95
  104.6 3.0 %convolution_bitcast_fusion.2 = f32[256,256]{0,1:T(8,128)S(1)} fusion(bf16[1024,256]{1,0:T(8,128)(2,1)} %get-tuple-element.229, bf16[1024,1024]{1,0:T(8,128)(2,1)} %get-tuple-element.228, f32[1024]{0:T(1024)S(1)} %get-tuple-element.227, f32[256]{0:T(256)S(1)} %multiply_reduce_fusion.4, bf16[128,1024]{1,0:T(8,128)(2,1)S(1)} %slice.103, ...), kind=kOutput, calls=%fused_computation.4.clone.1 | convolution fusion | flops 675020800 | bytes 3412992 | tf_op jit(solution)/shard_map/while/body/eval_jaxpr/dot_general | solution.py:42
  107.6 2.1 %collective-permute-done.1 = bf16[192,1024]{1,0:T(8,128)(2,1)S(1)} collective-permute-done((bf16[192,1024]{1,0:T(8,128)(2,1)S(1)}, bf16[192,1024]{1,0:T(8,128)(2,1)S(1)}, u32[]{:S(2)}, u32[]{:S(2)}) %collective-permute-start.1) | collective-permute-done | bytes 393248 | tf_op jit(solution)/shard_map/while/body/eval_jaxpr/ppermute | solution.py:95
  112.7 3.0 %convolution_bitcast_fusion.2 = f32[256,256]{0,1:T(8,128)S(1)} fusion(bf16[1024,256]{1,0:T(8,128)(2,1)} %get-tuple-element.229, bf16[1024,1024]{1,0:T(8,128)(2,1)} %get-tuple-element.228, f32[1024]{0:T(1024)S(1)} %get-tuple-element.227, f32[256]{0:T(256)S(1)} %multiply_reduce_fusion.4, bf16[128,1024]{1,0:T(8,128)(2,1)S(1)} %slice.103, ...), kind=kOutput, calls=%fused_computation.4.clone.1 | convolution fusion | flops 675020800 | bytes 3412992 | tf_op jit(solution)/shard_map/while/body/eval_jaxpr/dot_general | solution.py:42
  115.7 2.1 %collective-permute-done.1 = bf16[192,1024]{1,0:T(8,128)(2,1)S(1)} collective-permute-done((bf16[192,1024]{1,0:T(8,128)(2,1)S(1)}, bf16[192,1024]{1,0:T(8,128)(2,1)S(1)}, u32[]{:S(2)}, u32[]{:S(2)}) %collective-permute-start.1) | collective-permute-done | bytes 393248 | tf_op jit(solution)/shard_map/while/body/eval_jaxpr/ppermute | solution.py:95
  120.7 3.0 %convolution_bitcast_fusion.2 = f32[256,256]{0,1:T(8,128)S(1)} fusion(bf16[1024,256]{1,0:T(8,128)(2,1)} %get-tuple-element.229, bf16[1024,1024]{1,0:T(8,128)(2,1)} %get-tuple-element.228, f32[1024]{0:T(1024)S(1)} %get-tuple-element.227, f32[256]{0:T(256)S(1)} %multiply_reduce_fusion.4, bf16[128,1024]{1,0:T(8,128)(2,1)S(1)} %slice.103, ...), kind=kOutput, calls=%fused_computation.4.clone.1 | convolution fusion | flops 675020800 | bytes 3412992 | tf_op jit(solution)/shard_map/while/body/eval_jaxpr/dot_general | solution.py:42
  123.7 2.1 %collective-permute-done.1 = bf16[192,1024]{1,0:T(8,128)(2,1)S(1)} collective-permute-done((bf16[192,1024]{1,0:T(8,128)(2,1)S(1)}, bf16[192,1024]{1,0:T(8,128)(2,1)S(1)}, u32[]{:S(2)}, u32[]{:S(2)}) %collective-permute-start.1) | collective-permute-done | bytes 393248 | tf_op jit(solution)/shard_map/while/body/eval_jaxpr/ppermute | solution.py:95
  128.7 3.0 %convolution_bitcast_fusion.2 = f32[256,256]{0,1:T(8,128)S(1)} fusion(bf16[1024,256]{1,0:T(8,128)(2,1)} %get-tuple-element.229, bf16[1024,1024]{1,0:T(8,128)(2,1)} %get-tuple-element.228, f32[1024]{0:T(1024)S(1)} %get-tuple-element.227, f32[256]{0:T(256)S(1)} %multiply_reduce_fusion.4, bf16[128,1024]{1,0:T(8,128)(2,1)S(1)} %slice.103, ...), kind=kOutput, calls=%fused_computation.4.clone.1 | convolution fusion | flops 675020800 | bytes 3412992 | tf_op jit(solution)/shard_map/while/body/eval_jaxpr/dot_general | solution.py:42
  131.8 2.1 %collective-permute-done.1 = bf16[192,1024]{1,0:T(8,128)(2,1)S(1)} collective-permute-done((bf16[192,1024]{1,0:T(8,128)(2,1)S(1)}, bf16[192,1024]{1,0:T(8,128)(2,1)S(1)}, u32[]{:S(2)}, u32[]{:S(2)}) %collective-permute-start.1) | collective-permute-done | bytes 393248 | tf_op jit(solution)/shard_map/while/body/eval_jaxpr/ppermute | solution.py:95
  138.0 2.7 %collective-permute-done.5 = f32[256,128]{1,0:T(8,128)S(1)} collective-permute-done((f32[256,128]{1,0:T(8,128)S(1)}, f32[256,128]{1,0:T(8,128)S(1)}, u32[]{:S(2)}, u32[]{:S(2)}) %collective-permute-start.5) | collective-permute-done | bytes 131104 | tf_op jit(solution)/shard_map/ppermute | solution.py:95
  140.7 2.6 %maximum_add_fusion = f32[256,256]{1,0:T(8,128)S(1)} fusion(f32[256,128]{1,0:T(8,128)S(1)} %collective-permute-done.5, f32[256,128]{1,0:T(8,128)S(1)} %collective-permute-done.4, bf16[1024,256]{1,0:T(8,128)(2,1)} %add_convert_fusion, bf16[256,1024]{1,0:T(8,128)(2,1)} %copy-done.2, bf16[1024,1024]{1,0:T(8,128)(2,1)S(1)} %copy-done.1, ...), kind=kOutput, calls=%fused_computation.54 | convolution fusion | flops 674103296 | bytes 3675136 | tf_op jit(solution)/shard_map/dot_general | solution.py:42
  144.4 4.1 %collective-permute-done.6 = f32[2,2,2,16,256]{4,3,2,1,0:T(8,128)S(1)} collective-permute-done((f32[2,2,2,16,256]{4,3,2,1,0:T(8,128)S(1)}, f32[2,2,2,16,256]{4,3,2,1,0:T(8,128)S(1)}, u32[]{:S(2)}, u32[]{:S(2)}) %collective-permute-start.6) | collective-permute-done | bytes 131104 | tf_op jit(solution)/shard_map/ppermute | solution.py:62
  150.4 2.3 %collective-permute-done.7 = f32[2,2,16,256]{3,2,1,0:T(8,128)S(1)} collective-permute-done((f32[2,2,16,256]{3,2,1,0:T(8,128)S(1)}, f32[2,2,16,256]{3,2,1,0:T(8,128)S(1)}, u32[]{:S(2)}, u32[]{:S(2)}) %collective-permute-start.7) | collective-permute-done | bytes 65568 | tf_op jit(solution)/shard_map/ppermute | solution.py:62
  152.8 3.2 %collective-permute-start.8 = (f32[2,16,256]{2,1,0:T(8,128)S(1)}, f32[2,16,256]{2,1,0:T(8,128)S(1)}, u32[]{:S(2)}, u32[]{:S(2)}) collective-permute-start(f32[2,16,256]{2,1,0:T(8,128)S(1)} %dynamic-slice_bitcast_fusion.2), channel_id=1, source_target_pairs={{0,128},{16,144},{32,160},{48,176},{64,192},{80,208},{96,224},{112... | collective-permute-start | bytes 98312 | tf_op jit(solution)/shard_map/ppermute | solution.py:62
  157.3 7.6 %collective-permute-start.9 = (f32[16,256]{1,0:T(8,128)S(1)}, f32[16,256]{1,0:T(8,128)S(1)}, u32[]{:S(2)}, u32[]{:S(2)}) collective-permute-start(f32[16,256]{1,0:T(8,128)S(1)} %dynamic-slice_bitcast_fusion.3), channel_id=1, source_target_pairs={{0,64},{16,80},{32,96},{48,112},{64,0},{80,16},{96,32},{112,48},{1... | collective-permute-start | bytes 49160 | tf_op jit(solution)/shard_map/ppermute | solution.py:62
  (355 shorter events, 42.2 us)
Async XLA Ops:
  1.2 5.5 %copy-start.4 = (s32[1024,8]{0,1:T(8,128)S(1)}, s32[1024,8]{0,1:T(8,128)}, u32[]{:S(2)}) copy-start(s32[1024,8]{0,1:T(8,128)} %param.8) | copy-start | bytes 98308
  2.7 2.8 %copy-start.2 = (bf16[256,1024]{1,0:T(8,128)(2,1)}, bf16[256,1024]{1,0:T(8,128)(2,1)S(1)}, u32[]{:S(2)}) copy-start(bf16[256,1024]{1,0:T(8,128)(2,1)S(1)} %get-tuple-element.130) | copy-start | bytes 1572868
  2.7 4.2 %copy-start.3 = (s32[1024,256]{1,0:T(8,128)S(1)}, s32[1024,256]{1,0:T(8,128)}, u32[]{:S(2)}) copy-start(s32[1024,256]{1,0:T(8,128)} %param.9) | copy-start | bytes 3145732
  2.9 9.3 %collective-permute-start.2 = (bf16[192,1024]{1,0:T(8,128)(2,1)S(1)}, bf16[192,1024]{1,0:T(8,128)(2,1)S(1)}, u32[]{:S(2)}, u32[]{:S(2)}) collective-permute-start(bf16[192,1024]{1,0:T(8,128)(2,1)S(1)} %get-tuple-element.142), channel_id=1, source_target_pairs={{0,1},{1,4},{4,5},{5,8},{8,9},{9,12},{12,13},{13,14},{14,15},{15,1... | collective-permute-start | bytes 1179656 | tf_op jit(solution)/shard_map/ppermute | solution.py:95
  5.5 7.4 %collective-permute-start.3 = (bf16[192,1024]{1,0:T(8,128)(2,1)S(1)}, bf16[192,1024]{1,0:T(8,128)(2,1)S(1)}, u32[]{:S(2)}, u32[]{:S(2)}) collective-permute-start(bf16[192,1024]{1,0:T(8,128)(2,1)S(1)} %get-tuple-element.141), channel_id=1, source_target_pairs={{1,0},{4,1},{5,4},{8,5},{9,8},{12,9},{13,12},{14,13},{15,14},{10,1... | collective-permute-start | bytes 1179656 | tf_op jit(solution)/shard_map/ppermute | solution.py:95
  7.9 2.2 %copy-start = (s32[1024,1024]{1,0:T(8,128)S(1)}, s32[1024,1024]{1,0:T(8,128)}, u32[]{:S(2)}) copy-start(s32[1024,1024]{1,0:T(8,128)} %param.7) | copy-start | bytes 12582916
  13.3 7.6 %collective-permute-start.1 = (bf16[192,1024]{1,0:T(8,128)(2,1)S(1)}, bf16[192,1024]{1,0:T(8,128)(2,1)S(1)}, u32[]{:S(2)}, u32[]{:S(2)}) collective-permute-start(bf16[192,1024]{1,0:T(8,128)(2,1)S(1)} %pad_maximum_fusion.14), channel_id=1, source_target_pairs={{1,0},{4,1},{5,4},{8,5},{9,8},{12,9},{13,12},{14,13},{15,14},{10,1... | collective-permute-start | bytes 1179656 | tf_op jit(solution)/shard_map/while/body/eval_jaxpr/ppermute | solution.py:95
  14.1 6.8 %collective-permute-start = (bf16[192,1024]{1,0:T(8,128)(2,1)S(1)}, bf16[192,1024]{1,0:T(8,128)(2,1)S(1)}, u32[]{:S(2)}, u32[]{:S(2)}) collective-permute-start(bf16[192,1024]{1,0:T(8,128)(2,1)S(1)} %pad_maximum_fusion.13), channel_id=1, source_target_pairs={{0,1},{1,4},{4,5},{5,8},{8,9},{9,12},{12,13},{13,14},{14,15},{15,1... | collective-permute-start | bytes 1179656 | tf_op jit(solution)/shard_map/while/body/eval_jaxpr/ppermute | solution.py:95
  21.2 7.7 %collective-permute-start.1 = (bf16[192,1024]{1,0:T(8,128)(2,1)S(1)}, bf16[192,1024]{1,0:T(8,128)(2,1)S(1)}, u32[]{:S(2)}, u32[]{:S(2)}) collective-permute-start(bf16[192,1024]{1,0:T(8,128)(2,1)S(1)} %pad_maximum_fusion.14), channel_id=1, source_target_pairs={{1,0},{4,1},{5,4},{8,5},{9,8},{12,9},{13,12},{14,13},{15,14},{10,1... | collective-permute-start | bytes 1179656 | tf_op jit(solution)/shard_map/while/body/eval_jaxpr/ppermute | solution.py:95
  23.9 5.0 %collective-permute-start = (bf16[192,1024]{1,0:T(8,128)(2,1)S(1)}, bf16[192,1024]{1,0:T(8,128)(2,1)S(1)}, u32[]{:S(2)}, u32[]{:S(2)}) collective-permute-start(bf16[192,1024]{1,0:T(8,128)(2,1)S(1)} %pad_maximum_fusion.13), channel_id=1, source_target_pairs={{0,1},{1,4},{4,5},{5,8},{8,9},{9,12},{12,13},{13,14},{14,15},{15,1... | collective-permute-start | bytes 1179656 | tf_op jit(solution)/shard_map/while/body/eval_jaxpr/ppermute | solution.py:95
  29.3 8.1 %collective-permute-start.1 = (bf16[192,1024]{1,0:T(8,128)(2,1)S(1)}, bf16[192,1024]{1,0:T(8,128)(2,1)S(1)}, u32[]{:S(2)}, u32[]{:S(2)}) collective-permute-start(bf16[192,1024]{1,0:T(8,128)(2,1)S(1)} %pad_maximum_fusion.14), channel_id=1, source_target_pairs={{1,0},{4,1},{5,4},{8,5},{9,8},{12,9},{13,12},{14,13},{15,14},{10,1... | collective-permute-start | bytes 1179656 | tf_op jit(solution)/shard_map/while/body/eval_jaxpr/ppermute | solution.py:95
  31.9 5.4 %collective-permute-start = (bf16[192,1024]{1,0:T(8,128)(2,1)S(1)}, bf16[192,1024]{1,0:T(8,128)(2,1)S(1)}, u32[]{:S(2)}, u32[]{:S(2)}) collective-permute-start(bf16[192,1024]{1,0:T(8,128)(2,1)S(1)} %pad_maximum_fusion.13), channel_id=1, source_target_pairs={{0,1},{1,4},{4,5},{5,8},{8,9},{9,12},{12,13},{13,14},{14,15},{15,1... | collective-permute-start | bytes 1179656 | tf_op jit(solution)/shard_map/while/body/eval_jaxpr/ppermute | solution.py:95
  37.7 7.7 %collective-permute-start.1 = (bf16[192,1024]{1,0:T(8,128)(2,1)S(1)}, bf16[192,1024]{1,0:T(8,128)(2,1)S(1)}, u32[]{:S(2)}, u32[]{:S(2)}) collective-permute-start(bf16[192,1024]{1,0:T(8,128)(2,1)S(1)} %pad_maximum_fusion.14), channel_id=1, source_target_pairs={{1,0},{4,1},{5,4},{8,5},{9,8},{12,9},{13,12},{14,13},{15,14},{10,1... | collective-permute-start | bytes 1179656 | tf_op jit(solution)/shard_map/while/body/eval_jaxpr/ppermute | solution.py:95
  40.0 5.4 %collective-permute-start = (bf16[192,1024]{1,0:T(8,128)(2,1)S(1)}, bf16[192,1024]{1,0:T(8,128)(2,1)S(1)}, u32[]{:S(2)}, u32[]{:S(2)}) collective-permute-start(bf16[192,1024]{1,0:T(8,128)(2,1)S(1)} %pad_maximum_fusion.13), channel_id=1, source_target_pairs={{0,1},{1,4},{4,5},{5,8},{8,9},{9,12},{12,13},{13,14},{14,15},{15,1... | collective-permute-start | bytes 1179656 | tf_op jit(solution)/shard_map/while/body/eval_jaxpr/ppermute | solution.py:95
  45.7 7.7 %collective-permute-start.1 = (bf16[192,1024]{1,0:T(8,128)(2,1)S(1)}, bf16[192,1024]{1,0:T(8,128)(2,1)S(1)}, u32[]{:S(2)}, u32[]{:S(2)}) collective-permute-start(bf16[192,1024]{1,0:T(8,128)(2,1)S(1)} %pad_maximum_fusion.14), channel_id=1, source_target_pairs={{1,0},{4,1},{5,4},{8,5},{9,8},{12,9},{13,12},{14,13},{15,14},{10,1... | collective-permute-start | bytes 1179656 | tf_op jit(solution)/shard_map/while/body/eval_jaxpr/ppermute | solution.py:95
  48.0 5.4 %collective-permute-start = (bf16[192,1024]{1,0:T(8,128)(2,1)S(1)}, bf16[192,1024]{1,0:T(8,128)(2,1)S(1)}, u32[]{:S(2)}, u32[]{:S(2)}) collective-permute-start(bf16[192,1024]{1,0:T(8,128)(2,1)S(1)} %pad_maximum_fusion.13), channel_id=1, source_target_pairs={{0,1},{1,4},{4,5},{5,8},{8,9},{9,12},{12,13},{13,14},{14,15},{15,1... | collective-permute-start | bytes 1179656 | tf_op jit(solution)/shard_map/while/body/eval_jaxpr/ppermute | solution.py:95
  53.8 7.7 %collective-permute-start.1 = (bf16[192,1024]{1,0:T(8,128)(2,1)S(1)}, bf16[192,1024]{1,0:T(8,128)(2,1)S(1)}, u32[]{:S(2)}, u32[]{:S(2)}) collective-permute-start(bf16[192,1024]{1,0:T(8,128)(2,1)S(1)} %pad_maximum_fusion.14), channel_id=1, source_target_pairs={{1,0},{4,1},{5,4},{8,5},{9,8},{12,9},{13,12},{14,13},{15,14},{10,1... | collective-permute-start | bytes 1179656 | tf_op jit(solution)/shard_map/while/body/eval_jaxpr/ppermute | solution.py:95
  56.1 5.4 %collective-permute-start = (bf16[192,1024]{1,0:T(8,128)(2,1)S(1)}, bf16[192,1024]{1,0:T(8,128)(2,1)S(1)}, u32[]{:S(2)}, u32[]{:S(2)}) collective-permute-start(bf16[192,1024]{1,0:T(8,128)(2,1)S(1)} %pad_maximum_fusion.13), channel_id=1, source_target_pairs={{0,1},{1,4},{4,5},{5,8},{8,9},{9,12},{12,13},{13,14},{14,15},{15,1... | collective-permute-start | bytes 1179656 | tf_op jit(solution)/shard_map/while/body/eval_jaxpr/ppermute | solution.py:95
  61.8 7.7 %collective-permute-start.1 = (bf16[192,1024]{1,0:T(8,128)(2,1)S(1)}, bf16[192,1024]{1,0:T(8,128)(2,1)S(1)}, u32[]{:S(2)}, u32[]{:S(2)}) collective-permute-start(bf16[192,1024]{1,0:T(8,128)(2,1)S(1)} %pad_maximum_fusion.14), channel_id=1, source_target_pairs={{1,0},{4,1},{5,4},{8,5},{9,8},{12,9},{13,12},{14,13},{15,14},{10,1... | collective-permute-start | bytes 1179656 | tf_op jit(solution)/shard_map/while/body/eval_jaxpr/ppermute | solution.py:95
  64.1 5.4 %collective-permute-start = (bf16[192,1024]{1,0:T(8,128)(2,1)S(1)}, bf16[192,1024]{1,0:T(8,128)(2,1)S(1)}, u32[]{:S(2)}, u32[]{:S(2)}) collective-permute-start(bf16[192,1024]{1,0:T(8,128)(2,1)S(1)} %pad_maximum_fusion.13), channel_id=1, source_target_pairs={{0,1},{1,4},{4,5},{5,8},{8,9},{9,12},{12,13},{13,14},{14,15},{15,1... | collective-permute-start | bytes 1179656 | tf_op jit(solution)/shard_map/while/body/eval_jaxpr/ppermute | solution.py:95
  69.9 7.7 %collective-permute-start.1 = (bf16[192,1024]{1,0:T(8,128)(2,1)S(1)}, bf16[192,1024]{1,0:T(8,128)(2,1)S(1)}, u32[]{:S(2)}, u32[]{:S(2)}) collective-permute-start(bf16[192,1024]{1,0:T(8,128)(2,1)S(1)} %pad_maximum_fusion.14), channel_id=1, source_target_pairs={{1,0},{4,1},{5,4},{8,5},{9,8},{12,9},{13,12},{14,13},{15,14},{10,1... | collective-permute-start | bytes 1179656 | tf_op jit(solution)/shard_map/while/body/eval_jaxpr/ppermute | solution.py:95
  72.2 5.4 %collective-permute-start = (bf16[192,1024]{1,0:T(8,128)(2,1)S(1)}, bf16[192,1024]{1,0:T(8,128)(2,1)S(1)}, u32[]{:S(2)}, u32[]{:S(2)}) collective-permute-start(bf16[192,1024]{1,0:T(8,128)(2,1)S(1)} %pad_maximum_fusion.13), channel_id=1, source_target_pairs={{0,1},{1,4},{4,5},{5,8},{8,9},{9,12},{12,13},{13,14},{14,15},{15,1... | collective-permute-start | bytes 1179656 | tf_op jit(solution)/shard_map/while/body/eval_jaxpr/ppermute | solution.py:95
  77.9 7.7 %collective-permute-start.1 = (bf16[192,1024]{1,0:T(8,128)(2,1)S(1)}, bf16[192,1024]{1,0:T(8,128)(2,1)S(1)}, u32[]{:S(2)}, u32[]{:S(2)}) collective-permute-start(bf16[192,1024]{1,0:T(8,128)(2,1)S(1)} %pad_maximum_fusion.14), channel_id=1, source_target_pairs={{1,0},{4,1},{5,4},{8,5},{9,8},{12,9},{13,12},{14,13},{15,14},{10,1... | collective-permute-start | bytes 1179656 | tf_op jit(solution)/shard_map/while/body/eval_jaxpr/ppermute | solution.py:95
  80.2 5.4 %collective-permute-start = (bf16[192,1024]{1,0:T(8,128)(2,1)S(1)}, bf16[192,1024]{1,0:T(8,128)(2,1)S(1)}, u32[]{:S(2)}, u32[]{:S(2)}) collective-permute-start(bf16[192,1024]{1,0:T(8,128)(2,1)S(1)} %pad_maximum_fusion.13), channel_id=1, source_target_pairs={{0,1},{1,4},{4,5},{5,8},{8,9},{9,12},{12,13},{13,14},{14,15},{15,1... | collective-permute-start | bytes 1179656 | tf_op jit(solution)/shard_map/while/body/eval_jaxpr/ppermute | solution.py:95
  86.0 7.7 %collective-permute-start.1 = (bf16[192,1024]{1,0:T(8,128)(2,1)S(1)}, bf16[192,1024]{1,0:T(8,128)(2,1)S(1)}, u32[]{:S(2)}, u32[]{:S(2)}) collective-permute-start(bf16[192,1024]{1,0:T(8,128)(2,1)S(1)} %pad_maximum_fusion.14), channel_id=1, source_target_pairs={{1,0},{4,1},{5,4},{8,5},{9,8},{12,9},{13,12},{14,13},{15,14},{10,1... | collective-permute-start | bytes 1179656 | tf_op jit(solution)/shard_map/while/body/eval_jaxpr/ppermute | solution.py:95
  88.3 5.4 %collective-permute-start = (bf16[192,1024]{1,0:T(8,128)(2,1)S(1)}, bf16[192,1024]{1,0:T(8,128)(2,1)S(1)}, u32[]{:S(2)}, u32[]{:S(2)}) collective-permute-start(bf16[192,1024]{1,0:T(8,128)(2,1)S(1)} %pad_maximum_fusion.13), channel_id=1, source_target_pairs={{0,1},{1,4},{4,5},{5,8},{8,9},{9,12},{12,13},{13,14},{14,15},{15,1... | collective-permute-start | bytes 1179656 | tf_op jit(solution)/shard_map/while/body/eval_jaxpr/ppermute | solution.py:95
  94.0 7.7 %collective-permute-start.1 = (bf16[192,1024]{1,0:T(8,128)(2,1)S(1)}, bf16[192,1024]{1,0:T(8,128)(2,1)S(1)}, u32[]{:S(2)}, u32[]{:S(2)}) collective-permute-start(bf16[192,1024]{1,0:T(8,128)(2,1)S(1)} %pad_maximum_fusion.14), channel_id=1, source_target_pairs={{1,0},{4,1},{5,4},{8,5},{9,8},{12,9},{13,12},{14,13},{15,14},{10,1... | collective-permute-start | bytes 1179656 | tf_op jit(solution)/shard_map/while/body/eval_jaxpr/ppermute | solution.py:95
  96.3 5.4 %collective-permute-start = (bf16[192,1024]{1,0:T(8,128)(2,1)S(1)}, bf16[192,1024]{1,0:T(8,128)(2,1)S(1)}, u32[]{:S(2)}, u32[]{:S(2)}) collective-permute-start(bf16[192,1024]{1,0:T(8,128)(2,1)S(1)} %pad_maximum_fusion.13), channel_id=1, source_target_pairs={{0,1},{1,4},{4,5},{5,8},{8,9},{9,12},{12,13},{13,14},{14,15},{15,1... | collective-permute-start | bytes 1179656 | tf_op jit(solution)/shard_map/while/body/eval_jaxpr/ppermute | solution.py:95
  102.0 7.7 %collective-permute-start.1 = (bf16[192,1024]{1,0:T(8,128)(2,1)S(1)}, bf16[192,1024]{1,0:T(8,128)(2,1)S(1)}, u32[]{:S(2)}, u32[]{:S(2)}) collective-permute-start(bf16[192,1024]{1,0:T(8,128)(2,1)S(1)} %pad_maximum_fusion.14), channel_id=1, source_target_pairs={{1,0},{4,1},{5,4},{8,5},{9,8},{12,9},{13,12},{14,13},{15,14},{10,1... | collective-permute-start | bytes 1179656 | tf_op jit(solution)/shard_map/while/body/eval_jaxpr/ppermute | solution.py:95
  104.3 5.4 %collective-permute-start = (bf16[192,1024]{1,0:T(8,128)(2,1)S(1)}, bf16[192,1024]{1,0:T(8,128)(2,1)S(1)}, u32[]{:S(2)}, u32[]{:S(2)}) collective-permute-start(bf16[192,1024]{1,0:T(8,128)(2,1)S(1)} %pad_maximum_fusion.13), channel_id=1, source_target_pairs={{0,1},{1,4},{4,5},{5,8},{8,9},{9,12},{12,13},{13,14},{14,15},{15,1... | collective-permute-start | bytes 1179656 | tf_op jit(solution)/shard_map/while/body/eval_jaxpr/ppermute | solution.py:95
  110.1 7.7 %collective-permute-start.1 = (bf16[192,1024]{1,0:T(8,128)(2,1)S(1)}, bf16[192,1024]{1,0:T(8,128)(2,1)S(1)}, u32[]{:S(2)}, u32[]{:S(2)}) collective-permute-start(bf16[192,1024]{1,0:T(8,128)(2,1)S(1)} %pad_maximum_fusion.14), channel_id=1, source_target_pairs={{1,0},{4,1},{5,4},{8,5},{9,8},{12,9},{13,12},{14,13},{15,14},{10,1... | collective-permute-start | bytes 1179656 | tf_op jit(solution)/shard_map/while/body/eval_jaxpr/ppermute | solution.py:95
  112.4 5.4 %collective-permute-start = (bf16[192,1024]{1,0:T(8,128)(2,1)S(1)}, bf16[192,1024]{1,0:T(8,128)(2,1)S(1)}, u32[]{:S(2)}, u32[]{:S(2)}) collective-permute-start(bf16[192,1024]{1,0:T(8,128)(2,1)S(1)} %pad_maximum_fusion.13), channel_id=1, source_target_pairs={{0,1},{1,4},{4,5},{5,8},{8,9},{9,12},{12,13},{13,14},{14,15},{15,1... | collective-permute-start | bytes 1179656 | tf_op jit(solution)/shard_map/while/body/eval_jaxpr/ppermute | solution.py:95
  118.1 7.7 %collective-permute-start.1 = (bf16[192,1024]{1,0:T(8,128)(2,1)S(1)}, bf16[192,1024]{1,0:T(8,128)(2,1)S(1)}, u32[]{:S(2)}, u32[]{:S(2)}) collective-permute-start(bf16[192,1024]{1,0:T(8,128)(2,1)S(1)} %pad_maximum_fusion.14), channel_id=1, source_target_pairs={{1,0},{4,1},{5,4},{8,5},{9,8},{12,9},{13,12},{14,13},{15,14},{10,1... | collective-permute-start | bytes 1179656 | tf_op jit(solution)/shard_map/while/body/eval_jaxpr/ppermute | solution.py:95
  120.4 5.4 %collective-permute-start = (bf16[192,1024]{1,0:T(8,128)(2,1)S(1)}, bf16[192,1024]{1,0:T(8,128)(2,1)S(1)}, u32[]{:S(2)}, u32[]{:S(2)}) collective-permute-start(bf16[192,1024]{1,0:T(8,128)(2,1)S(1)} %pad_maximum_fusion.13), channel_id=1, source_target_pairs={{0,1},{1,4},{4,5},{5,8},{8,9},{9,12},{12,13},{13,14},{14,15},{15,1... | collective-permute-start | bytes 1179656 | tf_op jit(solution)/shard_map/while/body/eval_jaxpr/ppermute | solution.py:95
  126.2 7.7 %collective-permute-start.1 = (bf16[192,1024]{1,0:T(8,128)(2,1)S(1)}, bf16[192,1024]{1,0:T(8,128)(2,1)S(1)}, u32[]{:S(2)}, u32[]{:S(2)}) collective-permute-start(bf16[192,1024]{1,0:T(8,128)(2,1)S(1)} %pad_maximum_fusion.14), channel_id=1, source_target_pairs={{1,0},{4,1},{5,4},{8,5},{9,8},{12,9},{13,12},{14,13},{15,14},{10,1... | collective-permute-start | bytes 1179656 | tf_op jit(solution)/shard_map/while/body/eval_jaxpr/ppermute | solution.py:95
  128.5 5.4 %collective-permute-start = (bf16[192,1024]{1,0:T(8,128)(2,1)S(1)}, bf16[192,1024]{1,0:T(8,128)(2,1)S(1)}, u32[]{:S(2)}, u32[]{:S(2)}) collective-permute-start(bf16[192,1024]{1,0:T(8,128)(2,1)S(1)} %pad_maximum_fusion.13), channel_id=1, source_target_pairs={{0,1},{1,4},{4,5},{5,8},{8,9},{9,12},{12,13},{13,14},{14,15},{15,1... | collective-permute-start | bytes 1179656 | tf_op jit(solution)/shard_map/while/body/eval_jaxpr/ppermute | solution.py:95
  133.9 6.8 %copy-start.1 = (bf16[1024,1024]{1,0:T(8,128)(2,1)S(1)}, bf16[1024,1024]{1,0:T(8,128)(2,1)}, u32[]{:S(2)}) copy-start(bf16[1024,1024]{1,0:T(8,128)(2,1)} %get-tuple-element.237) | copy-start | bytes 6291460
  134.1 3.9 %collective-permute-start.4 = (f32[256,128]{1,0:T(8,128)S(1)}, f32[256,128]{1,0:T(8,128)S(1)}, u32[]{:S(2)}, u32[]{:S(2)}) collective-permute-start(f32[256,128]{1,0:T(8,128)S(1)} %add.186), channel_id=1, source_target_pairs={{0,1},{1,4},{4,5},{5,8},{8,9},{9,12},{12,13},{13,14},{14,15},{15,1... | collective-permute-start | bytes 393224 | tf_op jit(solution)/shard_map/ppermute | solution.py:95
  136.2 4.5 %collective-permute-start.5 = (f32[256,128]{1,0:T(8,128)S(1)}, f32[256,128]{1,0:T(8,128)S(1)}, u32[]{:S(2)}, u32[]{:S(2)}) collective-permute-start(f32[256,128]{1,0:T(8,128)S(1)} %add.189), channel_id=1, source_target_pairs={{1,0},{4,1},{5,4},{8,5},{9,8},{12,9},{13,12},{14,13},{15,14},{10,1... | collective-permute-start | bytes 393224 | tf_op jit(solution)/shard_map/ppermute | solution.py:95
  143.3 5.3 %collective-permute-start.6 = (f32[2,2,2,16,256]{4,3,2,1,0:T(8,128)S(1)}, f32[2,2,2,16,256]{4,3,2,1,0:T(8,128)S(1)}, u32[]{:S(2)}, u32[]{:S(2)}) collective-permute-start(f32[2,2,2,16,256]{4,3,2,1,0:T(8,128)S(1)} %dynamic-slice_bitcast_fusion), channel_id=1, source_target_pairs={{0,16},{16,0},{32,48},{48,32},{64,80},{80,64},{96,112},{112,96},{1... | collective-permute-start | bytes 393224 | tf_op jit(solution)/shard_map/ppermute | solution.py:62
  148.6 4.1 %collective-permute-start.7 = (f32[2,2,16,256]{3,2,1,0:T(8,128)S(1)}, f32[2,2,16,256]{3,2,1,0:T(8,128)S(1)}, u32[]{:S(2)}, u32[]{:S(2)}) collective-permute-start(f32[2,2,16,256]{3,2,1,0:T(8,128)S(1)} %dynamic-slice_bitcast_fusion.1), channel_id=1, source_target_pairs={{0,32},{16,48},{32,0},{48,16},{64,96},{80,112},{96,64},{112,80},{1... | collective-permute-start | bytes 196616 | tf_op jit(solution)/shard_map/ppermute | solution.py:62
  152.8 4.5 %collective-permute-start.8 = (f32[2,16,256]{2,1,0:T(8,128)S(1)}, f32[2,16,256]{2,1,0:T(8,128)S(1)}, u32[]{:S(2)}, u32[]{:S(2)}) collective-permute-start(f32[2,16,256]{2,1,0:T(8,128)S(1)} %dynamic-slice_bitcast_fusion.2), channel_id=1, source_target_pairs={{0,128},{16,144},{32,160},{48,176},{64,192},{80,208},{96,224},{112... | collective-permute-start | bytes 98312 | tf_op jit(solution)/shard_map/ppermute | solution.py:62
  157.3 8.7 %collective-permute-start.9 = (f32[16,256]{1,0:T(8,128)S(1)}, f32[16,256]{1,0:T(8,128)S(1)}, u32[]{:S(2)}, u32[]{:S(2)}) collective-permute-start(f32[16,256]{1,0:T(8,128)S(1)} %dynamic-slice_bitcast_fusion.3), channel_id=1, source_target_pairs={{0,64},{16,80},{32,96},{48,112},{64,0},{80,16},{96,32},{112,48},{1... | collective-permute-start | bytes 49160 | tf_op jit(solution)/shard_map/ppermute | solution.py:62

commit v5 on v3

--- a/solution.py
+++ b/solution.py
@@ -42,6 +42,14 @@
     return lax.dot_general(
         rhs_values, matern, (((0,), (1,)), ((), ())), preferred_element_type=jnp.float32
     )
+
+
+def exchange_scatter(sums, axis):
+    size = lax.axis_size(axis)
+    rows, cols = sums.shape
+    pieces = sums.reshape(size, rows // size, cols)
+    pieces = lax.all_to_all(pieces, axis, 0, 0, tiled=False)
+    return jnp.sum(pieces, axis=0)
 
 
 def halving_scatter(sums, axis):
@@ -113,7 +121,7 @@
     part_f, part_b = halves(points_f, points_b)
     sums_f, sums_b = send(sums_f + part_f, sums_b + part_b)
     gathered_sums = own + jnp.concatenate([sums_f, sums_b], axis=1)
-    owned_sums = halving_scatter(gathered_sums, "grp")
+    owned_sums = exchange_scatter(gathered_sums, "grp")
     source_total = src_codes.shape[0] * group_size * cycle_size
     return owned_sums.T * (4.0 / math.sqrt(source_total))
 

time: 157 us -> 157 us (level)
  the two profiles are of different devices: /device:TPU:6 before, /device:TPU:1 now
where the time goes in v5:
time: 157 us; the launch traced here: 155 us
  matrix products  46 us (29%)
  starting transfers between devices  42.7 us (27%)
  waiting for transfers between devices  24.2 us (15%)
  blocking collectives  21.3 us (14%)
  local copies, waits for them, and re-layouts  10.1 us (6%)
  other arithmetic  9.68 us (6%)
    dot_general x16, matrix products, kernel_block(): lax.dot_general(rhs_values, matern, (((0,), (1,)), ((), ())), preferred_e...  46 us
    ppermute x30, waiting for transfers between devices, send(): lax.ppermute(points_b, 'blk', backward)  24.1 us
    ppermute x30, starting transfers between devices, send(): lax.ppermute(points_f, 'blk', forward)  22.8 us
    all_to_all x1, blocking collectives, exchange_scatter(): pieces = lax.all_to_all(pieces, axis, 0, 0, tiled=False)  21.3 us
    ppermute x30, starting transfers between devices, send(): lax.ppermute(points_b, 'blk', backward)  19.9 us
    reduce_sum x17, other arithmetic, squares(): return jnp.sum(widened * widened, axis=1)  5.11 us
    unnamed x22, local copies, waits for them, and re-layouts  3.74 us
  transfers between devices with their start and end apart: 60, of which 16 were waited for; matrix products, arithmetic and copies ran while one was open for 34% of the time, Pallas kernels for 0%

profile of v5, /device:TPU:1, one launch (start us, length us, event | category | flops | bytes accessed | tf_op | source)
XLA Modules:
  0.0 155.1 jit_solution(12518713868063574555)
XLA Ops:
  1.2 1.5 multiply_reduce_fusion.4
  4.3 2.6 %collective-permute-start.4 = (bf16[128,1024]{1,0:T(8,128)(2,1)S(1)}, bf16[128,1024]{1,0:T(8,128)(2,1)S(1)}, u32[]{:S(2)}, u32[]{:S(2)}) collective-permute-start(bf16[128,1024]{1,0:T(8,128)(2,1)S(1)} %get-tuple-element.178), channel_id=1, source_target_pairs={{0,1},{1,4},{4,5},{5,8},{8,9},{9,12},{12,13},{13,14},{14,15},{15,1... | collective-permute-start | bytes 786440 | tf_op jit(solution)/shard_map/ppermute | solution.py:103
  15.3 3.2 %fusion.27 = f32[256,256]{1,0:T(8,128)} fusion(bf16[1024,256]{1,0:T(8,128)(2,1)} %add_convert_fusion, bf16[256,1024]{1,0:T(8,128)(2,1)S(1)} %constant_dynamic-update-slice_fusion.2, bf16[1024,1024]{1,0:T(8,128)(2,1)S(1)} %get-tuple-element.256, f32[256]{0:T(256)S(1)} %multiply_reduce_fusion.3, f32[1024]{0:T(1024)S(1)} %get-tuple-element.255), kind=kOutput, calls=%fused_computation.42 | convolution fusion | flops 673972224 | bytes 3412992 | tf_op jit(solution)/shard_map/dot_general | solution.py:42
  20.6 96.9 %while.22 = (s32[]{:T(128)}, bf16[128,1024]{1,0:T(8,128)(2,1)S(1)}, bf16[128,1024]{1,0:T(8,128)(2,1)S(1)}, f32[256,128]{0,1:T(8,128)S(1)}, f32[256,128]{0,1:T(8,...) while((s32[]{:T(128)}, bf16[128,1024]{1,0:T(8,128)(2,1)S(1)}, ...), condition=%wide.region_5.6_spmd, body=%wide.region_3.5_spmd.sunk | while | flops 674823936 | bytes 12589353 | solution.py:118
  23.8 2.9 %convolution_bitcast_fusion.2 = f32[256,256]{0,1:T(8,128)S(1)} fusion(bf16[1024,256]{1,0:T(8,128)(2,1)S(1)} %copy-done.7, bf16[256,1024]{1,0:T(8,128)(2,1)S(1)} %constant_dynamic-update-slice_fusion.9, bf16[1024,1024]{1,0:T(8,128)(2,1)} %get-tuple-element.278, f32[1024]{0:T(1024)S(1)} %get-tuple-element.277, f32[256]{0:T(256)S(1)} %multiply_reduce_fusion.6), kind=kOutput, calls=%fused_computation.4.clone.1 | convolution fusion | flops 673972224 | bytes 3412992 | tf_op jit(solution)/shard_map/while/body/eval_jaxpr/dot_general | solution.py:42
  26.8 1.6 %collective-permute-done.3 = f32[256,128]{0,1:T(8,128)S(1)} collective-permute-done((f32[256,128]{0,1:T(8,128)S(1)}, f32[256,128]{0,1:T(8,128)S(1)}, u32[]{:S(2)}, u32[]{:S(2)}) %collective-permute-start.3) | collective-permute-done | bytes 131104 | tf_op jit(solution)/shard_map/while/body/eval_jaxpr/ppermute | solution.py:103
  29.1 1.3 collective-permute-start.2
  31.3 2.9 %convolution_bitcast_fusion.2 = f32[256,256]{0,1:T(8,128)S(1)} fusion(bf16[1024,256]{1,0:T(8,128)(2,1)S(1)} %copy-done.7, bf16[256,1024]{1,0:T(8,128)(2,1)S(1)} %constant_dynamic-update-slice_fusion.9, bf16[1024,1024]{1,0:T(8,128)(2,1)} %get-tuple-element.278, f32[1024]{0:T(1024)S(1)} %get-tuple-element.277, f32[256]{0:T(256)S(1)} %multiply_reduce_fusion.6), kind=kOutput, calls=%fused_computation.4.clone.1 | convolution fusion | flops 673972224 | bytes 3412992 | tf_op jit(solution)/shard_map/while/body/eval_jaxpr/dot_general | solution.py:42
  34.2 1.6 %collective-permute-done.3 = f32[256,128]{0,1:T(8,128)S(1)} collective-permute-done((f32[256,128]{0,1:T(8,128)S(1)}, f32[256,128]{0,1:T(8,128)S(1)}, u32[]{:S(2)}, u32[]{:S(2)}) %collective-permute-start.3) | collective-permute-done | bytes 131104 | tf_op jit(solution)/shard_map/while/body/eval_jaxpr/ppermute | solution.py:103
  36.5 1.3 collective-permute-start.2
  38.7 2.9 %convolution_bitcast_fusion.2 = f32[256,256]{0,1:T(8,128)S(1)} fusion(bf16[1024,256]{1,0:T(8,128)(2,1)S(1)} %copy-done.7, bf16[256,1024]{1,0:T(8,128)(2,1)S(1)} %constant_dynamic-update-slice_fusion.9, bf16[1024,1024]{1,0:T(8,128)(2,1)} %get-tuple-element.278, f32[1024]{0:T(1024)S(1)} %get-tuple-element.277, f32[256]{0:T(256)S(1)} %multiply_reduce_fusion.6), kind=kOutput, calls=%fused_computation.4.clone.1 | convolution fusion | flops 673972224 | bytes 3412992 | tf_op jit(solution)/shard_map/while/body/eval_jaxpr/dot_general | solution.py:42
  41.6 1.6 %collective-permute-done.3 = f32[256,128]{0,1:T(8,128)S(1)} collective-permute-done((f32[256,128]{0,1:T(8,128)S(1)}, f32[256,128]{0,1:T(8,128)S(1)}, u32[]{:S(2)}, u32[]{:S(2)}) %collective-permute-start.3) | collective-permute-done | bytes 131104 | tf_op jit(solution)/shard_map/while/body/eval_jaxpr/ppermute | solution.py:103
  43.9 1.3 collective-permute-start.2
  46.1 2.9 %convolution_bitcast_fusion.2 = f32[256,256]{0,1:T(8,128)S(1)} fusion(bf16[1024,256]{1,0:T(8,128)(2,1)S(1)} %copy-done.7, bf16[256,1024]{1,0:T(8,128)(2,1)S(1)} %constant_dynamic-update-slice_fusion.9, bf16[1024,1024]{1,0:T(8,128)(2,1)} %get-tuple-element.278, f32[1024]{0:T(1024)S(1)} %get-tuple-element.277, f32[256]{0:T(256)S(1)} %multiply_reduce_fusion.6), kind=kOutput, calls=%fused_computation.4.clone.1 | convolution fusion | flops 673972224 | bytes 3412992 | tf_op jit(solution)/shard_map/while/body/eval_jaxpr/dot_general | solution.py:42
  49.1 1.6 %collective-permute-done.3 = f32[256,128]{0,1:T(8,128)S(1)} collective-permute-done((f32[256,128]{0,1:T(8,128)S(1)}, f32[256,128]{0,1:T(8,128)S(1)}, u32[]{:S(2)}, u32[]{:S(2)}) %collective-permute-start.3) | collective-permute-done | bytes 131104 | tf_op jit(solution)/shard_map/while/body/eval_jaxpr/ppermute | solution.py:103
  51.4 1.3 collective-permute-start.2
  53.6 2.9 %convolution_bitcast_fusion.2 = f32[256,256]{0,1:T(8,128)S(1)} fusion(bf16[1024,256]{1,0:T(8,128)(2,1)S(1)} %copy-done.7, bf16[256,1024]{1,0:T(8,128)(2,1)S(1)} %constant_dynamic-update-slice_fusion.9, bf16[1024,1024]{1,0:T(8,128)(2,1)} %get-tuple-element.278, f32[1024]{0:T(1024)S(1)} %get-tuple-element.277, f32[256]{0:T(256)S(1)} %multiply_reduce_fusion.6), kind=kOutput, calls=%fused_computation.4.clone.1 | convolution fusion | flops 673972224 | bytes 3412992 | tf_op jit(solution)/shard_map/while/body/eval_jaxpr/dot_general | solution.py:42
  56.5 1.6 %collective-permute-done.3 = f32[256,128]{0,1:T(8,128)S(1)} collective-permute-done((f32[256,128]{0,1:T(8,128)S(1)}, f32[256,128]{0,1:T(8,128)S(1)}, u32[]{:S(2)}, u32[]{:S(2)}) %collective-permute-start.3) | collective-permute-done | bytes 131104 | tf_op jit(solution)/shard_map/while/body/eval_jaxpr/ppermute | solution.py:103
  58.8 1.3 collective-permute-start.2
  61.0 2.9 %convolution_bitcast_fusion.2 = f32[256,256]{0,1:T(8,128)S(1)} fusion(bf16[1024,256]{1,0:T(8,128)(2,1)S(1)} %copy-done.7, bf16[256,1024]{1,0:T(8,128)(2,1)S(1)} %constant_dynamic-update-slice_fusion.9, bf16[1024,1024]{1,0:T(8,128)(2,1)} %get-tuple-element.278, f32[1024]{0:T(1024)S(1)} %get-tuple-element.277, f32[256]{0:T(256)S(1)} %multiply_reduce_fusion.6), kind=kOutput, calls=%fused_computation.4.clone.1 | convolution fusion | flops 673972224 | bytes 3412992 | tf_op jit(solution)/shard_map/while/body/eval_jaxpr/dot_general | solution.py:42
  63.9 1.6 %collective-permute-done.3 = f32[256,128]{0,1:T(8,128)S(1)} collective-permute-done((f32[256,128]{0,1:T(8,128)S(1)}, f32[256,128]{0,1:T(8,128)S(1)}, u32[]{:S(2)}, u32[]{:S(2)}) %collective-permute-start.3) | collective-permute-done | bytes 131104 | tf_op jit(solution)/shard_map/while/body/eval_jaxpr/ppermute | solution.py:103
  66.2 1.3 collective-permute-start.2
  68.4 2.9 %convolution_bitcast_fusion.2 = f32[256,256]{0,1:T(8,128)S(1)} fusion(bf16[1024,256]{1,0:T(8,128)(2,1)S(1)} %copy-done.7, bf16[256,1024]{1,0:T(8,128)(2,1)S(1)} %constant_dynamic-update-slice_fusion.9, bf16[1024,1024]{1,0:T(8,128)(2,1)} %get-tuple-element.278, f32[1024]{0:T(1024)S(1)} %get-tuple-element.277, f32[256]{0:T(256)S(1)} %multiply_reduce_fusion.6), kind=kOutput, calls=%fused_computation.4.clone.1 | convolution fusion | flops 673972224 | bytes 3412992 | tf_op jit(solution)/shard_map/while/body/eval_jaxpr/dot_general | solution.py:42
  71.4 1.6 %collective-permute-done.3 = f32[256,128]{0,1:T(8,128)S(1)} collective-permute-done((f32[256,128]{0,1:T(8,128)S(1)}, f32[256,128]{0,1:T(8,128)S(1)}, u32[]{:S(2)}, u32[]{:S(2)}) %collective-permute-start.3) | collective-permute-done | bytes 131104 | tf_op jit(solution)/shard_map/while/body/eval_jaxpr/ppermute | solution.py:103
  73.7 1.3 collective-permute-start.2
  75.9 2.9 %convolution_bitcast_fusion.2 = f32[256,256]{0,1:T(8,128)S(1)} fusion(bf16[1024,256]{1,0:T(8,128)(2,1)S(1)} %copy-done.7, bf16[256,1024]{1,0:T(8,128)(2,1)S(1)} %constant_dynamic-update-slice_fusion.9, bf16[1024,1024]{1,0:T(8,128)(2,1)} %get-tuple-element.278, f32[1024]{0:T(1024)S(1)} %get-tuple-element.277, f32[256]{0:T(256)S(1)} %multiply_reduce_fusion.6), kind=kOutput, calls=%fused_computation.4.clone.1 | convolution fusion | flops 673972224 | bytes 3412992 | tf_op jit(solution)/shard_map/while/body/eval_jaxpr/dot_general | solution.py:42
  78.8 1.6 %collective-permute-done.3 = f32[256,128]{0,1:T(8,128)S(1)} collective-permute-done((f32[256,128]{0,1:T(8,128)S(1)}, f32[256,128]{0,1:T(8,128)S(1)}, u32[]{:S(2)}, u32[]{:S(2)}) %collective-permute-start.3) | collective-permute-done | bytes 131104 | tf_op jit(solution)/shard_map/while/body/eval_jaxpr/ppermute | solution.py:103
  81.1 1.3 collective-permute-start.2
  83.3 2.9 %convolution_bitcast_fusion.2 = f32[256,256]{0,1:T(8,128)S(1)} fusion(bf16[1024,256]{1,0:T(8,128)(2,1)S(1)} %copy-done.7, bf16[256,1024]{1,0:T(8,128)(2,1)S(1)} %constant_dynamic-update-slice_fusion.9, bf16[1024,1024]{1,0:T(8,128)(2,1)} %get-tuple-element.278, f32[1024]{0:T(1024)S(1)} %get-tuple-element.277, f32[256]{0:T(256)S(1)} %multiply_reduce_fusion.6), kind=kOutput, calls=%fused_computation.4.clone.1 | convolution fusion | flops 673972224 | bytes 3412992 | tf_op jit(solution)/shard_map/while/body/eval_jaxpr/dot_general | solution.py:42
  86.2 1.6 %collective-permute-done.3 = f32[256,128]{0,1:T(8,128)S(1)} collective-permute-done((f32[256,128]{0,1:T(8,128)S(1)}, f32[256,128]{0,1:T(8,128)S(1)}, u32[]{:S(2)}, u32[]{:S(2)}) %collective-permute-start.3) | collective-permute-done | bytes 131104 | tf_op jit(solution)/shard_map/while/body/eval_jaxpr/ppermute | solution.py:103
  88.6 1.3 collective-permute-start.2
  90.7 2.9 %convolution_bitcast_fusion.2 = f32[256,256]{0,1:T(8,128)S(1)} fusion(bf16[1024,256]{1,0:T(8,128)(2,1)S(1)} %copy-done.7, bf16[256,1024]{1,0:T(8,128)(2,1)S(1)} %constant_dynamic-update-slice_fusion.9, bf16[1024,1024]{1,0:T(8,128)(2,1)} %get-tuple-element.278, f32[1024]{0:T(1024)S(1)} %get-tuple-element.277, f32[256]{0:T(256)S(1)} %multiply_reduce_fusion.6), kind=kOutput, calls=%fused_computation.4.clone.1 | convolution fusion | flops 673972224 | bytes 3412992 | tf_op jit(solution)/shard_map/while/body/eval_jaxpr/dot_general | solution.py:42
  93.7 1.6 %collective-permute-done.3 = f32[256,128]{0,1:T(8,128)S(1)} collective-permute-done((f32[256,128]{0,1:T(8,128)S(1)}, f32[256,128]{0,1:T(8,128)S(1)}, u32[]{:S(2)}, u32[]{:S(2)}) %collective-permute-start.3) | collective-permute-done | bytes 131104 | tf_op jit(solution)/shard_map/while/body/eval_jaxpr/ppermute | solution.py:103
  96.0 1.3 collective-permute-start.2
  98.2 2.9 %convolution_bitcast_fusion.2 = f32[256,256]{0,1:T(8,128)S(1)} fusion(bf16[1024,256]{1,0:T(8,128)(2,1)S(1)} %copy-done.7, bf16[256,1024]{1,0:T(8,128)(2,1)S(1)} %constant_dynamic-update-slice_fusion.9, bf16[1024,1024]{1,0:T(8,128)(2,1)} %get-tuple-element.278, f32[1024]{0:T(1024)S(1)} %get-tuple-element.277, f32[256]{0:T(256)S(1)} %multiply_reduce_fusion.6), kind=kOutput, calls=%fused_computation.4.clone.1 | convolution fusion | flops 673972224 | bytes 3412992 | tf_op jit(solution)/shard_map/while/body/eval_jaxpr/dot_general | solution.py:42
  101.1 1.6 %collective-permute-done.3 = f32[256,128]{0,1:T(8,128)S(1)} collective-permute-done((f32[256,128]{0,1:T(8,128)S(1)}, f32[256,128]{0,1:T(8,128)S(1)}, u32[]{:S(2)}, u32[]{:S(2)}) %collective-permute-start.3) | collective-permute-done | bytes 131104 | tf_op jit(solution)/shard_map/while/body/eval_jaxpr/ppermute | solution.py:103
  103.4 1.3 collective-permute-start.2
  105.6 2.9 %convolution_bitcast_fusion.2 = f32[256,256]{0,1:T(8,128)S(1)} fusion(bf16[1024,256]{1,0:T(8,128)(2,1)S(1)} %copy-done.7, bf16[256,1024]{1,0:T(8,128)(2,1)S(1)} %constant_dynamic-update-slice_fusion.9, bf16[1024,1024]{1,0:T(8,128)(2,1)} %get-tuple-element.278, f32[1024]{0:T(1024)S(1)} %get-tuple-element.277, f32[256]{0:T(256)S(1)} %multiply_reduce_fusion.6), kind=kOutput, calls=%fused_computation.4.clone.1 | convolution fusion | flops 673972224 | bytes 3412992 | tf_op jit(solution)/shard_map/while/body/eval_jaxpr/dot_general | solution.py:42
  108.6 1.6 %collective-permute-done.3 = f32[256,128]{0,1:T(8,128)S(1)} collective-permute-done((f32[256,128]{0,1:T(8,128)S(1)}, f32[256,128]{0,1:T(8,128)S(1)}, u32[]{:S(2)}, u32[]{:S(2)}) %collective-permute-start.3) | collective-permute-done | bytes 131104 | tf_op jit(solution)/shard_map/while/body/eval_jaxpr/ppermute | solution.py:103
  110.9 1.3 collective-permute-start.2
  113.0 2.9 %convolution_bitcast_fusion.2 = f32[256,256]{0,1:T(8,128)S(1)} fusion(bf16[1024,256]{1,0:T(8,128)(2,1)S(1)} %copy-done.7, bf16[256,1024]{1,0:T(8,128)(2,1)S(1)} %constant_dynamic-update-slice_fusion.9, bf16[1024,1024]{1,0:T(8,128)(2,1)} %get-tuple-element.278, f32[1024]{0:T(1024)S(1)} %get-tuple-element.277, f32[256]{0:T(256)S(1)} %multiply_reduce_fusion.6), kind=kOutput, calls=%fused_computation.4.clone.1 | convolution fusion | flops 673972224 | bytes 3412992 | tf_op jit(solution)/shard_map/while/body/eval_jaxpr/dot_general | solution.py:42
  116.0 1.6 %collective-permute-done.3 = f32[256,128]{0,1:T(8,128)S(1)} collective-permute-done((f32[256,128]{0,1:T(8,128)S(1)}, f32[256,128]{0,1:T(8,128)S(1)}, u32[]{:S(2)}, u32[]{:S(2)}) %collective-permute-start.3) | collective-permute-done | bytes 131104 | tf_op jit(solution)/shard_map/while/body/eval_jaxpr/ppermute | solution.py:103
  120.4 1.3 collective-permute-start.8
  121.7 2.6 %fusion.25 = f32[256,256]{1,0:T(8,128)S(1)} fusion(bf16[1024,256]{1,0:T(8,128)(2,1)} %get-tuple-element.292, bf16[256,1024]{1,0:T(8,128)(2,1)} %copy-done.5, bf16[1024,1024]{1,0:T(8,128)(2,1)S(1)} %copy-done.2, f32[256]{0:T(256)S(1)} %multiply_reduce_fusion.2, f32[1024]{0:T(1024)S(1)} %get-tuple-element.299), kind=kOutput, calls=%fused_computation.38 | convolution fusion | flops 673972224 | bytes 3412992 | tf_op jit(solution)/shard_map/dot_general | solution.py:42
  125.4 2.6 %collective-permute-start.11 = (f32[256,128]{1,0:T(8,128)S(1)}, f32[256,128]{1,0:T(8,128)S(1)}, u32[]{:S(2)}, u32[]{:S(2)}) collective-permute-start(f32[256,128]{1,0:T(8,128)S(1)} %get-tuple-element.180), channel_id=1, source_target_pairs={{1,0},{4,1},{5,4},{8,5},{9,8},{12,9},{13,12},{14,13},{15,14},{10,1... | collective-permute-start | bytes 393224 | tf_op jit(solution)/shard_map/ppermute | solution.py:103
  128.0 2.2 %collective-permute-done.11 = f32[256,128]{1,0:T(8,128)S(1)} collective-permute-done((f32[256,128]{1,0:T(8,128)S(1)}, f32[256,128]{1,0:T(8,128)S(1)}, u32[]{:S(2)}, u32[]{:S(2)}) %collective-permute-start.11) | collective-permute-done | bytes 131104 | tf_op jit(solution)/shard_map/ppermute | solution.py:103
  130.8 2.3 %maximum_add_fusion = f32[256,256]{1,0:T(8,128)S(1)} fusion(f32[256,128]{1,0:T(8,128)S(1)} %collective-permute-done.11, f32[256,128]{1,0:T(8,128)} %copy-done.10, bf16[1024,256]{1,0:T(8,128)(2,1)S(1)} %copy-done.8, bf16[256,1024]{1,0:T(8,128)(2,1)S(1)} %copy-done.4, bf16[1024,1024]{1,0:T(8,128)(2,1)S(1)} %copy-done.2, f32[1024]{0:T(1024)S(1)} %get-tuple-element.299, ...), kind=kOutput, calls=%fused_computation.68 | convolution fusion | flops 674103296 | bytes 3675136 | tf_op jit(solution)/shard_map/dot_general | solution.py:42
  133.2 21.3 %all_to_all.5 = f32[16,16,256]{2,1,0:T(8,128)S(1)} all-to-all(f32[16,16,256]{2,1,0:T(8,128)S(1)} %bitcast.39), channel_id=1, replica_groups=mesh['grp'=16,'blk'=16] {'grp'}, dimensions={0} | all-to-all | bytes 524288 | tf_op jit(solution)/shard_map/all_to_all | solution.py:51
  (270 shorter events, 40.2 us)
Async XLA Ops:
  4.3 8.0 %collective-permute-start.4 = (bf16[128,1024]{1,0:T(8,128)(2,1)S(1)}, bf16[128,1024]{1,0:T(8,128)(2,1)S(1)}, u32[]{:S(2)}, u32[]{:S(2)}) collective-permute-start(bf16[128,1024]{1,0:T(8,128)(2,1)S(1)} %get-tuple-element.178), channel_id=1, source_target_pairs={{0,1},{1,4},{4,5},{5,8},{8,9},{9,12},{12,13},{13,14},{14,15},{15,1... | collective-permute-start | bytes 786440 | tf_op jit(solution)/shard_map/ppermute | solution.py:103
  6.8 6.1 %collective-permute-start.6 = (bf16[128,1024]{1,0:T(8,128)(2,1)}, bf16[128,1024]{1,0:T(8,128)(2,1)}, u32[]{:S(2)}, u32[]{:S(2)}) collective-permute-start(bf16[128,1024]{1,0:T(8,128)(2,1)} %get-tuple-element.177), channel_id=1, source_target_pairs={{1,0},{4,1},{5,4},{8,5},{9,8},{12,9},{13,12},{14,13},{15,14},{10,1... | collective-permute-start | bytes 786440 | tf_op jit(solution)/shard_map/ppermute | solution.py:103
  14.1 5.6 %collective-permute-start.5 = (bf16[128,1024]{1,0:T(8,128)(2,1)S(1)}, bf16[128,1024]{1,0:T(8,128)(2,1)S(1)}, u32[]{:S(2)}, u32[]{:S(2)}) collective-permute-start(bf16[128,1024]{1,0:T(8,128)(2,1)S(1)} %collective-permute-done.4), channel_id=1, source_target_pairs={{0,1},{1,4},{4,5},{5,8},{8,9},{9,12},{12,13},{13,14},{14,15},{15,1... | collective-permute-start | bytes 786440 | tf_op jit(solution)/shard_map/ppermute | solution.py:103
  14.6 6.0 %collective-permute-start.7 = (bf16[128,1024]{1,0:T(8,128)(2,1)}, bf16[128,1024]{1,0:T(8,128)(2,1)S(1)}, u32[]{:S(2)}, u32[]{:S(2)}) collective-permute-start(bf16[128,1024]{1,0:T(8,128)(2,1)} %collective-permute-done.6), channel_id=1, source_target_pairs={{1,0},{4,1},{5,4},{8,5},{9,8},{12,9},{13,12},{14,13},{15,14},{10,1... | collective-permute-start | bytes 786440 | tf_op jit(solution)/shard_map/ppermute | solution.py:103
  20.7 7.6 %collective-permute-start = (bf16[128,1024]{1,0:T(8,128)(2,1)S(1)}, bf16[128,1024]{1,0:T(8,128)(2,1)S(1)}, u32[]{:S(2)}, u32[]{:S(2)}) collective-permute-start(bf16[128,1024]{1,0:T(8,128)(2,1)S(1)} %copy.30), channel_id=1, source_target_pairs={{0,1},{1,4},{4,5},{5,8},{8,9},{9,12},{12,13},{13,14},{14,15},{15,1... | collective-permute-start | bytes 786440 | tf_op jit(solution)/shard_map/while/body/eval_jaxpr/ppermute | solution.py:103
  20.9 7.4 %collective-permute-start.1 = (bf16[128,1024]{1,0:T(8,128)(2,1)S(1)}, bf16[128,1024]{1,0:T(8,128)(2,1)S(1)}, u32[]{:S(2)}, u32[]{:S(2)}) collective-permute-start(bf16[128,1024]{1,0:T(8,128)(2,1)S(1)} %copy.31), channel_id=1, source_target_pairs={{1,0},{4,1},{5,4},{8,5},{9,8},{12,9},{13,12},{14,13},{15,14},{10,1... | collective-permute-start | bytes 786440 | tf_op jit(solution)/shard_map/while/body/eval_jaxpr/ppermute | solution.py:103
  22.9 5.5 %collective-permute-start.3 = (f32[256,128]{0,1:T(8,128)S(1)}, f32[256,128]{0,1:T(8,128)S(1)}, u32[]{:S(2)}, u32[]{:S(2)}) collective-permute-start(f32[256,128]{0,1:T(8,128)S(1)} %add.269), channel_id=1, source_target_pairs={{1,0},{4,1},{5,4},{8,5},{9,8},{12,9},{13,12},{14,13},{15,14},{10,1... | collective-permute-start | bytes 393224 | tf_op jit(solution)/shard_map/while/body/eval_jaxpr/ppermute | solution.py:103
  28.4 7.4 %collective-permute-start = (bf16[128,1024]{1,0:T(8,128)(2,1)S(1)}, bf16[128,1024]{1,0:T(8,128)(2,1)S(1)}, u32[]{:S(2)}, u32[]{:S(2)}) collective-permute-start(bf16[128,1024]{1,0:T(8,128)(2,1)S(1)} %copy.30), channel_id=1, source_target_pairs={{0,1},{1,4},{4,5},{5,8},{8,9},{9,12},{12,13},{13,14},{14,15},{15,1... | collective-permute-start | bytes 786440 | tf_op jit(solution)/shard_map/while/body/eval_jaxpr/ppermute | solution.py:103
  28.5 7.3 %collective-permute-start.1 = (bf16[128,1024]{1,0:T(8,128)(2,1)S(1)}, bf16[128,1024]{1,0:T(8,128)(2,1)S(1)}, u32[]{:S(2)}, u32[]{:S(2)}) collective-permute-start(bf16[128,1024]{1,0:T(8,128)(2,1)S(1)} %copy.31), channel_id=1, source_target_pairs={{1,0},{4,1},{5,4},{8,5},{9,8},{12,9},{13,12},{14,13},{15,14},{10,1... | collective-permute-start | bytes 786440 | tf_op jit(solution)/shard_map/while/body/eval_jaxpr/ppermute | solution.py:103
  29.1 5.1 %collective-permute-start.2 = (f32[256,128]{0,1:T(8,128)S(1)}, f32[256,128]{0,1:T(8,128)S(1)}, u32[]{:S(2)}, u32[]{:S(2)}) collective-permute-start(f32[256,128]{0,1:T(8,128)S(1)} %add.268), channel_id=1, source_target_pairs={{0,1},{1,4},{4,5},{5,8},{8,9},{9,12},{12,13},{13,14},{14,15},{15,1... | collective-permute-start | bytes 393224 | tf_op jit(solution)/shard_map/while/body/eval_jaxpr/ppermute | solution.py:103
  30.4 5.3 %collective-permute-start.3 = (f32[256,128]{0,1:T(8,128)S(1)}, f32[256,128]{0,1:T(8,128)S(1)}, u32[]{:S(2)}, u32[]{:S(2)}) collective-permute-start(f32[256,128]{0,1:T(8,128)S(1)} %add.269), channel_id=1, source_target_pairs={{1,0},{4,1},{5,4},{8,5},{9,8},{12,9},{13,12},{14,13},{15,14},{10,1... | collective-permute-start | bytes 393224 | tf_op jit(solution)/shard_map/while/body/eval_jaxpr/ppermute | solution.py:103
  35.8 7.4 %collective-permute-start = (bf16[128,1024]{1,0:T(8,128)(2,1)S(1)}, bf16[128,1024]{1,0:T(8,128)(2,1)S(1)}, u32[]{:S(2)}, u32[]{:S(2)}) collective-permute-start(bf16[128,1024]{1,0:T(8,128)(2,1)S(1)} %copy.30), channel_id=1, source_target_pairs={{0,1},{1,4},{4,5},{5,8},{8,9},{9,12},{12,13},{13,14},{14,15},{15,1... | collective-permute-start | bytes 786440 | tf_op jit(solution)/shard_map/while/body/eval_jaxpr/ppermute | solution.py:103
  35.9 7.3 %collective-permute-start.1 = (bf16[128,1024]{1,0:T(8,128)(2,1)S(1)}, bf16[128,1024]{1,0:T(8,128)(2,1)S(1)}, u32[]{:S(2)}, u32[]{:S(2)}) collective-permute-start(bf16[128,1024]{1,0:T(8,128)(2,1)S(1)} %copy.31), channel_id=1, source_target_pairs={{1,0},{4,1},{5,4},{8,5},{9,8},{12,9},{13,12},{14,13},{15,14},{10,1... | collective-permute-start | bytes 786440 | tf_op jit(solution)/shard_map/while/body/eval_jaxpr/ppermute | solution.py:103
  36.5 5.1 %collective-permute-start.2 = (f32[256,128]{0,1:T(8,128)S(1)}, f32[256,128]{0,1:T(8,128)S(1)}, u32[]{:S(2)}, u32[]{:S(2)}) collective-permute-start(f32[256,128]{0,1:T(8,128)S(1)} %add.268), channel_id=1, source_target_pairs={{0,1},{1,4},{4,5},{5,8},{8,9},{9,12},{12,13},{13,14},{14,15},{15,1... | collective-permute-start | bytes 393224 | tf_op jit(solution)/shard_map/while/body/eval_jaxpr/ppermute | solution.py:103
  37.9 5.3 %collective-permute-start.3 = (f32[256,128]{0,1:T(8,128)S(1)}, f32[256,128]{0,1:T(8,128)S(1)}, u32[]{:S(2)}, u32[]{:S(2)}) collective-permute-start(f32[256,128]{0,1:T(8,128)S(1)} %add.269), channel_id=1, source_target_pairs={{1,0},{4,1},{5,4},{8,5},{9,8},{12,9},{13,12},{14,13},{15,14},{10,1... | collective-permute-start | bytes 393224 | tf_op jit(solution)/shard_map/while/body/eval_jaxpr/ppermute | solution.py:103
  43.2 7.4 %collective-permute-start = (bf16[128,1024]{1,0:T(8,128)(2,1)S(1)}, bf16[128,1024]{1,0:T(8,128)(2,1)S(1)}, u32[]{:S(2)}, u32[]{:S(2)}) collective-permute-start(bf16[128,1024]{1,0:T(8,128)(2,1)S(1)} %copy.30), channel_id=1, source_target_pairs={{0,1},{1,4},{4,5},{5,8},{8,9},{9,12},{12,13},{13,14},{14,15},{15,1... | collective-permute-start | bytes 786440 | tf_op jit(solution)/shard_map/while/body/eval_jaxpr/ppermute | solution.py:103
  43.4 7.3 %collective-permute-start.1 = (bf16[128,1024]{1,0:T(8,128)(2,1)S(1)}, bf16[128,1024]{1,0:T(8,128)(2,1)S(1)}, u32[]{:S(2)}, u32[]{:S(2)}) collective-permute-start(bf16[128,1024]{1,0:T(8,128)(2,1)S(1)} %copy.31), channel_id=1, source_target_pairs={{1,0},{4,1},{5,4},{8,5},{9,8},{12,9},{13,12},{14,13},{15,14},{10,1... | collective-permute-start | bytes 786440 | tf_op jit(solution)/shard_map/while/body/eval_jaxpr/ppermute | solution.py:103
  43.9 5.1 %collective-permute-start.2 = (f32[256,128]{0,1:T(8,128)S(1)}, f32[256,128]{0,1:T(8,128)S(1)}, u32[]{:S(2)}, u32[]{:S(2)}) collective-permute-start(f32[256,128]{0,1:T(8,128)S(1)} %add.268), channel_id=1, source_target_pairs={{0,1},{1,4},{4,5},{5,8},{8,9},{9,12},{12,13},{13,14},{14,15},{15,1... | collective-permute-start | bytes 393224 | tf_op jit(solution)/shard_map/while/body/eval_jaxpr/ppermute | solution.py:103
  45.3 5.3 %collective-permute-start.3 = (f32[256,128]{0,1:T(8,128)S(1)}, f32[256,128]{0,1:T(8,128)S(1)}, u32[]{:S(2)}, u32[]{:S(2)}) collective-permute-start(f32[256,128]{0,1:T(8,128)S(1)} %add.269), channel_id=1, source_target_pairs={{1,0},{4,1},{5,4},{8,5},{9,8},{12,9},{13,12},{14,13},{15,14},{10,1... | collective-permute-start | bytes 393224 | tf_op jit(solution)/shard_map/while/body/eval_jaxpr/ppermute | solution.py:103
  50.7 7.4 %collective-permute-start = (bf16[128,1024]{1,0:T(8,128)(2,1)S(1)}, bf16[128,1024]{1,0:T(8,128)(2,1)S(1)}, u32[]{:S(2)}, u32[]{:S(2)}) collective-permute-start(bf16[128,1024]{1,0:T(8,128)(2,1)S(1)} %copy.30), channel_id=1, source_target_pairs={{0,1},{1,4},{4,5},{5,8},{8,9},{9,12},{12,13},{13,14},{14,15},{15,1... | collective-permute-start | bytes 786440 | tf_op jit(solution)/shard_map/while/body/eval_jaxpr/ppermute | solution.py:103
  50.8 7.3 %collective-permute-start.1 = (bf16[128,1024]{1,0:T(8,128)(2,1)S(1)}, bf16[128,1024]{1,0:T(8,128)(2,1)S(1)}, u32[]{:S(2)}, u32[]{:S(2)}) collective-permute-start(bf16[128,1024]{1,0:T(8,128)(2,1)S(1)} %copy.31), channel_id=1, source_target_pairs={{1,0},{4,1},{5,4},{8,5},{9,8},{12,9},{13,12},{14,13},{15,14},{10,1... | collective-permute-start | bytes 786440 | tf_op jit(solution)/shard_map/while/body/eval_jaxpr/ppermute | solution.py:103
  51.4 5.1 %collective-permute-start.2 = (f32[256,128]{0,1:T(8,128)S(1)}, f32[256,128]{0,1:T(8,128)S(1)}, u32[]{:S(2)}, u32[]{:S(2)}) collective-permute-start(f32[256,128]{0,1:T(8,128)S(1)} %add.268), channel_id=1, source_target_pairs={{0,1},{1,4},{4,5},{5,8},{8,9},{9,12},{12,13},{13,14},{14,15},{15,1... | collective-permute-start | bytes 393224 | tf_op jit(solution)/shard_map/while/body/eval_jaxpr/ppermute | solution.py:103
  52.7 5.3 %collective-permute-start.3 = (f32[256,128]{0,1:T(8,128)S(1)}, f32[256,128]{0,1:T(8,128)S(1)}, u32[]{:S(2)}, u32[]{:S(2)}) collective-permute-start(f32[256,128]{0,1:T(8,128)S(1)} %add.269), channel_id=1, source_target_pairs={{1,0},{4,1},{5,4},{8,5},{9,8},{12,9},{13,12},{14,13},{15,14},{10,1... | collective-permute-start | bytes 393224 | tf_op jit(solution)/shard_map/while/body/eval_jaxpr/ppermute | solution.py:103
  58.1 7.4 %collective-permute-start = (bf16[128,1024]{1,0:T(8,128)(2,1)S(1)}, bf16[128,1024]{1,0:T(8,128)(2,1)S(1)}, u32[]{:S(2)}, u32[]{:S(2)}) collective-permute-start(bf16[128,1024]{1,0:T(8,128)(2,1)S(1)} %copy.30), channel_id=1, source_target_pairs={{0,1},{1,4},{4,5},{5,8},{8,9},{9,12},{12,13},{13,14},{14,15},{15,1... | collective-permute-start | bytes 786440 | tf_op jit(solution)/shard_map/while/body/eval_jaxpr/ppermute | solution.py:103
  58.2 7.3 %collective-permute-start.1 = (bf16[128,1024]{1,0:T(8,128)(2,1)S(1)}, bf16[128,1024]{1,0:T(8,128)(2,1)S(1)}, u32[]{:S(2)}, u32[]{:S(2)}) collective-permute-start(bf16[128,1024]{1,0:T(8,128)(2,1)S(1)} %copy.31), channel_id=1, source_target_pairs={{1,0},{4,1},{5,4},{8,5},{9,8},{12,9},{13,12},{14,13},{15,14},{10,1... | collective-permute-start | bytes 786440 | tf_op jit(solution)/shard_map/while/body/eval_jaxpr/ppermute | solution.py:103
  60.2 5.3 %collective-permute-start.3 = (f32[256,128]{0,1:T(8,128)S(1)}, f32[256,128]{0,1:T(8,128)S(1)}, u32[]{:S(2)}, u32[]{:S(2)}) collective-permute-start(f32[256,128]{0,1:T(8,128)S(1)} %add.269), channel_id=1, source_target_pairs={{1,0},{4,1},{5,4},{8,5},{9,8},{12,9},{13,12},{14,13},{15,14},{10,1... | collective-permute-start | bytes 393224 | tf_op jit(solution)/shard_map/while/body/eval_jaxpr/ppermute | solution.py:103
  65.5 7.4 %collective-permute-start = (bf16[128,1024]{1,0:T(8,128)(2,1)S(1)}, bf16[128,1024]{1,0:T(8,128)(2,1)S(1)}, u32[]{:S(2)}, u32[]{:S(2)}) collective-permute-start(bf16[128,1024]{1,0:T(8,128)(2,1)S(1)} %copy.30), channel_id=1, source_target_pairs={{0,1},{1,4},{4,5},{5,8},{8,9},{9,12},{12,13},{13,14},{14,15},{15,1... | collective-permute-start | bytes 786440 | tf_op jit(solution)/shard_map/while/body/eval_jaxpr/ppermute | solution.py:103
  65.7 7.3 %collective-permute-start.1 = (bf16[128,1024]{1,0:T(8,128)(2,1)S(1)}, bf16[128,1024]{1,0:T(8,128)(2,1)S(1)}, u32[]{:S(2)}, u32[]{:S(2)}) collective-permute-start(bf16[128,1024]{1,0:T(8,128)(2,1)S(1)} %copy.31), channel_id=1, source_target_pairs={{1,0},{4,1},{5,4},{8,5},{9,8},{12,9},{13,12},{14,13},{15,14},{10,1... | collective-permute-start | bytes 786440 | tf_op jit(solution)/shard_map/while/body/eval_jaxpr/ppermute | solution.py:103
  67.6 5.3 %collective-permute-start.3 = (f32[256,128]{0,1:T(8,128)S(1)}, f32[256,128]{0,1:T(8,128)S(1)}, u32[]{:S(2)}, u32[]{:S(2)}) collective-permute-start(f32[256,128]{0,1:T(8,128)S(1)} %add.269), channel_id=1, source_target_pairs={{1,0},{4,1},{5,4},{8,5},{9,8},{12,9},{13,12},{14,13},{15,14},{10,1... | collective-permute-start | bytes 393224 | tf_op jit(solution)/shard_map/while/body/eval_jaxpr/ppermute | solution.py:103
  73.0 7.4 %collective-permute-start = (bf16[128,1024]{1,0:T(8,128)(2,1)S(1)}, bf16[128,1024]{1,0:T(8,128)(2,1)S(1)}, u32[]{:S(2)}, u32[]{:S(2)}) collective-permute-start(bf16[128,1024]{1,0:T(8,128)(2,1)S(1)} %copy.30), channel_id=1, source_target_pairs={{0,1},{1,4},{4,5},{5,8},{8,9},{9,12},{12,13},{13,14},{14,15},{15,1... | collective-permute-start | bytes 786440 | tf_op jit(solution)/shard_map/while/body/eval_jaxpr/ppermute | solution.py:103
  73.1 7.3 %collective-permute-start.1 = (bf16[128,1024]{1,0:T(8,128)(2,1)S(1)}, bf16[128,1024]{1,0:T(8,128)(2,1)S(1)}, u32[]{:S(2)}, u32[]{:S(2)}) collective-permute-start(bf16[128,1024]{1,0:T(8,128)(2,1)S(1)} %copy.31), channel_id=1, source_target_pairs={{1,0},{4,1},{5,4},{8,5},{9,8},{12,9},{13,12},{14,13},{15,14},{10,1... | collective-permute-start | bytes 786440 | tf_op jit(solution)/shard_map/while/body/eval_jaxpr/ppermute | solution.py:103
  75.0 5.3 %collective-permute-start.3 = (f32[256,128]{0,1:T(8,128)S(1)}, f32[256,128]{0,1:T(8,128)S(1)}, u32[]{:S(2)}, u32[]{:S(2)}) collective-permute-start(f32[256,128]{0,1:T(8,128)S(1)} %add.269), channel_id=1, source_target_pairs={{1,0},{4,1},{5,4},{8,5},{9,8},{12,9},{13,12},{14,13},{15,14},{10,1... | collective-permute-start | bytes 393224 | tf_op jit(solution)/shard_map/while/body/eval_jaxpr/ppermute | solution.py:103
  80.4 7.4 %collective-permute-start = (bf16[128,1024]{1,0:T(8,128)(2,1)S(1)}, bf16[128,1024]{1,0:T(8,128)(2,1)S(1)}, u32[]{:S(2)}, u32[]{:S(2)}) collective-permute-start(bf16[128,1024]{1,0:T(8,128)(2,1)S(1)} %copy.30), channel_id=1, source_target_pairs={{0,1},{1,4},{4,5},{5,8},{8,9},{9,12},{12,13},{13,14},{14,15},{15,1... | collective-permute-start | bytes 786440 | tf_op jit(solution)/shard_map/while/body/eval_jaxpr/ppermute | solution.py:103
  80.5 7.3 %collective-permute-start.1 = (bf16[128,1024]{1,0:T(8,128)(2,1)S(1)}, bf16[128,1024]{1,0:T(8,128)(2,1)S(1)}, u32[]{:S(2)}, u32[]{:S(2)}) collective-permute-start(bf16[128,1024]{1,0:T(8,128)(2,1)S(1)} %copy.31), channel_id=1, source_target_pairs={{1,0},{4,1},{5,4},{8,5},{9,8},{12,9},{13,12},{14,13},{15,14},{10,1... | collective-permute-start | bytes 786440 | tf_op jit(solution)/shard_map/while/body/eval_jaxpr/ppermute | solution.py:103
  82.5 5.3 %collective-permute-start.3 = (f32[256,128]{0,1:T(8,128)S(1)}, f32[256,128]{0,1:T(8,128)S(1)}, u32[]{:S(2)}, u32[]{:S(2)}) collective-permute-start(f32[256,128]{0,1:T(8,128)S(1)} %add.269), channel_id=1, source_target_pairs={{1,0},{4,1},{5,4},{8,5},{9,8},{12,9},{13,12},{14,13},{15,14},{10,1... | collective-permute-start | bytes 393224 | tf_op jit(solution)/shard_map/while/body/eval_jaxpr/ppermute | solution.py:103
  87.8 7.4 %collective-permute-start = (bf16[128,1024]{1,0:T(8,128)(2,1)S(1)}, bf16[128,1024]{1,0:T(8,128)(2,1)S(1)}, u32[]{:S(2)}, u32[]{:S(2)}) collective-permute-start(bf16[128,1024]{1,0:T(8,128)(2,1)S(1)} %copy.30), channel_id=1, source_target_pairs={{0,1},{1,4},{4,5},{5,8},{8,9},{9,12},{12,13},{13,14},{14,15},{15,1... | collective-permute-start | bytes 786440 | tf_op jit(solution)/shard_map/while/body/eval_jaxpr/ppermute | solution.py:103
  88.0 7.3 %collective-permute-start.1 = (bf16[128,1024]{1,0:T(8,128)(2,1)S(1)}, bf16[128,1024]{1,0:T(8,128)(2,1)S(1)}, u32[]{:S(2)}, u32[]{:S(2)}) collective-permute-start(bf16[128,1024]{1,0:T(8,128)(2,1)S(1)} %copy.31), channel_id=1, source_target_pairs={{1,0},{4,1},{5,4},{8,5},{9,8},{12,9},{13,12},{14,13},{15,14},{10,1... | collective-permute-start | bytes 786440 | tf_op jit(solution)/shard_map/while/body/eval_jaxpr/ppermute | solution.py:103
  89.9 5.3 %collective-permute-start.3 = (f32[256,128]{0,1:T(8,128)S(1)}, f32[256,128]{0,1:T(8,128)S(1)}, u32[]{:S(2)}, u32[]{:S(2)}) collective-permute-start(f32[256,128]{0,1:T(8,128)S(1)} %add.269), channel_id=1, source_target_pairs={{1,0},{4,1},{5,4},{8,5},{9,8},{12,9},{13,12},{14,13},{15,14},{10,1... | collective-permute-start | bytes 393224 | tf_op jit(solution)/shard_map/while/body/eval_jaxpr/ppermute | solution.py:103
  95.3 7.4 %collective-permute-start = (bf16[128,1024]{1,0:T(8,128)(2,1)S(1)}, bf16[128,1024]{1,0:T(8,128)(2,1)S(1)}, u32[]{:S(2)}, u32[]{:S(2)}) collective-permute-start(bf16[128,1024]{1,0:T(8,128)(2,1)S(1)} %copy.30), channel_id=1, source_target_pairs={{0,1},{1,4},{4,5},{5,8},{8,9},{9,12},{12,13},{13,14},{14,15},{15,1... | collective-permute-start | bytes 786440 | tf_op jit(solution)/shard_map/while/body/eval_jaxpr/ppermute | solution.py:103
  95.4 7.3 %collective-permute-start.1 = (bf16[128,1024]{1,0:T(8,128)(2,1)S(1)}, bf16[128,1024]{1,0:T(8,128)(2,1)S(1)}, u32[]{:S(2)}, u32[]{:S(2)}) collective-permute-start(bf16[128,1024]{1,0:T(8,128)(2,1)S(1)} %copy.31), channel_id=1, source_target_pairs={{1,0},{4,1},{5,4},{8,5},{9,8},{12,9},{13,12},{14,13},{15,14},{10,1... | collective-permute-start | bytes 786440 | tf_op jit(solution)/shard_map/while/body/eval_jaxpr/ppermute | solution.py:103
  97.3 5.3 %collective-permute-start.3 = (f32[256,128]{0,1:T(8,128)S(1)}, f32[256,128]{0,1:T(8,128)S(1)}, u32[]{:S(2)}, u32[]{:S(2)}) collective-permute-start(f32[256,128]{0,1:T(8,128)S(1)} %add.269), channel_id=1, source_target_pairs={{1,0},{4,1},{5,4},{8,5},{9,8},{12,9},{13,12},{14,13},{15,14},{10,1... | collective-permute-start | bytes 393224 | tf_op jit(solution)/shard_map/while/body/eval_jaxpr/ppermute | solution.py:103
  102.7 7.4 %collective-permute-start = (bf16[128,1024]{1,0:T(8,128)(2,1)S(1)}, bf16[128,1024]{1,0:T(8,128)(2,1)S(1)}, u32[]{:S(2)}, u32[]{:S(2)}) collective-permute-start(bf16[128,1024]{1,0:T(8,128)(2,1)S(1)} %copy.30), channel_id=1, source_target_pairs={{0,1},{1,4},{4,5},{5,8},{8,9},{9,12},{12,13},{13,14},{14,15},{15,1... | collective-permute-start | bytes 786440 | tf_op jit(solution)/shard_map/while/body/eval_jaxpr/ppermute | solution.py:103
  102.8 7.3 %collective-permute-start.1 = (bf16[128,1024]{1,0:T(8,128)(2,1)S(1)}, bf16[128,1024]{1,0:T(8,128)(2,1)S(1)}, u32[]{:S(2)}, u32[]{:S(2)}) collective-permute-start(bf16[128,1024]{1,0:T(8,128)(2,1)S(1)} %copy.31), channel_id=1, source_target_pairs={{1,0},{4,1},{5,4},{8,5},{9,8},{12,9},{13,12},{14,13},{15,14},{10,1... | collective-permute-start | bytes 786440 | tf_op jit(solution)/shard_map/while/body/eval_jaxpr/ppermute | solution.py:103
  104.8 5.3 %collective-permute-start.3 = (f32[256,128]{0,1:T(8,128)S(1)}, f32[256,128]{0,1:T(8,128)S(1)}, u32[]{:S(2)}, u32[]{:S(2)}) collective-permute-start(f32[256,128]{0,1:T(8,128)S(1)} %add.269), channel_id=1, source_target_pairs={{1,0},{4,1},{5,4},{8,5},{9,8},{12,9},{13,12},{14,13},{15,14},{10,1... | collective-permute-start | bytes 393224 | tf_op jit(solution)/shard_map/while/body/eval_jaxpr/ppermute | solution.py:103
  110.2 7.4 %collective-permute-start = (bf16[128,1024]{1,0:T(8,128)(2,1)S(1)}, bf16[128,1024]{1,0:T(8,128)(2,1)S(1)}, u32[]{:S(2)}, u32[]{:S(2)}) collective-permute-start(bf16[128,1024]{1,0:T(8,128)(2,1)S(1)} %copy.30), channel_id=1, source_target_pairs={{0,1},{1,4},{4,5},{5,8},{8,9},{9,12},{12,13},{13,14},{14,15},{15,1... | collective-permute-start | bytes 786440 | tf_op jit(solution)/shard_map/while/body/eval_jaxpr/ppermute | solution.py:103
  110.3 7.3 %collective-permute-start.1 = (bf16[128,1024]{1,0:T(8,128)(2,1)S(1)}, bf16[128,1024]{1,0:T(8,128)(2,1)S(1)}, u32[]{:S(2)}, u32[]{:S(2)}) collective-permute-start(bf16[128,1024]{1,0:T(8,128)(2,1)S(1)} %copy.31), channel_id=1, source_target_pairs={{1,0},{4,1},{5,4},{8,5},{9,8},{12,9},{13,12},{14,13},{15,14},{10,1... | collective-permute-start | bytes 786440 | tf_op jit(solution)/shard_map/while/body/eval_jaxpr/ppermute | solution.py:103
  112.2 5.3 %collective-permute-start.3 = (f32[256,128]{0,1:T(8,128)S(1)}, f32[256,128]{0,1:T(8,128)S(1)}, u32[]{:S(2)}, u32[]{:S(2)}) collective-permute-start(f32[256,128]{0,1:T(8,128)S(1)} %add.269), channel_id=1, source_target_pairs={{1,0},{4,1},{5,4},{8,5},{9,8},{12,9},{13,12},{14,13},{15,14},{10,1... | collective-permute-start | bytes 393224 | tf_op jit(solution)/shard_map/while/body/eval_jaxpr/ppermute | solution.py:103
  117.8 6.6 %collective-permute-start.10 = (f32[256,128]{1,0:T(8,128)S(1)}, f32[256,128]{1,0:T(8,128)}, u32[]{:S(2)}, u32[]{:S(2)}) collective-permute-start(f32[256,128]{1,0:T(8,128)S(1)} %add.160), channel_id=1, source_target_pairs={{1,0},{4,1},{5,4},{8,5},{9,8},{12,9},{13,12},{14,13},{15,14},{10,1... | collective-permute-start | bytes 393224 | tf_op jit(solution)/shard_map/ppermute | solution.py:103
  (35 other events, 139.6 us)

commit v6 on v3

--- a/solution.py
+++ b/solution.py
@@ -42,6 +42,37 @@
     return lax.dot_general(
         rhs_values, matern, (((0,), (1,)), ((), ())), preferred_element_type=jnp.float32
     )
+
+
+def radix_scatter(sums, axis, groups=((0, 1), (2, 3))):
+    size = lax.axis_size(axis)
+    me = lax.axis_index(axis)
+    bits = size.bit_length() - 1
+    if size != 16:
+        return halving_scatter(sums, axis)
+    rows, cols = sums.shape
+    chunk = rows // size
+    parts = sums.reshape((2,) * bits + (chunk, cols))
+    remaining = list(range(bits - 1, -1, -1))
+
+    def select(values, group):
+        picked = parts
+        for bit in sorted(group, key=remaining.index, reverse=True):
+            picked = lax.dynamic_index_in_dim(picked, values[bit], remaining.index(bit), keepdims=False)
+        return picked
+
+    for group in groups:
+        mine = {bit: (me >> bit) & 1 for bit in group}
+        total = select(mine, group)
+        for code in range(1, 1 << len(group)):
+            offset = sum(((code >> k) & 1) << bit for k, bit in enumerate(group))
+            theirs = {bit: mine[bit] ^ ((offset >> bit) & 1) for bit in group}
+            route = [(i, i ^ offset) for i in range(size)]
+            total = total + lax.ppermute(select(theirs, group), axis, route)
+        parts = total
+        for bit in group:
+            remaining.remove(bit)
+    return parts.reshape(chunk, cols)
 
 
 def halving_scatter(sums, axis):
@@ -102,7 +133,7 @@
         return (next_f, next_b, sums_f, sums_b, part_f, part_b)
 
     points_f, points_b = send(targets_bf[:half], targets_bf[half:])
-    own = contribution(targets_bf)
+    own = lax.optimization_barrier(contribution(targets_bf))
     next_f, next_b = send(points_f, points_b)
     part_f, part_b = halves(points_f, points_b)
     zeros = jnp.zeros_like(part_f)
@@ -113,7 +144,7 @@
     part_f, part_b = halves(points_f, points_b)
     sums_f, sums_b = send(sums_f + part_f, sums_b + part_b)
     gathered_sums = own + jnp.concatenate([sums_f, sums_b], axis=1)
-    owned_sums = halving_scatter(gathered_sums, "grp")
+    owned_sums = radix_scatter(gathered_sums, "grp")
     source_total = src_codes.shape[0] * group_size * cycle_size
     return owned_sums.T * (4.0 / math.sqrt(source_total))
 

time: 157 us -> 159 us (1.013)
  the two profiles are of different devices: /device:TPU:6 before, /device:TPU:1 now
where the time goes in v6:
time: 159 us; the launch traced here: 158 us
  starting transfers between devices  53.7 us (34%)
  matrix products  45 us (28%)
  waiting for transfers between devices  37.1 us (23%)
  other arithmetic  11.3 us (7%)
  local copies, waits for them, and re-layouts  9.43 us (6%)
    dot_general x16, matrix products, kernel_block(): lax.dot_general(rhs_values, matern, (((0,), (1,)), ((), ())), preferred_e...  45 us
    ppermute x30, waiting for transfers between devices, send(): lax.ppermute(points_b, 'blk', backward)  25.4 us
    ppermute x30, starting transfers between devices, send(): lax.ppermute(points_f, 'blk', forward)  23.1 us
    ppermute x30, starting transfers between devices, send(): lax.ppermute(points_b, 'blk', backward)  17.5 us
    ppermute x6, starting transfers between devices, radix_scatter(): total = total + lax.ppermute(select(theirs, group), axis, route)  13.1 us
    ppermute x6, waiting for transfers between devices, radix_scatter(): total = total + lax.ppermute(select(theirs, group), axis, route)  11.6 us
    reduce_sum x17, other arithmetic, squares(): return jnp.sum(widened * widened, axis=1)  5.11 us
  transfers between devices with their start and end apart: 66, of which 23 were waited for; matrix products, arithmetic and copies ran while one was open for 34% of the time, Pallas kernels for 0%

profile of v6, /device:TPU:1, one launch (start us, length us, event | category | flops | bytes accessed | tf_op | source)
XLA Modules:
  0.0 157.7 jit_solution(4240660670491767826)
XLA Ops:
  1.2 1.5 multiply_reduce_fusion.4
  4.2 2.6 %collective-permute-start.4 = (bf16[128,1024]{1,0:T(8,128)(2,1)S(1)}, bf16[128,1024]{1,0:T(8,128)(2,1)S(1)}, u32[]{:S(2)}, u32[]{:S(2)}) collective-permute-start(bf16[128,1024]{1,0:T(8,128)(2,1)S(1)} %get-tuple-element.178), channel_id=1, source_target_pairs={{0,1},{1,4},{4,5},{5,8},{8,9},{9,12},{12,13},{13,14},{14,15},{15,1... | collective-permute-start | bytes 786440 | tf_op jit(solution)/shard_map/ppermute | solution.py:126
  15.2 3.2 %fusion.27 = f32[256,256]{1,0:T(8,128)} fusion(bf16[1024,256]{1,0:T(8,128)(2,1)} %add_convert_fusion, bf16[256,1024]{1,0:T(8,128)(2,1)S(1)} %constant_dynamic-update-slice_fusion.2, bf16[1024,1024]{1,0:T(8,128)(2,1)S(1)} %get-tuple-element.262, f32[256]{0:T(256)S(1)} %multiply_reduce_fusion.3, f32[1024]{0:T(1024)S(1)} %get-tuple-element.261), kind=kOutput, calls=%fused_computation.42 | convolution fusion | flops 673972224 | bytes 3412992 | tf_op jit(solution)/shard_map/dot_general | solution.py:42
  20.6 96.9 %while.22 = (s32[]{:T(128)}, bf16[128,1024]{1,0:T(8,128)(2,1)S(1)}, bf16[128,1024]{1,0:T(8,128)(2,1)S(1)}, f32[256,128]{0,1:T(8,128)S(1)}, f32[256,128]{0,1:T(8,...) while((s32[]{:T(128)}, bf16[128,1024]{1,0:T(8,128)(2,1)S(1)}, ...), condition=%wide.region_5.6_spmd, body=%wide.region_3.5_spmd.sunk | while | flops 674823936 | bytes 12589353 | solution.py:141
  23.7 2.9 %convolution_bitcast_fusion.2 = f32[256,256]{0,1:T(8,128)S(1)} fusion(bf16[1024,256]{1,0:T(8,128)(2,1)S(1)} %copy-done.7, bf16[256,1024]{1,0:T(8,128)(2,1)S(1)} %constant_dynamic-update-slice_fusion.9, bf16[1024,1024]{1,0:T(8,128)(2,1)} %get-tuple-element.284, f32[1024]{0:T(1024)S(1)} %get-tuple-element.283, f32[256]{0:T(256)S(1)} %multiply_reduce_fusion.6), kind=kOutput, calls=%fused_computation.4.clone.1 | convolution fusion | flops 673972224 | bytes 3412992 | tf_op jit(solution)/shard_map/while/body/eval_jaxpr/dot_general | solution.py:42
  26.7 1.6 collective-permute-done.3
  29.0 1.3 collective-permute-start.2
  31.2 2.9 %convolution_bitcast_fusion.2 = f32[256,256]{0,1:T(8,128)S(1)} fusion(bf16[1024,256]{1,0:T(8,128)(2,1)S(1)} %copy-done.7, bf16[256,1024]{1,0:T(8,128)(2,1)S(1)} %constant_dynamic-update-slice_fusion.9, bf16[1024,1024]{1,0:T(8,128)(2,1)} %get-tuple-element.284, f32[1024]{0:T(1024)S(1)} %get-tuple-element.283, f32[256]{0:T(256)S(1)} %multiply_reduce_fusion.6), kind=kOutput, calls=%fused_computation.4.clone.1 | convolution fusion | flops 673972224 | bytes 3412992 | tf_op jit(solution)/shard_map/while/body/eval_jaxpr/dot_general | solution.py:42
  34.1 1.6 collective-permute-done.3
  36.4 1.3 collective-permute-start.2
  38.6 2.9 %convolution_bitcast_fusion.2 = f32[256,256]{0,1:T(8,128)S(1)} fusion(bf16[1024,256]{1,0:T(8,128)(2,1)S(1)} %copy-done.7, bf16[256,1024]{1,0:T(8,128)(2,1)S(1)} %constant_dynamic-update-slice_fusion.9, bf16[1024,1024]{1,0:T(8,128)(2,1)} %get-tuple-element.284, f32[1024]{0:T(1024)S(1)} %get-tuple-element.283, f32[256]{0:T(256)S(1)} %multiply_reduce_fusion.6), kind=kOutput, calls=%fused_computation.4.clone.1 | convolution fusion | flops 673972224 | bytes 3412992 | tf_op jit(solution)/shard_map/while/body/eval_jaxpr/dot_general | solution.py:42
  41.6 1.6 collective-permute-done.3
  43.9 1.3 collective-permute-start.2
  46.1 2.9 %convolution_bitcast_fusion.2 = f32[256,256]{0,1:T(8,128)S(1)} fusion(bf16[1024,256]{1,0:T(8,128)(2,1)S(1)} %copy-done.7, bf16[256,1024]{1,0:T(8,128)(2,1)S(1)} %constant_dynamic-update-slice_fusion.9, bf16[1024,1024]{1,0:T(8,128)(2,1)} %get-tuple-element.284, f32[1024]{0:T(1024)S(1)} %get-tuple-element.283, f32[256]{0:T(256)S(1)} %multiply_reduce_fusion.6), kind=kOutput, calls=%fused_computation.4.clone.1 | convolution fusion | flops 673972224 | bytes 3412992 | tf_op jit(solution)/shard_map/while/body/eval_jaxpr/dot_general | solution.py:42
  49.0 1.6 collective-permute-done.3
  51.3 1.3 collective-permute-start.2
  53.5 2.9 %convolution_bitcast_fusion.2 = f32[256,256]{0,1:T(8,128)S(1)} fusion(bf16[1024,256]{1,0:T(8,128)(2,1)S(1)} %copy-done.7, bf16[256,1024]{1,0:T(8,128)(2,1)S(1)} %constant_dynamic-update-slice_fusion.9, bf16[1024,1024]{1,0:T(8,128)(2,1)} %get-tuple-element.284, f32[1024]{0:T(1024)S(1)} %get-tuple-element.283, f32[256]{0:T(256)S(1)} %multiply_reduce_fusion.6), kind=kOutput, calls=%fused_computation.4.clone.1 | convolution fusion | flops 673972224 | bytes 3412992 | tf_op jit(solution)/shard_map/while/body/eval_jaxpr/dot_general | solution.py:42
  56.4 1.6 collective-permute-done.3
  58.7 1.3 collective-permute-start.2
  60.9 2.9 %convolution_bitcast_fusion.2 = f32[256,256]{0,1:T(8,128)S(1)} fusion(bf16[1024,256]{1,0:T(8,128)(2,1)S(1)} %copy-done.7, bf16[256,1024]{1,0:T(8,128)(2,1)S(1)} %constant_dynamic-update-slice_fusion.9, bf16[1024,1024]{1,0:T(8,128)(2,1)} %get-tuple-element.284, f32[1024]{0:T(1024)S(1)} %get-tuple-element.283, f32[256]{0:T(256)S(1)} %multiply_reduce_fusion.6), kind=kOutput, calls=%fused_computation.4.clone.1 | convolution fusion | flops 673972224 | bytes 3412992 | tf_op jit(solution)/shard_map/while/body/eval_jaxpr/dot_general | solution.py:42
  63.9 1.6 collective-permute-done.3
  66.2 1.3 collective-permute-start.2
  68.4 2.9 %convolution_bitcast_fusion.2 = f32[256,256]{0,1:T(8,128)S(1)} fusion(bf16[1024,256]{1,0:T(8,128)(2,1)S(1)} %copy-done.7, bf16[256,1024]{1,0:T(8,128)(2,1)S(1)} %constant_dynamic-update-slice_fusion.9, bf16[1024,1024]{1,0:T(8,128)(2,1)} %get-tuple-element.284, f32[1024]{0:T(1024)S(1)} %get-tuple-element.283, f32[256]{0:T(256)S(1)} %multiply_reduce_fusion.6), kind=kOutput, calls=%fused_computation.4.clone.1 | convolution fusion | flops 673972224 | bytes 3412992 | tf_op jit(solution)/shard_map/while/body/eval_jaxpr/dot_general | solution.py:42
  71.3 1.6 collective-permute-done.3
  75.8 2.9 %convolution_bitcast_fusion.2 = f32[256,256]{0,1:T(8,128)S(1)} fusion(bf16[1024,256]{1,0:T(8,128)(2,1)S(1)} %copy-done.7, bf16[256,1024]{1,0:T(8,128)(2,1)S(1)} %constant_dynamic-update-slice_fusion.9, bf16[1024,1024]{1,0:T(8,128)(2,1)} %get-tuple-element.284, f32[1024]{0:T(1024)S(1)} %get-tuple-element.283, f32[256]{0:T(256)S(1)} %multiply_reduce_fusion.6), kind=kOutput, calls=%fused_computation.4.clone.1 | convolution fusion | flops 673972224 | bytes 3412992 | tf_op jit(solution)/shard_map/while/body/eval_jaxpr/dot_general | solution.py:42
  78.7 1.6 collective-permute-done.3
  83.2 2.9 %convolution_bitcast_fusion.2 = f32[256,256]{0,1:T(8,128)S(1)} fusion(bf16[1024,256]{1,0:T(8,128)(2,1)S(1)} %copy-done.7, bf16[256,1024]{1,0:T(8,128)(2,1)S(1)} %constant_dynamic-update-slice_fusion.9, bf16[1024,1024]{1,0:T(8,128)(2,1)} %get-tuple-element.284, f32[1024]{0:T(1024)S(1)} %get-tuple-element.283, f32[256]{0:T(256)S(1)} %multiply_reduce_fusion.6), kind=kOutput, calls=%fused_computation.4.clone.1 | convolution fusion | flops 673972224 | bytes 3412992 | tf_op jit(solution)/shard_map/while/body/eval_jaxpr/dot_general | solution.py:42
  86.2 1.6 collective-permute-done.3
  90.7 2.9 %convolution_bitcast_fusion.2 = f32[256,256]{0,1:T(8,128)S(1)} fusion(bf16[1024,256]{1,0:T(8,128)(2,1)S(1)} %copy-done.7, bf16[256,1024]{1,0:T(8,128)(2,1)S(1)} %constant_dynamic-update-slice_fusion.9, bf16[1024,1024]{1,0:T(8,128)(2,1)} %get-tuple-element.284, f32[1024]{0:T(1024)S(1)} %get-tuple-element.283, f32[256]{0:T(256)S(1)} %multiply_reduce_fusion.6), kind=kOutput, calls=%fused_computation.4.clone.1 | convolution fusion | flops 673972224 | bytes 3412992 | tf_op jit(solution)/shard_map/while/body/eval_jaxpr/dot_general | solution.py:42
  93.6 1.6 collective-permute-done.3
  98.1 2.9 %convolution_bitcast_fusion.2 = f32[256,256]{0,1:T(8,128)S(1)} fusion(bf16[1024,256]{1,0:T(8,128)(2,1)S(1)} %copy-done.7, bf16[256,1024]{1,0:T(8,128)(2,1)S(1)} %constant_dynamic-update-slice_fusion.9, bf16[1024,1024]{1,0:T(8,128)(2,1)} %get-tuple-element.284, f32[1024]{0:T(1024)S(1)} %get-tuple-element.283, f32[256]{0:T(256)S(1)} %multiply_reduce_fusion.6), kind=kOutput, calls=%fused_computation.4.clone.1 | convolution fusion | flops 673972224 | bytes 3412992 | tf_op jit(solution)/shard_map/while/body/eval_jaxpr/dot_general | solution.py:42
  101.0 1.6 collective-permute-done.3
  105.5 2.9 %convolution_bitcast_fusion.2 = f32[256,256]{0,1:T(8,128)S(1)} fusion(bf16[1024,256]{1,0:T(8,128)(2,1)S(1)} %copy-done.7, bf16[256,1024]{1,0:T(8,128)(2,1)S(1)} %constant_dynamic-update-slice_fusion.9, bf16[1024,1024]{1,0:T(8,128)(2,1)} %get-tuple-element.284, f32[1024]{0:T(1024)S(1)} %get-tuple-element.283, f32[256]{0:T(256)S(1)} %multiply_reduce_fusion.6), kind=kOutput, calls=%fused_computation.4.clone.1 | convolution fusion | flops 673972224 | bytes 3412992 | tf_op jit(solution)/shard_map/while/body/eval_jaxpr/dot_general | solution.py:42
  108.5 1.6 collective-permute-done.3
  113.0 2.9 %convolution_bitcast_fusion.2 = f32[256,256]{0,1:T(8,128)S(1)} fusion(bf16[1024,256]{1,0:T(8,128)(2,1)S(1)} %copy-done.7, bf16[256,1024]{1,0:T(8,128)(2,1)S(1)} %constant_dynamic-update-slice_fusion.9, bf16[1024,1024]{1,0:T(8,128)(2,1)} %get-tuple-element.284, f32[1024]{0:T(1024)S(1)} %get-tuple-element.283, f32[256]{0:T(256)S(1)} %multiply_reduce_fusion.6), kind=kOutput, calls=%fused_computation.4.clone.1 | convolution fusion | flops 673972224 | bytes 3412992 | tf_op jit(solution)/shard_map/while/body/eval_jaxpr/dot_general | solution.py:42
  115.9 1.6 collective-permute-done.3
  120.4 2.6 %fusion.25 = f32[256,256]{1,0:T(8,128)S(1)} fusion(bf16[1024,256]{1,0:T(8,128)(2,1)} %get-tuple-element.298, bf16[256,1024]{1,0:T(8,128)(2,1)} %copy-done.5, bf16[1024,1024]{1,0:T(8,128)(2,1)S(1)} %copy-done.2, f32[256]{0:T(256)S(1)} %multiply_reduce_fusion.2, f32[1024]{0:T(1024)S(1)} %get-tuple-element.316), kind=kOutput, calls=%fused_computation.38 | convolution fusion | flops 673972224 | bytes 3412992 | tf_op jit(solution)/shard_map/dot_general | solution.py:42
  123.0 1.6 %collective-permute-done.10 = f32[256,128]{1,0:T(8,128)} collective-permute-done((f32[256,128]{1,0:T(8,128)}, f32[256,128]{1,0:T(8,128)}, u32[]{:S(2)}, u32[]{:S(2)}) %collective-permute-start.10) | collective-permute-done | bytes 131104 | tf_op jit(solution)/shard_map/ppermute | solution.py:126
  124.6 1.6 %slice_add_fusion.1 = (f32[256,128]{1,0:T(8,128)S(1)}, f32[256,128]{1,0:T(8,128)}) fusion(f32[256,128]{1,0:T(8,128)} %collective-permute-done.8, f32[256,256]{1,0:T(8,128)S(1)} %fusion.25, f32[256,128]{1,0:T(8,128)} %collective-permute-done.10), kind=kLoop, calls=%fused_computation.70 | loop fusion | flops 65536 | bytes 786432 | tf_op jit(solution)/shard_map/add | solution.py:145
  126.6 1.4 collective-permute-start.9
  128.0 1.4 fusion.29
  129.4 1.8 %collective-permute-done.11 = f32[256,128]{1,0:T(8,128)} collective-permute-done((f32[256,128]{1,0:T(8,128)}, f32[256,128]{1,0:T(8,128)}, u32[]{:S(2)}, u32[]{:S(2)}) %collective-permute-start.11) | collective-permute-done | bytes 131104 | tf_op jit(solution)/shard_map/ppermute | solution.py:126
  132.3 4.0 %collective-permute-start.14 = (f32[2,2,16,256]{3,2,1,0:T(8,128)S(1)}, f32[2,2,16,256]{3,2,1,0:T(8,128)S(1)}, u32[]{:S(2)}, u32[]{:S(2)}) collective-permute-start(f32[2,2,16,256]{3,2,1,0:T(8,128)S(1)} %get-tuple-element.180), channel_id=1, source_target_pairs={{0,48},{16,32},{32,16},{48,0},{64,112},{80,96},{96,80},{112,64},{1... | collective-permute-start | bytes 196616 | tf_op jit(solution)/shard_map/ppermute | solution.py:71
  136.7 1.3 collective-permute-done.14
  138.1 3.7 %collective-permute-done.13 = f32[2,2,16,256]{3,2,1,0:T(8,128)S(1)} collective-permute-done((f32[2,2,16,256]{3,2,1,0:T(8,128)S(1)}, f32[2,2,16,256]{3,2,1,0:T(8,128)S(1)}, u32[]{:S(2)}, u32[]{:S(2)}) %collective-permute-start.13) | collective-permute-done | bytes 65568 | tf_op jit(solution)/shard_map/ppermute | solution.py:71
  142.2 8.3 %collective-permute-start.17 = (f32[16,256]{1,0:T(8,128)S(1)}, f32[16,256]{1,0:T(8,128)S(1)}, u32[]{:S(2)}, u32[]{:S(2)}) collective-permute-start(f32[16,256]{1,0:T(8,128)S(1)} %get-tuple-element.187), channel_id=1, source_target_pairs={{0,192},{16,208},{32,224},{48,240},{64,128},{80,144},{96,160},{112... | collective-permute-start | bytes 49160 | tf_op jit(solution)/shard_map/ppermute | solution.py:71
  151.6 3.0 %collective-permute-done.16 = f32[16,256]{1,0:T(8,128)S(1)} collective-permute-done((f32[16,256]{1,0:T(8,128)S(1)}, f32[16,256]{1,0:T(8,128)S(1)}, u32[]{:S(2)}, u32[]{:S(2)}) %collective-permute-start.16) | collective-permute-done | bytes 16416 | tf_op jit(solution)/shard_map/ppermute | solution.py:71
  154.6 2.5 %collective-permute-done.15 = f32[16,256]{1,0:T(8,128)S(1)} collective-permute-done((f32[16,256]{1,0:T(8,128)S(1)}, f32[16,256]{1,0:T(8,128)S(1)}, u32[]{:S(2)}, u32[]{:S(2)}) %collective-permute-start.15) | collective-permute-done | bytes 16416 | tf_op jit(solution)/shard_map/ppermute | solution.py:71
  (282 shorter events, 49.9 us)
Async XLA Ops:
  4.2 7.9 %collective-permute-start.4 = (bf16[128,1024]{1,0:T(8,128)(2,1)S(1)}, bf16[128,1024]{1,0:T(8,128)(2,1)S(1)}, u32[]{:S(2)}, u32[]{:S(2)}) collective-permute-start(bf16[128,1024]{1,0:T(8,128)(2,1)S(1)} %get-tuple-element.178), channel_id=1, source_target_pairs={{0,1},{1,4},{4,5},{5,8},{8,9},{9,12},{12,13},{13,14},{14,15},{15,1... | collective-permute-start | bytes 786440 | tf_op jit(solution)/shard_map/ppermute | solution.py:126
  6.8 6.1 %collective-permute-start.6 = (bf16[128,1024]{1,0:T(8,128)(2,1)}, bf16[128,1024]{1,0:T(8,128)(2,1)}, u32[]{:S(2)}, u32[]{:S(2)}) collective-permute-start(bf16[128,1024]{1,0:T(8,128)(2,1)} %get-tuple-element.177), channel_id=1, source_target_pairs={{1,0},{4,1},{5,4},{8,5},{9,8},{12,9},{13,12},{14,13},{15,14},{10,1... | collective-permute-start | bytes 786440 | tf_op jit(solution)/shard_map/ppermute | solution.py:126
  14.1 5.5 %collective-permute-start.5 = (bf16[128,1024]{1,0:T(8,128)(2,1)S(1)}, bf16[128,1024]{1,0:T(8,128)(2,1)S(1)}, u32[]{:S(2)}, u32[]{:S(2)}) collective-permute-start(bf16[128,1024]{1,0:T(8,128)(2,1)S(1)} %collective-permute-done.4), channel_id=1, source_target_pairs={{0,1},{1,4},{4,5},{5,8},{8,9},{9,12},{12,13},{13,14},{14,15},{15,1... | collective-permute-start | bytes 786440 | tf_op jit(solution)/shard_map/ppermute | solution.py:126
  14.5 6.0 %collective-permute-start.7 = (bf16[128,1024]{1,0:T(8,128)(2,1)}, bf16[128,1024]{1,0:T(8,128)(2,1)S(1)}, u32[]{:S(2)}, u32[]{:S(2)}) collective-permute-start(bf16[128,1024]{1,0:T(8,128)(2,1)} %collective-permute-done.6), channel_id=1, source_target_pairs={{1,0},{4,1},{5,4},{8,5},{9,8},{12,9},{13,12},{14,13},{15,14},{10,1... | collective-permute-start | bytes 786440 | tf_op jit(solution)/shard_map/ppermute | solution.py:126
  20.6 7.6 %collective-permute-start = (bf16[128,1024]{1,0:T(8,128)(2,1)S(1)}, bf16[128,1024]{1,0:T(8,128)(2,1)S(1)}, u32[]{:S(2)}, u32[]{:S(2)}) collective-permute-start(bf16[128,1024]{1,0:T(8,128)(2,1)S(1)} %copy.30), channel_id=1, source_target_pairs={{0,1},{1,4},{4,5},{5,8},{8,9},{9,12},{12,13},{13,14},{14,15},{15,1... | collective-permute-start | bytes 786440 | tf_op jit(solution)/shard_map/while/body/eval_jaxpr/ppermute | solution.py:126
  20.9 7.4 %collective-permute-start.1 = (bf16[128,1024]{1,0:T(8,128)(2,1)S(1)}, bf16[128,1024]{1,0:T(8,128)(2,1)S(1)}, u32[]{:S(2)}, u32[]{:S(2)}) collective-permute-start(bf16[128,1024]{1,0:T(8,128)(2,1)S(1)} %copy.31), channel_id=1, source_target_pairs={{1,0},{4,1},{5,4},{8,5},{9,8},{12,9},{13,12},{14,13},{15,14},{10,1... | collective-permute-start | bytes 786440 | tf_op jit(solution)/shard_map/while/body/eval_jaxpr/ppermute | solution.py:126
  22.8 5.5 %collective-permute-start.3 = (f32[256,128]{0,1:T(8,128)S(1)}, f32[256,128]{0,1:T(8,128)S(1)}, u32[]{:S(2)}, u32[]{:S(2)}) collective-permute-start(f32[256,128]{0,1:T(8,128)S(1)} %add.397), channel_id=1, source_target_pairs={{1,0},{4,1},{5,4},{8,5},{9,8},{12,9},{13,12},{14,13},{15,14},{10,1... | collective-permute-start | bytes 393224 | tf_op jit(solution)/shard_map/while/body/eval_jaxpr/ppermute | solution.py:126
  28.3 7.4 %collective-permute-start = (bf16[128,1024]{1,0:T(8,128)(2,1)S(1)}, bf16[128,1024]{1,0:T(8,128)(2,1)S(1)}, u32[]{:S(2)}, u32[]{:S(2)}) collective-permute-start(bf16[128,1024]{1,0:T(8,128)(2,1)S(1)} %copy.30), channel_id=1, source_target_pairs={{0,1},{1,4},{4,5},{5,8},{8,9},{9,12},{12,13},{13,14},{14,15},{15,1... | collective-permute-start | bytes 786440 | tf_op jit(solution)/shard_map/while/body/eval_jaxpr/ppermute | solution.py:126
  28.4 7.3 %collective-permute-start.1 = (bf16[128,1024]{1,0:T(8,128)(2,1)S(1)}, bf16[128,1024]{1,0:T(8,128)(2,1)S(1)}, u32[]{:S(2)}, u32[]{:S(2)}) collective-permute-start(bf16[128,1024]{1,0:T(8,128)(2,1)S(1)} %copy.31), channel_id=1, source_target_pairs={{1,0},{4,1},{5,4},{8,5},{9,8},{12,9},{13,12},{14,13},{15,14},{10,1... | collective-permute-start | bytes 786440 | tf_op jit(solution)/shard_map/while/body/eval_jaxpr/ppermute | solution.py:126
  30.4 5.3 %collective-permute-start.3 = (f32[256,128]{0,1:T(8,128)S(1)}, f32[256,128]{0,1:T(8,128)S(1)}, u32[]{:S(2)}, u32[]{:S(2)}) collective-permute-start(f32[256,128]{0,1:T(8,128)S(1)} %add.397), channel_id=1, source_target_pairs={{1,0},{4,1},{5,4},{8,5},{9,8},{12,9},{13,12},{14,13},{15,14},{10,1... | collective-permute-start | bytes 393224 | tf_op jit(solution)/shard_map/while/body/eval_jaxpr/ppermute | solution.py:126
  35.7 7.4 %collective-permute-start = (bf16[128,1024]{1,0:T(8,128)(2,1)S(1)}, bf16[128,1024]{1,0:T(8,128)(2,1)S(1)}, u32[]{:S(2)}, u32[]{:S(2)}) collective-permute-start(bf16[128,1024]{1,0:T(8,128)(2,1)S(1)} %copy.30), channel_id=1, source_target_pairs={{0,1},{1,4},{4,5},{5,8},{8,9},{9,12},{12,13},{13,14},{14,15},{15,1... | collective-permute-start | bytes 786440 | tf_op jit(solution)/shard_map/while/body/eval_jaxpr/ppermute | solution.py:126
  35.8 7.3 %collective-permute-start.1 = (bf16[128,1024]{1,0:T(8,128)(2,1)S(1)}, bf16[128,1024]{1,0:T(8,128)(2,1)S(1)}, u32[]{:S(2)}, u32[]{:S(2)}) collective-permute-start(bf16[128,1024]{1,0:T(8,128)(2,1)S(1)} %copy.31), channel_id=1, source_target_pairs={{1,0},{4,1},{5,4},{8,5},{9,8},{12,9},{13,12},{14,13},{15,14},{10,1... | collective-permute-start | bytes 786440 | tf_op jit(solution)/shard_map/while/body/eval_jaxpr/ppermute | solution.py:126
  37.8 5.3 %collective-permute-start.3 = (f32[256,128]{0,1:T(8,128)S(1)}, f32[256,128]{0,1:T(8,128)S(1)}, u32[]{:S(2)}, u32[]{:S(2)}) collective-permute-start(f32[256,128]{0,1:T(8,128)S(1)} %add.397), channel_id=1, source_target_pairs={{1,0},{4,1},{5,4},{8,5},{9,8},{12,9},{13,12},{14,13},{15,14},{10,1... | collective-permute-start | bytes 393224 | tf_op jit(solution)/shard_map/while/body/eval_jaxpr/ppermute | solution.py:126
  43.2 7.4 %collective-permute-start = (bf16[128,1024]{1,0:T(8,128)(2,1)S(1)}, bf16[128,1024]{1,0:T(8,128)(2,1)S(1)}, u32[]{:S(2)}, u32[]{:S(2)}) collective-permute-start(bf16[128,1024]{1,0:T(8,128)(2,1)S(1)} %copy.30), channel_id=1, source_target_pairs={{0,1},{1,4},{4,5},{5,8},{8,9},{9,12},{12,13},{13,14},{14,15},{15,1... | collective-permute-start | bytes 786440 | tf_op jit(solution)/shard_map/while/body/eval_jaxpr/ppermute | solution.py:126
  43.3 7.3 %collective-permute-start.1 = (bf16[128,1024]{1,0:T(8,128)(2,1)S(1)}, bf16[128,1024]{1,0:T(8,128)(2,1)S(1)}, u32[]{:S(2)}, u32[]{:S(2)}) collective-permute-start(bf16[128,1024]{1,0:T(8,128)(2,1)S(1)} %copy.31), channel_id=1, source_target_pairs={{1,0},{4,1},{5,4},{8,5},{9,8},{12,9},{13,12},{14,13},{15,14},{10,1... | collective-permute-start | bytes 786440 | tf_op jit(solution)/shard_map/while/body/eval_jaxpr/ppermute | solution.py:126
  45.2 5.3 %collective-permute-start.3 = (f32[256,128]{0,1:T(8,128)S(1)}, f32[256,128]{0,1:T(8,128)S(1)}, u32[]{:S(2)}, u32[]{:S(2)}) collective-permute-start(f32[256,128]{0,1:T(8,128)S(1)} %add.397), channel_id=1, source_target_pairs={{1,0},{4,1},{5,4},{8,5},{9,8},{12,9},{13,12},{14,13},{15,14},{10,1... | collective-permute-start | bytes 393224 | tf_op jit(solution)/shard_map/while/body/eval_jaxpr/ppermute | solution.py:126
  50.6 7.4 %collective-permute-start = (bf16[128,1024]{1,0:T(8,128)(2,1)S(1)}, bf16[128,1024]{1,0:T(8,128)(2,1)S(1)}, u32[]{:S(2)}, u32[]{:S(2)}) collective-permute-start(bf16[128,1024]{1,0:T(8,128)(2,1)S(1)} %copy.30), channel_id=1, source_target_pairs={{0,1},{1,4},{4,5},{5,8},{8,9},{9,12},{12,13},{13,14},{14,15},{15,1... | collective-permute-start | bytes 786440 | tf_op jit(solution)/shard_map/while/body/eval_jaxpr/ppermute | solution.py:126
  50.7 7.3 %collective-permute-start.1 = (bf16[128,1024]{1,0:T(8,128)(2,1)S(1)}, bf16[128,1024]{1,0:T(8,128)(2,1)S(1)}, u32[]{:S(2)}, u32[]{:S(2)}) collective-permute-start(bf16[128,1024]{1,0:T(8,128)(2,1)S(1)} %copy.31), channel_id=1, source_target_pairs={{1,0},{4,1},{5,4},{8,5},{9,8},{12,9},{13,12},{14,13},{15,14},{10,1... | collective-permute-start | bytes 786440 | tf_op jit(solution)/shard_map/while/body/eval_jaxpr/ppermute | solution.py:126
  52.7 5.3 %collective-permute-start.3 = (f32[256,128]{0,1:T(8,128)S(1)}, f32[256,128]{0,1:T(8,128)S(1)}, u32[]{:S(2)}, u32[]{:S(2)}) collective-permute-start(f32[256,128]{0,1:T(8,128)S(1)} %add.397), channel_id=1, source_target_pairs={{1,0},{4,1},{5,4},{8,5},{9,8},{12,9},{13,12},{14,13},{15,14},{10,1... | collective-permute-start | bytes 393224 | tf_op jit(solution)/shard_map/while/body/eval_jaxpr/ppermute | solution.py:126
  58.0 7.4 %collective-permute-start = (bf16[128,1024]{1,0:T(8,128)(2,1)S(1)}, bf16[128,1024]{1,0:T(8,128)(2,1)S(1)}, u32[]{:S(2)}, u32[]{:S(2)}) collective-permute-start(bf16[128,1024]{1,0:T(8,128)(2,1)S(1)} %copy.30), channel_id=1, source_target_pairs={{0,1},{1,4},{4,5},{5,8},{8,9},{9,12},{12,13},{13,14},{14,15},{15,1... | collective-permute-start | bytes 786440 | tf_op jit(solution)/shard_map/while/body/eval_jaxpr/ppermute | solution.py:126
  58.2 7.3 %collective-permute-start.1 = (bf16[128,1024]{1,0:T(8,128)(2,1)S(1)}, bf16[128,1024]{1,0:T(8,128)(2,1)S(1)}, u32[]{:S(2)}, u32[]{:S(2)}) collective-permute-start(bf16[128,1024]{1,0:T(8,128)(2,1)S(1)} %copy.31), channel_id=1, source_target_pairs={{1,0},{4,1},{5,4},{8,5},{9,8},{12,9},{13,12},{14,13},{15,14},{10,1... | collective-permute-start | bytes 786440 | tf_op jit(solution)/shard_map/while/body/eval_jaxpr/ppermute | solution.py:126
  60.1 5.3 %collective-permute-start.3 = (f32[256,128]{0,1:T(8,128)S(1)}, f32[256,128]{0,1:T(8,128)S(1)}, u32[]{:S(2)}, u32[]{:S(2)}) collective-permute-start(f32[256,128]{0,1:T(8,128)S(1)} %add.397), channel_id=1, source_target_pairs={{1,0},{4,1},{5,4},{8,5},{9,8},{12,9},{13,12},{14,13},{15,14},{10,1... | collective-permute-start | bytes 393224 | tf_op jit(solution)/shard_map/while/body/eval_jaxpr/ppermute | solution.py:126
  65.5 7.4 %collective-permute-start = (bf16[128,1024]{1,0:T(8,128)(2,1)S(1)}, bf16[128,1024]{1,0:T(8,128)(2,1)S(1)}, u32[]{:S(2)}, u32[]{:S(2)}) collective-permute-start(bf16[128,1024]{1,0:T(8,128)(2,1)S(1)} %copy.30), channel_id=1, source_target_pairs={{0,1},{1,4},{4,5},{5,8},{8,9},{9,12},{12,13},{13,14},{14,15},{15,1... | collective-permute-start | bytes 786440 | tf_op jit(solution)/shard_map/while/body/eval_jaxpr/ppermute | solution.py:126
  65.6 7.3 %collective-permute-start.1 = (bf16[128,1024]{1,0:T(8,128)(2,1)S(1)}, bf16[128,1024]{1,0:T(8,128)(2,1)S(1)}, u32[]{:S(2)}, u32[]{:S(2)}) collective-permute-start(bf16[128,1024]{1,0:T(8,128)(2,1)S(1)} %copy.31), channel_id=1, source_target_pairs={{1,0},{4,1},{5,4},{8,5},{9,8},{12,9},{13,12},{14,13},{15,14},{10,1... | collective-permute-start | bytes 786440 | tf_op jit(solution)/shard_map/while/body/eval_jaxpr/ppermute | solution.py:126
  67.5 5.3 %collective-permute-start.3 = (f32[256,128]{0,1:T(8,128)S(1)}, f32[256,128]{0,1:T(8,128)S(1)}, u32[]{:S(2)}, u32[]{:S(2)}) collective-permute-start(f32[256,128]{0,1:T(8,128)S(1)} %add.397), channel_id=1, source_target_pairs={{1,0},{4,1},{5,4},{8,5},{9,8},{12,9},{13,12},{14,13},{15,14},{10,1... | collective-permute-start | bytes 393224 | tf_op jit(solution)/shard_map/while/body/eval_jaxpr/ppermute | solution.py:126
  72.9 7.4 %collective-permute-start = (bf16[128,1024]{1,0:T(8,128)(2,1)S(1)}, bf16[128,1024]{1,0:T(8,128)(2,1)S(1)}, u32[]{:S(2)}, u32[]{:S(2)}) collective-permute-start(bf16[128,1024]{1,0:T(8,128)(2,1)S(1)} %copy.30), channel_id=1, source_target_pairs={{0,1},{1,4},{4,5},{5,8},{8,9},{9,12},{12,13},{13,14},{14,15},{15,1... | collective-permute-start | bytes 786440 | tf_op jit(solution)/shard_map/while/body/eval_jaxpr/ppermute | solution.py:126
  73.0 7.3 %collective-permute-start.1 = (bf16[128,1024]{1,0:T(8,128)(2,1)S(1)}, bf16[128,1024]{1,0:T(8,128)(2,1)S(1)}, u32[]{:S(2)}, u32[]{:S(2)}) collective-permute-start(bf16[128,1024]{1,0:T(8,128)(2,1)S(1)} %copy.31), channel_id=1, source_target_pairs={{1,0},{4,1},{5,4},{8,5},{9,8},{12,9},{13,12},{14,13},{15,14},{10,1... | collective-permute-start | bytes 786440 | tf_op jit(solution)/shard_map/while/body/eval_jaxpr/ppermute | solution.py:126
  75.0 5.3 %collective-permute-start.3 = (f32[256,128]{0,1:T(8,128)S(1)}, f32[256,128]{0,1:T(8,128)S(1)}, u32[]{:S(2)}, u32[]{:S(2)}) collective-permute-start(f32[256,128]{0,1:T(8,128)S(1)} %add.397), channel_id=1, source_target_pairs={{1,0},{4,1},{5,4},{8,5},{9,8},{12,9},{13,12},{14,13},{15,14},{10,1... | collective-permute-start | bytes 393224 | tf_op jit(solution)/shard_map/while/body/eval_jaxpr/ppermute | solution.py:126
  80.3 7.4 %collective-permute-start = (bf16[128,1024]{1,0:T(8,128)(2,1)S(1)}, bf16[128,1024]{1,0:T(8,128)(2,1)S(1)}, u32[]{:S(2)}, u32[]{:S(2)}) collective-permute-start(bf16[128,1024]{1,0:T(8,128)(2,1)S(1)} %copy.30), channel_id=1, source_target_pairs={{0,1},{1,4},{4,5},{5,8},{8,9},{9,12},{12,13},{13,14},{14,15},{15,1... | collective-permute-start | bytes 786440 | tf_op jit(solution)/shard_map/while/body/eval_jaxpr/ppermute | solution.py:126
  80.5 7.3 %collective-permute-start.1 = (bf16[128,1024]{1,0:T(8,128)(2,1)S(1)}, bf16[128,1024]{1,0:T(8,128)(2,1)S(1)}, u32[]{:S(2)}, u32[]{:S(2)}) collective-permute-start(bf16[128,1024]{1,0:T(8,128)(2,1)S(1)} %copy.31), channel_id=1, source_target_pairs={{1,0},{4,1},{5,4},{8,5},{9,8},{12,9},{13,12},{14,13},{15,14},{10,1... | collective-permute-start | bytes 786440 | tf_op jit(solution)/shard_map/while/body/eval_jaxpr/ppermute | solution.py:126
  82.4 5.3 %collective-permute-start.3 = (f32[256,128]{0,1:T(8,128)S(1)}, f32[256,128]{0,1:T(8,128)S(1)}, u32[]{:S(2)}, u32[]{:S(2)}) collective-permute-start(f32[256,128]{0,1:T(8,128)S(1)} %add.397), channel_id=1, source_target_pairs={{1,0},{4,1},{5,4},{8,5},{9,8},{12,9},{13,12},{14,13},{15,14},{10,1... | collective-permute-start | bytes 393224 | tf_op jit(solution)/shard_map/while/body/eval_jaxpr/ppermute | solution.py:126
  87.8 7.4 %collective-permute-start = (bf16[128,1024]{1,0:T(8,128)(2,1)S(1)}, bf16[128,1024]{1,0:T(8,128)(2,1)S(1)}, u32[]{:S(2)}, u32[]{:S(2)}) collective-permute-start(bf16[128,1024]{1,0:T(8,128)(2,1)S(1)} %copy.30), channel_id=1, source_target_pairs={{0,1},{1,4},{4,5},{5,8},{8,9},{9,12},{12,13},{13,14},{14,15},{15,1... | collective-permute-start | bytes 786440 | tf_op jit(solution)/shard_map/while/body/eval_jaxpr/ppermute | solution.py:126
  87.9 7.3 %collective-permute-start.1 = (bf16[128,1024]{1,0:T(8,128)(2,1)S(1)}, bf16[128,1024]{1,0:T(8,128)(2,1)S(1)}, u32[]{:S(2)}, u32[]{:S(2)}) collective-permute-start(bf16[128,1024]{1,0:T(8,128)(2,1)S(1)} %copy.31), channel_id=1, source_target_pairs={{1,0},{4,1},{5,4},{8,5},{9,8},{12,9},{13,12},{14,13},{15,14},{10,1... | collective-permute-start | bytes 786440 | tf_op jit(solution)/shard_map/while/body/eval_jaxpr/ppermute | solution.py:126
  89.8 5.3 %collective-permute-start.3 = (f32[256,128]{0,1:T(8,128)S(1)}, f32[256,128]{0,1:T(8,128)S(1)}, u32[]{:S(2)}, u32[]{:S(2)}) collective-permute-start(f32[256,128]{0,1:T(8,128)S(1)} %add.397), channel_id=1, source_target_pairs={{1,0},{4,1},{5,4},{8,5},{9,8},{12,9},{13,12},{14,13},{15,14},{10,1... | collective-permute-start | bytes 393224 | tf_op jit(solution)/shard_map/while/body/eval_jaxpr/ppermute | solution.py:126
  95.2 7.4 %collective-permute-start = (bf16[128,1024]{1,0:T(8,128)(2,1)S(1)}, bf16[128,1024]{1,0:T(8,128)(2,1)S(1)}, u32[]{:S(2)}, u32[]{:S(2)}) collective-permute-start(bf16[128,1024]{1,0:T(8,128)(2,1)S(1)} %copy.30), channel_id=1, source_target_pairs={{0,1},{1,4},{4,5},{5,8},{8,9},{9,12},{12,13},{13,14},{14,15},{15,1... | collective-permute-start | bytes 786440 | tf_op jit(solution)/shard_map/while/body/eval_jaxpr/ppermute | solution.py:126
  95.3 7.3 %collective-permute-start.1 = (bf16[128,1024]{1,0:T(8,128)(2,1)S(1)}, bf16[128,1024]{1,0:T(8,128)(2,1)S(1)}, u32[]{:S(2)}, u32[]{:S(2)}) collective-permute-start(bf16[128,1024]{1,0:T(8,128)(2,1)S(1)} %copy.31), channel_id=1, source_target_pairs={{1,0},{4,1},{5,4},{8,5},{9,8},{12,9},{13,12},{14,13},{15,14},{10,1... | collective-permute-start | bytes 786440 | tf_op jit(solution)/shard_map/while/body/eval_jaxpr/ppermute | solution.py:126
  97.3 5.3 %collective-permute-start.3 = (f32[256,128]{0,1:T(8,128)S(1)}, f32[256,128]{0,1:T(8,128)S(1)}, u32[]{:S(2)}, u32[]{:S(2)}) collective-permute-start(f32[256,128]{0,1:T(8,128)S(1)} %add.397), channel_id=1, source_target_pairs={{1,0},{4,1},{5,4},{8,5},{9,8},{12,9},{13,12},{14,13},{15,14},{10,1... | collective-permute-start | bytes 393224 | tf_op jit(solution)/shard_map/while/body/eval_jaxpr/ppermute | solution.py:126
  102.7 7.4 %collective-permute-start = (bf16[128,1024]{1,0:T(8,128)(2,1)S(1)}, bf16[128,1024]{1,0:T(8,128)(2,1)S(1)}, u32[]{:S(2)}, u32[]{:S(2)}) collective-permute-start(bf16[128,1024]{1,0:T(8,128)(2,1)S(1)} %copy.30), channel_id=1, source_target_pairs={{0,1},{1,4},{4,5},{5,8},{8,9},{9,12},{12,13},{13,14},{14,15},{15,1... | collective-permute-start | bytes 786440 | tf_op jit(solution)/shard_map/while/body/eval_jaxpr/ppermute | solution.py:126
  102.8 7.3 %collective-permute-start.1 = (bf16[128,1024]{1,0:T(8,128)(2,1)S(1)}, bf16[128,1024]{1,0:T(8,128)(2,1)S(1)}, u32[]{:S(2)}, u32[]{:S(2)}) collective-permute-start(bf16[128,1024]{1,0:T(8,128)(2,1)S(1)} %copy.31), channel_id=1, source_target_pairs={{1,0},{4,1},{5,4},{8,5},{9,8},{12,9},{13,12},{14,13},{15,14},{10,1... | collective-permute-start | bytes 786440 | tf_op jit(solution)/shard_map/while/body/eval_jaxpr/ppermute | solution.py:126
  104.7 5.3 %collective-permute-start.3 = (f32[256,128]{0,1:T(8,128)S(1)}, f32[256,128]{0,1:T(8,128)S(1)}, u32[]{:S(2)}, u32[]{:S(2)}) collective-permute-start(f32[256,128]{0,1:T(8,128)S(1)} %add.397), channel_id=1, source_target_pairs={{1,0},{4,1},{5,4},{8,5},{9,8},{12,9},{13,12},{14,13},{15,14},{10,1... | collective-permute-start | bytes 393224 | tf_op jit(solution)/shard_map/while/body/eval_jaxpr/ppermute | solution.py:126
  110.1 7.4 %collective-permute-start = (bf16[128,1024]{1,0:T(8,128)(2,1)S(1)}, bf16[128,1024]{1,0:T(8,128)(2,1)S(1)}, u32[]{:S(2)}, u32[]{:S(2)}) collective-permute-start(bf16[128,1024]{1,0:T(8,128)(2,1)S(1)} %copy.30), channel_id=1, source_target_pairs={{0,1},{1,4},{4,5},{5,8},{8,9},{9,12},{12,13},{13,14},{14,15},{15,1... | collective-permute-start | bytes 786440 | tf_op jit(solution)/shard_map/while/body/eval_jaxpr/ppermute | solution.py:126
  110.2 7.3 %collective-permute-start.1 = (bf16[128,1024]{1,0:T(8,128)(2,1)S(1)}, bf16[128,1024]{1,0:T(8,128)(2,1)S(1)}, u32[]{:S(2)}, u32[]{:S(2)}) collective-permute-start(bf16[128,1024]{1,0:T(8,128)(2,1)S(1)} %copy.31), channel_id=1, source_target_pairs={{1,0},{4,1},{5,4},{8,5},{9,8},{12,9},{13,12},{14,13},{15,14},{10,1... | collective-permute-start | bytes 786440 | tf_op jit(solution)/shard_map/while/body/eval_jaxpr/ppermute | solution.py:126
  112.1 5.3 %collective-permute-start.3 = (f32[256,128]{0,1:T(8,128)S(1)}, f32[256,128]{0,1:T(8,128)S(1)}, u32[]{:S(2)}, u32[]{:S(2)}) collective-permute-start(f32[256,128]{0,1:T(8,128)S(1)} %add.397), channel_id=1, source_target_pairs={{1,0},{4,1},{5,4},{8,5},{9,8},{12,9},{13,12},{14,13},{15,14},{10,1... | collective-permute-start | bytes 393224 | tf_op jit(solution)/shard_map/while/body/eval_jaxpr/ppermute | solution.py:126
  132.3 5.8 %collective-permute-start.14 = (f32[2,2,16,256]{3,2,1,0:T(8,128)S(1)}, f32[2,2,16,256]{3,2,1,0:T(8,128)S(1)}, u32[]{:S(2)}, u32[]{:S(2)}) collective-permute-start(f32[2,2,16,256]{3,2,1,0:T(8,128)S(1)} %get-tuple-element.180), channel_id=1, source_target_pairs={{0,48},{16,32},{32,16},{48,0},{64,112},{80,96},{96,80},{112,64},{1... | collective-permute-start | bytes 196616 | tf_op jit(solution)/shard_map/ppermute | solution.py:71
  136.3 5.4 %collective-permute-start.13 = (f32[2,2,16,256]{3,2,1,0:T(8,128)S(1)}, f32[2,2,16,256]{3,2,1,0:T(8,128)S(1)}, u32[]{:S(2)}, u32[]{:S(2)}) collective-permute-start(f32[2,2,16,256]{3,2,1,0:T(8,128)S(1)} %get-tuple-element.181), channel_id=1, source_target_pairs={{0,32},{16,48},{32,0},{48,16},{64,96},{80,112},{96,64},{112,80},{1... | collective-permute-start | bytes 196616 | tf_op jit(solution)/shard_map/ppermute | solution.py:71
  136.3 5.8 %collective-permute-start.12 = (f32[2,2,16,256]{3,2,1,0:T(8,128)S(1)}, f32[2,2,16,256]{3,2,1,0:T(8,128)S(1)}, u32[]{:S(2)}, u32[]{:S(2)}) collective-permute-start(f32[2,2,16,256]{3,2,1,0:T(8,128)S(1)} %get-tuple-element.179), channel_id=1, source_target_pairs={{0,16},{16,0},{32,48},{48,32},{64,80},{80,64},{96,112},{112,96},{1... | collective-permute-start | bytes 196616 | tf_op jit(solution)/shard_map/ppermute | solution.py:71
  142.2 9.4 %collective-permute-start.17 = (f32[16,256]{1,0:T(8,128)S(1)}, f32[16,256]{1,0:T(8,128)S(1)}, u32[]{:S(2)}, u32[]{:S(2)}) collective-permute-start(f32[16,256]{1,0:T(8,128)S(1)} %get-tuple-element.187), channel_id=1, source_target_pairs={{0,192},{16,208},{32,224},{48,240},{64,128},{80,144},{96,160},{112... | collective-permute-start | bytes 49160 | tf_op jit(solution)/shard_map/ppermute | solution.py:71
  150.6 6.5 %collective-permute-start.15 = (f32[16,256]{1,0:T(8,128)S(1)}, f32[16,256]{1,0:T(8,128)S(1)}, u32[]{:S(2)}, u32[]{:S(2)}) collective-permute-start(f32[16,256]{1,0:T(8,128)S(1)} %get-tuple-element.186), channel_id=1, source_target_pairs={{0,64},{16,80},{32,96},{48,112},{64,0},{80,16},{96,32},{112,48},{1... | collective-permute-start | bytes 49160 | tf_op jit(solution)/shard_map/ppermute | solution.py:71
  (40 other events, 166.1 us)

commit v7 on v3

--- a/solution.py
+++ b/solution.py
@@ -102,7 +102,7 @@
         return (next_f, next_b, sums_f, sums_b, part_f, part_b)
 
     points_f, points_b = send(targets_bf[:half], targets_bf[half:])
-    own = contribution(targets_bf)
+    own = lax.optimization_barrier(contribution(targets_bf))
     next_f, next_b = send(points_f, points_b)
     part_f, part_b = halves(points_f, points_b)
     zeros = jnp.zeros_like(part_f)

time: 157 us -> 159 us (1.013)
  other arithmetic: 8.01 us -> 11.3 us
  waiting for transfers between devices: 19.7 us -> 16.9 us
    ppermute x30, starting transfers between devices: 31.4 us -> 33.9 us  [send(): lax.ppermute(points_f, 'blk', forward)]
    add x3, other arithmetic: 0.06 us -> 2.34 us  [per_device(): sums_f, sums_b = send(sums_f + part_f, sums_b + part_b)]
    ppermute x30, waiting for transfers between devices: 6.64 us -> 4.66 us  [send(): lax.ppermute(points_f, 'blk', forward)]
    unnamed x18 -> x20, local copies, waits for them, and re-layouts: 3.2 us -> 3.06 us
  transfers between devices with their start and end apart: 64 -> 64, of which waited for: 20 -> 20; matrix products, arithmetic and copies ran while one was open for 34% -> 35% of each run, Pallas kernels for 0% -> 0%
where the time goes in v7:
time: 159 us; the launch traced here: 158 us
  starting transfers between devices  73.7 us (46%)
  matrix products  45.1 us (28%)
  waiting for transfers between devices  16.9 us (11%)
  other arithmetic  11.3 us (7%)
  local copies, waits for them, and re-layouts  9.45 us (6%)
    dot_general x16, matrix products, kernel_block(): lax.dot_general(rhs_values, matern, (((0,), (1,)), ((), ())), preferred_e...  45.1 us
    ppermute x30, starting transfers between devices, send(): lax.ppermute(points_f, 'blk', forward)  33.9 us
    ppermute x30, starting transfers between devices, send(): lax.ppermute(points_b, 'blk', backward)  24.3 us
    ppermute x4, starting transfers between devices, halving_scatter(): parts = kept + lax.ppermute(sent, axis, route)  15.5 us
    ppermute x4, waiting for transfers between devices, halving_scatter(): parts = kept + lax.ppermute(sent, axis, route)  10.7 us
    reduce_sum x17, other arithmetic, squares(): return jnp.sum(widened * widened, axis=1)  5.11 us
    ppermute x30, waiting for transfers between devices, send(): lax.ppermute(points_f, 'blk', forward)  4.66 us
  transfers between devices with their start and end apart: 64, of which 20 were waited for; matrix products, arithmetic and copies ran while one was open for 35% of the time, Pallas kernels for 0%

profile of v7, /device:TPU:6, one launch (start us, length us, event | category | flops | bytes accessed | tf_op | source)
XLA Modules:
  0.0 157.7 jit_solution(3636238718426814145)
XLA Ops:
  1.2 1.5 multiply_reduce_fusion.4
  4.2 1.7 %collective-permute-start.6 = (bf16[128,1024]{1,0:T(8,128)(2,1)}, bf16[128,1024]{1,0:T(8,128)(2,1)}, u32[]{:S(2)}, u32[]{:S(2)}) collective-permute-start(bf16[128,1024]{1,0:T(8,128)(2,1)} %get-tuple-element.177), channel_id=1, source_target_pairs={{1,0},{4,1},{5,4},{8,5},{9,8},{12,9},{13,12},{14,13},{15,14},{10,1... | collective-permute-start | bytes 786440 | tf_op jit(solution)/shard_map/ppermute | solution.py:95
  13.7 3.2 %fusion.27 = f32[256,256]{1,0:T(8,128)} fusion(bf16[1024,256]{1,0:T(8,128)(2,1)} %add_convert_fusion, bf16[256,1024]{1,0:T(8,128)(2,1)S(1)} %constant_dynamic-update-slice_fusion.2, bf16[1024,1024]{1,0:T(8,128)(2,1)S(1)} %get-tuple-element.256, f32[256]{0:T(256)S(1)} %multiply_reduce_fusion.3, f32[1024]{0:T(1024)S(1)} %get-tuple-element.255), kind=kOutput, calls=%fused_computation.42 | convolution fusion | flops 673972224 | bytes 3412992 | tf_op jit(solution)/shard_map/dot_general | solution.py:42
  18.1 96.6 %while.22 = (s32[]{:T(128)}, bf16[128,1024]{1,0:T(8,128)(2,1)S(1)}, bf16[128,1024]{1,0:T(8,128)(2,1)S(1)}, f32[256,128]{0,1:T(8,128)S(1)}, f32[256,128]{0,1:T(8,...) while((s32[]{:T(128)}, bf16[128,1024]{1,0:T(8,128)(2,1)S(1)}, ...), condition=%wide.region_5.6_spmd, body=%wide.region_3.5_spmd.sunk | while | flops 674823936 | bytes 12589353 | solution.py:110
  18.2 1.6 %collective-permute-start = (bf16[128,1024]{1,0:T(8,128)(2,1)S(1)}, bf16[128,1024]{1,0:T(8,128)(2,1)S(1)}, u32[]{:S(2)}, u32[]{:S(2)}) collective-permute-start(bf16[128,1024]{1,0:T(8,128)(2,1)S(1)} %copy.30), channel_id=1, source_target_pairs={{0,1},{1,4},{4,5},{5,8},{8,9},{9,12},{12,13},{13,14},{14,15},{15,1... | collective-permute-start | bytes 786440 | tf_op jit(solution)/shard_map/while/body/eval_jaxpr/ppermute | solution.py:95
  20.5 1.5 collective-permute-start.3
  22.3 2.9 %convolution_bitcast_fusion.2 = f32[256,256]{0,1:T(8,128)S(1)} fusion(bf16[1024,256]{1,0:T(8,128)(2,1)S(1)} %copy-done.7, bf16[256,1024]{1,0:T(8,128)(2,1)S(1)} %constant_dynamic-update-slice_fusion.9, bf16[1024,1024]{1,0:T(8,128)(2,1)} %get-tuple-element.278, f32[1024]{0:T(1024)S(1)} %get-tuple-element.277, f32[256]{0:T(256)S(1)} %multiply_reduce_fusion.6), kind=kOutput, calls=%fused_computation.4.clone.1 | convolution fusion | flops 673972224 | bytes 3412992 | tf_op jit(solution)/shard_map/while/body/eval_jaxpr/dot_general | solution.py:42
  25.5 1.8 %collective-permute-start = (bf16[128,1024]{1,0:T(8,128)(2,1)S(1)}, bf16[128,1024]{1,0:T(8,128)(2,1)S(1)}, u32[]{:S(2)}, u32[]{:S(2)}) collective-permute-start(bf16[128,1024]{1,0:T(8,128)(2,1)S(1)} %copy.30), channel_id=1, source_target_pairs={{0,1},{1,4},{4,5},{5,8},{8,9},{9,12},{12,13},{13,14},{14,15},{15,1... | collective-permute-start | bytes 786440 | tf_op jit(solution)/shard_map/while/body/eval_jaxpr/ppermute | solution.py:95
  29.7 2.9 %convolution_bitcast_fusion.2 = f32[256,256]{0,1:T(8,128)S(1)} fusion(bf16[1024,256]{1,0:T(8,128)(2,1)S(1)} %copy-done.7, bf16[256,1024]{1,0:T(8,128)(2,1)S(1)} %constant_dynamic-update-slice_fusion.9, bf16[1024,1024]{1,0:T(8,128)(2,1)} %get-tuple-element.278, f32[1024]{0:T(1024)S(1)} %get-tuple-element.277, f32[256]{0:T(256)S(1)} %multiply_reduce_fusion.6), kind=kOutput, calls=%fused_computation.4.clone.1 | convolution fusion | flops 673972224 | bytes 3412992 | tf_op jit(solution)/shard_map/while/body/eval_jaxpr/dot_general | solution.py:42
  32.9 1.9 %collective-permute-start = (bf16[128,1024]{1,0:T(8,128)(2,1)S(1)}, bf16[128,1024]{1,0:T(8,128)(2,1)S(1)}, u32[]{:S(2)}, u32[]{:S(2)}) collective-permute-start(bf16[128,1024]{1,0:T(8,128)(2,1)S(1)} %copy.30), channel_id=1, source_target_pairs={{0,1},{1,4},{4,5},{5,8},{8,9},{9,12},{12,13},{13,14},{14,15},{15,1... | collective-permute-start | bytes 786440 | tf_op jit(solution)/shard_map/while/body/eval_jaxpr/ppermute | solution.py:95
  37.2 2.9 %convolution_bitcast_fusion.2 = f32[256,256]{0,1:T(8,128)S(1)} fusion(bf16[1024,256]{1,0:T(8,128)(2,1)S(1)} %copy-done.7, bf16[256,1024]{1,0:T(8,128)(2,1)S(1)} %constant_dynamic-update-slice_fusion.9, bf16[1024,1024]{1,0:T(8,128)(2,1)} %get-tuple-element.278, f32[1024]{0:T(1024)S(1)} %get-tuple-element.277, f32[256]{0:T(256)S(1)} %multiply_reduce_fusion.6), kind=kOutput, calls=%fused_computation.4.clone.1 | convolution fusion | flops 673972224 | bytes 3412992 | tf_op jit(solution)/shard_map/while/body/eval_jaxpr/dot_general | solution.py:42
  40.4 1.9 %collective-permute-start = (bf16[128,1024]{1,0:T(8,128)(2,1)S(1)}, bf16[128,1024]{1,0:T(8,128)(2,1)S(1)}, u32[]{:S(2)}, u32[]{:S(2)}) collective-permute-start(bf16[128,1024]{1,0:T(8,128)(2,1)S(1)} %copy.30), channel_id=1, source_target_pairs={{0,1},{1,4},{4,5},{5,8},{8,9},{9,12},{12,13},{13,14},{14,15},{15,1... | collective-permute-start | bytes 786440 | tf_op jit(solution)/shard_map/while/body/eval_jaxpr/ppermute | solution.py:95
  44.6 2.9 %convolution_bitcast_fusion.2 = f32[256,256]{0,1:T(8,128)S(1)} fusion(bf16[1024,256]{1,0:T(8,128)(2,1)S(1)} %copy-done.7, bf16[256,1024]{1,0:T(8,128)(2,1)S(1)} %constant_dynamic-update-slice_fusion.9, bf16[1024,1024]{1,0:T(8,128)(2,1)} %get-tuple-element.278, f32[1024]{0:T(1024)S(1)} %get-tuple-element.277, f32[256]{0:T(256)S(1)} %multiply_reduce_fusion.6), kind=kOutput, calls=%fused_computation.4.clone.1 | convolution fusion | flops 673972224 | bytes 3412992 | tf_op jit(solution)/shard_map/while/body/eval_jaxpr/dot_general | solution.py:42
  47.8 1.9 %collective-permute-start = (bf16[128,1024]{1,0:T(8,128)(2,1)S(1)}, bf16[128,1024]{1,0:T(8,128)(2,1)S(1)}, u32[]{:S(2)}, u32[]{:S(2)}) collective-permute-start(bf16[128,1024]{1,0:T(8,128)(2,1)S(1)} %copy.30), channel_id=1, source_target_pairs={{0,1},{1,4},{4,5},{5,8},{8,9},{9,12},{12,13},{13,14},{14,15},{15,1... | collective-permute-start | bytes 786440 | tf_op jit(solution)/shard_map/while/body/eval_jaxpr/ppermute | solution.py:95
  52.0 2.9 %convolution_bitcast_fusion.2 = f32[256,256]{0,1:T(8,128)S(1)} fusion(bf16[1024,256]{1,0:T(8,128)(2,1)S(1)} %copy-done.7, bf16[256,1024]{1,0:T(8,128)(2,1)S(1)} %constant_dynamic-update-slice_fusion.9, bf16[1024,1024]{1,0:T(8,128)(2,1)} %get-tuple-element.278, f32[1024]{0:T(1024)S(1)} %get-tuple-element.277, f32[256]{0:T(256)S(1)} %multiply_reduce_fusion.6), kind=kOutput, calls=%fused_computation.4.clone.1 | convolution fusion | flops 673972224 | bytes 3412992 | tf_op jit(solution)/shard_map/while/body/eval_jaxpr/dot_general | solution.py:42
  55.3 1.9 %collective-permute-start = (bf16[128,1024]{1,0:T(8,128)(2,1)S(1)}, bf16[128,1024]{1,0:T(8,128)(2,1)S(1)}, u32[]{:S(2)}, u32[]{:S(2)}) collective-permute-start(bf16[128,1024]{1,0:T(8,128)(2,1)S(1)} %copy.30), channel_id=1, source_target_pairs={{0,1},{1,4},{4,5},{5,8},{8,9},{9,12},{12,13},{13,14},{14,15},{15,1... | collective-permute-start | bytes 786440 | tf_op jit(solution)/shard_map/while/body/eval_jaxpr/ppermute | solution.py:95
  57.8 1.4 collective-permute-start.3
  59.5 2.9 %convolution_bitcast_fusion.2 = f32[256,256]{0,1:T(8,128)S(1)} fusion(bf16[1024,256]{1,0:T(8,128)(2,1)S(1)} %copy-done.7, bf16[256,1024]{1,0:T(8,128)(2,1)S(1)} %constant_dynamic-update-slice_fusion.9, bf16[1024,1024]{1,0:T(8,128)(2,1)} %get-tuple-element.278, f32[1024]{0:T(1024)S(1)} %get-tuple-element.277, f32[256]{0:T(256)S(1)} %multiply_reduce_fusion.6), kind=kOutput, calls=%fused_computation.4.clone.1 | convolution fusion | flops 673972224 | bytes 3412992 | tf_op jit(solution)/shard_map/while/body/eval_jaxpr/dot_general | solution.py:42
  62.7 1.9 %collective-permute-start = (bf16[128,1024]{1,0:T(8,128)(2,1)S(1)}, bf16[128,1024]{1,0:T(8,128)(2,1)S(1)}, u32[]{:S(2)}, u32[]{:S(2)}) collective-permute-start(bf16[128,1024]{1,0:T(8,128)(2,1)S(1)} %copy.30), channel_id=1, source_target_pairs={{0,1},{1,4},{4,5},{5,8},{8,9},{9,12},{12,13},{13,14},{14,15},{15,1... | collective-permute-start | bytes 786440 | tf_op jit(solution)/shard_map/while/body/eval_jaxpr/ppermute | solution.py:95
  66.9 2.9 %convolution_bitcast_fusion.2 = f32[256,256]{0,1:T(8,128)S(1)} fusion(bf16[1024,256]{1,0:T(8,128)(2,1)S(1)} %copy-done.7, bf16[256,1024]{1,0:T(8,128)(2,1)S(1)} %constant_dynamic-update-slice_fusion.9, bf16[1024,1024]{1,0:T(8,128)(2,1)} %get-tuple-element.278, f32[1024]{0:T(1024)S(1)} %get-tuple-element.277, f32[256]{0:T(256)S(1)} %multiply_reduce_fusion.6), kind=kOutput, calls=%fused_computation.4.clone.1 | convolution fusion | flops 673972224 | bytes 3412992 | tf_op jit(solution)/shard_map/while/body/eval_jaxpr/dot_general | solution.py:42
  70.1 1.9 %collective-permute-start = (bf16[128,1024]{1,0:T(8,128)(2,1)S(1)}, bf16[128,1024]{1,0:T(8,128)(2,1)S(1)}, u32[]{:S(2)}, u32[]{:S(2)}) collective-permute-start(bf16[128,1024]{1,0:T(8,128)(2,1)S(1)} %copy.30), channel_id=1, source_target_pairs={{0,1},{1,4},{4,5},{5,8},{8,9},{9,12},{12,13},{13,14},{14,15},{15,1... | collective-permute-start | bytes 786440 | tf_op jit(solution)/shard_map/while/body/eval_jaxpr/ppermute | solution.py:95
  72.7 1.4 collective-permute-start.3
  74.3 2.9 %convolution_bitcast_fusion.2 = f32[256,256]{0,1:T(8,128)S(1)} fusion(bf16[1024,256]{1,0:T(8,128)(2,1)S(1)} %copy-done.7, bf16[256,1024]{1,0:T(8,128)(2,1)S(1)} %constant_dynamic-update-slice_fusion.9, bf16[1024,1024]{1,0:T(8,128)(2,1)} %get-tuple-element.278, f32[1024]{0:T(1024)S(1)} %get-tuple-element.277, f32[256]{0:T(256)S(1)} %multiply_reduce_fusion.6), kind=kOutput, calls=%fused_computation.4.clone.1 | convolution fusion | flops 673972224 | bytes 3412992 | tf_op jit(solution)/shard_map/while/body/eval_jaxpr/dot_general | solution.py:42
  77.6 1.9 %collective-permute-start = (bf16[128,1024]{1,0:T(8,128)(2,1)S(1)}, bf16[128,1024]{1,0:T(8,128)(2,1)S(1)}, u32[]{:S(2)}, u32[]{:S(2)}) collective-permute-start(bf16[128,1024]{1,0:T(8,128)(2,1)S(1)} %copy.30), channel_id=1, source_target_pairs={{0,1},{1,4},{4,5},{5,8},{8,9},{9,12},{12,13},{13,14},{14,15},{15,1... | collective-permute-start | bytes 786440 | tf_op jit(solution)/shard_map/while/body/eval_jaxpr/ppermute | solution.py:95
  81.8 2.9 %convolution_bitcast_fusion.2 = f32[256,256]{0,1:T(8,128)S(1)} fusion(bf16[1024,256]{1,0:T(8,128)(2,1)S(1)} %copy-done.7, bf16[256,1024]{1,0:T(8,128)(2,1)S(1)} %constant_dynamic-update-slice_fusion.9, bf16[1024,1024]{1,0:T(8,128)(2,1)} %get-tuple-element.278, f32[1024]{0:T(1024)S(1)} %get-tuple-element.277, f32[256]{0:T(256)S(1)} %multiply_reduce_fusion.6), kind=kOutput, calls=%fused_computation.4.clone.1 | convolution fusion | flops 673972224 | bytes 3412992 | tf_op jit(solution)/shard_map/while/body/eval_jaxpr/dot_general | solution.py:42
  85.0 1.9 %collective-permute-start = (bf16[128,1024]{1,0:T(8,128)(2,1)S(1)}, bf16[128,1024]{1,0:T(8,128)(2,1)S(1)}, u32[]{:S(2)}, u32[]{:S(2)}) collective-permute-start(bf16[128,1024]{1,0:T(8,128)(2,1)S(1)} %copy.30), channel_id=1, source_target_pairs={{0,1},{1,4},{4,5},{5,8},{8,9},{9,12},{12,13},{13,14},{14,15},{15,1... | collective-permute-start | bytes 786440 | tf_op jit(solution)/shard_map/while/body/eval_jaxpr/ppermute | solution.py:95
  89.2 2.9 %convolution_bitcast_fusion.2 = f32[256,256]{0,1:T(8,128)S(1)} fusion(bf16[1024,256]{1,0:T(8,128)(2,1)S(1)} %copy-done.7, bf16[256,1024]{1,0:T(8,128)(2,1)S(1)} %constant_dynamic-update-slice_fusion.9, bf16[1024,1024]{1,0:T(8,128)(2,1)} %get-tuple-element.278, f32[1024]{0:T(1024)S(1)} %get-tuple-element.277, f32[256]{0:T(256)S(1)} %multiply_reduce_fusion.6), kind=kOutput, calls=%fused_computation.4.clone.1 | convolution fusion | flops 673972224 | bytes 3412992 | tf_op jit(solution)/shard_map/while/body/eval_jaxpr/dot_general | solution.py:42
  92.4 1.9 %collective-permute-start = (bf16[128,1024]{1,0:T(8,128)(2,1)S(1)}, bf16[128,1024]{1,0:T(8,128)(2,1)S(1)}, u32[]{:S(2)}, u32[]{:S(2)}) collective-permute-start(bf16[128,1024]{1,0:T(8,128)(2,1)S(1)} %copy.30), channel_id=1, source_target_pairs={{0,1},{1,4},{4,5},{5,8},{8,9},{9,12},{12,13},{13,14},{14,15},{15,1... | collective-permute-start | bytes 786440 | tf_op jit(solution)/shard_map/while/body/eval_jaxpr/ppermute | solution.py:95
  96.6 2.9 %convolution_bitcast_fusion.2 = f32[256,256]{0,1:T(8,128)S(1)} fusion(bf16[1024,256]{1,0:T(8,128)(2,1)S(1)} %copy-done.7, bf16[256,1024]{1,0:T(8,128)(2,1)S(1)} %constant_dynamic-update-slice_fusion.9, bf16[1024,1024]{1,0:T(8,128)(2,1)} %get-tuple-element.278, f32[1024]{0:T(1024)S(1)} %get-tuple-element.277, f32[256]{0:T(256)S(1)} %multiply_reduce_fusion.6), kind=kOutput, calls=%fused_computation.4.clone.1 | convolution fusion | flops 673972224 | bytes 3412992 | tf_op jit(solution)/shard_map/while/body/eval_jaxpr/dot_general | solution.py:42
  99.9 1.9 %collective-permute-start = (bf16[128,1024]{1,0:T(8,128)(2,1)S(1)}, bf16[128,1024]{1,0:T(8,128)(2,1)S(1)}, u32[]{:S(2)}, u32[]{:S(2)}) collective-permute-start(bf16[128,1024]{1,0:T(8,128)(2,1)S(1)} %copy.30), channel_id=1, source_target_pairs={{0,1},{1,4},{4,5},{5,8},{8,9},{9,12},{12,13},{13,14},{14,15},{15,1... | collective-permute-start | bytes 786440 | tf_op jit(solution)/shard_map/while/body/eval_jaxpr/ppermute | solution.py:95
  104.1 2.9 %convolution_bitcast_fusion.2 = f32[256,256]{0,1:T(8,128)S(1)} fusion(bf16[1024,256]{1,0:T(8,128)(2,1)S(1)} %copy-done.7, bf16[256,1024]{1,0:T(8,128)(2,1)S(1)} %constant_dynamic-update-slice_fusion.9, bf16[1024,1024]{1,0:T(8,128)(2,1)} %get-tuple-element.278, f32[1024]{0:T(1024)S(1)} %get-tuple-element.277, f32[256]{0:T(256)S(1)} %multiply_reduce_fusion.6), kind=kOutput, calls=%fused_computation.4.clone.1 | convolution fusion | flops 673972224 | bytes 3412992 | tf_op jit(solution)/shard_map/while/body/eval_jaxpr/dot_general | solution.py:42
  107.3 1.9 %collective-permute-start = (bf16[128,1024]{1,0:T(8,128)(2,1)S(1)}, bf16[128,1024]{1,0:T(8,128)(2,1)S(1)}, u32[]{:S(2)}, u32[]{:S(2)}) collective-permute-start(bf16[128,1024]{1,0:T(8,128)(2,1)S(1)} %copy.30), channel_id=1, source_target_pairs={{0,1},{1,4},{4,5},{5,8},{8,9},{9,12},{12,13},{13,14},{14,15},{15,1... | collective-permute-start | bytes 786440 | tf_op jit(solution)/shard_map/while/body/eval_jaxpr/ppermute | solution.py:95
  111.5 2.9 %convolution_bitcast_fusion.2 = f32[256,256]{0,1:T(8,128)S(1)} fusion(bf16[1024,256]{1,0:T(8,128)(2,1)S(1)} %copy-done.7, bf16[256,1024]{1,0:T(8,128)(2,1)S(1)} %constant_dynamic-update-slice_fusion.9, bf16[1024,1024]{1,0:T(8,128)(2,1)} %get-tuple-element.278, f32[1024]{0:T(1024)S(1)} %get-tuple-element.277, f32[256]{0:T(256)S(1)} %multiply_reduce_fusion.6), kind=kOutput, calls=%fused_computation.4.clone.1 | convolution fusion | flops 673972224 | bytes 3412992 | tf_op jit(solution)/shard_map/while/body/eval_jaxpr/dot_general | solution.py:42
  114.9 2.0 %collective-permute-start.8 = (f32[256,128]{1,0:T(8,128)S(1)}, f32[256,128]{1,0:T(8,128)}, u32[]{:S(2)}, u32[]{:S(2)}) collective-permute-start(f32[256,128]{1,0:T(8,128)S(1)} %add.198), channel_id=1, source_target_pairs={{0,1},{1,4},{4,5},{5,8},{8,9},{9,12},{12,13},{13,14},{14,15},{15,1... | collective-permute-start | bytes 393224 | tf_op jit(solution)/shard_map/ppermute | solution.py:95
  118.9 2.7 %fusion.25 = f32[256,256]{1,0:T(8,128)S(1)} fusion(bf16[1024,256]{1,0:T(8,128)(2,1)} %get-tuple-element.292, bf16[256,1024]{1,0:T(8,128)(2,1)} %copy-done.5, bf16[1024,1024]{1,0:T(8,128)(2,1)S(1)} %copy-done.2, f32[256]{0:T(256)S(1)} %multiply_reduce_fusion.2, f32[1024]{0:T(1024)S(1)} %get-tuple-element.306), kind=kOutput, calls=%fused_computation.38 | convolution fusion | flops 673972224 | bytes 3412992 | tf_op jit(solution)/shard_map/dot_general | solution.py:42
  121.8 1.7 %slice_add_fusion.1 = (f32[256,128]{1,0:T(8,128)S(1)}, f32[256,128]{1,0:T(8,128)}) fusion(f32[256,128]{1,0:T(8,128)} %collective-permute-done.8, f32[256,256]{1,0:T(8,128)S(1)} %fusion.25, f32[256,128]{1,0:T(8,128)} %collective-permute-done.10), kind=kLoop, calls=%fused_computation.70 | loop fusion | flops 65536 | bytes 786432 | tf_op jit(solution)/shard_map/add | solution.py:114
  123.4 1.9 %collective-permute-start.11 = (f32[256,128]{1,0:T(8,128)}, f32[256,128]{1,0:T(8,128)}, u32[]{:S(2)}, u32[]{:S(2)}) collective-permute-start(f32[256,128]{1,0:T(8,128)} %get-tuple-element.180), channel_id=1, source_target_pairs={{1,0},{4,1},{5,4},{8,5},{9,8},{12,9},{13,12},{14,13},{15,14},{10,1... | collective-permute-start | bytes 393224 | tf_op jit(solution)/shard_map/ppermute | solution.py:95
  125.3 1.4 fusion.29
  126.8 1.4 collective-permute-done.11
  128.1 1.7 %collective-permute-done.9 = f32[256,128]{1,0:T(8,128)} collective-permute-done((f32[256,128]{1,0:T(8,128)S(1)}, f32[256,128]{1,0:T(8,128)}, u32[]{:S(2)}, u32[]{:S(2)}) %collective-permute-start.9) | collective-permute-done | bytes 131104 | tf_op jit(solution)/shard_map/ppermute | solution.py:95
  130.8 2.0 %collective-permute-start.12 = (f32[2,2,2,16,256]{4,3,2,1,0:T(8,128)S(1)}, f32[2,2,2,16,256]{4,3,2,1,0:T(8,128)S(1)}, u32[]{:S(2)}, u32[]{:S(2)}) collective-permute-start(f32[2,2,2,16,256]{4,3,2,1,0:T(8,128)S(1)} %dynamic-slice_bitcast_fusion), channel_id=1, source_target_pairs={{0,16},{16,0},{32,48},{48,32},{64,80},{80,64},{96,112},{112,96},{1... | collective-permute-start | bytes 393224 | tf_op jit(solution)/shard_map/ppermute | solution.py:62
  132.8 3.8 %collective-permute-done.12 = f32[2,2,2,16,256]{4,3,2,1,0:T(8,128)S(1)} collective-permute-done((f32[2,2,2,16,256]{4,3,2,1,0:T(8,128)S(1)}, f32[2,2,2,16,256]{4,3,2,1,0:T(8,128)S(1)}, u32[]{:S(2)}, u32[]{:S(2)}) %collective-permute-start.12) | collective-permute-done | bytes 131104 | tf_op jit(solution)/shard_map/ppermute | solution.py:62
  136.7 3.3 %collective-permute-start.13 = (f32[2,2,16,256]{3,2,1,0:T(8,128)S(1)}, f32[2,2,16,256]{3,2,1,0:T(8,128)S(1)}, u32[]{:S(2)}, u32[]{:S(2)}) collective-permute-start(f32[2,2,16,256]{3,2,1,0:T(8,128)S(1)} %dynamic-slice_bitcast_fusion.1), channel_id=1, source_target_pairs={{0,32},{16,48},{32,0},{48,16},{64,96},{80,112},{96,64},{112,80},{1... | collective-permute-start | bytes 196616 | tf_op jit(solution)/shard_map/ppermute | solution.py:62
  140.0 2.7 %collective-permute-done.13 = f32[2,2,16,256]{3,2,1,0:T(8,128)S(1)} collective-permute-done((f32[2,2,16,256]{3,2,1,0:T(8,128)S(1)}, f32[2,2,16,256]{3,2,1,0:T(8,128)S(1)}, u32[]{:S(2)}, u32[]{:S(2)}) %collective-permute-start.13) | collective-permute-done | bytes 65568 | tf_op jit(solution)/shard_map/ppermute | solution.py:62
  142.8 3.2 %collective-permute-start.14 = (f32[2,16,256]{2,1,0:T(8,128)S(1)}, f32[2,16,256]{2,1,0:T(8,128)S(1)}, u32[]{:S(2)}, u32[]{:S(2)}) collective-permute-start(f32[2,16,256]{2,1,0:T(8,128)S(1)} %dynamic-slice_bitcast_fusion.2), channel_id=1, source_target_pairs={{0,128},{16,144},{32,160},{48,176},{64,192},{80,208},{96,224},{112... | collective-permute-start | bytes 98312 | tf_op jit(solution)/shard_map/ppermute | solution.py:62
  146.0 2.3 %collective-permute-done.14 = f32[2,16,256]{2,1,0:T(8,128)S(1)} collective-permute-done((f32[2,16,256]{2,1,0:T(8,128)S(1)}, f32[2,16,256]{2,1,0:T(8,128)S(1)}, u32[]{:S(2)}, u32[]{:S(2)}) %collective-permute-start.14) | collective-permute-done | bytes 32800 | tf_op jit(solution)/shard_map/ppermute | solution.py:62
  148.3 7.0 %collective-permute-start.15 = (f32[16,256]{1,0:T(8,128)S(1)}, f32[16,256]{1,0:T(8,128)S(1)}, u32[]{:S(2)}, u32[]{:S(2)}) collective-permute-start(f32[16,256]{1,0:T(8,128)S(1)} %dynamic-slice_bitcast_fusion.3), channel_id=1, source_target_pairs={{0,64},{16,80},{32,96},{48,112},{64,0},{80,16},{96,32},{112,48},{1... | collective-permute-start | bytes 49160 | tf_op jit(solution)/shard_map/ppermute | solution.py:62
  155.3 1.8 %collective-permute-done.15 = f32[16,256]{1,0:T(8,128)S(1)} collective-permute-done((f32[16,256]{1,0:T(8,128)S(1)}, f32[16,256]{1,0:T(8,128)S(1)}, u32[]{:S(2)}, u32[]{:S(2)}) %collective-permute-start.15) | collective-permute-done | bytes 16416 | tf_op jit(solution)/shard_map/ppermute | solution.py:62
  (282 shorter events, 45.2 us)
Async XLA Ops:
  4.2 6.5 %collective-permute-start.4 = (bf16[128,1024]{1,0:T(8,128)(2,1)S(1)}, bf16[128,1024]{1,0:T(8,128)(2,1)S(1)}, u32[]{:S(2)}, u32[]{:S(2)}) collective-permute-start(bf16[128,1024]{1,0:T(8,128)(2,1)S(1)} %get-tuple-element.178), channel_id=1, source_target_pairs={{0,1},{1,4},{4,5},{5,8},{8,9},{9,12},{12,13},{13,14},{14,15},{15,1... | collective-permute-start | bytes 786440 | tf_op jit(solution)/shard_map/ppermute | solution.py:95
  4.2 6.5 %collective-permute-start.6 = (bf16[128,1024]{1,0:T(8,128)(2,1)}, bf16[128,1024]{1,0:T(8,128)(2,1)}, u32[]{:S(2)}, u32[]{:S(2)}) collective-permute-start(bf16[128,1024]{1,0:T(8,128)(2,1)} %get-tuple-element.177), channel_id=1, source_target_pairs={{1,0},{4,1},{5,4},{8,5},{9,8},{12,9},{13,12},{14,13},{15,14},{10,1... | collective-permute-start | bytes 786440 | tf_op jit(solution)/shard_map/ppermute | solution.py:95
  11.9 6.2 %collective-permute-start.5 = (bf16[128,1024]{1,0:T(8,128)(2,1)S(1)}, bf16[128,1024]{1,0:T(8,128)(2,1)S(1)}, u32[]{:S(2)}, u32[]{:S(2)}) collective-permute-start(bf16[128,1024]{1,0:T(8,128)(2,1)S(1)} %collective-permute-done.4), channel_id=1, source_target_pairs={{0,1},{1,4},{4,5},{5,8},{8,9},{9,12},{12,13},{13,14},{14,15},{15,1... | collective-permute-start | bytes 786440 | tf_op jit(solution)/shard_map/ppermute | solution.py:95
  18.2 7.3 %collective-permute-start = (bf16[128,1024]{1,0:T(8,128)(2,1)S(1)}, bf16[128,1024]{1,0:T(8,128)(2,1)S(1)}, u32[]{:S(2)}, u32[]{:S(2)}) collective-permute-start(bf16[128,1024]{1,0:T(8,128)(2,1)S(1)} %copy.30), channel_id=1, source_target_pairs={{0,1},{1,4},{4,5},{5,8},{8,9},{9,12},{12,13},{13,14},{14,15},{15,1... | collective-permute-start | bytes 786440 | tf_op jit(solution)/shard_map/while/body/eval_jaxpr/ppermute | solution.py:95
  19.8 5.6 %collective-permute-start.1 = (bf16[128,1024]{1,0:T(8,128)(2,1)S(1)}, bf16[128,1024]{1,0:T(8,128)(2,1)S(1)}, u32[]{:S(2)}, u32[]{:S(2)}) collective-permute-start(bf16[128,1024]{1,0:T(8,128)(2,1)S(1)} %copy.31), channel_id=1, source_target_pairs={{1,0},{4,1},{5,4},{8,5},{9,8},{12,9},{13,12},{14,13},{15,14},{10,1... | collective-permute-start | bytes 786440 | tf_op jit(solution)/shard_map/while/body/eval_jaxpr/ppermute | solution.py:95
  20.1 5.3 %collective-permute-start.2 = (f32[256,128]{0,1:T(8,128)S(1)}, f32[256,128]{0,1:T(8,128)S(1)}, u32[]{:S(2)}, u32[]{:S(2)}) collective-permute-start(f32[256,128]{0,1:T(8,128)S(1)} %add.322), channel_id=1, source_target_pairs={{0,1},{1,4},{4,5},{5,8},{8,9},{9,12},{12,13},{13,14},{14,15},{15,1... | collective-permute-start | bytes 393224 | tf_op jit(solution)/shard_map/while/body/eval_jaxpr/ppermute | solution.py:95
  20.5 4.9 %collective-permute-start.3 = (f32[256,128]{0,1:T(8,128)S(1)}, f32[256,128]{0,1:T(8,128)S(1)}, u32[]{:S(2)}, u32[]{:S(2)}) collective-permute-start(f32[256,128]{0,1:T(8,128)S(1)} %add.323), channel_id=1, source_target_pairs={{1,0},{4,1},{5,4},{8,5},{9,8},{12,9},{13,12},{14,13},{15,14},{10,1... | collective-permute-start | bytes 393224 | tf_op jit(solution)/shard_map/while/body/eval_jaxpr/ppermute | solution.py:95
  25.5 7.4 %collective-permute-start = (bf16[128,1024]{1,0:T(8,128)(2,1)S(1)}, bf16[128,1024]{1,0:T(8,128)(2,1)S(1)}, u32[]{:S(2)}, u32[]{:S(2)}) collective-permute-start(bf16[128,1024]{1,0:T(8,128)(2,1)S(1)} %copy.30), channel_id=1, source_target_pairs={{0,1},{1,4},{4,5},{5,8},{8,9},{9,12},{12,13},{13,14},{14,15},{15,1... | collective-permute-start | bytes 786440 | tf_op jit(solution)/shard_map/while/body/eval_jaxpr/ppermute | solution.py:95
  27.4 5.5 %collective-permute-start.1 = (bf16[128,1024]{1,0:T(8,128)(2,1)S(1)}, bf16[128,1024]{1,0:T(8,128)(2,1)S(1)}, u32[]{:S(2)}, u32[]{:S(2)}) collective-permute-start(bf16[128,1024]{1,0:T(8,128)(2,1)S(1)} %copy.31), channel_id=1, source_target_pairs={{1,0},{4,1},{5,4},{8,5},{9,8},{12,9},{13,12},{14,13},{15,14},{10,1... | collective-permute-start | bytes 786440 | tf_op jit(solution)/shard_map/while/body/eval_jaxpr/ppermute | solution.py:95
  27.6 5.3 %collective-permute-start.2 = (f32[256,128]{0,1:T(8,128)S(1)}, f32[256,128]{0,1:T(8,128)S(1)}, u32[]{:S(2)}, u32[]{:S(2)}) collective-permute-start(f32[256,128]{0,1:T(8,128)S(1)} %add.322), channel_id=1, source_target_pairs={{0,1},{1,4},{4,5},{5,8},{8,9},{9,12},{12,13},{13,14},{14,15},{15,1... | collective-permute-start | bytes 393224 | tf_op jit(solution)/shard_map/while/body/eval_jaxpr/ppermute | solution.py:95
  32.9 7.4 %collective-permute-start = (bf16[128,1024]{1,0:T(8,128)(2,1)S(1)}, bf16[128,1024]{1,0:T(8,128)(2,1)S(1)}, u32[]{:S(2)}, u32[]{:S(2)}) collective-permute-start(bf16[128,1024]{1,0:T(8,128)(2,1)S(1)} %copy.30), channel_id=1, source_target_pairs={{0,1},{1,4},{4,5},{5,8},{8,9},{9,12},{12,13},{13,14},{14,15},{15,1... | collective-permute-start | bytes 786440 | tf_op jit(solution)/shard_map/while/body/eval_jaxpr/ppermute | solution.py:95
  34.8 5.5 %collective-permute-start.1 = (bf16[128,1024]{1,0:T(8,128)(2,1)S(1)}, bf16[128,1024]{1,0:T(8,128)(2,1)S(1)}, u32[]{:S(2)}, u32[]{:S(2)}) collective-permute-start(bf16[128,1024]{1,0:T(8,128)(2,1)S(1)} %copy.31), channel_id=1, source_target_pairs={{1,0},{4,1},{5,4},{8,5},{9,8},{12,9},{13,12},{14,13},{15,14},{10,1... | collective-permute-start | bytes 786440 | tf_op jit(solution)/shard_map/while/body/eval_jaxpr/ppermute | solution.py:95
  35.0 5.3 %collective-permute-start.2 = (f32[256,128]{0,1:T(8,128)S(1)}, f32[256,128]{0,1:T(8,128)S(1)}, u32[]{:S(2)}, u32[]{:S(2)}) collective-permute-start(f32[256,128]{0,1:T(8,128)S(1)} %add.322), channel_id=1, source_target_pairs={{0,1},{1,4},{4,5},{5,8},{8,9},{9,12},{12,13},{13,14},{14,15},{15,1... | collective-permute-start | bytes 393224 | tf_op jit(solution)/shard_map/while/body/eval_jaxpr/ppermute | solution.py:95
  40.4 7.4 %collective-permute-start = (bf16[128,1024]{1,0:T(8,128)(2,1)S(1)}, bf16[128,1024]{1,0:T(8,128)(2,1)S(1)}, u32[]{:S(2)}, u32[]{:S(2)}) collective-permute-start(bf16[128,1024]{1,0:T(8,128)(2,1)S(1)} %copy.30), channel_id=1, source_target_pairs={{0,1},{1,4},{4,5},{5,8},{8,9},{9,12},{12,13},{13,14},{14,15},{15,1... | collective-permute-start | bytes 786440 | tf_op jit(solution)/shard_map/while/body/eval_jaxpr/ppermute | solution.py:95
  42.3 5.5 %collective-permute-start.1 = (bf16[128,1024]{1,0:T(8,128)(2,1)S(1)}, bf16[128,1024]{1,0:T(8,128)(2,1)S(1)}, u32[]{:S(2)}, u32[]{:S(2)}) collective-permute-start(bf16[128,1024]{1,0:T(8,128)(2,1)S(1)} %copy.31), channel_id=1, source_target_pairs={{1,0},{4,1},{5,4},{8,5},{9,8},{12,9},{13,12},{14,13},{15,14},{10,1... | collective-permute-start | bytes 786440 | tf_op jit(solution)/shard_map/while/body/eval_jaxpr/ppermute | solution.py:95
  42.4 5.3 %collective-permute-start.2 = (f32[256,128]{0,1:T(8,128)S(1)}, f32[256,128]{0,1:T(8,128)S(1)}, u32[]{:S(2)}, u32[]{:S(2)}) collective-permute-start(f32[256,128]{0,1:T(8,128)S(1)} %add.322), channel_id=1, source_target_pairs={{0,1},{1,4},{4,5},{5,8},{8,9},{9,12},{12,13},{13,14},{14,15},{15,1... | collective-permute-start | bytes 393224 | tf_op jit(solution)/shard_map/while/body/eval_jaxpr/ppermute | solution.py:95
  47.8 7.4 %collective-permute-start = (bf16[128,1024]{1,0:T(8,128)(2,1)S(1)}, bf16[128,1024]{1,0:T(8,128)(2,1)S(1)}, u32[]{:S(2)}, u32[]{:S(2)}) collective-permute-start(bf16[128,1024]{1,0:T(8,128)(2,1)S(1)} %copy.30), channel_id=1, source_target_pairs={{0,1},{1,4},{4,5},{5,8},{8,9},{9,12},{12,13},{13,14},{14,15},{15,1... | collective-permute-start | bytes 786440 | tf_op jit(solution)/shard_map/while/body/eval_jaxpr/ppermute | solution.py:95
  49.7 5.5 %collective-permute-start.1 = (bf16[128,1024]{1,0:T(8,128)(2,1)S(1)}, bf16[128,1024]{1,0:T(8,128)(2,1)S(1)}, u32[]{:S(2)}, u32[]{:S(2)}) collective-permute-start(bf16[128,1024]{1,0:T(8,128)(2,1)S(1)} %copy.31), channel_id=1, source_target_pairs={{1,0},{4,1},{5,4},{8,5},{9,8},{12,9},{13,12},{14,13},{15,14},{10,1... | collective-permute-start | bytes 786440 | tf_op jit(solution)/shard_map/while/body/eval_jaxpr/ppermute | solution.py:95
  49.9 5.3 %collective-permute-start.2 = (f32[256,128]{0,1:T(8,128)S(1)}, f32[256,128]{0,1:T(8,128)S(1)}, u32[]{:S(2)}, u32[]{:S(2)}) collective-permute-start(f32[256,128]{0,1:T(8,128)S(1)} %add.322), channel_id=1, source_target_pairs={{0,1},{1,4},{4,5},{5,8},{8,9},{9,12},{12,13},{13,14},{14,15},{15,1... | collective-permute-start | bytes 393224 | tf_op jit(solution)/shard_map/while/body/eval_jaxpr/ppermute | solution.py:95
  55.3 7.4 %collective-permute-start = (bf16[128,1024]{1,0:T(8,128)(2,1)S(1)}, bf16[128,1024]{1,0:T(8,128)(2,1)S(1)}, u32[]{:S(2)}, u32[]{:S(2)}) collective-permute-start(bf16[128,1024]{1,0:T(8,128)(2,1)S(1)} %copy.30), channel_id=1, source_target_pairs={{0,1},{1,4},{4,5},{5,8},{8,9},{9,12},{12,13},{13,14},{14,15},{15,1... | collective-permute-start | bytes 786440 | tf_op jit(solution)/shard_map/while/body/eval_jaxpr/ppermute | solution.py:95
  57.1 5.5 %collective-permute-start.1 = (bf16[128,1024]{1,0:T(8,128)(2,1)S(1)}, bf16[128,1024]{1,0:T(8,128)(2,1)S(1)}, u32[]{:S(2)}, u32[]{:S(2)}) collective-permute-start(bf16[128,1024]{1,0:T(8,128)(2,1)S(1)} %copy.31), channel_id=1, source_target_pairs={{1,0},{4,1},{5,4},{8,5},{9,8},{12,9},{13,12},{14,13},{15,14},{10,1... | collective-permute-start | bytes 786440 | tf_op jit(solution)/shard_map/while/body/eval_jaxpr/ppermute | solution.py:95
  57.3 5.3 %collective-permute-start.2 = (f32[256,128]{0,1:T(8,128)S(1)}, f32[256,128]{0,1:T(8,128)S(1)}, u32[]{:S(2)}, u32[]{:S(2)}) collective-permute-start(f32[256,128]{0,1:T(8,128)S(1)} %add.322), channel_id=1, source_target_pairs={{0,1},{1,4},{4,5},{5,8},{8,9},{9,12},{12,13},{13,14},{14,15},{15,1... | collective-permute-start | bytes 393224 | tf_op jit(solution)/shard_map/while/body/eval_jaxpr/ppermute | solution.py:95
  62.7 7.4 %collective-permute-start = (bf16[128,1024]{1,0:T(8,128)(2,1)S(1)}, bf16[128,1024]{1,0:T(8,128)(2,1)S(1)}, u32[]{:S(2)}, u32[]{:S(2)}) collective-permute-start(bf16[128,1024]{1,0:T(8,128)(2,1)S(1)} %copy.30), channel_id=1, source_target_pairs={{0,1},{1,4},{4,5},{5,8},{8,9},{9,12},{12,13},{13,14},{14,15},{15,1... | collective-permute-start | bytes 786440 | tf_op jit(solution)/shard_map/while/body/eval_jaxpr/ppermute | solution.py:95
  64.6 5.5 %collective-permute-start.1 = (bf16[128,1024]{1,0:T(8,128)(2,1)S(1)}, bf16[128,1024]{1,0:T(8,128)(2,1)S(1)}, u32[]{:S(2)}, u32[]{:S(2)}) collective-permute-start(bf16[128,1024]{1,0:T(8,128)(2,1)S(1)} %copy.31), channel_id=1, source_target_pairs={{1,0},{4,1},{5,4},{8,5},{9,8},{12,9},{13,12},{14,13},{15,14},{10,1... | collective-permute-start | bytes 786440 | tf_op jit(solution)/shard_map/while/body/eval_jaxpr/ppermute | solution.py:95
  64.7 5.3 %collective-permute-start.2 = (f32[256,128]{0,1:T(8,128)S(1)}, f32[256,128]{0,1:T(8,128)S(1)}, u32[]{:S(2)}, u32[]{:S(2)}) collective-permute-start(f32[256,128]{0,1:T(8,128)S(1)} %add.322), channel_id=1, source_target_pairs={{0,1},{1,4},{4,5},{5,8},{8,9},{9,12},{12,13},{13,14},{14,15},{15,1... | collective-permute-start | bytes 393224 | tf_op jit(solution)/shard_map/while/body/eval_jaxpr/ppermute | solution.py:95
  70.1 7.4 %collective-permute-start = (bf16[128,1024]{1,0:T(8,128)(2,1)S(1)}, bf16[128,1024]{1,0:T(8,128)(2,1)S(1)}, u32[]{:S(2)}, u32[]{:S(2)}) collective-permute-start(bf16[128,1024]{1,0:T(8,128)(2,1)S(1)} %copy.30), channel_id=1, source_target_pairs={{0,1},{1,4},{4,5},{5,8},{8,9},{9,12},{12,13},{13,14},{14,15},{15,1... | collective-permute-start | bytes 786440 | tf_op jit(solution)/shard_map/while/body/eval_jaxpr/ppermute | solution.py:95
  72.0 5.5 %collective-permute-start.1 = (bf16[128,1024]{1,0:T(8,128)(2,1)S(1)}, bf16[128,1024]{1,0:T(8,128)(2,1)S(1)}, u32[]{:S(2)}, u32[]{:S(2)}) collective-permute-start(bf16[128,1024]{1,0:T(8,128)(2,1)S(1)} %copy.31), channel_id=1, source_target_pairs={{1,0},{4,1},{5,4},{8,5},{9,8},{12,9},{13,12},{14,13},{15,14},{10,1... | collective-permute-start | bytes 786440 | tf_op jit(solution)/shard_map/while/body/eval_jaxpr/ppermute | solution.py:95
  72.2 5.3 %collective-permute-start.2 = (f32[256,128]{0,1:T(8,128)S(1)}, f32[256,128]{0,1:T(8,128)S(1)}, u32[]{:S(2)}, u32[]{:S(2)}) collective-permute-start(f32[256,128]{0,1:T(8,128)S(1)} %add.322), channel_id=1, source_target_pairs={{0,1},{1,4},{4,5},{5,8},{8,9},{9,12},{12,13},{13,14},{14,15},{15,1... | collective-permute-start | bytes 393224 | tf_op jit(solution)/shard_map/while/body/eval_jaxpr/ppermute | solution.py:95
  77.6 7.4 %collective-permute-start = (bf16[128,1024]{1,0:T(8,128)(2,1)S(1)}, bf16[128,1024]{1,0:T(8,128)(2,1)S(1)}, u32[]{:S(2)}, u32[]{:S(2)}) collective-permute-start(bf16[128,1024]{1,0:T(8,128)(2,1)S(1)} %copy.30), channel_id=1, source_target_pairs={{0,1},{1,4},{4,5},{5,8},{8,9},{9,12},{12,13},{13,14},{14,15},{15,1... | collective-permute-start | bytes 786440 | tf_op jit(solution)/shard_map/while/body/eval_jaxpr/ppermute | solution.py:95
  79.4 5.5 %collective-permute-start.1 = (bf16[128,1024]{1,0:T(8,128)(2,1)S(1)}, bf16[128,1024]{1,0:T(8,128)(2,1)S(1)}, u32[]{:S(2)}, u32[]{:S(2)}) collective-permute-start(bf16[128,1024]{1,0:T(8,128)(2,1)S(1)} %copy.31), channel_id=1, source_target_pairs={{1,0},{4,1},{5,4},{8,5},{9,8},{12,9},{13,12},{14,13},{15,14},{10,1... | collective-permute-start | bytes 786440 | tf_op jit(solution)/shard_map/while/body/eval_jaxpr/ppermute | solution.py:95
  79.6 5.3 %collective-permute-start.2 = (f32[256,128]{0,1:T(8,128)S(1)}, f32[256,128]{0,1:T(8,128)S(1)}, u32[]{:S(2)}, u32[]{:S(2)}) collective-permute-start(f32[256,128]{0,1:T(8,128)S(1)} %add.322), channel_id=1, source_target_pairs={{0,1},{1,4},{4,5},{5,8},{8,9},{9,12},{12,13},{13,14},{14,15},{15,1... | collective-permute-start | bytes 393224 | tf_op jit(solution)/shard_map/while/body/eval_jaxpr/ppermute | solution.py:95
  85.0 7.4 %collective-permute-start = (bf16[128,1024]{1,0:T(8,128)(2,1)S(1)}, bf16[128,1024]{1,0:T(8,128)(2,1)S(1)}, u32[]{:S(2)}, u32[]{:S(2)}) collective-permute-start(bf16[128,1024]{1,0:T(8,128)(2,1)S(1)} %copy.30), channel_id=1, source_target_pairs={{0,1},{1,4},{4,5},{5,8},{8,9},{9,12},{12,13},{13,14},{14,15},{15,1... | collective-permute-start | bytes 786440 | tf_op jit(solution)/shard_map/while/body/eval_jaxpr/ppermute | solution.py:95
  86.9 5.5 %collective-permute-start.1 = (bf16[128,1024]{1,0:T(8,128)(2,1)S(1)}, bf16[128,1024]{1,0:T(8,128)(2,1)S(1)}, u32[]{:S(2)}, u32[]{:S(2)}) collective-permute-start(bf16[128,1024]{1,0:T(8,128)(2,1)S(1)} %copy.31), channel_id=1, source_target_pairs={{1,0},{4,1},{5,4},{8,5},{9,8},{12,9},{13,12},{14,13},{15,14},{10,1... | collective-permute-start | bytes 786440 | tf_op jit(solution)/shard_map/while/body/eval_jaxpr/ppermute | solution.py:95
  87.0 5.3 %collective-permute-start.2 = (f32[256,128]{0,1:T(8,128)S(1)}, f32[256,128]{0,1:T(8,128)S(1)}, u32[]{:S(2)}, u32[]{:S(2)}) collective-permute-start(f32[256,128]{0,1:T(8,128)S(1)} %add.322), channel_id=1, source_target_pairs={{0,1},{1,4},{4,5},{5,8},{8,9},{9,12},{12,13},{13,14},{14,15},{15,1... | collective-permute-start | bytes 393224 | tf_op jit(solution)/shard_map/while/body/eval_jaxpr/ppermute | solution.py:95
  92.4 7.4 %collective-permute-start = (bf16[128,1024]{1,0:T(8,128)(2,1)S(1)}, bf16[128,1024]{1,0:T(8,128)(2,1)S(1)}, u32[]{:S(2)}, u32[]{:S(2)}) collective-permute-start(bf16[128,1024]{1,0:T(8,128)(2,1)S(1)} %copy.30), channel_id=1, source_target_pairs={{0,1},{1,4},{4,5},{5,8},{8,9},{9,12},{12,13},{13,14},{14,15},{15,1... | collective-permute-start | bytes 786440 | tf_op jit(solution)/shard_map/while/body/eval_jaxpr/ppermute | solution.py:95
  94.3 5.5 %collective-permute-start.1 = (bf16[128,1024]{1,0:T(8,128)(2,1)S(1)}, bf16[128,1024]{1,0:T(8,128)(2,1)S(1)}, u32[]{:S(2)}, u32[]{:S(2)}) collective-permute-start(bf16[128,1024]{1,0:T(8,128)(2,1)S(1)} %copy.31), channel_id=1, source_target_pairs={{1,0},{4,1},{5,4},{8,5},{9,8},{12,9},{13,12},{14,13},{15,14},{10,1... | collective-permute-start | bytes 786440 | tf_op jit(solution)/shard_map/while/body/eval_jaxpr/ppermute | solution.py:95
  94.5 5.3 %collective-permute-start.2 = (f32[256,128]{0,1:T(8,128)S(1)}, f32[256,128]{0,1:T(8,128)S(1)}, u32[]{:S(2)}, u32[]{:S(2)}) collective-permute-start(f32[256,128]{0,1:T(8,128)S(1)} %add.322), channel_id=1, source_target_pairs={{0,1},{1,4},{4,5},{5,8},{8,9},{9,12},{12,13},{13,14},{14,15},{15,1... | collective-permute-start | bytes 393224 | tf_op jit(solution)/shard_map/while/body/eval_jaxpr/ppermute | solution.py:95
  99.9 7.4 %collective-permute-start = (bf16[128,1024]{1,0:T(8,128)(2,1)S(1)}, bf16[128,1024]{1,0:T(8,128)(2,1)S(1)}, u32[]{:S(2)}, u32[]{:S(2)}) collective-permute-start(bf16[128,1024]{1,0:T(8,128)(2,1)S(1)} %copy.30), channel_id=1, source_target_pairs={{0,1},{1,4},{4,5},{5,8},{8,9},{9,12},{12,13},{13,14},{14,15},{15,1... | collective-permute-start | bytes 786440 | tf_op jit(solution)/shard_map/while/body/eval_jaxpr/ppermute | solution.py:95
  101.7 5.5 %collective-permute-start.1 = (bf16[128,1024]{1,0:T(8,128)(2,1)S(1)}, bf16[128,1024]{1,0:T(8,128)(2,1)S(1)}, u32[]{:S(2)}, u32[]{:S(2)}) collective-permute-start(bf16[128,1024]{1,0:T(8,128)(2,1)S(1)} %copy.31), channel_id=1, source_target_pairs={{1,0},{4,1},{5,4},{8,5},{9,8},{12,9},{13,12},{14,13},{15,14},{10,1... | collective-permute-start | bytes 786440 | tf_op jit(solution)/shard_map/while/body/eval_jaxpr/ppermute | solution.py:95
  101.9 5.3 %collective-permute-start.2 = (f32[256,128]{0,1:T(8,128)S(1)}, f32[256,128]{0,1:T(8,128)S(1)}, u32[]{:S(2)}, u32[]{:S(2)}) collective-permute-start(f32[256,128]{0,1:T(8,128)S(1)} %add.322), channel_id=1, source_target_pairs={{0,1},{1,4},{4,5},{5,8},{8,9},{9,12},{12,13},{13,14},{14,15},{15,1... | collective-permute-start | bytes 393224 | tf_op jit(solution)/shard_map/while/body/eval_jaxpr/ppermute | solution.py:95
  107.3 7.4 %collective-permute-start = (bf16[128,1024]{1,0:T(8,128)(2,1)S(1)}, bf16[128,1024]{1,0:T(8,128)(2,1)S(1)}, u32[]{:S(2)}, u32[]{:S(2)}) collective-permute-start(bf16[128,1024]{1,0:T(8,128)(2,1)S(1)} %copy.30), channel_id=1, source_target_pairs={{0,1},{1,4},{4,5},{5,8},{8,9},{9,12},{12,13},{13,14},{14,15},{15,1... | collective-permute-start | bytes 786440 | tf_op jit(solution)/shard_map/while/body/eval_jaxpr/ppermute | solution.py:95
  109.2 5.5 %collective-permute-start.1 = (bf16[128,1024]{1,0:T(8,128)(2,1)S(1)}, bf16[128,1024]{1,0:T(8,128)(2,1)S(1)}, u32[]{:S(2)}, u32[]{:S(2)}) collective-permute-start(bf16[128,1024]{1,0:T(8,128)(2,1)S(1)} %copy.31), channel_id=1, source_target_pairs={{1,0},{4,1},{5,4},{8,5},{9,8},{12,9},{13,12},{14,13},{15,14},{10,1... | collective-permute-start | bytes 786440 | tf_op jit(solution)/shard_map/while/body/eval_jaxpr/ppermute | solution.py:95
  109.4 5.3 %collective-permute-start.2 = (f32[256,128]{0,1:T(8,128)S(1)}, f32[256,128]{0,1:T(8,128)S(1)}, u32[]{:S(2)}, u32[]{:S(2)}) collective-permute-start(f32[256,128]{0,1:T(8,128)S(1)} %add.322), channel_id=1, source_target_pairs={{0,1},{1,4},{4,5},{5,8},{8,9},{9,12},{12,13},{13,14},{14,15},{15,1... | collective-permute-start | bytes 393224 | tf_op jit(solution)/shard_map/while/body/eval_jaxpr/ppermute | solution.py:95
  114.9 6.7 %collective-permute-start.8 = (f32[256,128]{1,0:T(8,128)S(1)}, f32[256,128]{1,0:T(8,128)}, u32[]{:S(2)}, u32[]{:S(2)}) collective-permute-start(f32[256,128]{1,0:T(8,128)S(1)} %add.198), channel_id=1, source_target_pairs={{0,1},{1,4},{4,5},{5,8},{8,9},{9,12},{12,13},{13,14},{14,15},{15,1... | collective-permute-start | bytes 393224 | tf_op jit(solution)/shard_map/ppermute | solution.py:95
  130.8 5.8 %collective-permute-start.12 = (f32[2,2,2,16,256]{4,3,2,1,0:T(8,128)S(1)}, f32[2,2,2,16,256]{4,3,2,1,0:T(8,128)S(1)}, u32[]{:S(2)}, u32[]{:S(2)}) collective-permute-start(f32[2,2,2,16,256]{4,3,2,1,0:T(8,128)S(1)} %dynamic-slice_bitcast_fusion), channel_id=1, source_target_pairs={{0,16},{16,0},{32,48},{48,32},{64,80},{80,64},{96,112},{112,96},{1... | collective-permute-start | bytes 393224 | tf_op jit(solution)/shard_map/ppermute | solution.py:62
  136.7 6.1 %collective-permute-start.13 = (f32[2,2,16,256]{3,2,1,0:T(8,128)S(1)}, f32[2,2,16,256]{3,2,1,0:T(8,128)S(1)}, u32[]{:S(2)}, u32[]{:S(2)}) collective-permute-start(f32[2,2,16,256]{3,2,1,0:T(8,128)S(1)} %dynamic-slice_bitcast_fusion.1), channel_id=1, source_target_pairs={{0,32},{16,48},{32,0},{48,16},{64,96},{80,112},{96,64},{112,80},{1... | collective-permute-start | bytes 196616 | tf_op jit(solution)/shard_map/ppermute | solution.py:62
  142.8 5.5 %collective-permute-start.14 = (f32[2,16,256]{2,1,0:T(8,128)S(1)}, f32[2,16,256]{2,1,0:T(8,128)S(1)}, u32[]{:S(2)}, u32[]{:S(2)}) collective-permute-start(f32[2,16,256]{2,1,0:T(8,128)S(1)} %dynamic-slice_bitcast_fusion.2), channel_id=1, source_target_pairs={{0,128},{16,144},{32,160},{48,176},{64,192},{80,208},{96,224},{112... | collective-permute-start | bytes 98312 | tf_op jit(solution)/shard_map/ppermute | solution.py:62
  148.3 8.8 %collective-permute-start.15 = (f32[16,256]{1,0:T(8,128)S(1)}, f32[16,256]{1,0:T(8,128)S(1)}, u32[]{:S(2)}, u32[]{:S(2)}) collective-permute-start(f32[16,256]{1,0:T(8,128)S(1)} %dynamic-slice_bitcast_fusion.3), channel_id=1, source_target_pairs={{0,64},{16,80},{32,96},{48,112},{64,0},{80,16},{96,32},{112,48},{1... | collective-permute-start | bytes 49160 | tf_op jit(solution)/shard_map/ppermute | solution.py:62
  (38 other events, 163.7 us)

commit v8 on v5

--- a/solution.py
+++ b/solution.py
@@ -111,17 +111,16 @@
 
     points_f, points_b = send(targets_bf[:half], targets_bf[half:])
     own = contribution(targets_bf)
-    next_f, next_b = send(points_f, points_b)
-    part_f, part_b = halves(points_f, points_b)
-    zeros = jnp.zeros_like(part_f)
-    carried = (next_f, next_b, zeros, zeros, part_f, part_b)
-    carried = lax.fori_loop(0, cycle_size - 3, advance, carried)
+    zeros = jnp.zeros_like(own[:, :half])
+    carried = (points_f, points_b, zeros, zeros, own[:, :half], own[:, half:])
+    carried = lax.fori_loop(0, cycle_size - 2, advance, carried)
     points_f, points_b, sums_f, sums_b, part_f, part_b = carried
     sums_f, sums_b = send(sums_f + part_f, sums_b + part_b)
     part_f, part_b = halves(points_f, points_b)
-    sums_f, sums_b = send(sums_f + part_f, sums_b + part_b)
-    gathered_sums = own + jnp.concatenate([sums_f, sums_b], axis=1)
-    owned_sums = exchange_scatter(gathered_sums, "grp")
+    complete = jnp.concatenate([sums_f + part_f, sums_b + part_b], axis=1)
+    owned = exchange_scatter(complete, "grp")
+    mine_f, mine_b = send(owned[:, :half], owned[:, half:])
+    owned_sums = jnp.concatenate([mine_f, mine_b], axis=1)
     source_total = src_codes.shape[0] * group_size * cycle_size
     return owned_sums.T * (4.0 / math.sqrt(source_total))
 

time: 157 us -> 154 us (0.981)
  local copies, waits for them, and re-layouts: 10.1 us -> 6.05 us
  starting transfers between devices: 42.7 us -> 45.9 us
  other arithmetic: 9.68 us -> 8.03 us
    ppermute x30 -> x31, starting transfers between devices: 22.8 us -> 28.3 us  [send(): lax.ppermute(points_f, 'blk', forward)]
    ppermute x30 -> x31, starting transfers between devices: 19.9 us -> 17.6 us  [send(): lax.ppermute(points_b, 'blk', backward)]
    unnamed x22 -> x13, local copies, waits for them, and re-layouts: 3.74 us -> 1.67 us
    add x3 -> x2, other arithmetic: 1.68 us -> 0.04 us  [per_device(): sums_f, sums_b = send(sums_f + part_f, sums_b + part_b)]
    ppermute x30 -> x31, waiting for transfers between devices: 24.1 us -> 24.2 us  [send(): lax.ppermute(points_b, 'blk', backward)]
  transfers between devices with their start and end apart: 60 -> 62, of which waited for: 16 -> 16; matrix products, arithmetic and copies ran while one was open for 34% -> 35% of each run, Pallas kernels for 0% -> 0%
where the time goes in v8:
time: 154 us; the launch traced here: 153 us
  matrix products  46.1 us (30%)
  starting transfers between devices  45.9 us (30%)
  waiting for transfers between devices  25.1 us (16%)
  blocking collectives  20.8 us (14%)
  other arithmetic  8.03 us (5%)
  local copies, waits for them, and re-layouts  6.05 us (4%)
    dot_general x16, matrix products, kernel_block(): lax.dot_general(rhs_values, matern, (((0,), (1,)), ((), ())), preferred_e...  46.1 us
    ppermute x31, starting transfers between devices, send(): lax.ppermute(points_f, 'blk', forward)  28.3 us
    ppermute x31, waiting for transfers between devices, send(): lax.ppermute(points_b, 'blk', backward)  24.2 us
    all_to_all x1, blocking collectives, exchange_scatter(): pieces = lax.all_to_all(pieces, axis, 0, 0, tiled=False)  20.8 us
    ppermute x31, starting transfers between devices, send(): lax.ppermute(points_b, 'blk', backward)  17.6 us
    reduce_sum x17, other arithmetic, squares(): return jnp.sum(widened * widened, axis=1)  5.19 us
  transfers between devices with their start and end apart: 62, of which 16 were waited for; matrix products, arithmetic and copies ran while one was open for 35% of the time, Pallas kernels for 0%

profile of v8, /device:TPU:1, one launch (start us, length us, event | category | flops | bytes accessed | tf_op | source)
XLA Modules:
  0.0 153.1 jit_solution(2670639487075964942)
XLA Ops:
  1.2 1.6 %multiply_reduce_fusion.3 = (f32[256]{0:T(256)S(1)}, bf16[256,1024]{1,0:T(8,128)(2,1)S(1)}) fusion(f32[32,8,8,128]{3,2,1,0:T(8,128)S(1)} %bitcast.35, s32[256,1024]{1,0:T(8,128)} %param.10), kind=kLoop, calls=%fused_computation.40 | loop fusion | flops 1572608 | bytes 2622464 | tf_op jit(solution)/shard_map/reduce_sum | solution.py:31
  3.6 2.6 %collective-permute-start.4 = (bf16[128,1024]{1,0:T(8,128)(2,1)}, bf16[128,1024]{1,0:T(8,128)(2,1)S(1)}, u32[]{:S(2)}, u32[]{:S(2)}) collective-permute-start(bf16[128,1024]{1,0:T(8,128)(2,1)} %get-tuple-element.188), channel_id=1, source_target_pairs={{0,1},{1,4},{4,5},{5,8},{8,9},{9,12},{12,13},{13,14},{14,15},{15,1... | collective-permute-start | bytes 786440 | tf_op jit(solution)/shard_map/ppermute | solution.py:103
  11.1 2.8 %fusion.24 = f32[256,256]{1,0:T(8,128)S(1)} fusion(bf16[1024,256]{1,0:T(8,128)(2,1)} %add_convert_fusion, bf16[256,1024]{1,0:T(8,128)(2,1)S(1)} %get-tuple-element.182, bf16[1024,1024]{1,0:T(8,128)(2,1)S(1)} %get-tuple-element.268, f32[1024]{0:T(1024)S(1)} %get-tuple-element.267, f32[256]{0:T(256)S(1)} %get-tuple-element.181), kind=kOutput, calls=%fused_computation.38 | convolution fusion | flops 673972224 | bytes 3412992 | tf_op jit(solution)/shard_map/dot_general | solution.py:42
  14.2 105.3 %while.22 = (s32[]{:T(128)}, bf16[128,1024]{1,0:T(8,128)(2,1)S(1)}, bf16[128,1024]{1,0:T(8,128)(2,1)S(1)}, f32[256,128]{0,1:T(8,128)S(1)}, f32[256,128]{0,1:T(8,...) while((s32[]{:T(128)}, bf16[128,1024]{1,0:T(8,128)(2,1)S(1)}, ...), condition=%wide.region_4.5_spmd, body=%wide.region_2.4_spmd.sunk | while | flops 674823936 | bytes 12589353 | solution.py:116
  18.4 2.9 %convolution_bitcast_fusion.2 = f32[256,256]{0,1:T(8,128)S(1)} fusion(bf16[1024,256]{1,0:T(8,128)(2,1)S(1)} %copy-done.5, bf16[256,1024]{1,0:T(8,128)(2,1)S(1)} %constant_dynamic-update-slice_fusion.7, bf16[1024,1024]{1,0:T(8,128)(2,1)} %get-tuple-element.290, f32[1024]{0:T(1024)S(1)} %get-tuple-element.289, f32[256]{0:T(256)S(1)} %multiply_reduce_fusion.5), kind=kOutput, calls=%fused_computation.4.clone.1 | convolution fusion | flops 673972224 | bytes 3412992 | tf_op jit(solution)/shard_map/while/body/eval_jaxpr/dot_general | solution.py:42
  21.3 1.6 %collective-permute-done.3 = f32[256,128]{0,1:T(8,128)S(1)} collective-permute-done((f32[256,128]{0,1:T(8,128)S(1)}, f32[256,128]{0,1:T(8,128)S(1)}, u32[]{:S(2)}, u32[]{:S(2)}) %collective-permute-start.3) | collective-permute-done | bytes 131104 | tf_op jit(solution)/shard_map/while/body/eval_jaxpr/ppermute | solution.py:103
  23.6 1.3 collective-permute-start.2
  25.8 2.9 %convolution_bitcast_fusion.2 = f32[256,256]{0,1:T(8,128)S(1)} fusion(bf16[1024,256]{1,0:T(8,128)(2,1)S(1)} %copy-done.5, bf16[256,1024]{1,0:T(8,128)(2,1)S(1)} %constant_dynamic-update-slice_fusion.7, bf16[1024,1024]{1,0:T(8,128)(2,1)} %get-tuple-element.290, f32[1024]{0:T(1024)S(1)} %get-tuple-element.289, f32[256]{0:T(256)S(1)} %multiply_reduce_fusion.5), kind=kOutput, calls=%fused_computation.4.clone.1 | convolution fusion | flops 673972224 | bytes 3412992 | tf_op jit(solution)/shard_map/while/body/eval_jaxpr/dot_general | solution.py:42
  28.8 1.6 %collective-permute-done.3 = f32[256,128]{0,1:T(8,128)S(1)} collective-permute-done((f32[256,128]{0,1:T(8,128)S(1)}, f32[256,128]{0,1:T(8,128)S(1)}, u32[]{:S(2)}, u32[]{:S(2)}) %collective-permute-start.3) | collective-permute-done | bytes 131104 | tf_op jit(solution)/shard_map/while/body/eval_jaxpr/ppermute | solution.py:103
  31.1 1.3 collective-permute-start.2
  33.2 2.9 %convolution_bitcast_fusion.2 = f32[256,256]{0,1:T(8,128)S(1)} fusion(bf16[1024,256]{1,0:T(8,128)(2,1)S(1)} %copy-done.5, bf16[256,1024]{1,0:T(8,128)(2,1)S(1)} %constant_dynamic-update-slice_fusion.7, bf16[1024,1024]{1,0:T(8,128)(2,1)} %get-tuple-element.290, f32[1024]{0:T(1024)S(1)} %get-tuple-element.289, f32[256]{0:T(256)S(1)} %multiply_reduce_fusion.5), kind=kOutput, calls=%fused_computation.4.clone.1 | convolution fusion | flops 673972224 | bytes 3412992 | tf_op jit(solution)/shard_map/while/body/eval_jaxpr/dot_general | solution.py:42
  36.2 1.6 %collective-permute-done.3 = f32[256,128]{0,1:T(8,128)S(1)} collective-permute-done((f32[256,128]{0,1:T(8,128)S(1)}, f32[256,128]{0,1:T(8,128)S(1)}, u32[]{:S(2)}, u32[]{:S(2)}) %collective-permute-start.3) | collective-permute-done | bytes 131104 | tf_op jit(solution)/shard_map/while/body/eval_jaxpr/ppermute | solution.py:103
  38.5 1.3 collective-permute-start.2
  40.7 2.9 %convolution_bitcast_fusion.2 = f32[256,256]{0,1:T(8,128)S(1)} fusion(bf16[1024,256]{1,0:T(8,128)(2,1)S(1)} %copy-done.5, bf16[256,1024]{1,0:T(8,128)(2,1)S(1)} %constant_dynamic-update-slice_fusion.7, bf16[1024,1024]{1,0:T(8,128)(2,1)} %get-tuple-element.290, f32[1024]{0:T(1024)S(1)} %get-tuple-element.289, f32[256]{0:T(256)S(1)} %multiply_reduce_fusion.5), kind=kOutput, calls=%fused_computation.4.clone.1 | convolution fusion | flops 673972224 | bytes 3412992 | tf_op jit(solution)/shard_map/while/body/eval_jaxpr/dot_general | solution.py:42
  43.6 1.6 %collective-permute-done.3 = f32[256,128]{0,1:T(8,128)S(1)} collective-permute-done((f32[256,128]{0,1:T(8,128)S(1)}, f32[256,128]{0,1:T(8,128)S(1)}, u32[]{:S(2)}, u32[]{:S(2)}) %collective-permute-start.3) | collective-permute-done | bytes 131104 | tf_op jit(solution)/shard_map/while/body/eval_jaxpr/ppermute | solution.py:103
  45.9 1.3 collective-permute-start.2
  48.1 2.9 %convolution_bitcast_fusion.2 = f32[256,256]{0,1:T(8,128)S(1)} fusion(bf16[1024,256]{1,0:T(8,128)(2,1)S(1)} %copy-done.5, bf16[256,1024]{1,0:T(8,128)(2,1)S(1)} %constant_dynamic-update-slice_fusion.7, bf16[1024,1024]{1,0:T(8,128)(2,1)} %get-tuple-element.290, f32[1024]{0:T(1024)S(1)} %get-tuple-element.289, f32[256]{0:T(256)S(1)} %multiply_reduce_fusion.5), kind=kOutput, calls=%fused_computation.4.clone.1 | convolution fusion | flops 673972224 | bytes 3412992 | tf_op jit(solution)/shard_map/while/body/eval_jaxpr/dot_general | solution.py:42
  51.1 1.6 %collective-permute-done.3 = f32[256,128]{0,1:T(8,128)S(1)} collective-permute-done((f32[256,128]{0,1:T(8,128)S(1)}, f32[256,128]{0,1:T(8,128)S(1)}, u32[]{:S(2)}, u32[]{:S(2)}) %collective-permute-start.3) | collective-permute-done | bytes 131104 | tf_op jit(solution)/shard_map/while/body/eval_jaxpr/ppermute | solution.py:103
  53.4 1.3 collective-permute-start.2
  55.5 2.9 %convolution_bitcast_fusion.2 = f32[256,256]{0,1:T(8,128)S(1)} fusion(bf16[1024,256]{1,0:T(8,128)(2,1)S(1)} %copy-done.5, bf16[256,1024]{1,0:T(8,128)(2,1)S(1)} %constant_dynamic-update-slice_fusion.7, bf16[1024,1024]{1,0:T(8,128)(2,1)} %get-tuple-element.290, f32[1024]{0:T(1024)S(1)} %get-tuple-element.289, f32[256]{0:T(256)S(1)} %multiply_reduce_fusion.5), kind=kOutput, calls=%fused_computation.4.clone.1 | convolution fusion | flops 673972224 | bytes 3412992 | tf_op jit(solution)/shard_map/while/body/eval_jaxpr/dot_general | solution.py:42
  58.5 1.6 %collective-permute-done.3 = f32[256,128]{0,1:T(8,128)S(1)} collective-permute-done((f32[256,128]{0,1:T(8,128)S(1)}, f32[256,128]{0,1:T(8,128)S(1)}, u32[]{:S(2)}, u32[]{:S(2)}) %collective-permute-start.3) | collective-permute-done | bytes 131104 | tf_op jit(solution)/shard_map/while/body/eval_jaxpr/ppermute | solution.py:103
  60.8 1.3 collective-permute-start.2
  63.0 2.9 %convolution_bitcast_fusion.2 = f32[256,256]{0,1:T(8,128)S(1)} fusion(bf16[1024,256]{1,0:T(8,128)(2,1)S(1)} %copy-done.5, bf16[256,1024]{1,0:T(8,128)(2,1)S(1)} %constant_dynamic-update-slice_fusion.7, bf16[1024,1024]{1,0:T(8,128)(2,1)} %get-tuple-element.290, f32[1024]{0:T(1024)S(1)} %get-tuple-element.289, f32[256]{0:T(256)S(1)} %multiply_reduce_fusion.5), kind=kOutput, calls=%fused_computation.4.clone.1 | convolution fusion | flops 673972224 | bytes 3412992 | tf_op jit(solution)/shard_map/while/body/eval_jaxpr/dot_general | solution.py:42
  65.9 1.6 %collective-permute-done.3 = f32[256,128]{0,1:T(8,128)S(1)} collective-permute-done((f32[256,128]{0,1:T(8,128)S(1)}, f32[256,128]{0,1:T(8,128)S(1)}, u32[]{:S(2)}, u32[]{:S(2)}) %collective-permute-start.3) | collective-permute-done | bytes 131104 | tf_op jit(solution)/shard_map/while/body/eval_jaxpr/ppermute | solution.py:103
  68.2 1.3 collective-permute-start.2
  70.4 2.9 %convolution_bitcast_fusion.2 = f32[256,256]{0,1:T(8,128)S(1)} fusion(bf16[1024,256]{1,0:T(8,128)(2,1)S(1)} %copy-done.5, bf16[256,1024]{1,0:T(8,128)(2,1)S(1)} %constant_dynamic-update-slice_fusion.7, bf16[1024,1024]{1,0:T(8,128)(2,1)} %get-tuple-element.290, f32[1024]{0:T(1024)S(1)} %get-tuple-element.289, f32[256]{0:T(256)S(1)} %multiply_reduce_fusion.5), kind=kOutput, calls=%fused_computation.4.clone.1 | convolution fusion | flops 673972224 | bytes 3412992 | tf_op jit(solution)/shard_map/while/body/eval_jaxpr/dot_general | solution.py:42
  73.4 1.6 %collective-permute-done.3 = f32[256,128]{0,1:T(8,128)S(1)} collective-permute-done((f32[256,128]{0,1:T(8,128)S(1)}, f32[256,128]{0,1:T(8,128)S(1)}, u32[]{:S(2)}, u32[]{:S(2)}) %collective-permute-start.3) | collective-permute-done | bytes 131104 | tf_op jit(solution)/shard_map/while/body/eval_jaxpr/ppermute | solution.py:103
  75.7 1.3 collective-permute-start.2
  77.9 2.9 %convolution_bitcast_fusion.2 = f32[256,256]{0,1:T(8,128)S(1)} fusion(bf16[1024,256]{1,0:T(8,128)(2,1)S(1)} %copy-done.5, bf16[256,1024]{1,0:T(8,128)(2,1)S(1)} %constant_dynamic-update-slice_fusion.7, bf16[1024,1024]{1,0:T(8,128)(2,1)} %get-tuple-element.290, f32[1024]{0:T(1024)S(1)} %get-tuple-element.289, f32[256]{0:T(256)S(1)} %multiply_reduce_fusion.5), kind=kOutput, calls=%fused_computation.4.clone.1 | convolution fusion | flops 673972224 | bytes 3412992 | tf_op jit(solution)/shard_map/while/body/eval_jaxpr/dot_general | solution.py:42
  80.8 1.6 %collective-permute-done.3 = f32[256,128]{0,1:T(8,128)S(1)} collective-permute-done((f32[256,128]{0,1:T(8,128)S(1)}, f32[256,128]{0,1:T(8,128)S(1)}, u32[]{:S(2)}, u32[]{:S(2)}) %collective-permute-start.3) | collective-permute-done | bytes 131104 | tf_op jit(solution)/shard_map/while/body/eval_jaxpr/ppermute | solution.py:103
  83.1 1.3 collective-permute-start.2
  85.3 2.9 %convolution_bitcast_fusion.2 = f32[256,256]{0,1:T(8,128)S(1)} fusion(bf16[1024,256]{1,0:T(8,128)(2,1)S(1)} %copy-done.5, bf16[256,1024]{1,0:T(8,128)(2,1)S(1)} %constant_dynamic-update-slice_fusion.7, bf16[1024,1024]{1,0:T(8,128)(2,1)} %get-tuple-element.290, f32[1024]{0:T(1024)S(1)} %get-tuple-element.289, f32[256]{0:T(256)S(1)} %multiply_reduce_fusion.5), kind=kOutput, calls=%fused_computation.4.clone.1 | convolution fusion | flops 673972224 | bytes 3412992 | tf_op jit(solution)/shard_map/while/body/eval_jaxpr/dot_general | solution.py:42
  88.2 1.6 %collective-permute-done.3 = f32[256,128]{0,1:T(8,128)S(1)} collective-permute-done((f32[256,128]{0,1:T(8,128)S(1)}, f32[256,128]{0,1:T(8,128)S(1)}, u32[]{:S(2)}, u32[]{:S(2)}) %collective-permute-start.3) | collective-permute-done | bytes 131104 | tf_op jit(solution)/shard_map/while/body/eval_jaxpr/ppermute | solution.py:103
  92.7 2.9 %convolution_bitcast_fusion.2 = f32[256,256]{0,1:T(8,128)S(1)} fusion(bf16[1024,256]{1,0:T(8,128)(2,1)S(1)} %copy-done.5, bf16[256,1024]{1,0:T(8,128)(2,1)S(1)} %constant_dynamic-update-slice_fusion.7, bf16[1024,1024]{1,0:T(8,128)(2,1)} %get-tuple-element.290, f32[1024]{0:T(1024)S(1)} %get-tuple-element.289, f32[256]{0:T(256)S(1)} %multiply_reduce_fusion.5), kind=kOutput, calls=%fused_computation.4.clone.1 | convolution fusion | flops 673972224 | bytes 3412992 | tf_op jit(solution)/shard_map/while/body/eval_jaxpr/dot_general | solution.py:42
  95.7 1.6 %collective-permute-done.3 = f32[256,128]{0,1:T(8,128)S(1)} collective-permute-done((f32[256,128]{0,1:T(8,128)S(1)}, f32[256,128]{0,1:T(8,128)S(1)}, u32[]{:S(2)}, u32[]{:S(2)}) %collective-permute-start.3) | collective-permute-done | bytes 131104 | tf_op jit(solution)/shard_map/while/body/eval_jaxpr/ppermute | solution.py:103
  98.0 1.3 collective-permute-start.2
  100.2 2.9 %convolution_bitcast_fusion.2 = f32[256,256]{0,1:T(8,128)S(1)} fusion(bf16[1024,256]{1,0:T(8,128)(2,1)S(1)} %copy-done.5, bf16[256,1024]{1,0:T(8,128)(2,1)S(1)} %constant_dynamic-update-slice_fusion.7, bf16[1024,1024]{1,0:T(8,128)(2,1)} %get-tuple-element.290, f32[1024]{0:T(1024)S(1)} %get-tuple-element.289, f32[256]{0:T(256)S(1)} %multiply_reduce_fusion.5), kind=kOutput, calls=%fused_computation.4.clone.1 | convolution fusion | flops 673972224 | bytes 3412992 | tf_op jit(solution)/shard_map/while/body/eval_jaxpr/dot_general | solution.py:42
  103.1 1.6 %collective-permute-done.3 = f32[256,128]{0,1:T(8,128)S(1)} collective-permute-done((f32[256,128]{0,1:T(8,128)S(1)}, f32[256,128]{0,1:T(8,128)S(1)}, u32[]{:S(2)}, u32[]{:S(2)}) %collective-permute-start.3) | collective-permute-done | bytes 131104 | tf_op jit(solution)/shard_map/while/body/eval_jaxpr/ppermute | solution.py:103
  107.6 2.9 %convolution_bitcast_fusion.2 = f32[256,256]{0,1:T(8,128)S(1)} fusion(bf16[1024,256]{1,0:T(8,128)(2,1)S(1)} %copy-done.5, bf16[256,1024]{1,0:T(8,128)(2,1)S(1)} %constant_dynamic-update-slice_fusion.7, bf16[1024,1024]{1,0:T(8,128)(2,1)} %get-tuple-element.290, f32[1024]{0:T(1024)S(1)} %get-tuple-element.289, f32[256]{0:T(256)S(1)} %multiply_reduce_fusion.5), kind=kOutput, calls=%fused_computation.4.clone.1 | convolution fusion | flops 673972224 | bytes 3412992 | tf_op jit(solution)/shard_map/while/body/eval_jaxpr/dot_general | solution.py:42
  110.5 1.6 %collective-permute-done.3 = f32[256,128]{0,1:T(8,128)S(1)} collective-permute-done((f32[256,128]{0,1:T(8,128)S(1)}, f32[256,128]{0,1:T(8,128)S(1)}, u32[]{:S(2)}, u32[]{:S(2)}) %collective-permute-start.3) | collective-permute-done | bytes 131104 | tf_op jit(solution)/shard_map/while/body/eval_jaxpr/ppermute | solution.py:103
  112.9 1.3 collective-permute-start.2
  115.0 2.9 %convolution_bitcast_fusion.2 = f32[256,256]{0,1:T(8,128)S(1)} fusion(bf16[1024,256]{1,0:T(8,128)(2,1)S(1)} %copy-done.5, bf16[256,1024]{1,0:T(8,128)(2,1)S(1)} %constant_dynamic-update-slice_fusion.7, bf16[1024,1024]{1,0:T(8,128)(2,1)} %get-tuple-element.290, f32[1024]{0:T(1024)S(1)} %get-tuple-element.289, f32[256]{0:T(256)S(1)} %multiply_reduce_fusion.5), kind=kOutput, calls=%fused_computation.4.clone.1 | convolution fusion | flops 673972224 | bytes 3412992 | tf_op jit(solution)/shard_map/while/body/eval_jaxpr/dot_general | solution.py:42
  118.0 1.6 %collective-permute-done.3 = f32[256,128]{0,1:T(8,128)S(1)} collective-permute-done((f32[256,128]{0,1:T(8,128)S(1)}, f32[256,128]{0,1:T(8,128)S(1)}, u32[]{:S(2)}, u32[]{:S(2)}) %collective-permute-start.3) | collective-permute-done | bytes 131104 | tf_op jit(solution)/shard_map/while/body/eval_jaxpr/ppermute | solution.py:103
  120.9 1.3 collective-permute-start.6
  122.3 2.5 %fusion.22 = f32[256,256]{0,1:T(8,128)S(1)} fusion(bf16[1024,256]{1,0:T(8,128)(2,1)} %get-tuple-element.304, bf16[256,1024]{1,0:T(8,128)(2,1)} %copy-done.3, bf16[1024,1024]{1,0:T(8,128)(2,1)S(1)} %copy-done.2, f32[256]{0:T(256)S(1)} %multiply_reduce_fusion.2, f32[1024]{0:T(1024)S(1)} %get-tuple-element.313), kind=kOutput, calls=%fused_computation.34 | convolution fusion | flops 673972224 | bytes 3412992 | tf_op jit(solution)/shard_map/dot_general | solution.py:42
  125.0 20.8 %all_to_all.5 = f32[16,16,256]{2,1,0:T(8,128)S(1)} all-to-all(f32[16,16,256]{2,1,0:T(8,128)S(1)} %bitcast.36), channel_id=1, replica_groups=mesh['grp'=16,'blk'=16] {'grp'}, dimensions={0} | all-to-all | bytes 524288 | tf_op jit(solution)/shard_map/all_to_all | solution.py:51
  145.8 3.5 %collective-permute-start.8 = (f32[16,128]{1,0:T(8,128)S(1)}, f32[16,128]{1,0:T(8,128)S(1)}, u32[]{:S(2)}, u32[]{:S(2)}) collective-permute-start(f32[16,128]{1,0:T(8,128)S(1)} %get-tuple-element.193), channel_id=1, source_target_pairs={{0,1},{1,4},{4,5},{5,8},{8,9},{9,12},{12,13},{13,14},{14,15},{15,1... | collective-permute-start | bytes 24584 | tf_op jit(solution)/shard_map/ppermute | solution.py:103
  150.2 2.3 %collective-permute-done.9 = f32[16,128]{1,0:T(8,128)S(1)} collective-permute-done((f32[16,128]{1,0:T(8,128)S(1)}, f32[16,128]{1,0:T(8,128)S(1)}, u32[]{:S(2)}, u32[]{:S(2)}) %collective-permute-start.9) | collective-permute-done | bytes 8224 | tf_op jit(solution)/shard_map/ppermute | solution.py:103
  (272 shorter events, 37.1 us)
Async XLA Ops:
  3.6 10.5 %collective-permute-start.4 = (bf16[128,1024]{1,0:T(8,128)(2,1)}, bf16[128,1024]{1,0:T(8,128)(2,1)S(1)}, u32[]{:S(2)}, u32[]{:S(2)}) collective-permute-start(bf16[128,1024]{1,0:T(8,128)(2,1)} %get-tuple-element.188), channel_id=1, source_target_pairs={{0,1},{1,4},{4,5},{5,8},{8,9},{9,12},{12,13},{13,14},{14,15},{15,1... | collective-permute-start | bytes 786440 | tf_op jit(solution)/shard_map/ppermute | solution.py:103
  6.2 7.9 %collective-permute-start.5 = (bf16[128,1024]{1,0:T(8,128)(2,1)}, bf16[128,1024]{1,0:T(8,128)(2,1)S(1)}, u32[]{:S(2)}, u32[]{:S(2)}) collective-permute-start(bf16[128,1024]{1,0:T(8,128)(2,1)} %get-tuple-element.187), channel_id=1, source_target_pairs={{1,0},{4,1},{5,4},{8,5},{9,8},{12,9},{13,12},{14,13},{15,14},{10,1... | collective-permute-start | bytes 786440 | tf_op jit(solution)/shard_map/ppermute | solution.py:103
  14.3 8.6 %collective-permute-start = (bf16[128,1024]{1,0:T(8,128)(2,1)S(1)}, bf16[128,1024]{1,0:T(8,128)(2,1)S(1)}, u32[]{:S(2)}, u32[]{:S(2)}) collective-permute-start(bf16[128,1024]{1,0:T(8,128)(2,1)S(1)} %copy.30), channel_id=1, source_target_pairs={{0,1},{1,4},{4,5},{5,8},{8,9},{9,12},{12,13},{13,14},{14,15},{15,1... | collective-permute-start | bytes 786440 | tf_op jit(solution)/shard_map/while/body/eval_jaxpr/ppermute | solution.py:103
  15.5 7.4 %collective-permute-start.1 = (bf16[128,1024]{1,0:T(8,128)(2,1)S(1)}, bf16[128,1024]{1,0:T(8,128)(2,1)S(1)}, u32[]{:S(2)}, u32[]{:S(2)}) collective-permute-start(bf16[128,1024]{1,0:T(8,128)(2,1)S(1)} %copy.31), channel_id=1, source_target_pairs={{1,0},{4,1},{5,4},{8,5},{9,8},{12,9},{13,12},{14,13},{15,14},{10,1... | collective-permute-start | bytes 786440 | tf_op jit(solution)/shard_map/while/body/eval_jaxpr/ppermute | solution.py:103
  17.4 5.5 %collective-permute-start.3 = (f32[256,128]{0,1:T(8,128)S(1)}, f32[256,128]{0,1:T(8,128)S(1)}, u32[]{:S(2)}, u32[]{:S(2)}) collective-permute-start(f32[256,128]{0,1:T(8,128)S(1)} %add.215), channel_id=1, source_target_pairs={{1,0},{4,1},{5,4},{8,5},{9,8},{12,9},{13,12},{14,13},{15,14},{10,1... | collective-permute-start | bytes 393224 | tf_op jit(solution)/shard_map/while/body/eval_jaxpr/ppermute | solution.py:103
  22.9 7.4 %collective-permute-start = (bf16[128,1024]{1,0:T(8,128)(2,1)S(1)}, bf16[128,1024]{1,0:T(8,128)(2,1)S(1)}, u32[]{:S(2)}, u32[]{:S(2)}) collective-permute-start(bf16[128,1024]{1,0:T(8,128)(2,1)S(1)} %copy.30), channel_id=1, source_target_pairs={{0,1},{1,4},{4,5},{5,8},{8,9},{9,12},{12,13},{13,14},{14,15},{15,1... | collective-permute-start | bytes 786440 | tf_op jit(solution)/shard_map/while/body/eval_jaxpr/ppermute | solution.py:103
  23.0 7.3 %collective-permute-start.1 = (bf16[128,1024]{1,0:T(8,128)(2,1)S(1)}, bf16[128,1024]{1,0:T(8,128)(2,1)S(1)}, u32[]{:S(2)}, u32[]{:S(2)}) collective-permute-start(bf16[128,1024]{1,0:T(8,128)(2,1)S(1)} %copy.31), channel_id=1, source_target_pairs={{1,0},{4,1},{5,4},{8,5},{9,8},{12,9},{13,12},{14,13},{15,14},{10,1... | collective-permute-start | bytes 786440 | tf_op jit(solution)/shard_map/while/body/eval_jaxpr/ppermute | solution.py:103
  25.0 5.3 %collective-permute-start.3 = (f32[256,128]{0,1:T(8,128)S(1)}, f32[256,128]{0,1:T(8,128)S(1)}, u32[]{:S(2)}, u32[]{:S(2)}) collective-permute-start(f32[256,128]{0,1:T(8,128)S(1)} %add.215), channel_id=1, source_target_pairs={{1,0},{4,1},{5,4},{8,5},{9,8},{12,9},{13,12},{14,13},{15,14},{10,1... | collective-permute-start | bytes 393224 | tf_op jit(solution)/shard_map/while/body/eval_jaxpr/ppermute | solution.py:103
  30.4 7.4 %collective-permute-start = (bf16[128,1024]{1,0:T(8,128)(2,1)S(1)}, bf16[128,1024]{1,0:T(8,128)(2,1)S(1)}, u32[]{:S(2)}, u32[]{:S(2)}) collective-permute-start(bf16[128,1024]{1,0:T(8,128)(2,1)S(1)} %copy.30), channel_id=1, source_target_pairs={{0,1},{1,4},{4,5},{5,8},{8,9},{9,12},{12,13},{13,14},{14,15},{15,1... | collective-permute-start | bytes 786440 | tf_op jit(solution)/shard_map/while/body/eval_jaxpr/ppermute | solution.py:103
  30.5 7.3 %collective-permute-start.1 = (bf16[128,1024]{1,0:T(8,128)(2,1)S(1)}, bf16[128,1024]{1,0:T(8,128)(2,1)S(1)}, u32[]{:S(2)}, u32[]{:S(2)}) collective-permute-start(bf16[128,1024]{1,0:T(8,128)(2,1)S(1)} %copy.31), channel_id=1, source_target_pairs={{1,0},{4,1},{5,4},{8,5},{9,8},{12,9},{13,12},{14,13},{15,14},{10,1... | collective-permute-start | bytes 786440 | tf_op jit(solution)/shard_map/while/body/eval_jaxpr/ppermute | solution.py:103
  32.4 5.3 %collective-permute-start.3 = (f32[256,128]{0,1:T(8,128)S(1)}, f32[256,128]{0,1:T(8,128)S(1)}, u32[]{:S(2)}, u32[]{:S(2)}) collective-permute-start(f32[256,128]{0,1:T(8,128)S(1)} %add.215), channel_id=1, source_target_pairs={{1,0},{4,1},{5,4},{8,5},{9,8},{12,9},{13,12},{14,13},{15,14},{10,1... | collective-permute-start | bytes 393224 | tf_op jit(solution)/shard_map/while/body/eval_jaxpr/ppermute | solution.py:103
  37.8 7.4 %collective-permute-start = (bf16[128,1024]{1,0:T(8,128)(2,1)S(1)}, bf16[128,1024]{1,0:T(8,128)(2,1)S(1)}, u32[]{:S(2)}, u32[]{:S(2)}) collective-permute-start(bf16[128,1024]{1,0:T(8,128)(2,1)S(1)} %copy.30), channel_id=1, source_target_pairs={{0,1},{1,4},{4,5},{5,8},{8,9},{9,12},{12,13},{13,14},{14,15},{15,1... | collective-permute-start | bytes 786440 | tf_op jit(solution)/shard_map/while/body/eval_jaxpr/ppermute | solution.py:103
  37.9 7.3 %collective-permute-start.1 = (bf16[128,1024]{1,0:T(8,128)(2,1)S(1)}, bf16[128,1024]{1,0:T(8,128)(2,1)S(1)}, u32[]{:S(2)}, u32[]{:S(2)}) collective-permute-start(bf16[128,1024]{1,0:T(8,128)(2,1)S(1)} %copy.31), channel_id=1, source_target_pairs={{1,0},{4,1},{5,4},{8,5},{9,8},{12,9},{13,12},{14,13},{15,14},{10,1... | collective-permute-start | bytes 786440 | tf_op jit(solution)/shard_map/while/body/eval_jaxpr/ppermute | solution.py:103
  39.8 5.3 %collective-permute-start.3 = (f32[256,128]{0,1:T(8,128)S(1)}, f32[256,128]{0,1:T(8,128)S(1)}, u32[]{:S(2)}, u32[]{:S(2)}) collective-permute-start(f32[256,128]{0,1:T(8,128)S(1)} %add.215), channel_id=1, source_target_pairs={{1,0},{4,1},{5,4},{8,5},{9,8},{12,9},{13,12},{14,13},{15,14},{10,1... | collective-permute-start | bytes 393224 | tf_op jit(solution)/shard_map/while/body/eval_jaxpr/ppermute | solution.py:103
  45.2 7.4 %collective-permute-start = (bf16[128,1024]{1,0:T(8,128)(2,1)S(1)}, bf16[128,1024]{1,0:T(8,128)(2,1)S(1)}, u32[]{:S(2)}, u32[]{:S(2)}) collective-permute-start(bf16[128,1024]{1,0:T(8,128)(2,1)S(1)} %copy.30), channel_id=1, source_target_pairs={{0,1},{1,4},{4,5},{5,8},{8,9},{9,12},{12,13},{13,14},{14,15},{15,1... | collective-permute-start | bytes 786440 | tf_op jit(solution)/shard_map/while/body/eval_jaxpr/ppermute | solution.py:103
  45.3 7.3 %collective-permute-start.1 = (bf16[128,1024]{1,0:T(8,128)(2,1)S(1)}, bf16[128,1024]{1,0:T(8,128)(2,1)S(1)}, u32[]{:S(2)}, u32[]{:S(2)}) collective-permute-start(bf16[128,1024]{1,0:T(8,128)(2,1)S(1)} %copy.31), channel_id=1, source_target_pairs={{1,0},{4,1},{5,4},{8,5},{9,8},{12,9},{13,12},{14,13},{15,14},{10,1... | collective-permute-start | bytes 786440 | tf_op jit(solution)/shard_map/while/body/eval_jaxpr/ppermute | solution.py:103
  47.3 5.3 %collective-permute-start.3 = (f32[256,128]{0,1:T(8,128)S(1)}, f32[256,128]{0,1:T(8,128)S(1)}, u32[]{:S(2)}, u32[]{:S(2)}) collective-permute-start(f32[256,128]{0,1:T(8,128)S(1)} %add.215), channel_id=1, source_target_pairs={{1,0},{4,1},{5,4},{8,5},{9,8},{12,9},{13,12},{14,13},{15,14},{10,1... | collective-permute-start | bytes 393224 | tf_op jit(solution)/shard_map/while/body/eval_jaxpr/ppermute | solution.py:103
  52.7 7.4 %collective-permute-start = (bf16[128,1024]{1,0:T(8,128)(2,1)S(1)}, bf16[128,1024]{1,0:T(8,128)(2,1)S(1)}, u32[]{:S(2)}, u32[]{:S(2)}) collective-permute-start(bf16[128,1024]{1,0:T(8,128)(2,1)S(1)} %copy.30), channel_id=1, source_target_pairs={{0,1},{1,4},{4,5},{5,8},{8,9},{9,12},{12,13},{13,14},{14,15},{15,1... | collective-permute-start | bytes 786440 | tf_op jit(solution)/shard_map/while/body/eval_jaxpr/ppermute | solution.py:103
  52.8 7.3 %collective-permute-start.1 = (bf16[128,1024]{1,0:T(8,128)(2,1)S(1)}, bf16[128,1024]{1,0:T(8,128)(2,1)S(1)}, u32[]{:S(2)}, u32[]{:S(2)}) collective-permute-start(bf16[128,1024]{1,0:T(8,128)(2,1)S(1)} %copy.31), channel_id=1, source_target_pairs={{1,0},{4,1},{5,4},{8,5},{9,8},{12,9},{13,12},{14,13},{15,14},{10,1... | collective-permute-start | bytes 786440 | tf_op jit(solution)/shard_map/while/body/eval_jaxpr/ppermute | solution.py:103
  53.4 5.1 %collective-permute-start.2 = (f32[256,128]{0,1:T(8,128)S(1)}, f32[256,128]{0,1:T(8,128)S(1)}, u32[]{:S(2)}, u32[]{:S(2)}) collective-permute-start(f32[256,128]{0,1:T(8,128)S(1)} %add.214), channel_id=1, source_target_pairs={{0,1},{1,4},{4,5},{5,8},{8,9},{9,12},{12,13},{13,14},{14,15},{15,1... | collective-permute-start | bytes 393224 | tf_op jit(solution)/shard_map/while/body/eval_jaxpr/ppermute | solution.py:103
  54.7 5.3 %collective-permute-start.3 = (f32[256,128]{0,1:T(8,128)S(1)}, f32[256,128]{0,1:T(8,128)S(1)}, u32[]{:S(2)}, u32[]{:S(2)}) collective-permute-start(f32[256,128]{0,1:T(8,128)S(1)} %add.215), channel_id=1, source_target_pairs={{1,0},{4,1},{5,4},{8,5},{9,8},{12,9},{13,12},{14,13},{15,14},{10,1... | collective-permute-start | bytes 393224 | tf_op jit(solution)/shard_map/while/body/eval_jaxpr/ppermute | solution.py:103
  60.1 7.4 %collective-permute-start = (bf16[128,1024]{1,0:T(8,128)(2,1)S(1)}, bf16[128,1024]{1,0:T(8,128)(2,1)S(1)}, u32[]{:S(2)}, u32[]{:S(2)}) collective-permute-start(bf16[128,1024]{1,0:T(8,128)(2,1)S(1)} %copy.30), channel_id=1, source_target_pairs={{0,1},{1,4},{4,5},{5,8},{8,9},{9,12},{12,13},{13,14},{14,15},{15,1... | collective-permute-start | bytes 786440 | tf_op jit(solution)/shard_map/while/body/eval_jaxpr/ppermute | solution.py:103
  60.2 7.3 %collective-permute-start.1 = (bf16[128,1024]{1,0:T(8,128)(2,1)S(1)}, bf16[128,1024]{1,0:T(8,128)(2,1)S(1)}, u32[]{:S(2)}, u32[]{:S(2)}) collective-permute-start(bf16[128,1024]{1,0:T(8,128)(2,1)S(1)} %copy.31), channel_id=1, source_target_pairs={{1,0},{4,1},{5,4},{8,5},{9,8},{12,9},{13,12},{14,13},{15,14},{10,1... | collective-permute-start | bytes 786440 | tf_op jit(solution)/shard_map/while/body/eval_jaxpr/ppermute | solution.py:103
  62.2 5.3 %collective-permute-start.3 = (f32[256,128]{0,1:T(8,128)S(1)}, f32[256,128]{0,1:T(8,128)S(1)}, u32[]{:S(2)}, u32[]{:S(2)}) collective-permute-start(f32[256,128]{0,1:T(8,128)S(1)} %add.215), channel_id=1, source_target_pairs={{1,0},{4,1},{5,4},{8,5},{9,8},{12,9},{13,12},{14,13},{15,14},{10,1... | collective-permute-start | bytes 393224 | tf_op jit(solution)/shard_map/while/body/eval_jaxpr/ppermute | solution.py:103
  67.5 7.4 %collective-permute-start = (bf16[128,1024]{1,0:T(8,128)(2,1)S(1)}, bf16[128,1024]{1,0:T(8,128)(2,1)S(1)}, u32[]{:S(2)}, u32[]{:S(2)}) collective-permute-start(bf16[128,1024]{1,0:T(8,128)(2,1)S(1)} %copy.30), channel_id=1, source_target_pairs={{0,1},{1,4},{4,5},{5,8},{8,9},{9,12},{12,13},{13,14},{14,15},{15,1... | collective-permute-start | bytes 786440 | tf_op jit(solution)/shard_map/while/body/eval_jaxpr/ppermute | solution.py:103
  67.7 7.3 %collective-permute-start.1 = (bf16[128,1024]{1,0:T(8,128)(2,1)S(1)}, bf16[128,1024]{1,0:T(8,128)(2,1)S(1)}, u32[]{:S(2)}, u32[]{:S(2)}) collective-permute-start(bf16[128,1024]{1,0:T(8,128)(2,1)S(1)} %copy.31), channel_id=1, source_target_pairs={{1,0},{4,1},{5,4},{8,5},{9,8},{12,9},{13,12},{14,13},{15,14},{10,1... | collective-permute-start | bytes 786440 | tf_op jit(solution)/shard_map/while/body/eval_jaxpr/ppermute | solution.py:103
  68.2 5.1 %collective-permute-start.2 = (f32[256,128]{0,1:T(8,128)S(1)}, f32[256,128]{0,1:T(8,128)S(1)}, u32[]{:S(2)}, u32[]{:S(2)}) collective-permute-start(f32[256,128]{0,1:T(8,128)S(1)} %add.214), channel_id=1, source_target_pairs={{0,1},{1,4},{4,5},{5,8},{8,9},{9,12},{12,13},{13,14},{14,15},{15,1... | collective-permute-start | bytes 393224 | tf_op jit(solution)/shard_map/while/body/eval_jaxpr/ppermute | solution.py:103
  69.6 5.3 %collective-permute-start.3 = (f32[256,128]{0,1:T(8,128)S(1)}, f32[256,128]{0,1:T(8,128)S(1)}, u32[]{:S(2)}, u32[]{:S(2)}) collective-permute-start(f32[256,128]{0,1:T(8,128)S(1)} %add.215), channel_id=1, source_target_pairs={{1,0},{4,1},{5,4},{8,5},{9,8},{12,9},{13,12},{14,13},{15,14},{10,1... | collective-permute-start | bytes 393224 | tf_op jit(solution)/shard_map/while/body/eval_jaxpr/ppermute | solution.py:103
  75.0 7.4 %collective-permute-start = (bf16[128,1024]{1,0:T(8,128)(2,1)S(1)}, bf16[128,1024]{1,0:T(8,128)(2,1)S(1)}, u32[]{:S(2)}, u32[]{:S(2)}) collective-permute-start(bf16[128,1024]{1,0:T(8,128)(2,1)S(1)} %copy.30), channel_id=1, source_target_pairs={{0,1},{1,4},{4,5},{5,8},{8,9},{9,12},{12,13},{13,14},{14,15},{15,1... | collective-permute-start | bytes 786440 | tf_op jit(solution)/shard_map/while/body/eval_jaxpr/ppermute | solution.py:103
  75.1 7.3 %collective-permute-start.1 = (bf16[128,1024]{1,0:T(8,128)(2,1)S(1)}, bf16[128,1024]{1,0:T(8,128)(2,1)S(1)}, u32[]{:S(2)}, u32[]{:S(2)}) collective-permute-start(bf16[128,1024]{1,0:T(8,128)(2,1)S(1)} %copy.31), channel_id=1, source_target_pairs={{1,0},{4,1},{5,4},{8,5},{9,8},{12,9},{13,12},{14,13},{15,14},{10,1... | collective-permute-start | bytes 786440 | tf_op jit(solution)/shard_map/while/body/eval_jaxpr/ppermute | solution.py:103
  77.0 5.3 %collective-permute-start.3 = (f32[256,128]{0,1:T(8,128)S(1)}, f32[256,128]{0,1:T(8,128)S(1)}, u32[]{:S(2)}, u32[]{:S(2)}) collective-permute-start(f32[256,128]{0,1:T(8,128)S(1)} %add.215), channel_id=1, source_target_pairs={{1,0},{4,1},{5,4},{8,5},{9,8},{12,9},{13,12},{14,13},{15,14},{10,1... | collective-permute-start | bytes 393224 | tf_op jit(solution)/shard_map/while/body/eval_jaxpr/ppermute | solution.py:103
  82.4 7.4 %collective-permute-start = (bf16[128,1024]{1,0:T(8,128)(2,1)S(1)}, bf16[128,1024]{1,0:T(8,128)(2,1)S(1)}, u32[]{:S(2)}, u32[]{:S(2)}) collective-permute-start(bf16[128,1024]{1,0:T(8,128)(2,1)S(1)} %copy.30), channel_id=1, source_target_pairs={{0,1},{1,4},{4,5},{5,8},{8,9},{9,12},{12,13},{13,14},{14,15},{15,1... | collective-permute-start | bytes 786440 | tf_op jit(solution)/shard_map/while/body/eval_jaxpr/ppermute | solution.py:103
  82.5 7.3 %collective-permute-start.1 = (bf16[128,1024]{1,0:T(8,128)(2,1)S(1)}, bf16[128,1024]{1,0:T(8,128)(2,1)S(1)}, u32[]{:S(2)}, u32[]{:S(2)}) collective-permute-start(bf16[128,1024]{1,0:T(8,128)(2,1)S(1)} %copy.31), channel_id=1, source_target_pairs={{1,0},{4,1},{5,4},{8,5},{9,8},{12,9},{13,12},{14,13},{15,14},{10,1... | collective-permute-start | bytes 786440 | tf_op jit(solution)/shard_map/while/body/eval_jaxpr/ppermute | solution.py:103
  83.1 5.1 %collective-permute-start.2 = (f32[256,128]{0,1:T(8,128)S(1)}, f32[256,128]{0,1:T(8,128)S(1)}, u32[]{:S(2)}, u32[]{:S(2)}) collective-permute-start(f32[256,128]{0,1:T(8,128)S(1)} %add.214), channel_id=1, source_target_pairs={{0,1},{1,4},{4,5},{5,8},{8,9},{9,12},{12,13},{13,14},{14,15},{15,1... | collective-permute-start | bytes 393224 | tf_op jit(solution)/shard_map/while/body/eval_jaxpr/ppermute | solution.py:103
  84.5 5.3 %collective-permute-start.3 = (f32[256,128]{0,1:T(8,128)S(1)}, f32[256,128]{0,1:T(8,128)S(1)}, u32[]{:S(2)}, u32[]{:S(2)}) collective-permute-start(f32[256,128]{0,1:T(8,128)S(1)} %add.215), channel_id=1, source_target_pairs={{1,0},{4,1},{5,4},{8,5},{9,8},{12,9},{13,12},{14,13},{15,14},{10,1... | collective-permute-start | bytes 393224 | tf_op jit(solution)/shard_map/while/body/eval_jaxpr/ppermute | solution.py:103
  89.8 7.4 %collective-permute-start = (bf16[128,1024]{1,0:T(8,128)(2,1)S(1)}, bf16[128,1024]{1,0:T(8,128)(2,1)S(1)}, u32[]{:S(2)}, u32[]{:S(2)}) collective-permute-start(bf16[128,1024]{1,0:T(8,128)(2,1)S(1)} %copy.30), channel_id=1, source_target_pairs={{0,1},{1,4},{4,5},{5,8},{8,9},{9,12},{12,13},{13,14},{14,15},{15,1... | collective-permute-start | bytes 786440 | tf_op jit(solution)/shard_map/while/body/eval_jaxpr/ppermute | solution.py:103
  90.0 7.3 %collective-permute-start.1 = (bf16[128,1024]{1,0:T(8,128)(2,1)S(1)}, bf16[128,1024]{1,0:T(8,128)(2,1)S(1)}, u32[]{:S(2)}, u32[]{:S(2)}) collective-permute-start(bf16[128,1024]{1,0:T(8,128)(2,1)S(1)} %copy.31), channel_id=1, source_target_pairs={{1,0},{4,1},{5,4},{8,5},{9,8},{12,9},{13,12},{14,13},{15,14},{10,1... | collective-permute-start | bytes 786440 | tf_op jit(solution)/shard_map/while/body/eval_jaxpr/ppermute | solution.py:103
  91.9 5.3 %collective-permute-start.3 = (f32[256,128]{0,1:T(8,128)S(1)}, f32[256,128]{0,1:T(8,128)S(1)}, u32[]{:S(2)}, u32[]{:S(2)}) collective-permute-start(f32[256,128]{0,1:T(8,128)S(1)} %add.215), channel_id=1, source_target_pairs={{1,0},{4,1},{5,4},{8,5},{9,8},{12,9},{13,12},{14,13},{15,14},{10,1... | collective-permute-start | bytes 393224 | tf_op jit(solution)/shard_map/while/body/eval_jaxpr/ppermute | solution.py:103
  97.3 7.4 %collective-permute-start = (bf16[128,1024]{1,0:T(8,128)(2,1)S(1)}, bf16[128,1024]{1,0:T(8,128)(2,1)S(1)}, u32[]{:S(2)}, u32[]{:S(2)}) collective-permute-start(bf16[128,1024]{1,0:T(8,128)(2,1)S(1)} %copy.30), channel_id=1, source_target_pairs={{0,1},{1,4},{4,5},{5,8},{8,9},{9,12},{12,13},{13,14},{14,15},{15,1... | collective-permute-start | bytes 786440 | tf_op jit(solution)/shard_map/while/body/eval_jaxpr/ppermute | solution.py:103
  97.4 7.3 %collective-permute-start.1 = (bf16[128,1024]{1,0:T(8,128)(2,1)S(1)}, bf16[128,1024]{1,0:T(8,128)(2,1)S(1)}, u32[]{:S(2)}, u32[]{:S(2)}) collective-permute-start(bf16[128,1024]{1,0:T(8,128)(2,1)S(1)} %copy.31), channel_id=1, source_target_pairs={{1,0},{4,1},{5,4},{8,5},{9,8},{12,9},{13,12},{14,13},{15,14},{10,1... | collective-permute-start | bytes 786440 | tf_op jit(solution)/shard_map/while/body/eval_jaxpr/ppermute | solution.py:103
  99.3 5.3 %collective-permute-start.3 = (f32[256,128]{0,1:T(8,128)S(1)}, f32[256,128]{0,1:T(8,128)S(1)}, u32[]{:S(2)}, u32[]{:S(2)}) collective-permute-start(f32[256,128]{0,1:T(8,128)S(1)} %add.215), channel_id=1, source_target_pairs={{1,0},{4,1},{5,4},{8,5},{9,8},{12,9},{13,12},{14,13},{15,14},{10,1... | collective-permute-start | bytes 393224 | tf_op jit(solution)/shard_map/while/body/eval_jaxpr/ppermute | solution.py:103
  104.7 7.4 %collective-permute-start = (bf16[128,1024]{1,0:T(8,128)(2,1)S(1)}, bf16[128,1024]{1,0:T(8,128)(2,1)S(1)}, u32[]{:S(2)}, u32[]{:S(2)}) collective-permute-start(bf16[128,1024]{1,0:T(8,128)(2,1)S(1)} %copy.30), channel_id=1, source_target_pairs={{0,1},{1,4},{4,5},{5,8},{8,9},{9,12},{12,13},{13,14},{14,15},{15,1... | collective-permute-start | bytes 786440 | tf_op jit(solution)/shard_map/while/body/eval_jaxpr/ppermute | solution.py:103
  104.8 7.3 %collective-permute-start.1 = (bf16[128,1024]{1,0:T(8,128)(2,1)S(1)}, bf16[128,1024]{1,0:T(8,128)(2,1)S(1)}, u32[]{:S(2)}, u32[]{:S(2)}) collective-permute-start(bf16[128,1024]{1,0:T(8,128)(2,1)S(1)} %copy.31), channel_id=1, source_target_pairs={{1,0},{4,1},{5,4},{8,5},{9,8},{12,9},{13,12},{14,13},{15,14},{10,1... | collective-permute-start | bytes 786440 | tf_op jit(solution)/shard_map/while/body/eval_jaxpr/ppermute | solution.py:103
  106.8 5.3 %collective-permute-start.3 = (f32[256,128]{0,1:T(8,128)S(1)}, f32[256,128]{0,1:T(8,128)S(1)}, u32[]{:S(2)}, u32[]{:S(2)}) collective-permute-start(f32[256,128]{0,1:T(8,128)S(1)} %add.215), channel_id=1, source_target_pairs={{1,0},{4,1},{5,4},{8,5},{9,8},{12,9},{13,12},{14,13},{15,14},{10,1... | collective-permute-start | bytes 393224 | tf_op jit(solution)/shard_map/while/body/eval_jaxpr/ppermute | solution.py:103
  112.1 7.4 %collective-permute-start = (bf16[128,1024]{1,0:T(8,128)(2,1)S(1)}, bf16[128,1024]{1,0:T(8,128)(2,1)S(1)}, u32[]{:S(2)}, u32[]{:S(2)}) collective-permute-start(bf16[128,1024]{1,0:T(8,128)(2,1)S(1)} %copy.30), channel_id=1, source_target_pairs={{0,1},{1,4},{4,5},{5,8},{8,9},{9,12},{12,13},{13,14},{14,15},{15,1... | collective-permute-start | bytes 786440 | tf_op jit(solution)/shard_map/while/body/eval_jaxpr/ppermute | solution.py:103
  112.3 7.3 %collective-permute-start.1 = (bf16[128,1024]{1,0:T(8,128)(2,1)S(1)}, bf16[128,1024]{1,0:T(8,128)(2,1)S(1)}, u32[]{:S(2)}, u32[]{:S(2)}) collective-permute-start(bf16[128,1024]{1,0:T(8,128)(2,1)S(1)} %copy.31), channel_id=1, source_target_pairs={{1,0},{4,1},{5,4},{8,5},{9,8},{12,9},{13,12},{14,13},{15,14},{10,1... | collective-permute-start | bytes 786440 | tf_op jit(solution)/shard_map/while/body/eval_jaxpr/ppermute | solution.py:103
  114.2 5.3 %collective-permute-start.3 = (f32[256,128]{0,1:T(8,128)S(1)}, f32[256,128]{0,1:T(8,128)S(1)}, u32[]{:S(2)}, u32[]{:S(2)}) collective-permute-start(f32[256,128]{0,1:T(8,128)S(1)} %add.215), channel_id=1, source_target_pairs={{1,0},{4,1},{5,4},{8,5},{9,8},{12,9},{13,12},{14,13},{15,14},{10,1... | collective-permute-start | bytes 393224 | tf_op jit(solution)/shard_map/while/body/eval_jaxpr/ppermute | solution.py:103
  119.6 5.2 %collective-permute-start.7 = (f32[256,128]{0,1:T(8,128)S(1)}, f32[256,128]{0,1:T(8,128)S(1)}, u32[]{:S(2)}, u32[]{:S(2)}) collective-permute-start(f32[256,128]{0,1:T(8,128)S(1)} %add.136), channel_id=1, source_target_pairs={{1,0},{4,1},{5,4},{8,5},{9,8},{12,9},{13,12},{14,13},{15,14},{10,1... | collective-permute-start | bytes 393224 | tf_op jit(solution)/shard_map/ppermute | solution.py:103
  (34 other events, 129.7 us)

commit v9 on v8

--- a/solution.py
+++ b/solution.py
@@ -42,6 +42,22 @@
     return lax.dot_general(
         rhs_values, matern, (((0,), (1,)), ((), ())), preferred_element_type=jnp.float32
     )
+
+
+def staged_scatter(sums, axis, inner=8):
+    size = lax.axis_size(axis)
+    outer = size // inner
+    if size != outer * inner or outer < 2:
+        return exchange_scatter(sums, axis)
+    rows, cols = sums.shape
+    chunk = rows // size
+    pieces = sums.reshape(outer, inner, chunk, cols)
+    near = [[o * inner + i for i in range(inner)] for o in range(outer)]
+    pieces = lax.all_to_all(pieces, axis, 1, 1, axis_index_groups=near, tiled=True)
+    pieces = jnp.sum(pieces.reshape(outer, inner, chunk, cols), axis=1)
+    far = [[o * inner + i for o in range(outer)] for i in range(inner)]
+    pieces = lax.all_to_all(pieces, axis, 0, 0, axis_index_groups=far, tiled=True)
+    return jnp.sum(pieces, axis=0)
 
 
 def exchange_scatter(sums, axis):
@@ -118,7 +134,7 @@
     sums_f, sums_b = send(sums_f + part_f, sums_b + part_b)
     part_f, part_b = halves(points_f, points_b)
     complete = jnp.concatenate([sums_f + part_f, sums_b + part_b], axis=1)
-    owned = exchange_scatter(complete, "grp")
+    owned = staged_scatter(complete, "grp")
     mine_f, mine_b = send(owned[:, :half], owned[:, half:])
     owned_sums = jnp.concatenate([mine_f, mine_b], axis=1)
     source_total = src_codes.shape[0] * group_size * cycle_size

time: 154 us -> 161 us (1.045)
  blocking collectives: 20.8 us -> 26.5 us
    all_to_all x1 -> x2, blocking collectives: 20.8 us -> 26.5 us  [the longest x1 18.2 us: staged_scatter(): lax.all_to_all(pieces, axis, 1, 1, axis_index_groups=near, tiled=True)]
  transfers between devices with their start and end apart: 62 -> 62, of which waited for: 16 -> 16; matrix products, arithmetic and copies ran while one was open for 35% -> 34% of each run, Pallas kernels for 0% -> 0%
where the time goes in v9:
time: 161 us; the launch traced here: 160 us
  starting transfers between devices  47.4 us (29%)
  matrix products  46.1 us (29%)
  blocking collectives  26.5 us (16%)
  waiting for transfers between devices  25.1 us (16%)
  other arithmetic  8.03 us (5%)
  local copies, waits for them, and re-layouts  6.08 us (4%)
    dot_general x16, matrix products, kernel_block(): lax.dot_general(rhs_values, matern, (((0,), (1,)), ((), ())), preferred_e...  46.1 us
    ppermute x31, starting transfers between devices, send(): lax.ppermute(points_f, 'blk', forward)  29.8 us
    ppermute x31, waiting for transfers between devices, send(): lax.ppermute(points_b, 'blk', backward)  24.2 us
    all_to_all x1, blocking collectives, staged_scatter(): lax.all_to_all(pieces, axis, 1, 1, axis_index_groups=near, tiled=True)  18.2 us
    ppermute x31, starting transfers between devices, send(): lax.ppermute(points_b, 'blk', backward)  17.6 us
    all_to_all x1, blocking collectives, staged_scatter(): lax.all_to_all(pieces, axis, 0, 0, axis_index_groups=far, tiled=True)  8.27 us
    reduce_sum x17, other arithmetic, squares(): return jnp.sum(widened * widened, axis=1)  5.19 us
  transfers between devices with their start and end apart: 62, of which 16 were waited for; matrix products, arithmetic and copies ran while one was open for 34% of the time, Pallas kernels for 0%

profile of v9, /device:TPU:1, one launch (start us, length us, event | category | flops | bytes accessed | tf_op | source)
XLA Modules:
  0.0 160.3 jit_solution(13723445722678594621)
XLA Ops:
  1.2 1.6 multiply_reduce_fusion.3
  3.6 2.6 %collective-permute-start.4 = (bf16[128,1024]{1,0:T(8,128)(2,1)}, bf16[128,1024]{1,0:T(8,128)(2,1)S(1)}, u32[]{:S(2)}, u32[]{:S(2)}) collective-permute-start(bf16[128,1024]{1,0:T(8,128)(2,1)} %get-tuple-element.208), channel_id=1, source_target_pairs={{0,1},{1,4},{4,5},{5,8},{8,9},{9,12},{12,13},{13,14},{14,15},{15,1... | collective-permute-start | bytes 786440 | tf_op jit(solution)/shard_map/ppermute | solution.py:119
  11.0 2.8 %fusion.24 = f32[256,256]{1,0:T(8,128)S(1)} fusion(bf16[1024,256]{1,0:T(8,128)(2,1)} %add_convert_fusion, bf16[256,1024]{1,0:T(8,128)(2,1)S(1)} %get-tuple-element.202, bf16[1024,1024]{1,0:T(8,128)(2,1)S(1)} %get-tuple-element.288, f32[1024]{0:T(1024)S(1)} %get-tuple-element.287, f32[256]{0:T(256)S(1)} %get-tuple-element.201), kind=kOutput, calls=%fused_computation.38 | convolution fusion | flops 673972224 | bytes 3412992 | tf_op jit(solution)/shard_map/dot_general | solution.py:42
  14.2 105.3 %while.22 = (s32[]{:T(128)}, bf16[128,1024]{1,0:T(8,128)(2,1)S(1)}, bf16[128,1024]{1,0:T(8,128)(2,1)S(1)}, f32[256,128]{0,1:T(8,128)S(1)}, f32[256,128]{0,1:T(8,...) while((s32[]{:T(128)}, bf16[128,1024]{1,0:T(8,128)(2,1)S(1)}, ...), condition=%wide.region_4.5_spmd, body=%wide.region_2.4_spmd.sunk | while | flops 674823936 | bytes 12589353 | solution.py:132
  18.4 2.9 %convolution_bitcast_fusion.2 = f32[256,256]{0,1:T(8,128)S(1)} fusion(bf16[1024,256]{1,0:T(8,128)(2,1)S(1)} %copy-done.5, bf16[256,1024]{1,0:T(8,128)(2,1)S(1)} %constant_dynamic-update-slice_fusion.7, bf16[1024,1024]{1,0:T(8,128)(2,1)} %get-tuple-element.310, f32[1024]{0:T(1024)S(1)} %get-tuple-element.309, f32[256]{0:T(256)S(1)} %multiply_reduce_fusion.5), kind=kOutput, calls=%fused_computation.4.clone.1 | convolution fusion | flops 673972224 | bytes 3412992 | tf_op jit(solution)/shard_map/while/body/eval_jaxpr/dot_general | solution.py:42
  21.3 1.6 collective-permute-done.3
  23.6 1.3 collective-permute-start.2
  25.8 2.9 %convolution_bitcast_fusion.2 = f32[256,256]{0,1:T(8,128)S(1)} fusion(bf16[1024,256]{1,0:T(8,128)(2,1)S(1)} %copy-done.5, bf16[256,1024]{1,0:T(8,128)(2,1)S(1)} %constant_dynamic-update-slice_fusion.7, bf16[1024,1024]{1,0:T(8,128)(2,1)} %get-tuple-element.310, f32[1024]{0:T(1024)S(1)} %get-tuple-element.309, f32[256]{0:T(256)S(1)} %multiply_reduce_fusion.5), kind=kOutput, calls=%fused_computation.4.clone.1 | convolution fusion | flops 673972224 | bytes 3412992 | tf_op jit(solution)/shard_map/while/body/eval_jaxpr/dot_general | solution.py:42
  28.8 1.6 collective-permute-done.3
  31.1 1.3 collective-permute-start.2
  33.2 2.9 %convolution_bitcast_fusion.2 = f32[256,256]{0,1:T(8,128)S(1)} fusion(bf16[1024,256]{1,0:T(8,128)(2,1)S(1)} %copy-done.5, bf16[256,1024]{1,0:T(8,128)(2,1)S(1)} %constant_dynamic-update-slice_fusion.7, bf16[1024,1024]{1,0:T(8,128)(2,1)} %get-tuple-element.310, f32[1024]{0:T(1024)S(1)} %get-tuple-element.309, f32[256]{0:T(256)S(1)} %multiply_reduce_fusion.5), kind=kOutput, calls=%fused_computation.4.clone.1 | convolution fusion | flops 673972224 | bytes 3412992 | tf_op jit(solution)/shard_map/while/body/eval_jaxpr/dot_general | solution.py:42
  36.2 1.6 collective-permute-done.3
  38.5 1.3 collective-permute-start.2
  40.7 2.9 %convolution_bitcast_fusion.2 = f32[256,256]{0,1:T(8,128)S(1)} fusion(bf16[1024,256]{1,0:T(8,128)(2,1)S(1)} %copy-done.5, bf16[256,1024]{1,0:T(8,128)(2,1)S(1)} %constant_dynamic-update-slice_fusion.7, bf16[1024,1024]{1,0:T(8,128)(2,1)} %get-tuple-element.310, f32[1024]{0:T(1024)S(1)} %get-tuple-element.309, f32[256]{0:T(256)S(1)} %multiply_reduce_fusion.5), kind=kOutput, calls=%fused_computation.4.clone.1 | convolution fusion | flops 673972224 | bytes 3412992 | tf_op jit(solution)/shard_map/while/body/eval_jaxpr/dot_general | solution.py:42
  43.6 1.6 collective-permute-done.3
  45.9 1.3 collective-permute-start.2
  48.1 2.9 %convolution_bitcast_fusion.2 = f32[256,256]{0,1:T(8,128)S(1)} fusion(bf16[1024,256]{1,0:T(8,128)(2,1)S(1)} %copy-done.5, bf16[256,1024]{1,0:T(8,128)(2,1)S(1)} %constant_dynamic-update-slice_fusion.7, bf16[1024,1024]{1,0:T(8,128)(2,1)} %get-tuple-element.310, f32[1024]{0:T(1024)S(1)} %get-tuple-element.309, f32[256]{0:T(256)S(1)} %multiply_reduce_fusion.5), kind=kOutput, calls=%fused_computation.4.clone.1 | convolution fusion | flops 673972224 | bytes 3412992 | tf_op jit(solution)/shard_map/while/body/eval_jaxpr/dot_general | solution.py:42
  51.1 1.6 collective-permute-done.3
  53.4 1.3 collective-permute-start.2
  55.5 2.9 %convolution_bitcast_fusion.2 = f32[256,256]{0,1:T(8,128)S(1)} fusion(bf16[1024,256]{1,0:T(8,128)(2,1)S(1)} %copy-done.5, bf16[256,1024]{1,0:T(8,128)(2,1)S(1)} %constant_dynamic-update-slice_fusion.7, bf16[1024,1024]{1,0:T(8,128)(2,1)} %get-tuple-element.310, f32[1024]{0:T(1024)S(1)} %get-tuple-element.309, f32[256]{0:T(256)S(1)} %multiply_reduce_fusion.5), kind=kOutput, calls=%fused_computation.4.clone.1 | convolution fusion | flops 673972224 | bytes 3412992 | tf_op jit(solution)/shard_map/while/body/eval_jaxpr/dot_general | solution.py:42
  58.5 1.6 collective-permute-done.3
  60.8 1.3 collective-permute-start.2
  63.0 2.9 %convolution_bitcast_fusion.2 = f32[256,256]{0,1:T(8,128)S(1)} fusion(bf16[1024,256]{1,0:T(8,128)(2,1)S(1)} %copy-done.5, bf16[256,1024]{1,0:T(8,128)(2,1)S(1)} %constant_dynamic-update-slice_fusion.7, bf16[1024,1024]{1,0:T(8,128)(2,1)} %get-tuple-element.310, f32[1024]{0:T(1024)S(1)} %get-tuple-element.309, f32[256]{0:T(256)S(1)} %multiply_reduce_fusion.5), kind=kOutput, calls=%fused_computation.4.clone.1 | convolution fusion | flops 673972224 | bytes 3412992 | tf_op jit(solution)/shard_map/while/body/eval_jaxpr/dot_general | solution.py:42
  65.9 1.6 collective-permute-done.3
  68.2 1.3 collective-permute-start.2
  70.4 2.9 %convolution_bitcast_fusion.2 = f32[256,256]{0,1:T(8,128)S(1)} fusion(bf16[1024,256]{1,0:T(8,128)(2,1)S(1)} %copy-done.5, bf16[256,1024]{1,0:T(8,128)(2,1)S(1)} %constant_dynamic-update-slice_fusion.7, bf16[1024,1024]{1,0:T(8,128)(2,1)} %get-tuple-element.310, f32[1024]{0:T(1024)S(1)} %get-tuple-element.309, f32[256]{0:T(256)S(1)} %multiply_reduce_fusion.5), kind=kOutput, calls=%fused_computation.4.clone.1 | convolution fusion | flops 673972224 | bytes 3412992 | tf_op jit(solution)/shard_map/while/body/eval_jaxpr/dot_general | solution.py:42
  73.4 1.6 collective-permute-done.3
  77.9 2.9 %convolution_bitcast_fusion.2 = f32[256,256]{0,1:T(8,128)S(1)} fusion(bf16[1024,256]{1,0:T(8,128)(2,1)S(1)} %copy-done.5, bf16[256,1024]{1,0:T(8,128)(2,1)S(1)} %constant_dynamic-update-slice_fusion.7, bf16[1024,1024]{1,0:T(8,128)(2,1)} %get-tuple-element.310, f32[1024]{0:T(1024)S(1)} %get-tuple-element.309, f32[256]{0:T(256)S(1)} %multiply_reduce_fusion.5), kind=kOutput, calls=%fused_computation.4.clone.1 | convolution fusion | flops 673972224 | bytes 3412992 | tf_op jit(solution)/shard_map/while/body/eval_jaxpr/dot_general | solution.py:42
  80.8 1.6 collective-permute-done.3
  83.1 1.3 collective-permute-start.2
  85.3 2.9 %convolution_bitcast_fusion.2 = f32[256,256]{0,1:T(8,128)S(1)} fusion(bf16[1024,256]{1,0:T(8,128)(2,1)S(1)} %copy-done.5, bf16[256,1024]{1,0:T(8,128)(2,1)S(1)} %constant_dynamic-update-slice_fusion.7, bf16[1024,1024]{1,0:T(8,128)(2,1)} %get-tuple-element.310, f32[1024]{0:T(1024)S(1)} %get-tuple-element.309, f32[256]{0:T(256)S(1)} %multiply_reduce_fusion.5), kind=kOutput, calls=%fused_computation.4.clone.1 | convolution fusion | flops 673972224 | bytes 3412992 | tf_op jit(solution)/shard_map/while/body/eval_jaxpr/dot_general | solution.py:42
  88.2 1.6 collective-permute-done.3
  92.7 2.9 %convolution_bitcast_fusion.2 = f32[256,256]{0,1:T(8,128)S(1)} fusion(bf16[1024,256]{1,0:T(8,128)(2,1)S(1)} %copy-done.5, bf16[256,1024]{1,0:T(8,128)(2,1)S(1)} %constant_dynamic-update-slice_fusion.7, bf16[1024,1024]{1,0:T(8,128)(2,1)} %get-tuple-element.310, f32[1024]{0:T(1024)S(1)} %get-tuple-element.309, f32[256]{0:T(256)S(1)} %multiply_reduce_fusion.5), kind=kOutput, calls=%fused_computation.4.clone.1 | convolution fusion | flops 673972224 | bytes 3412992 | tf_op jit(solution)/shard_map/while/body/eval_jaxpr/dot_general | solution.py:42
  95.7 1.6 collective-permute-done.3
  98.0 1.3 collective-permute-start.2
  100.2 2.9 %convolution_bitcast_fusion.2 = f32[256,256]{0,1:T(8,128)S(1)} fusion(bf16[1024,256]{1,0:T(8,128)(2,1)S(1)} %copy-done.5, bf16[256,1024]{1,0:T(8,128)(2,1)S(1)} %constant_dynamic-update-slice_fusion.7, bf16[1024,1024]{1,0:T(8,128)(2,1)} %get-tuple-element.310, f32[1024]{0:T(1024)S(1)} %get-tuple-element.309, f32[256]{0:T(256)S(1)} %multiply_reduce_fusion.5), kind=kOutput, calls=%fused_computation.4.clone.1 | convolution fusion | flops 673972224 | bytes 3412992 | tf_op jit(solution)/shard_map/while/body/eval_jaxpr/dot_general | solution.py:42
  103.1 1.6 collective-permute-done.3
  107.6 2.9 %convolution_bitcast_fusion.2 = f32[256,256]{0,1:T(8,128)S(1)} fusion(bf16[1024,256]{1,0:T(8,128)(2,1)S(1)} %copy-done.5, bf16[256,1024]{1,0:T(8,128)(2,1)S(1)} %constant_dynamic-update-slice_fusion.7, bf16[1024,1024]{1,0:T(8,128)(2,1)} %get-tuple-element.310, f32[1024]{0:T(1024)S(1)} %get-tuple-element.309, f32[256]{0:T(256)S(1)} %multiply_reduce_fusion.5), kind=kOutput, calls=%fused_computation.4.clone.1 | convolution fusion | flops 673972224 | bytes 3412992 | tf_op jit(solution)/shard_map/while/body/eval_jaxpr/dot_general | solution.py:42
  110.5 1.6 collective-permute-done.3
  112.9 1.3 collective-permute-start.2
  115.0 2.9 %convolution_bitcast_fusion.2 = f32[256,256]{0,1:T(8,128)S(1)} fusion(bf16[1024,256]{1,0:T(8,128)(2,1)S(1)} %copy-done.5, bf16[256,1024]{1,0:T(8,128)(2,1)S(1)} %constant_dynamic-update-slice_fusion.7, bf16[1024,1024]{1,0:T(8,128)(2,1)} %get-tuple-element.310, f32[1024]{0:T(1024)S(1)} %get-tuple-element.309, f32[256]{0:T(256)S(1)} %multiply_reduce_fusion.5), kind=kOutput, calls=%fused_computation.4.clone.1 | convolution fusion | flops 673972224 | bytes 3412992 | tf_op jit(solution)/shard_map/while/body/eval_jaxpr/dot_general | solution.py:42
  118.0 1.6 collective-permute-done.3
  120.9 1.3 collective-permute-start.6
  122.3 2.5 %fusion.22 = f32[256,256]{0,1:T(8,128)S(1)} fusion(bf16[1024,256]{1,0:T(8,128)(2,1)} %get-tuple-element.324, bf16[256,1024]{1,0:T(8,128)(2,1)} %copy-done.3, bf16[1024,1024]{1,0:T(8,128)(2,1)S(1)} %copy-done.2, f32[256]{0:T(256)S(1)} %multiply_reduce_fusion.2, f32[1024]{0:T(1024)S(1)} %get-tuple-element.333), kind=kOutput, calls=%fused_computation.34 | convolution fusion | flops 673972224 | bytes 3412992 | tf_op jit(solution)/shard_map/dot_general | solution.py:42
  125.0 18.2 %all_to_all.10 = f32[2,8,16,256]{3,2,0,1:T(8,128)S(1)} all-to-all(f32[2,8,16,256]{3,2,0,1:T(8,128)S(1)} %copy.26), channel_id=1, replica_groups={{0,16,32,48,64,80,96,112},{128,144,160,176,192,208,224,240},{1,17,33,49..., dimensions={1} | all-to-all | bytes 524288 | tf_op jit(solution)/shard_map/all_to_all | solution.py:56
  143.3 8.3 %all_to_all.11 = f32[2,16,256]{2,1,0:T(8,128)S(1)} all-to-all(f32[2,16,256]{2,1,0:T(8,128)S(1)} %reduce_sum.60), channel_id=1, replica_groups={{0,128},{16,144},{32,160},{48,176},{64,192},{80,208},{96,224},{112,240}..., dimensions={0} | all-to-all | bytes 65536 | tf_op jit(solution)/shard_map/all_to_all | solution.py:59
  151.5 5.1 %collective-permute-start.8 = (f32[16,128]{1,0:T(8,128)S(1)}, f32[16,128]{1,0:T(8,128)S(1)}, u32[]{:S(2)}, u32[]{:S(2)}) collective-permute-start(f32[16,128]{1,0:T(8,128)S(1)} %get-tuple-element.213), channel_id=1, source_target_pairs={{0,1},{1,4},{4,5},{5,8},{8,9},{9,12},{12,13},{13,14},{14,15},{15,1... | collective-permute-start | bytes 24584 | tf_op jit(solution)/shard_map/ppermute | solution.py:119
  157.4 2.3 %collective-permute-done.9 = f32[16,128]{1,0:T(8,128)S(1)} collective-permute-done((f32[16,128]{1,0:T(8,128)S(1)}, f32[16,128]{1,0:T(8,128)S(1)}, u32[]{:S(2)}, u32[]{:S(2)}) %collective-permute-start.9) | collective-permute-done | bytes 8224 | tf_op jit(solution)/shard_map/ppermute | solution.py:119
  (275 shorter events, 38.5 us)
Async XLA Ops:
  3.6 10.5 %collective-permute-start.4 = (bf16[128,1024]{1,0:T(8,128)(2,1)}, bf16[128,1024]{1,0:T(8,128)(2,1)S(1)}, u32[]{:S(2)}, u32[]{:S(2)}) collective-permute-start(bf16[128,1024]{1,0:T(8,128)(2,1)} %get-tuple-element.208), channel_id=1, source_target_pairs={{0,1},{1,4},{4,5},{5,8},{8,9},{9,12},{12,13},{13,14},{14,15},{15,1... | collective-permute-start | bytes 786440 | tf_op jit(solution)/shard_map/ppermute | solution.py:119
  6.2 7.9 %collective-permute-start.5 = (bf16[128,1024]{1,0:T(8,128)(2,1)}, bf16[128,1024]{1,0:T(8,128)(2,1)S(1)}, u32[]{:S(2)}, u32[]{:S(2)}) collective-permute-start(bf16[128,1024]{1,0:T(8,128)(2,1)} %get-tuple-element.207), channel_id=1, source_target_pairs={{1,0},{4,1},{5,4},{8,5},{9,8},{12,9},{13,12},{14,13},{15,14},{10,1... | collective-permute-start | bytes 786440 | tf_op jit(solution)/shard_map/ppermute | solution.py:119
  14.3 8.6 %collective-permute-start = (bf16[128,1024]{1,0:T(8,128)(2,1)S(1)}, bf16[128,1024]{1,0:T(8,128)(2,1)S(1)}, u32[]{:S(2)}, u32[]{:S(2)}) collective-permute-start(bf16[128,1024]{1,0:T(8,128)(2,1)S(1)} %copy.42), channel_id=1, source_target_pairs={{0,1},{1,4},{4,5},{5,8},{8,9},{9,12},{12,13},{13,14},{14,15},{15,1... | collective-permute-start | bytes 786440 | tf_op jit(solution)/shard_map/while/body/eval_jaxpr/ppermute | solution.py:119
  15.5 7.4 %collective-permute-start.1 = (bf16[128,1024]{1,0:T(8,128)(2,1)S(1)}, bf16[128,1024]{1,0:T(8,128)(2,1)S(1)}, u32[]{:S(2)}, u32[]{:S(2)}) collective-permute-start(bf16[128,1024]{1,0:T(8,128)(2,1)S(1)} %copy.43), channel_id=1, source_target_pairs={{1,0},{4,1},{5,4},{8,5},{9,8},{12,9},{13,12},{14,13},{15,14},{10,1... | collective-permute-start | bytes 786440 | tf_op jit(solution)/shard_map/while/body/eval_jaxpr/ppermute | solution.py:119
  17.4 5.5 %collective-permute-start.3 = (f32[256,128]{0,1:T(8,128)S(1)}, f32[256,128]{0,1:T(8,128)S(1)}, u32[]{:S(2)}, u32[]{:S(2)}) collective-permute-start(f32[256,128]{0,1:T(8,128)S(1)} %add.215), channel_id=1, source_target_pairs={{1,0},{4,1},{5,4},{8,5},{9,8},{12,9},{13,12},{14,13},{15,14},{10,1... | collective-permute-start | bytes 393224 | tf_op jit(solution)/shard_map/while/body/eval_jaxpr/ppermute | solution.py:119
  22.9 7.4 %collective-permute-start = (bf16[128,1024]{1,0:T(8,128)(2,1)S(1)}, bf16[128,1024]{1,0:T(8,128)(2,1)S(1)}, u32[]{:S(2)}, u32[]{:S(2)}) collective-permute-start(bf16[128,1024]{1,0:T(8,128)(2,1)S(1)} %copy.42), channel_id=1, source_target_pairs={{0,1},{1,4},{4,5},{5,8},{8,9},{9,12},{12,13},{13,14},{14,15},{15,1... | collective-permute-start | bytes 786440 | tf_op jit(solution)/shard_map/while/body/eval_jaxpr/ppermute | solution.py:119
  23.0 7.3 %collective-permute-start.1 = (bf16[128,1024]{1,0:T(8,128)(2,1)S(1)}, bf16[128,1024]{1,0:T(8,128)(2,1)S(1)}, u32[]{:S(2)}, u32[]{:S(2)}) collective-permute-start(bf16[128,1024]{1,0:T(8,128)(2,1)S(1)} %copy.43), channel_id=1, source_target_pairs={{1,0},{4,1},{5,4},{8,5},{9,8},{12,9},{13,12},{14,13},{15,14},{10,1... | collective-permute-start | bytes 786440 | tf_op jit(solution)/shard_map/while/body/eval_jaxpr/ppermute | solution.py:119
  25.0 5.3 %collective-permute-start.3 = (f32[256,128]{0,1:T(8,128)S(1)}, f32[256,128]{0,1:T(8,128)S(1)}, u32[]{:S(2)}, u32[]{:S(2)}) collective-permute-start(f32[256,128]{0,1:T(8,128)S(1)} %add.215), channel_id=1, source_target_pairs={{1,0},{4,1},{5,4},{8,5},{9,8},{12,9},{13,12},{14,13},{15,14},{10,1... | collective-permute-start | bytes 393224 | tf_op jit(solution)/shard_map/while/body/eval_jaxpr/ppermute | solution.py:119
  30.4 7.4 %collective-permute-start = (bf16[128,1024]{1,0:T(8,128)(2,1)S(1)}, bf16[128,1024]{1,0:T(8,128)(2,1)S(1)}, u32[]{:S(2)}, u32[]{:S(2)}) collective-permute-start(bf16[128,1024]{1,0:T(8,128)(2,1)S(1)} %copy.42), channel_id=1, source_target_pairs={{0,1},{1,4},{4,5},{5,8},{8,9},{9,12},{12,13},{13,14},{14,15},{15,1... | collective-permute-start | bytes 786440 | tf_op jit(solution)/shard_map/while/body/eval_jaxpr/ppermute | solution.py:119
  30.5 7.3 %collective-permute-start.1 = (bf16[128,1024]{1,0:T(8,128)(2,1)S(1)}, bf16[128,1024]{1,0:T(8,128)(2,1)S(1)}, u32[]{:S(2)}, u32[]{:S(2)}) collective-permute-start(bf16[128,1024]{1,0:T(8,128)(2,1)S(1)} %copy.43), channel_id=1, source_target_pairs={{1,0},{4,1},{5,4},{8,5},{9,8},{12,9},{13,12},{14,13},{15,14},{10,1... | collective-permute-start | bytes 786440 | tf_op jit(solution)/shard_map/while/body/eval_jaxpr/ppermute | solution.py:119
  31.1 5.1 %collective-permute-start.2 = (f32[256,128]{0,1:T(8,128)S(1)}, f32[256,128]{0,1:T(8,128)S(1)}, u32[]{:S(2)}, u32[]{:S(2)}) collective-permute-start(f32[256,128]{0,1:T(8,128)S(1)} %add.214), channel_id=1, source_target_pairs={{0,1},{1,4},{4,5},{5,8},{8,9},{9,12},{12,13},{13,14},{14,15},{15,1... | collective-permute-start | bytes 393224 | tf_op jit(solution)/shard_map/while/body/eval_jaxpr/ppermute | solution.py:119
  32.4 5.3 %collective-permute-start.3 = (f32[256,128]{0,1:T(8,128)S(1)}, f32[256,128]{0,1:T(8,128)S(1)}, u32[]{:S(2)}, u32[]{:S(2)}) collective-permute-start(f32[256,128]{0,1:T(8,128)S(1)} %add.215), channel_id=1, source_target_pairs={{1,0},{4,1},{5,4},{8,5},{9,8},{12,9},{13,12},{14,13},{15,14},{10,1... | collective-permute-start | bytes 393224 | tf_op jit(solution)/shard_map/while/body/eval_jaxpr/ppermute | solution.py:119
  37.8 7.4 %collective-permute-start = (bf16[128,1024]{1,0:T(8,128)(2,1)S(1)}, bf16[128,1024]{1,0:T(8,128)(2,1)S(1)}, u32[]{:S(2)}, u32[]{:S(2)}) collective-permute-start(bf16[128,1024]{1,0:T(8,128)(2,1)S(1)} %copy.42), channel_id=1, source_target_pairs={{0,1},{1,4},{4,5},{5,8},{8,9},{9,12},{12,13},{13,14},{14,15},{15,1... | collective-permute-start | bytes 786440 | tf_op jit(solution)/shard_map/while/body/eval_jaxpr/ppermute | solution.py:119
  37.9 7.3 %collective-permute-start.1 = (bf16[128,1024]{1,0:T(8,128)(2,1)S(1)}, bf16[128,1024]{1,0:T(8,128)(2,1)S(1)}, u32[]{:S(2)}, u32[]{:S(2)}) collective-permute-start(bf16[128,1024]{1,0:T(8,128)(2,1)S(1)} %copy.43), channel_id=1, source_target_pairs={{1,0},{4,1},{5,4},{8,5},{9,8},{12,9},{13,12},{14,13},{15,14},{10,1... | collective-permute-start | bytes 786440 | tf_op jit(solution)/shard_map/while/body/eval_jaxpr/ppermute | solution.py:119
  39.8 5.3 %collective-permute-start.3 = (f32[256,128]{0,1:T(8,128)S(1)}, f32[256,128]{0,1:T(8,128)S(1)}, u32[]{:S(2)}, u32[]{:S(2)}) collective-permute-start(f32[256,128]{0,1:T(8,128)S(1)} %add.215), channel_id=1, source_target_pairs={{1,0},{4,1},{5,4},{8,5},{9,8},{12,9},{13,12},{14,13},{15,14},{10,1... | collective-permute-start | bytes 393224 | tf_op jit(solution)/shard_map/while/body/eval_jaxpr/ppermute | solution.py:119
  45.2 7.4 %collective-permute-start = (bf16[128,1024]{1,0:T(8,128)(2,1)S(1)}, bf16[128,1024]{1,0:T(8,128)(2,1)S(1)}, u32[]{:S(2)}, u32[]{:S(2)}) collective-permute-start(bf16[128,1024]{1,0:T(8,128)(2,1)S(1)} %copy.42), channel_id=1, source_target_pairs={{0,1},{1,4},{4,5},{5,8},{8,9},{9,12},{12,13},{13,14},{14,15},{15,1... | collective-permute-start | bytes 786440 | tf_op jit(solution)/shard_map/while/body/eval_jaxpr/ppermute | solution.py:119
  45.3 7.3 %collective-permute-start.1 = (bf16[128,1024]{1,0:T(8,128)(2,1)S(1)}, bf16[128,1024]{1,0:T(8,128)(2,1)S(1)}, u32[]{:S(2)}, u32[]{:S(2)}) collective-permute-start(bf16[128,1024]{1,0:T(8,128)(2,1)S(1)} %copy.43), channel_id=1, source_target_pairs={{1,0},{4,1},{5,4},{8,5},{9,8},{12,9},{13,12},{14,13},{15,14},{10,1... | collective-permute-start | bytes 786440 | tf_op jit(solution)/shard_map/while/body/eval_jaxpr/ppermute | solution.py:119
  47.3 5.3 %collective-permute-start.3 = (f32[256,128]{0,1:T(8,128)S(1)}, f32[256,128]{0,1:T(8,128)S(1)}, u32[]{:S(2)}, u32[]{:S(2)}) collective-permute-start(f32[256,128]{0,1:T(8,128)S(1)} %add.215), channel_id=1, source_target_pairs={{1,0},{4,1},{5,4},{8,5},{9,8},{12,9},{13,12},{14,13},{15,14},{10,1... | collective-permute-start | bytes 393224 | tf_op jit(solution)/shard_map/while/body/eval_jaxpr/ppermute | solution.py:119
  52.7 7.4 %collective-permute-start = (bf16[128,1024]{1,0:T(8,128)(2,1)S(1)}, bf16[128,1024]{1,0:T(8,128)(2,1)S(1)}, u32[]{:S(2)}, u32[]{:S(2)}) collective-permute-start(bf16[128,1024]{1,0:T(8,128)(2,1)S(1)} %copy.42), channel_id=1, source_target_pairs={{0,1},{1,4},{4,5},{5,8},{8,9},{9,12},{12,13},{13,14},{14,15},{15,1... | collective-permute-start | bytes 786440 | tf_op jit(solution)/shard_map/while/body/eval_jaxpr/ppermute | solution.py:119
  52.8 7.3 %collective-permute-start.1 = (bf16[128,1024]{1,0:T(8,128)(2,1)S(1)}, bf16[128,1024]{1,0:T(8,128)(2,1)S(1)}, u32[]{:S(2)}, u32[]{:S(2)}) collective-permute-start(bf16[128,1024]{1,0:T(8,128)(2,1)S(1)} %copy.43), channel_id=1, source_target_pairs={{1,0},{4,1},{5,4},{8,5},{9,8},{12,9},{13,12},{14,13},{15,14},{10,1... | collective-permute-start | bytes 786440 | tf_op jit(solution)/shard_map/while/body/eval_jaxpr/ppermute | solution.py:119
  54.7 5.3 %collective-permute-start.3 = (f32[256,128]{0,1:T(8,128)S(1)}, f32[256,128]{0,1:T(8,128)S(1)}, u32[]{:S(2)}, u32[]{:S(2)}) collective-permute-start(f32[256,128]{0,1:T(8,128)S(1)} %add.215), channel_id=1, source_target_pairs={{1,0},{4,1},{5,4},{8,5},{9,8},{12,9},{13,12},{14,13},{15,14},{10,1... | collective-permute-start | bytes 393224 | tf_op jit(solution)/shard_map/while/body/eval_jaxpr/ppermute | solution.py:119
  60.1 7.4 %collective-permute-start = (bf16[128,1024]{1,0:T(8,128)(2,1)S(1)}, bf16[128,1024]{1,0:T(8,128)(2,1)S(1)}, u32[]{:S(2)}, u32[]{:S(2)}) collective-permute-start(bf16[128,1024]{1,0:T(8,128)(2,1)S(1)} %copy.42), channel_id=1, source_target_pairs={{0,1},{1,4},{4,5},{5,8},{8,9},{9,12},{12,13},{13,14},{14,15},{15,1... | collective-permute-start | bytes 786440 | tf_op jit(solution)/shard_map/while/body/eval_jaxpr/ppermute | solution.py:119
  60.2 7.3 %collective-permute-start.1 = (bf16[128,1024]{1,0:T(8,128)(2,1)S(1)}, bf16[128,1024]{1,0:T(8,128)(2,1)S(1)}, u32[]{:S(2)}, u32[]{:S(2)}) collective-permute-start(bf16[128,1024]{1,0:T(8,128)(2,1)S(1)} %copy.43), channel_id=1, source_target_pairs={{1,0},{4,1},{5,4},{8,5},{9,8},{12,9},{13,12},{14,13},{15,14},{10,1... | collective-permute-start | bytes 786440 | tf_op jit(solution)/shard_map/while/body/eval_jaxpr/ppermute | solution.py:119
  62.2 5.3 %collective-permute-start.3 = (f32[256,128]{0,1:T(8,128)S(1)}, f32[256,128]{0,1:T(8,128)S(1)}, u32[]{:S(2)}, u32[]{:S(2)}) collective-permute-start(f32[256,128]{0,1:T(8,128)S(1)} %add.215), channel_id=1, source_target_pairs={{1,0},{4,1},{5,4},{8,5},{9,8},{12,9},{13,12},{14,13},{15,14},{10,1... | collective-permute-start | bytes 393224 | tf_op jit(solution)/shard_map/while/body/eval_jaxpr/ppermute | solution.py:119
  67.5 7.4 %collective-permute-start = (bf16[128,1024]{1,0:T(8,128)(2,1)S(1)}, bf16[128,1024]{1,0:T(8,128)(2,1)S(1)}, u32[]{:S(2)}, u32[]{:S(2)}) collective-permute-start(bf16[128,1024]{1,0:T(8,128)(2,1)S(1)} %copy.42), channel_id=1, source_target_pairs={{0,1},{1,4},{4,5},{5,8},{8,9},{9,12},{12,13},{13,14},{14,15},{15,1... | collective-permute-start | bytes 786440 | tf_op jit(solution)/shard_map/while/body/eval_jaxpr/ppermute | solution.py:119
  67.7 7.3 %collective-permute-start.1 = (bf16[128,1024]{1,0:T(8,128)(2,1)S(1)}, bf16[128,1024]{1,0:T(8,128)(2,1)S(1)}, u32[]{:S(2)}, u32[]{:S(2)}) collective-permute-start(bf16[128,1024]{1,0:T(8,128)(2,1)S(1)} %copy.43), channel_id=1, source_target_pairs={{1,0},{4,1},{5,4},{8,5},{9,8},{12,9},{13,12},{14,13},{15,14},{10,1... | collective-permute-start | bytes 786440 | tf_op jit(solution)/shard_map/while/body/eval_jaxpr/ppermute | solution.py:119
  69.6 5.3 %collective-permute-start.3 = (f32[256,128]{0,1:T(8,128)S(1)}, f32[256,128]{0,1:T(8,128)S(1)}, u32[]{:S(2)}, u32[]{:S(2)}) collective-permute-start(f32[256,128]{0,1:T(8,128)S(1)} %add.215), channel_id=1, source_target_pairs={{1,0},{4,1},{5,4},{8,5},{9,8},{12,9},{13,12},{14,13},{15,14},{10,1... | collective-permute-start | bytes 393224 | tf_op jit(solution)/shard_map/while/body/eval_jaxpr/ppermute | solution.py:119
  75.0 7.4 %collective-permute-start = (bf16[128,1024]{1,0:T(8,128)(2,1)S(1)}, bf16[128,1024]{1,0:T(8,128)(2,1)S(1)}, u32[]{:S(2)}, u32[]{:S(2)}) collective-permute-start(bf16[128,1024]{1,0:T(8,128)(2,1)S(1)} %copy.42), channel_id=1, source_target_pairs={{0,1},{1,4},{4,5},{5,8},{8,9},{9,12},{12,13},{13,14},{14,15},{15,1... | collective-permute-start | bytes 786440 | tf_op jit(solution)/shard_map/while/body/eval_jaxpr/ppermute | solution.py:119
  75.1 7.3 %collective-permute-start.1 = (bf16[128,1024]{1,0:T(8,128)(2,1)S(1)}, bf16[128,1024]{1,0:T(8,128)(2,1)S(1)}, u32[]{:S(2)}, u32[]{:S(2)}) collective-permute-start(bf16[128,1024]{1,0:T(8,128)(2,1)S(1)} %copy.43), channel_id=1, source_target_pairs={{1,0},{4,1},{5,4},{8,5},{9,8},{12,9},{13,12},{14,13},{15,14},{10,1... | collective-permute-start | bytes 786440 | tf_op jit(solution)/shard_map/while/body/eval_jaxpr/ppermute | solution.py:119
  77.0 5.3 %collective-permute-start.3 = (f32[256,128]{0,1:T(8,128)S(1)}, f32[256,128]{0,1:T(8,128)S(1)}, u32[]{:S(2)}, u32[]{:S(2)}) collective-permute-start(f32[256,128]{0,1:T(8,128)S(1)} %add.215), channel_id=1, source_target_pairs={{1,0},{4,1},{5,4},{8,5},{9,8},{12,9},{13,12},{14,13},{15,14},{10,1... | collective-permute-start | bytes 393224 | tf_op jit(solution)/shard_map/while/body/eval_jaxpr/ppermute | solution.py:119
  82.4 7.4 %collective-permute-start = (bf16[128,1024]{1,0:T(8,128)(2,1)S(1)}, bf16[128,1024]{1,0:T(8,128)(2,1)S(1)}, u32[]{:S(2)}, u32[]{:S(2)}) collective-permute-start(bf16[128,1024]{1,0:T(8,128)(2,1)S(1)} %copy.42), channel_id=1, source_target_pairs={{0,1},{1,4},{4,5},{5,8},{8,9},{9,12},{12,13},{13,14},{14,15},{15,1... | collective-permute-start | bytes 786440 | tf_op jit(solution)/shard_map/while/body/eval_jaxpr/ppermute | solution.py:119
  82.5 7.3 %collective-permute-start.1 = (bf16[128,1024]{1,0:T(8,128)(2,1)S(1)}, bf16[128,1024]{1,0:T(8,128)(2,1)S(1)}, u32[]{:S(2)}, u32[]{:S(2)}) collective-permute-start(bf16[128,1024]{1,0:T(8,128)(2,1)S(1)} %copy.43), channel_id=1, source_target_pairs={{1,0},{4,1},{5,4},{8,5},{9,8},{12,9},{13,12},{14,13},{15,14},{10,1... | collective-permute-start | bytes 786440 | tf_op jit(solution)/shard_map/while/body/eval_jaxpr/ppermute | solution.py:119
  83.1 5.1 %collective-permute-start.2 = (f32[256,128]{0,1:T(8,128)S(1)}, f32[256,128]{0,1:T(8,128)S(1)}, u32[]{:S(2)}, u32[]{:S(2)}) collective-permute-start(f32[256,128]{0,1:T(8,128)S(1)} %add.214), channel_id=1, source_target_pairs={{0,1},{1,4},{4,5},{5,8},{8,9},{9,12},{12,13},{13,14},{14,15},{15,1... | collective-permute-start | bytes 393224 | tf_op jit(solution)/shard_map/while/body/eval_jaxpr/ppermute | solution.py:119
  84.5 5.3 %collective-permute-start.3 = (f32[256,128]{0,1:T(8,128)S(1)}, f32[256,128]{0,1:T(8,128)S(1)}, u32[]{:S(2)}, u32[]{:S(2)}) collective-permute-start(f32[256,128]{0,1:T(8,128)S(1)} %add.215), channel_id=1, source_target_pairs={{1,0},{4,1},{5,4},{8,5},{9,8},{12,9},{13,12},{14,13},{15,14},{10,1... | collective-permute-start | bytes 393224 | tf_op jit(solution)/shard_map/while/body/eval_jaxpr/ppermute | solution.py:119
  89.8 7.4 %collective-permute-start = (bf16[128,1024]{1,0:T(8,128)(2,1)S(1)}, bf16[128,1024]{1,0:T(8,128)(2,1)S(1)}, u32[]{:S(2)}, u32[]{:S(2)}) collective-permute-start(bf16[128,1024]{1,0:T(8,128)(2,1)S(1)} %copy.42), channel_id=1, source_target_pairs={{0,1},{1,4},{4,5},{5,8},{8,9},{9,12},{12,13},{13,14},{14,15},{15,1... | collective-permute-start | bytes 786440 | tf_op jit(solution)/shard_map/while/body/eval_jaxpr/ppermute | solution.py:119
  90.0 7.3 %collective-permute-start.1 = (bf16[128,1024]{1,0:T(8,128)(2,1)S(1)}, bf16[128,1024]{1,0:T(8,128)(2,1)S(1)}, u32[]{:S(2)}, u32[]{:S(2)}) collective-permute-start(bf16[128,1024]{1,0:T(8,128)(2,1)S(1)} %copy.43), channel_id=1, source_target_pairs={{1,0},{4,1},{5,4},{8,5},{9,8},{12,9},{13,12},{14,13},{15,14},{10,1... | collective-permute-start | bytes 786440 | tf_op jit(solution)/shard_map/while/body/eval_jaxpr/ppermute | solution.py:119
  91.9 5.3 %collective-permute-start.3 = (f32[256,128]{0,1:T(8,128)S(1)}, f32[256,128]{0,1:T(8,128)S(1)}, u32[]{:S(2)}, u32[]{:S(2)}) collective-permute-start(f32[256,128]{0,1:T(8,128)S(1)} %add.215), channel_id=1, source_target_pairs={{1,0},{4,1},{5,4},{8,5},{9,8},{12,9},{13,12},{14,13},{15,14},{10,1... | collective-permute-start | bytes 393224 | tf_op jit(solution)/shard_map/while/body/eval_jaxpr/ppermute | solution.py:119
  97.3 7.4 %collective-permute-start = (bf16[128,1024]{1,0:T(8,128)(2,1)S(1)}, bf16[128,1024]{1,0:T(8,128)(2,1)S(1)}, u32[]{:S(2)}, u32[]{:S(2)}) collective-permute-start(bf16[128,1024]{1,0:T(8,128)(2,1)S(1)} %copy.42), channel_id=1, source_target_pairs={{0,1},{1,4},{4,5},{5,8},{8,9},{9,12},{12,13},{13,14},{14,15},{15,1... | collective-permute-start | bytes 786440 | tf_op jit(solution)/shard_map/while/body/eval_jaxpr/ppermute | solution.py:119
  97.4 7.3 %collective-permute-start.1 = (bf16[128,1024]{1,0:T(8,128)(2,1)S(1)}, bf16[128,1024]{1,0:T(8,128)(2,1)S(1)}, u32[]{:S(2)}, u32[]{:S(2)}) collective-permute-start(bf16[128,1024]{1,0:T(8,128)(2,1)S(1)} %copy.43), channel_id=1, source_target_pairs={{1,0},{4,1},{5,4},{8,5},{9,8},{12,9},{13,12},{14,13},{15,14},{10,1... | collective-permute-start | bytes 786440 | tf_op jit(solution)/shard_map/while/body/eval_jaxpr/ppermute | solution.py:119
  99.3 5.3 %collective-permute-start.3 = (f32[256,128]{0,1:T(8,128)S(1)}, f32[256,128]{0,1:T(8,128)S(1)}, u32[]{:S(2)}, u32[]{:S(2)}) collective-permute-start(f32[256,128]{0,1:T(8,128)S(1)} %add.215), channel_id=1, source_target_pairs={{1,0},{4,1},{5,4},{8,5},{9,8},{12,9},{13,12},{14,13},{15,14},{10,1... | collective-permute-start | bytes 393224 | tf_op jit(solution)/shard_map/while/body/eval_jaxpr/ppermute | solution.py:119
  104.7 7.4 %collective-permute-start = (bf16[128,1024]{1,0:T(8,128)(2,1)S(1)}, bf16[128,1024]{1,0:T(8,128)(2,1)S(1)}, u32[]{:S(2)}, u32[]{:S(2)}) collective-permute-start(bf16[128,1024]{1,0:T(8,128)(2,1)S(1)} %copy.42), channel_id=1, source_target_pairs={{0,1},{1,4},{4,5},{5,8},{8,9},{9,12},{12,13},{13,14},{14,15},{15,1... | collective-permute-start | bytes 786440 | tf_op jit(solution)/shard_map/while/body/eval_jaxpr/ppermute | solution.py:119
  104.8 7.3 %collective-permute-start.1 = (bf16[128,1024]{1,0:T(8,128)(2,1)S(1)}, bf16[128,1024]{1,0:T(8,128)(2,1)S(1)}, u32[]{:S(2)}, u32[]{:S(2)}) collective-permute-start(bf16[128,1024]{1,0:T(8,128)(2,1)S(1)} %copy.43), channel_id=1, source_target_pairs={{1,0},{4,1},{5,4},{8,5},{9,8},{12,9},{13,12},{14,13},{15,14},{10,1... | collective-permute-start | bytes 786440 | tf_op jit(solution)/shard_map/while/body/eval_jaxpr/ppermute | solution.py:119
  106.8 5.3 %collective-permute-start.3 = (f32[256,128]{0,1:T(8,128)S(1)}, f32[256,128]{0,1:T(8,128)S(1)}, u32[]{:S(2)}, u32[]{:S(2)}) collective-permute-start(f32[256,128]{0,1:T(8,128)S(1)} %add.215), channel_id=1, source_target_pairs={{1,0},{4,1},{5,4},{8,5},{9,8},{12,9},{13,12},{14,13},{15,14},{10,1... | collective-permute-start | bytes 393224 | tf_op jit(solution)/shard_map/while/body/eval_jaxpr/ppermute | solution.py:119
  112.1 7.4 %collective-permute-start = (bf16[128,1024]{1,0:T(8,128)(2,1)S(1)}, bf16[128,1024]{1,0:T(8,128)(2,1)S(1)}, u32[]{:S(2)}, u32[]{:S(2)}) collective-permute-start(bf16[128,1024]{1,0:T(8,128)(2,1)S(1)} %copy.42), channel_id=1, source_target_pairs={{0,1},{1,4},{4,5},{5,8},{8,9},{9,12},{12,13},{13,14},{14,15},{15,1... | collective-permute-start | bytes 786440 | tf_op jit(solution)/shard_map/while/body/eval_jaxpr/ppermute | solution.py:119
  112.3 7.3 %collective-permute-start.1 = (bf16[128,1024]{1,0:T(8,128)(2,1)S(1)}, bf16[128,1024]{1,0:T(8,128)(2,1)S(1)}, u32[]{:S(2)}, u32[]{:S(2)}) collective-permute-start(bf16[128,1024]{1,0:T(8,128)(2,1)S(1)} %copy.43), channel_id=1, source_target_pairs={{1,0},{4,1},{5,4},{8,5},{9,8},{12,9},{13,12},{14,13},{15,14},{10,1... | collective-permute-start | bytes 786440 | tf_op jit(solution)/shard_map/while/body/eval_jaxpr/ppermute | solution.py:119
  114.2 5.3 %collective-permute-start.3 = (f32[256,128]{0,1:T(8,128)S(1)}, f32[256,128]{0,1:T(8,128)S(1)}, u32[]{:S(2)}, u32[]{:S(2)}) collective-permute-start(f32[256,128]{0,1:T(8,128)S(1)} %add.215), channel_id=1, source_target_pairs={{1,0},{4,1},{5,4},{8,5},{9,8},{12,9},{13,12},{14,13},{15,14},{10,1... | collective-permute-start | bytes 393224 | tf_op jit(solution)/shard_map/while/body/eval_jaxpr/ppermute | solution.py:119
  119.6 5.2 %collective-permute-start.7 = (f32[256,128]{0,1:T(8,128)S(1)}, f32[256,128]{0,1:T(8,128)S(1)}, u32[]{:S(2)}, u32[]{:S(2)}) collective-permute-start(f32[256,128]{0,1:T(8,128)S(1)} %add.136), channel_id=1, source_target_pairs={{1,0},{4,1},{5,4},{8,5},{9,8},{12,9},{13,12},{14,13},{15,14},{10,1... | collective-permute-start | bytes 393224 | tf_op jit(solution)/shard_map/ppermute | solution.py:119
  151.5 5.9 %collective-permute-start.8 = (f32[16,128]{1,0:T(8,128)S(1)}, f32[16,128]{1,0:T(8,128)S(1)}, u32[]{:S(2)}, u32[]{:S(2)}) collective-permute-start(f32[16,128]{1,0:T(8,128)S(1)} %get-tuple-element.213), channel_id=1, source_target_pairs={{0,1},{1,4},{4,5},{5,8},{8,9},{9,12},{12,13},{13,14},{14,15},{15,1... | collective-permute-start | bytes 24584 | tf_op jit(solution)/shard_map/ppermute | solution.py:119
  (34 other events, 130.5 us)

commit v10 on v8

--- a/solution.py
+++ b/solution.py
@@ -21,9 +21,10 @@
     for level_index in range(4):
         factor = factor + jnp.where(exponents == level_index, 2.0 ** (level_index - 9), 0.0)
     scaled_codes = (
-        codes.reshape(points, blocks, columns // blocks).astype(jnp.float32) * factor[:, :, None]
+        codes.reshape(points, blocks, columns // blocks).astype(jnp.bfloat16)
+        * factor.astype(jnp.bfloat16)[:, :, None]
     )
-    return scaled_codes.reshape(points, columns).astype(jnp.bfloat16)
+    return scaled_codes.reshape(points, columns)
 
 
 def squares(points_bf):

time: 154 us -> 157 us (1.019)
    mul x2, local copies, waits for them, and re-layouts: 1.47 us -> 3.25 us  [dequantize(): codes.reshape(points, blocks, columns // blocks).astype(jnp.bfloat16)]
  transfers between devices with their start and end apart: 62 -> 62, of which waited for: 16 -> 16; matrix products, arithmetic and copies ran while one was open for 35% -> 38% of each run, Pallas kernels for 0% -> 0%
where the time goes in v10:
time: 157 us; the launch traced here: 156 us
  matrix products  47.6 us (30%)
  starting transfers between devices  45.8 us (29%)
  waiting for transfers between devices  24 us (15%)
  blocking collectives  20.8 us (13%)
  other arithmetic  9.58 us (6%)
  local copies, waits for them, and re-layouts  7.51 us (5%)
    dot_general x16, matrix products, kernel_block(): lax.dot_general(rhs_values, matern, (((0,), (1,)), ((), ())), preferred_e...  47.6 us
    ppermute x31, starting transfers between devices, send(): lax.ppermute(points_f, 'blk', forward)  28.3 us
    ppermute x31, waiting for transfers between devices, send(): lax.ppermute(points_b, 'blk', backward)  23.1 us
    all_to_all x1, blocking collectives, exchange_scatter(): pieces = lax.all_to_all(pieces, axis, 0, 0, tiled=False)  20.8 us
    ppermute x31, starting transfers between devices, send(): lax.ppermute(points_b, 'blk', backward)  17.6 us
    reduce_sum x17, other arithmetic, squares(): return jnp.sum(widened * widened, axis=1)  5.07 us
    mul x2, local copies, waits for them, and re-layouts, dequantize(): codes.reshape(points, blocks, columns // blocks).astype(jnp.bfloat16)  3.25 us
  transfers between devices with their start and end apart: 62, of which 16 were waited for; matrix products, arithmetic and copies ran while one was open for 38% of the time, Pallas kernels for 0%

profile of v10, /device:TPU:1, one launch (start us, length us, event | category | flops | bytes accessed | tf_op | source)
XLA Modules:
  0.0 156.4 jit_solution(4903519213891827660)
XLA Ops:
  3.4 2.6 %collective-permute-start.4 = (bf16[128,1024]{1,0:T(8,128)(2,1)}, bf16[128,1024]{1,0:T(8,128)(2,1)S(1)}, u32[]{:S(2)}, u32[]{:S(2)}) collective-permute-start(bf16[128,1024]{1,0:T(8,128)(2,1)} %bitcast.35), channel_id=1, source_target_pairs={{0,1},{1,4},{4,5},{5,8},{8,9},{9,12},{12,13},{13,14},{14,15},{15,1... | collective-permute-start | bytes 786440 | tf_op jit(solution)/shard_map/ppermute | solution.py:104
  9.2 2.9 %mul.102 = bf16[1024,8,128]{2,1,0:T(8,128)(2,1)S(1)} broadcast(bf16[1024,8]{1,0:T(8,128)(2,1)S(1)} %copy.11), dimensions={0,1} | broadcast | bytes 2113536 | tf_op jit(solution)/shard_map/mul | solution.py:24
  12.1 2.1 %multiply_reduce_fusion.1 = (f32[1024]{0:T(1024)S(1)}, bf16[1024,1024]{1,0:T(8,128)(2,1)}) fusion(bf16[128,8,8,128]{3,2,1,0:T(8,128)(2,1)S(1)} %bitcast.44, s32[1024,1024]{1,0:T(8,128)S(1)} %copy-done.1), kind=kLoop, calls=%fused_computation.20 | loop fusion | flops 5241856 | bytes 8392704 | tf_op jit(solution)/shard_map/reduce_sum | solution.py:32
  14.2 3.2 %fusion.22 = f32[256,256]{1,0:T(8,128)S(1)} fusion(bf16[1024,256]{1,0:T(8,128)(2,1)} %add_convert_fusion, bf16[1024,1024]{1,0:T(8,128)(2,1)} %get-tuple-element.266, f32[1024]{0:T(1024)S(1)} %get-tuple-element.265, f32[256]{0:T(256)S(1)} %multiply_reduce_fusion.3, bf16[32,8,8,128]{3,2,1,0:T(8,128)(2,1)S(1)} %bitcast.46, s32[256,1024]{1,0:T(8,128)S(1)} %copy-done), kind=kOutput, calls=%fused_computation.35 | convolution fusion | flops 674496512 | bytes 4461568 | tf_op jit(solution)/shard_map/dot_general | solution.py:43
  17.7 105.2 %while.22 = (s32[]{:T(128)}, bf16[128,1024]{1,0:T(8,128)(2,1)S(1)}, bf16[128,1024]{1,0:T(8,128)(2,1)S(1)}, f32[256,128]{0,1:T(8,128)S(1)}, f32[256,128]{0,1:T(8,...) while((s32[]{:T(128)}, bf16[128,1024]{1,0:T(8,128)(2,1)S(1)}, ...), condition=%wide.region_4.5_spmd, body=%wide.region_2.4_spmd.sunk | while | flops 674823936 | bytes 10492173 | solution.py:117
  21.8 3.0 %convolution_bitcast_fusion.2 = f32[256,256]{0,1:T(8,128)S(1)} fusion(bf16[1024,256]{1,0:T(8,128)(2,1)} %get-tuple-element.289, bf16[256,1024]{1,0:T(8,128)(2,1)S(1)} %constant_dynamic-update-slice_fusion.7, bf16[1024,1024]{1,0:T(8,128)(2,1)} %get-tuple-element.288, f32[1024]{0:T(1024)S(1)} %get-tuple-element.287, f32[256]{0:T(256)S(1)} %multiply_reduce_fusion.5), kind=kOutput, calls=%fused_computation.4.clone.1 | convolution fusion | flops 673972224 | bytes 3412992 | tf_op jit(solution)/shard_map/while/body/eval_jaxpr/dot_general | solution.py:43
  24.8 1.5 collective-permute-done.3
  27.1 1.3 collective-permute-start.2
  29.2 3.0 %convolution_bitcast_fusion.2 = f32[256,256]{0,1:T(8,128)S(1)} fusion(bf16[1024,256]{1,0:T(8,128)(2,1)} %get-tuple-element.289, bf16[256,1024]{1,0:T(8,128)(2,1)S(1)} %constant_dynamic-update-slice_fusion.7, bf16[1024,1024]{1,0:T(8,128)(2,1)} %get-tuple-element.288, f32[1024]{0:T(1024)S(1)} %get-tuple-element.287, f32[256]{0:T(256)S(1)} %multiply_reduce_fusion.5), kind=kOutput, calls=%fused_computation.4.clone.1 | convolution fusion | flops 673972224 | bytes 3412992 | tf_op jit(solution)/shard_map/while/body/eval_jaxpr/dot_general | solution.py:43
  32.3 1.5 collective-permute-done.3
  34.5 1.3 collective-permute-start.2
  36.7 3.0 %convolution_bitcast_fusion.2 = f32[256,256]{0,1:T(8,128)S(1)} fusion(bf16[1024,256]{1,0:T(8,128)(2,1)} %get-tuple-element.289, bf16[256,1024]{1,0:T(8,128)(2,1)S(1)} %constant_dynamic-update-slice_fusion.7, bf16[1024,1024]{1,0:T(8,128)(2,1)} %get-tuple-element.288, f32[1024]{0:T(1024)S(1)} %get-tuple-element.287, f32[256]{0:T(256)S(1)} %multiply_reduce_fusion.5), kind=kOutput, calls=%fused_computation.4.clone.1 | convolution fusion | flops 673972224 | bytes 3412992 | tf_op jit(solution)/shard_map/while/body/eval_jaxpr/dot_general | solution.py:43
  39.7 1.5 collective-permute-done.3
  41.9 1.3 collective-permute-start.2
  44.1 3.0 %convolution_bitcast_fusion.2 = f32[256,256]{0,1:T(8,128)S(1)} fusion(bf16[1024,256]{1,0:T(8,128)(2,1)} %get-tuple-element.289, bf16[256,1024]{1,0:T(8,128)(2,1)S(1)} %constant_dynamic-update-slice_fusion.7, bf16[1024,1024]{1,0:T(8,128)(2,1)} %get-tuple-element.288, f32[1024]{0:T(1024)S(1)} %get-tuple-element.287, f32[256]{0:T(256)S(1)} %multiply_reduce_fusion.5), kind=kOutput, calls=%fused_computation.4.clone.1 | convolution fusion | flops 673972224 | bytes 3412992 | tf_op jit(solution)/shard_map/while/body/eval_jaxpr/dot_general | solution.py:43
  47.1 1.5 collective-permute-done.3
  49.4 1.3 collective-permute-start.2
  51.5 3.0 %convolution_bitcast_fusion.2 = f32[256,256]{0,1:T(8,128)S(1)} fusion(bf16[1024,256]{1,0:T(8,128)(2,1)} %get-tuple-element.289, bf16[256,1024]{1,0:T(8,128)(2,1)S(1)} %constant_dynamic-update-slice_fusion.7, bf16[1024,1024]{1,0:T(8,128)(2,1)} %get-tuple-element.288, f32[1024]{0:T(1024)S(1)} %get-tuple-element.287, f32[256]{0:T(256)S(1)} %multiply_reduce_fusion.5), kind=kOutput, calls=%fused_computation.4.clone.1 | convolution fusion | flops 673972224 | bytes 3412992 | tf_op jit(solution)/shard_map/while/body/eval_jaxpr/dot_general | solution.py:43
  54.6 1.5 collective-permute-done.3
  56.8 1.3 collective-permute-start.2
  59.0 3.0 %convolution_bitcast_fusion.2 = f32[256,256]{0,1:T(8,128)S(1)} fusion(bf16[1024,256]{1,0:T(8,128)(2,1)} %get-tuple-element.289, bf16[256,1024]{1,0:T(8,128)(2,1)S(1)} %constant_dynamic-update-slice_fusion.7, bf16[1024,1024]{1,0:T(8,128)(2,1)} %get-tuple-element.288, f32[1024]{0:T(1024)S(1)} %get-tuple-element.287, f32[256]{0:T(256)S(1)} %multiply_reduce_fusion.5), kind=kOutput, calls=%fused_computation.4.clone.1 | convolution fusion | flops 673972224 | bytes 3412992 | tf_op jit(solution)/shard_map/while/body/eval_jaxpr/dot_general | solution.py:43
  62.0 1.5 collective-permute-done.3
  64.2 1.3 collective-permute-start.2
  66.4 3.0 %convolution_bitcast_fusion.2 = f32[256,256]{0,1:T(8,128)S(1)} fusion(bf16[1024,256]{1,0:T(8,128)(2,1)} %get-tuple-element.289, bf16[256,1024]{1,0:T(8,128)(2,1)S(1)} %constant_dynamic-update-slice_fusion.7, bf16[1024,1024]{1,0:T(8,128)(2,1)} %get-tuple-element.288, f32[1024]{0:T(1024)S(1)} %get-tuple-element.287, f32[256]{0:T(256)S(1)} %multiply_reduce_fusion.5), kind=kOutput, calls=%fused_computation.4.clone.1 | convolution fusion | flops 673972224 | bytes 3412992 | tf_op jit(solution)/shard_map/while/body/eval_jaxpr/dot_general | solution.py:43
  69.4 1.5 collective-permute-done.3
  71.6 1.3 collective-permute-start.2
  73.8 3.0 %convolution_bitcast_fusion.2 = f32[256,256]{0,1:T(8,128)S(1)} fusion(bf16[1024,256]{1,0:T(8,128)(2,1)} %get-tuple-element.289, bf16[256,1024]{1,0:T(8,128)(2,1)S(1)} %constant_dynamic-update-slice_fusion.7, bf16[1024,1024]{1,0:T(8,128)(2,1)} %get-tuple-element.288, f32[1024]{0:T(1024)S(1)} %get-tuple-element.287, f32[256]{0:T(256)S(1)} %multiply_reduce_fusion.5), kind=kOutput, calls=%fused_computation.4.clone.1 | convolution fusion | flops 673972224 | bytes 3412992 | tf_op jit(solution)/shard_map/while/body/eval_jaxpr/dot_general | solution.py:43
  76.8 1.5 collective-permute-done.3
  79.1 1.3 collective-permute-start.2
  81.2 3.0 %convolution_bitcast_fusion.2 = f32[256,256]{0,1:T(8,128)S(1)} fusion(bf16[1024,256]{1,0:T(8,128)(2,1)} %get-tuple-element.289, bf16[256,1024]{1,0:T(8,128)(2,1)S(1)} %constant_dynamic-update-slice_fusion.7, bf16[1024,1024]{1,0:T(8,128)(2,1)} %get-tuple-element.288, f32[1024]{0:T(1024)S(1)} %get-tuple-element.287, f32[256]{0:T(256)S(1)} %multiply_reduce_fusion.5), kind=kOutput, calls=%fused_computation.4.clone.1 | convolution fusion | flops 673972224 | bytes 3412992 | tf_op jit(solution)/shard_map/while/body/eval_jaxpr/dot_general | solution.py:43
  84.3 1.5 collective-permute-done.3
  86.5 1.3 collective-permute-start.2
  88.7 3.0 %convolution_bitcast_fusion.2 = f32[256,256]{0,1:T(8,128)S(1)} fusion(bf16[1024,256]{1,0:T(8,128)(2,1)} %get-tuple-element.289, bf16[256,1024]{1,0:T(8,128)(2,1)S(1)} %constant_dynamic-update-slice_fusion.7, bf16[1024,1024]{1,0:T(8,128)(2,1)} %get-tuple-element.288, f32[1024]{0:T(1024)S(1)} %get-tuple-element.287, f32[256]{0:T(256)S(1)} %multiply_reduce_fusion.5), kind=kOutput, calls=%fused_computation.4.clone.1 | convolution fusion | flops 673972224 | bytes 3412992 | tf_op jit(solution)/shard_map/while/body/eval_jaxpr/dot_general | solution.py:43
  91.7 1.5 collective-permute-done.3
  93.9 1.3 collective-permute-start.2
  96.1 3.0 %convolution_bitcast_fusion.2 = f32[256,256]{0,1:T(8,128)S(1)} fusion(bf16[1024,256]{1,0:T(8,128)(2,1)} %get-tuple-element.289, bf16[256,1024]{1,0:T(8,128)(2,1)S(1)} %constant_dynamic-update-slice_fusion.7, bf16[1024,1024]{1,0:T(8,128)(2,1)} %get-tuple-element.288, f32[1024]{0:T(1024)S(1)} %get-tuple-element.287, f32[256]{0:T(256)S(1)} %multiply_reduce_fusion.5), kind=kOutput, calls=%fused_computation.4.clone.1 | convolution fusion | flops 673972224 | bytes 3412992 | tf_op jit(solution)/shard_map/while/body/eval_jaxpr/dot_general | solution.py:43
  99.1 1.5 collective-permute-done.3
  103.5 3.0 %convolution_bitcast_fusion.2 = f32[256,256]{0,1:T(8,128)S(1)} fusion(bf16[1024,256]{1,0:T(8,128)(2,1)} %get-tuple-element.289, bf16[256,1024]{1,0:T(8,128)(2,1)S(1)} %constant_dynamic-update-slice_fusion.7, bf16[1024,1024]{1,0:T(8,128)(2,1)} %get-tuple-element.288, f32[1024]{0:T(1024)S(1)} %get-tuple-element.287, f32[256]{0:T(256)S(1)} %multiply_reduce_fusion.5), kind=kOutput, calls=%fused_computation.4.clone.1 | convolution fusion | flops 673972224 | bytes 3412992 | tf_op jit(solution)/shard_map/while/body/eval_jaxpr/dot_general | solution.py:43
  106.6 1.5 collective-permute-done.3
  111.0 3.0 %convolution_bitcast_fusion.2 = f32[256,256]{0,1:T(8,128)S(1)} fusion(bf16[1024,256]{1,0:T(8,128)(2,1)} %get-tuple-element.289, bf16[256,1024]{1,0:T(8,128)(2,1)S(1)} %constant_dynamic-update-slice_fusion.7, bf16[1024,1024]{1,0:T(8,128)(2,1)} %get-tuple-element.288, f32[1024]{0:T(1024)S(1)} %get-tuple-element.287, f32[256]{0:T(256)S(1)} %multiply_reduce_fusion.5), kind=kOutput, calls=%fused_computation.4.clone.1 | convolution fusion | flops 673972224 | bytes 3412992 | tf_op jit(solution)/shard_map/while/body/eval_jaxpr/dot_general | solution.py:43
  114.0 1.5 collective-permute-done.3
  118.4 3.0 %convolution_bitcast_fusion.2 = f32[256,256]{0,1:T(8,128)S(1)} fusion(bf16[1024,256]{1,0:T(8,128)(2,1)} %get-tuple-element.289, bf16[256,1024]{1,0:T(8,128)(2,1)S(1)} %constant_dynamic-update-slice_fusion.7, bf16[1024,1024]{1,0:T(8,128)(2,1)} %get-tuple-element.288, f32[1024]{0:T(1024)S(1)} %get-tuple-element.287, f32[256]{0:T(256)S(1)} %multiply_reduce_fusion.5), kind=kOutput, calls=%fused_computation.4.clone.1 | convolution fusion | flops 673972224 | bytes 3412992 | tf_op jit(solution)/shard_map/while/body/eval_jaxpr/dot_general | solution.py:43
  121.4 1.5 collective-permute-done.3
  124.3 1.3 collective-permute-start.6
  125.6 2.5 %fusion.20 = f32[256,256]{0,1:T(8,128)S(1)} fusion(bf16[1024,256]{1,0:T(8,128)(2,1)} %add_convert_fusion, bf16[256,1024]{1,0:T(8,128)(2,1)} %copy-done.3, bf16[1024,1024]{1,0:T(8,128)(2,1)S(1)} %copy-done.2, f32[256]{0:T(256)S(1)} %multiply_reduce_fusion.2, f32[1024]{0:T(1024)S(1)} %get-tuple-element.310), kind=kOutput, calls=%fused_computation.31 | convolution fusion | flops 673972224 | bytes 3412992 | tf_op jit(solution)/shard_map/dot_general | solution.py:43
  128.3 20.8 %all_to_all.5 = f32[16,16,256]{2,1,0:T(8,128)S(1)} all-to-all(f32[16,16,256]{2,1,0:T(8,128)S(1)} %bitcast.47), channel_id=1, replica_groups=mesh['grp'=16,'blk'=16] {'grp'}, dimensions={0} | all-to-all | bytes 524288 | tf_op jit(solution)/shard_map/all_to_all | solution.py:52
  149.2 3.5 %collective-permute-start.8 = (f32[16,128]{1,0:T(8,128)S(1)}, f32[16,128]{1,0:T(8,128)S(1)}, u32[]{:S(2)}, u32[]{:S(2)}) collective-permute-start(f32[16,128]{1,0:T(8,128)S(1)} %get-tuple-element.191), channel_id=1, source_target_pairs={{0,1},{1,4},{4,5},{5,8},{8,9},{9,12},{12,13},{13,14},{14,15},{15,1... | collective-permute-start | bytes 24584 | tf_op jit(solution)/shard_map/ppermute | solution.py:104
  153.5 2.3 %collective-permute-done.9 = f32[16,128]{1,0:T(8,128)S(1)} collective-permute-done((f32[16,128]{1,0:T(8,128)S(1)}, f32[16,128]{1,0:T(8,128)S(1)}, u32[]{:S(2)}, u32[]{:S(2)}) %collective-permute-start.9) | collective-permute-done | bytes 8224 | tf_op jit(solution)/shard_map/ppermute | solution.py:104
  (249 shorter events, 38.1 us)
Async XLA Ops:
  3.4 14.2 %collective-permute-start.4 = (bf16[128,1024]{1,0:T(8,128)(2,1)}, bf16[128,1024]{1,0:T(8,128)(2,1)S(1)}, u32[]{:S(2)}, u32[]{:S(2)}) collective-permute-start(bf16[128,1024]{1,0:T(8,128)(2,1)} %bitcast.35), channel_id=1, source_target_pairs={{0,1},{1,4},{4,5},{5,8},{8,9},{9,12},{12,13},{13,14},{14,15},{15,1... | collective-permute-start | bytes 786440 | tf_op jit(solution)/shard_map/ppermute | solution.py:104
  6.8 10.8 %collective-permute-start.5 = (bf16[128,1024]{1,0:T(8,128)(2,1)}, bf16[128,1024]{1,0:T(8,128)(2,1)S(1)}, u32[]{:S(2)}, u32[]{:S(2)}) collective-permute-start(bf16[128,1024]{1,0:T(8,128)(2,1)} %bitcast.34), channel_id=1, source_target_pairs={{1,0},{4,1},{5,4},{8,5},{9,8},{12,9},{13,12},{14,13},{15,14},{10,1... | collective-permute-start | bytes 786440 | tf_op jit(solution)/shard_map/ppermute | solution.py:104
  17.7 8.6 %collective-permute-start = (bf16[128,1024]{1,0:T(8,128)(2,1)S(1)}, bf16[128,1024]{1,0:T(8,128)(2,1)S(1)}, u32[]{:S(2)}, u32[]{:S(2)}) collective-permute-start(bf16[128,1024]{1,0:T(8,128)(2,1)S(1)} %copy.40), channel_id=1, source_target_pairs={{0,1},{1,4},{4,5},{5,8},{8,9},{9,12},{12,13},{13,14},{14,15},{15,1... | collective-permute-start | bytes 786440 | tf_op jit(solution)/shard_map/while/body/eval_jaxpr/ppermute | solution.py:104
  18.9 7.4 %collective-permute-start.1 = (bf16[128,1024]{1,0:T(8,128)(2,1)S(1)}, bf16[128,1024]{1,0:T(8,128)(2,1)S(1)}, u32[]{:S(2)}, u32[]{:S(2)}) collective-permute-start(bf16[128,1024]{1,0:T(8,128)(2,1)S(1)} %copy.41), channel_id=1, source_target_pairs={{1,0},{4,1},{5,4},{8,5},{9,8},{12,9},{13,12},{14,13},{15,14},{10,1... | collective-permute-start | bytes 786440 | tf_op jit(solution)/shard_map/while/body/eval_jaxpr/ppermute | solution.py:104
  20.9 5.5 %collective-permute-start.3 = (f32[256,128]{0,1:T(8,128)S(1)}, f32[256,128]{0,1:T(8,128)S(1)}, u32[]{:S(2)}, u32[]{:S(2)}) collective-permute-start(f32[256,128]{0,1:T(8,128)S(1)} %add.215), channel_id=1, source_target_pairs={{1,0},{4,1},{5,4},{8,5},{9,8},{12,9},{13,12},{14,13},{15,14},{10,1... | collective-permute-start | bytes 393224 | tf_op jit(solution)/shard_map/while/body/eval_jaxpr/ppermute | solution.py:104
  26.4 7.4 %collective-permute-start = (bf16[128,1024]{1,0:T(8,128)(2,1)S(1)}, bf16[128,1024]{1,0:T(8,128)(2,1)S(1)}, u32[]{:S(2)}, u32[]{:S(2)}) collective-permute-start(bf16[128,1024]{1,0:T(8,128)(2,1)S(1)} %copy.40), channel_id=1, source_target_pairs={{0,1},{1,4},{4,5},{5,8},{8,9},{9,12},{12,13},{13,14},{14,15},{15,1... | collective-permute-start | bytes 786440 | tf_op jit(solution)/shard_map/while/body/eval_jaxpr/ppermute | solution.py:104
  26.5 7.3 %collective-permute-start.1 = (bf16[128,1024]{1,0:T(8,128)(2,1)S(1)}, bf16[128,1024]{1,0:T(8,128)(2,1)S(1)}, u32[]{:S(2)}, u32[]{:S(2)}) collective-permute-start(bf16[128,1024]{1,0:T(8,128)(2,1)S(1)} %copy.41), channel_id=1, source_target_pairs={{1,0},{4,1},{5,4},{8,5},{9,8},{12,9},{13,12},{14,13},{15,14},{10,1... | collective-permute-start | bytes 786440 | tf_op jit(solution)/shard_map/while/body/eval_jaxpr/ppermute | solution.py:104
  28.4 5.3 %collective-permute-start.3 = (f32[256,128]{0,1:T(8,128)S(1)}, f32[256,128]{0,1:T(8,128)S(1)}, u32[]{:S(2)}, u32[]{:S(2)}) collective-permute-start(f32[256,128]{0,1:T(8,128)S(1)} %add.215), channel_id=1, source_target_pairs={{1,0},{4,1},{5,4},{8,5},{9,8},{12,9},{13,12},{14,13},{15,14},{10,1... | collective-permute-start | bytes 393224 | tf_op jit(solution)/shard_map/while/body/eval_jaxpr/ppermute | solution.py:104
  33.8 7.4 %collective-permute-start = (bf16[128,1024]{1,0:T(8,128)(2,1)S(1)}, bf16[128,1024]{1,0:T(8,128)(2,1)S(1)}, u32[]{:S(2)}, u32[]{:S(2)}) collective-permute-start(bf16[128,1024]{1,0:T(8,128)(2,1)S(1)} %copy.40), channel_id=1, source_target_pairs={{0,1},{1,4},{4,5},{5,8},{8,9},{9,12},{12,13},{13,14},{14,15},{15,1... | collective-permute-start | bytes 786440 | tf_op jit(solution)/shard_map/while/body/eval_jaxpr/ppermute | solution.py:104
  33.9 7.3 %collective-permute-start.1 = (bf16[128,1024]{1,0:T(8,128)(2,1)S(1)}, bf16[128,1024]{1,0:T(8,128)(2,1)S(1)}, u32[]{:S(2)}, u32[]{:S(2)}) collective-permute-start(bf16[128,1024]{1,0:T(8,128)(2,1)S(1)} %copy.41), channel_id=1, source_target_pairs={{1,0},{4,1},{5,4},{8,5},{9,8},{12,9},{13,12},{14,13},{15,14},{10,1... | collective-permute-start | bytes 786440 | tf_op jit(solution)/shard_map/while/body/eval_jaxpr/ppermute | solution.py:104
  35.9 5.3 %collective-permute-start.3 = (f32[256,128]{0,1:T(8,128)S(1)}, f32[256,128]{0,1:T(8,128)S(1)}, u32[]{:S(2)}, u32[]{:S(2)}) collective-permute-start(f32[256,128]{0,1:T(8,128)S(1)} %add.215), channel_id=1, source_target_pairs={{1,0},{4,1},{5,4},{8,5},{9,8},{12,9},{13,12},{14,13},{15,14},{10,1... | collective-permute-start | bytes 393224 | tf_op jit(solution)/shard_map/while/body/eval_jaxpr/ppermute | solution.py:104
  41.2 7.4 %collective-permute-start = (bf16[128,1024]{1,0:T(8,128)(2,1)S(1)}, bf16[128,1024]{1,0:T(8,128)(2,1)S(1)}, u32[]{:S(2)}, u32[]{:S(2)}) collective-permute-start(bf16[128,1024]{1,0:T(8,128)(2,1)S(1)} %copy.40), channel_id=1, source_target_pairs={{0,1},{1,4},{4,5},{5,8},{8,9},{9,12},{12,13},{13,14},{14,15},{15,1... | collective-permute-start | bytes 786440 | tf_op jit(solution)/shard_map/while/body/eval_jaxpr/ppermute | solution.py:104
  41.3 7.3 %collective-permute-start.1 = (bf16[128,1024]{1,0:T(8,128)(2,1)S(1)}, bf16[128,1024]{1,0:T(8,128)(2,1)S(1)}, u32[]{:S(2)}, u32[]{:S(2)}) collective-permute-start(bf16[128,1024]{1,0:T(8,128)(2,1)S(1)} %copy.41), channel_id=1, source_target_pairs={{1,0},{4,1},{5,4},{8,5},{9,8},{12,9},{13,12},{14,13},{15,14},{10,1... | collective-permute-start | bytes 786440 | tf_op jit(solution)/shard_map/while/body/eval_jaxpr/ppermute | solution.py:104
  43.3 5.3 %collective-permute-start.3 = (f32[256,128]{0,1:T(8,128)S(1)}, f32[256,128]{0,1:T(8,128)S(1)}, u32[]{:S(2)}, u32[]{:S(2)}) collective-permute-start(f32[256,128]{0,1:T(8,128)S(1)} %add.215), channel_id=1, source_target_pairs={{1,0},{4,1},{5,4},{8,5},{9,8},{12,9},{13,12},{14,13},{15,14},{10,1... | collective-permute-start | bytes 393224 | tf_op jit(solution)/shard_map/while/body/eval_jaxpr/ppermute | solution.py:104
  48.6 7.4 %collective-permute-start = (bf16[128,1024]{1,0:T(8,128)(2,1)S(1)}, bf16[128,1024]{1,0:T(8,128)(2,1)S(1)}, u32[]{:S(2)}, u32[]{:S(2)}) collective-permute-start(bf16[128,1024]{1,0:T(8,128)(2,1)S(1)} %copy.40), channel_id=1, source_target_pairs={{0,1},{1,4},{4,5},{5,8},{8,9},{9,12},{12,13},{13,14},{14,15},{15,1... | collective-permute-start | bytes 786440 | tf_op jit(solution)/shard_map/while/body/eval_jaxpr/ppermute | solution.py:104
  48.8 7.3 %collective-permute-start.1 = (bf16[128,1024]{1,0:T(8,128)(2,1)S(1)}, bf16[128,1024]{1,0:T(8,128)(2,1)S(1)}, u32[]{:S(2)}, u32[]{:S(2)}) collective-permute-start(bf16[128,1024]{1,0:T(8,128)(2,1)S(1)} %copy.41), channel_id=1, source_target_pairs={{1,0},{4,1},{5,4},{8,5},{9,8},{12,9},{13,12},{14,13},{15,14},{10,1... | collective-permute-start | bytes 786440 | tf_op jit(solution)/shard_map/while/body/eval_jaxpr/ppermute | solution.py:104
  50.7 5.3 %collective-permute-start.3 = (f32[256,128]{0,1:T(8,128)S(1)}, f32[256,128]{0,1:T(8,128)S(1)}, u32[]{:S(2)}, u32[]{:S(2)}) collective-permute-start(f32[256,128]{0,1:T(8,128)S(1)} %add.215), channel_id=1, source_target_pairs={{1,0},{4,1},{5,4},{8,5},{9,8},{12,9},{13,12},{14,13},{15,14},{10,1... | collective-permute-start | bytes 393224 | tf_op jit(solution)/shard_map/while/body/eval_jaxpr/ppermute | solution.py:104
  56.1 7.4 %collective-permute-start = (bf16[128,1024]{1,0:T(8,128)(2,1)S(1)}, bf16[128,1024]{1,0:T(8,128)(2,1)S(1)}, u32[]{:S(2)}, u32[]{:S(2)}) collective-permute-start(bf16[128,1024]{1,0:T(8,128)(2,1)S(1)} %copy.40), channel_id=1, source_target_pairs={{0,1},{1,4},{4,5},{5,8},{8,9},{9,12},{12,13},{13,14},{14,15},{15,1... | collective-permute-start | bytes 786440 | tf_op jit(solution)/shard_map/while/body/eval_jaxpr/ppermute | solution.py:104
  56.2 7.3 %collective-permute-start.1 = (bf16[128,1024]{1,0:T(8,128)(2,1)S(1)}, bf16[128,1024]{1,0:T(8,128)(2,1)S(1)}, u32[]{:S(2)}, u32[]{:S(2)}) collective-permute-start(bf16[128,1024]{1,0:T(8,128)(2,1)S(1)} %copy.41), channel_id=1, source_target_pairs={{1,0},{4,1},{5,4},{8,5},{9,8},{12,9},{13,12},{14,13},{15,14},{10,1... | collective-permute-start | bytes 786440 | tf_op jit(solution)/shard_map/while/body/eval_jaxpr/ppermute | solution.py:104
  58.1 5.3 %collective-permute-start.3 = (f32[256,128]{0,1:T(8,128)S(1)}, f32[256,128]{0,1:T(8,128)S(1)}, u32[]{:S(2)}, u32[]{:S(2)}) collective-permute-start(f32[256,128]{0,1:T(8,128)S(1)} %add.215), channel_id=1, source_target_pairs={{1,0},{4,1},{5,4},{8,5},{9,8},{12,9},{13,12},{14,13},{15,14},{10,1... | collective-permute-start | bytes 393224 | tf_op jit(solution)/shard_map/while/body/eval_jaxpr/ppermute | solution.py:104
  63.5 7.4 %collective-permute-start = (bf16[128,1024]{1,0:T(8,128)(2,1)S(1)}, bf16[128,1024]{1,0:T(8,128)(2,1)S(1)}, u32[]{:S(2)}, u32[]{:S(2)}) collective-permute-start(bf16[128,1024]{1,0:T(8,128)(2,1)S(1)} %copy.40), channel_id=1, source_target_pairs={{0,1},{1,4},{4,5},{5,8},{8,9},{9,12},{12,13},{13,14},{14,15},{15,1... | collective-permute-start | bytes 786440 | tf_op jit(solution)/shard_map/while/body/eval_jaxpr/ppermute | solution.py:104
  63.6 7.3 %collective-permute-start.1 = (bf16[128,1024]{1,0:T(8,128)(2,1)S(1)}, bf16[128,1024]{1,0:T(8,128)(2,1)S(1)}, u32[]{:S(2)}, u32[]{:S(2)}) collective-permute-start(bf16[128,1024]{1,0:T(8,128)(2,1)S(1)} %copy.41), channel_id=1, source_target_pairs={{1,0},{4,1},{5,4},{8,5},{9,8},{12,9},{13,12},{14,13},{15,14},{10,1... | collective-permute-start | bytes 786440 | tf_op jit(solution)/shard_map/while/body/eval_jaxpr/ppermute | solution.py:104
  64.2 5.2 %collective-permute-start.2 = (f32[256,128]{0,1:T(8,128)S(1)}, f32[256,128]{0,1:T(8,128)S(1)}, u32[]{:S(2)}, u32[]{:S(2)}) collective-permute-start(f32[256,128]{0,1:T(8,128)S(1)} %add.214), channel_id=1, source_target_pairs={{0,1},{1,4},{4,5},{5,8},{8,9},{9,12},{12,13},{13,14},{14,15},{15,1... | collective-permute-start | bytes 393224 | tf_op jit(solution)/shard_map/while/body/eval_jaxpr/ppermute | solution.py:104
  65.6 5.3 %collective-permute-start.3 = (f32[256,128]{0,1:T(8,128)S(1)}, f32[256,128]{0,1:T(8,128)S(1)}, u32[]{:S(2)}, u32[]{:S(2)}) collective-permute-start(f32[256,128]{0,1:T(8,128)S(1)} %add.215), channel_id=1, source_target_pairs={{1,0},{4,1},{5,4},{8,5},{9,8},{12,9},{13,12},{14,13},{15,14},{10,1... | collective-permute-start | bytes 393224 | tf_op jit(solution)/shard_map/while/body/eval_jaxpr/ppermute | solution.py:104
  70.9 7.4 %collective-permute-start = (bf16[128,1024]{1,0:T(8,128)(2,1)S(1)}, bf16[128,1024]{1,0:T(8,128)(2,1)S(1)}, u32[]{:S(2)}, u32[]{:S(2)}) collective-permute-start(bf16[128,1024]{1,0:T(8,128)(2,1)S(1)} %copy.40), channel_id=1, source_target_pairs={{0,1},{1,4},{4,5},{5,8},{8,9},{9,12},{12,13},{13,14},{14,15},{15,1... | collective-permute-start | bytes 786440 | tf_op jit(solution)/shard_map/while/body/eval_jaxpr/ppermute | solution.py:104
  71.1 7.3 %collective-permute-start.1 = (bf16[128,1024]{1,0:T(8,128)(2,1)S(1)}, bf16[128,1024]{1,0:T(8,128)(2,1)S(1)}, u32[]{:S(2)}, u32[]{:S(2)}) collective-permute-start(bf16[128,1024]{1,0:T(8,128)(2,1)S(1)} %copy.41), channel_id=1, source_target_pairs={{1,0},{4,1},{5,4},{8,5},{9,8},{12,9},{13,12},{14,13},{15,14},{10,1... | collective-permute-start | bytes 786440 | tf_op jit(solution)/shard_map/while/body/eval_jaxpr/ppermute | solution.py:104
  73.0 5.3 %collective-permute-start.3 = (f32[256,128]{0,1:T(8,128)S(1)}, f32[256,128]{0,1:T(8,128)S(1)}, u32[]{:S(2)}, u32[]{:S(2)}) collective-permute-start(f32[256,128]{0,1:T(8,128)S(1)} %add.215), channel_id=1, source_target_pairs={{1,0},{4,1},{5,4},{8,5},{9,8},{12,9},{13,12},{14,13},{15,14},{10,1... | collective-permute-start | bytes 393224 | tf_op jit(solution)/shard_map/while/body/eval_jaxpr/ppermute | solution.py:104
  78.4 7.4 %collective-permute-start = (bf16[128,1024]{1,0:T(8,128)(2,1)S(1)}, bf16[128,1024]{1,0:T(8,128)(2,1)S(1)}, u32[]{:S(2)}, u32[]{:S(2)}) collective-permute-start(bf16[128,1024]{1,0:T(8,128)(2,1)S(1)} %copy.40), channel_id=1, source_target_pairs={{0,1},{1,4},{4,5},{5,8},{8,9},{9,12},{12,13},{13,14},{14,15},{15,1... | collective-permute-start | bytes 786440 | tf_op jit(solution)/shard_map/while/body/eval_jaxpr/ppermute | solution.py:104
  78.5 7.3 %collective-permute-start.1 = (bf16[128,1024]{1,0:T(8,128)(2,1)S(1)}, bf16[128,1024]{1,0:T(8,128)(2,1)S(1)}, u32[]{:S(2)}, u32[]{:S(2)}) collective-permute-start(bf16[128,1024]{1,0:T(8,128)(2,1)S(1)} %copy.41), channel_id=1, source_target_pairs={{1,0},{4,1},{5,4},{8,5},{9,8},{12,9},{13,12},{14,13},{15,14},{10,1... | collective-permute-start | bytes 786440 | tf_op jit(solution)/shard_map/while/body/eval_jaxpr/ppermute | solution.py:104
  79.1 5.2 %collective-permute-start.2 = (f32[256,128]{0,1:T(8,128)S(1)}, f32[256,128]{0,1:T(8,128)S(1)}, u32[]{:S(2)}, u32[]{:S(2)}) collective-permute-start(f32[256,128]{0,1:T(8,128)S(1)} %add.214), channel_id=1, source_target_pairs={{0,1},{1,4},{4,5},{5,8},{8,9},{9,12},{12,13},{13,14},{14,15},{15,1... | collective-permute-start | bytes 393224 | tf_op jit(solution)/shard_map/while/body/eval_jaxpr/ppermute | solution.py:104
  80.4 5.3 %collective-permute-start.3 = (f32[256,128]{0,1:T(8,128)S(1)}, f32[256,128]{0,1:T(8,128)S(1)}, u32[]{:S(2)}, u32[]{:S(2)}) collective-permute-start(f32[256,128]{0,1:T(8,128)S(1)} %add.215), channel_id=1, source_target_pairs={{1,0},{4,1},{5,4},{8,5},{9,8},{12,9},{13,12},{14,13},{15,14},{10,1... | collective-permute-start | bytes 393224 | tf_op jit(solution)/shard_map/while/body/eval_jaxpr/ppermute | solution.py:104
  85.8 7.4 %collective-permute-start = (bf16[128,1024]{1,0:T(8,128)(2,1)S(1)}, bf16[128,1024]{1,0:T(8,128)(2,1)S(1)}, u32[]{:S(2)}, u32[]{:S(2)}) collective-permute-start(bf16[128,1024]{1,0:T(8,128)(2,1)S(1)} %copy.40), channel_id=1, source_target_pairs={{0,1},{1,4},{4,5},{5,8},{8,9},{9,12},{12,13},{13,14},{14,15},{15,1... | collective-permute-start | bytes 786440 | tf_op jit(solution)/shard_map/while/body/eval_jaxpr/ppermute | solution.py:104
  85.9 7.3 %collective-permute-start.1 = (bf16[128,1024]{1,0:T(8,128)(2,1)S(1)}, bf16[128,1024]{1,0:T(8,128)(2,1)S(1)}, u32[]{:S(2)}, u32[]{:S(2)}) collective-permute-start(bf16[128,1024]{1,0:T(8,128)(2,1)S(1)} %copy.41), channel_id=1, source_target_pairs={{1,0},{4,1},{5,4},{8,5},{9,8},{12,9},{13,12},{14,13},{15,14},{10,1... | collective-permute-start | bytes 786440 | tf_op jit(solution)/shard_map/while/body/eval_jaxpr/ppermute | solution.py:104
  86.5 5.2 %collective-permute-start.2 = (f32[256,128]{0,1:T(8,128)S(1)}, f32[256,128]{0,1:T(8,128)S(1)}, u32[]{:S(2)}, u32[]{:S(2)}) collective-permute-start(f32[256,128]{0,1:T(8,128)S(1)} %add.214), channel_id=1, source_target_pairs={{0,1},{1,4},{4,5},{5,8},{8,9},{9,12},{12,13},{13,14},{14,15},{15,1... | collective-permute-start | bytes 393224 | tf_op jit(solution)/shard_map/while/body/eval_jaxpr/ppermute | solution.py:104
  87.8 5.3 %collective-permute-start.3 = (f32[256,128]{0,1:T(8,128)S(1)}, f32[256,128]{0,1:T(8,128)S(1)}, u32[]{:S(2)}, u32[]{:S(2)}) collective-permute-start(f32[256,128]{0,1:T(8,128)S(1)} %add.215), channel_id=1, source_target_pairs={{1,0},{4,1},{5,4},{8,5},{9,8},{12,9},{13,12},{14,13},{15,14},{10,1... | collective-permute-start | bytes 393224 | tf_op jit(solution)/shard_map/while/body/eval_jaxpr/ppermute | solution.py:104
  93.2 7.4 %collective-permute-start = (bf16[128,1024]{1,0:T(8,128)(2,1)S(1)}, bf16[128,1024]{1,0:T(8,128)(2,1)S(1)}, u32[]{:S(2)}, u32[]{:S(2)}) collective-permute-start(bf16[128,1024]{1,0:T(8,128)(2,1)S(1)} %copy.40), channel_id=1, source_target_pairs={{0,1},{1,4},{4,5},{5,8},{8,9},{9,12},{12,13},{13,14},{14,15},{15,1... | collective-permute-start | bytes 786440 | tf_op jit(solution)/shard_map/while/body/eval_jaxpr/ppermute | solution.py:104
  93.3 7.3 %collective-permute-start.1 = (bf16[128,1024]{1,0:T(8,128)(2,1)S(1)}, bf16[128,1024]{1,0:T(8,128)(2,1)S(1)}, u32[]{:S(2)}, u32[]{:S(2)}) collective-permute-start(bf16[128,1024]{1,0:T(8,128)(2,1)S(1)} %copy.41), channel_id=1, source_target_pairs={{1,0},{4,1},{5,4},{8,5},{9,8},{12,9},{13,12},{14,13},{15,14},{10,1... | collective-permute-start | bytes 786440 | tf_op jit(solution)/shard_map/while/body/eval_jaxpr/ppermute | solution.py:104
  93.9 5.2 %collective-permute-start.2 = (f32[256,128]{0,1:T(8,128)S(1)}, f32[256,128]{0,1:T(8,128)S(1)}, u32[]{:S(2)}, u32[]{:S(2)}) collective-permute-start(f32[256,128]{0,1:T(8,128)S(1)} %add.214), channel_id=1, source_target_pairs={{0,1},{1,4},{4,5},{5,8},{8,9},{9,12},{12,13},{13,14},{14,15},{15,1... | collective-permute-start | bytes 393224 | tf_op jit(solution)/shard_map/while/body/eval_jaxpr/ppermute | solution.py:104
  95.3 5.3 %collective-permute-start.3 = (f32[256,128]{0,1:T(8,128)S(1)}, f32[256,128]{0,1:T(8,128)S(1)}, u32[]{:S(2)}, u32[]{:S(2)}) collective-permute-start(f32[256,128]{0,1:T(8,128)S(1)} %add.215), channel_id=1, source_target_pairs={{1,0},{4,1},{5,4},{8,5},{9,8},{12,9},{13,12},{14,13},{15,14},{10,1... | collective-permute-start | bytes 393224 | tf_op jit(solution)/shard_map/while/body/eval_jaxpr/ppermute | solution.py:104
  100.6 7.4 %collective-permute-start = (bf16[128,1024]{1,0:T(8,128)(2,1)S(1)}, bf16[128,1024]{1,0:T(8,128)(2,1)S(1)}, u32[]{:S(2)}, u32[]{:S(2)}) collective-permute-start(bf16[128,1024]{1,0:T(8,128)(2,1)S(1)} %copy.40), channel_id=1, source_target_pairs={{0,1},{1,4},{4,5},{5,8},{8,9},{9,12},{12,13},{13,14},{14,15},{15,1... | collective-permute-start | bytes 786440 | tf_op jit(solution)/shard_map/while/body/eval_jaxpr/ppermute | solution.py:104
  100.8 7.3 %collective-permute-start.1 = (bf16[128,1024]{1,0:T(8,128)(2,1)S(1)}, bf16[128,1024]{1,0:T(8,128)(2,1)S(1)}, u32[]{:S(2)}, u32[]{:S(2)}) collective-permute-start(bf16[128,1024]{1,0:T(8,128)(2,1)S(1)} %copy.41), channel_id=1, source_target_pairs={{1,0},{4,1},{5,4},{8,5},{9,8},{12,9},{13,12},{14,13},{15,14},{10,1... | collective-permute-start | bytes 786440 | tf_op jit(solution)/shard_map/while/body/eval_jaxpr/ppermute | solution.py:104
  102.7 5.3 %collective-permute-start.3 = (f32[256,128]{0,1:T(8,128)S(1)}, f32[256,128]{0,1:T(8,128)S(1)}, u32[]{:S(2)}, u32[]{:S(2)}) collective-permute-start(f32[256,128]{0,1:T(8,128)S(1)} %add.215), channel_id=1, source_target_pairs={{1,0},{4,1},{5,4},{8,5},{9,8},{12,9},{13,12},{14,13},{15,14},{10,1... | collective-permute-start | bytes 393224 | tf_op jit(solution)/shard_map/while/body/eval_jaxpr/ppermute | solution.py:104
  108.1 7.4 %collective-permute-start = (bf16[128,1024]{1,0:T(8,128)(2,1)S(1)}, bf16[128,1024]{1,0:T(8,128)(2,1)S(1)}, u32[]{:S(2)}, u32[]{:S(2)}) collective-permute-start(bf16[128,1024]{1,0:T(8,128)(2,1)S(1)} %copy.40), channel_id=1, source_target_pairs={{0,1},{1,4},{4,5},{5,8},{8,9},{9,12},{12,13},{13,14},{14,15},{15,1... | collective-permute-start | bytes 786440 | tf_op jit(solution)/shard_map/while/body/eval_jaxpr/ppermute | solution.py:104
  108.2 7.3 %collective-permute-start.1 = (bf16[128,1024]{1,0:T(8,128)(2,1)S(1)}, bf16[128,1024]{1,0:T(8,128)(2,1)S(1)}, u32[]{:S(2)}, u32[]{:S(2)}) collective-permute-start(bf16[128,1024]{1,0:T(8,128)(2,1)S(1)} %copy.41), channel_id=1, source_target_pairs={{1,0},{4,1},{5,4},{8,5},{9,8},{12,9},{13,12},{14,13},{15,14},{10,1... | collective-permute-start | bytes 786440 | tf_op jit(solution)/shard_map/while/body/eval_jaxpr/ppermute | solution.py:104
  110.1 5.3 %collective-permute-start.3 = (f32[256,128]{0,1:T(8,128)S(1)}, f32[256,128]{0,1:T(8,128)S(1)}, u32[]{:S(2)}, u32[]{:S(2)}) collective-permute-start(f32[256,128]{0,1:T(8,128)S(1)} %add.215), channel_id=1, source_target_pairs={{1,0},{4,1},{5,4},{8,5},{9,8},{12,9},{13,12},{14,13},{15,14},{10,1... | collective-permute-start | bytes 393224 | tf_op jit(solution)/shard_map/while/body/eval_jaxpr/ppermute | solution.py:104
  115.5 7.4 %collective-permute-start = (bf16[128,1024]{1,0:T(8,128)(2,1)S(1)}, bf16[128,1024]{1,0:T(8,128)(2,1)S(1)}, u32[]{:S(2)}, u32[]{:S(2)}) collective-permute-start(bf16[128,1024]{1,0:T(8,128)(2,1)S(1)} %copy.40), channel_id=1, source_target_pairs={{0,1},{1,4},{4,5},{5,8},{8,9},{9,12},{12,13},{13,14},{14,15},{15,1... | collective-permute-start | bytes 786440 | tf_op jit(solution)/shard_map/while/body/eval_jaxpr/ppermute | solution.py:104
  115.6 7.3 %collective-permute-start.1 = (bf16[128,1024]{1,0:T(8,128)(2,1)S(1)}, bf16[128,1024]{1,0:T(8,128)(2,1)S(1)}, u32[]{:S(2)}, u32[]{:S(2)}) collective-permute-start(bf16[128,1024]{1,0:T(8,128)(2,1)S(1)} %copy.41), channel_id=1, source_target_pairs={{1,0},{4,1},{5,4},{8,5},{9,8},{12,9},{13,12},{14,13},{15,14},{10,1... | collective-permute-start | bytes 786440 | tf_op jit(solution)/shard_map/while/body/eval_jaxpr/ppermute | solution.py:104
  117.6 5.3 %collective-permute-start.3 = (f32[256,128]{0,1:T(8,128)S(1)}, f32[256,128]{0,1:T(8,128)S(1)}, u32[]{:S(2)}, u32[]{:S(2)}) collective-permute-start(f32[256,128]{0,1:T(8,128)S(1)} %add.215), channel_id=1, source_target_pairs={{1,0},{4,1},{5,4},{8,5},{9,8},{12,9},{13,12},{14,13},{15,14},{10,1... | collective-permute-start | bytes 393224 | tf_op jit(solution)/shard_map/while/body/eval_jaxpr/ppermute | solution.py:104
  (20 other events, 92.6 us)
